TPU v7x, 512 devices: a whole 4x8x8 slice. The times are simulated.
512 devices in a mesh: blk: 256 (over z, x_hi, y, core), rep: 2 (over x_lo).
Axes of the slice: x: 4 (x_hi: 2, x_lo: 2; x = x_hi * 2 + x_lo), y: 8, z: 8, core: 2. Of those that a mesh axis runs over, the one named last changes fastest.
Arguments:
- samples: bfloat16 [8192, 16, 2048], P('blk', 'rep'), may hold values from -60 to 60, as said below
- offsets: int32 [4, 8192], P(None, 'blk'), may hold values from 0 to 31
- bad_mask: int32 [8192], P('blk'), may hold values 0 or 1
Outputs:
- correlations: float32 [8192, 4, 257], P('blk')
- mirrored: float32 [8192, 4, 257], P('blk')
Inputs may be any that keep to these rules, and one draw needn't show every extreme that they name: `samples`: samples vary in scale between channels and segments; channels near one another share a delayed common source.
All inputs are finite; a program needn't handle non-finite values. No bound on the sum of `bad_mask` on one device may be relied on, other than what follows from the above.
Results may differ from a plain program's by a relative error of at most 0.0017.
Values may be sent and summed in bfloat16 or wider, within the bound.
No kernel may reach another device: no remote copies, remote signals or barrier semaphores. Data moves between devices by JAX's collectives and lax.ppermute only.
A program may use at most 64 MiB of HBM per device.

v0:
```python
import math

import jax
import jax.numpy as jnp
from jax import lax
from jax.sharding import PartitionSpec as P

LAGS = 128


def shifted(x, axis, by):
    length = lax.axis_size(axis)
    return lax.ppermute(x, axis, [(i, (i + by) % length) for i in range(length)])


def forward_table(length):
    half_len = length // 2
    sample_idx = lax.iota(jnp.int32, length)
    bin_idx = lax.iota(jnp.int32, half_len)
    phase = sample_idx[:, None] * bin_idx[None, :] % length
    angle = phase.astype(jnp.float32) * (2.0 * math.pi / length)
    return jnp.concatenate([jnp.cos(angle), -jnp.sin(angle)], axis=1).astype(jnp.bfloat16)


def inverse_table(length, lag_half):
    half_len = length // 2
    bin_idx = lax.iota(jnp.int32, half_len)
    lag_idx = lax.iota(jnp.int32, 2 * lag_half + 1) - lag_half
    phase = bin_idx[:, None] * (lag_idx[None, :] % length) % length
    angle = phase.astype(jnp.float32) * (2.0 * math.pi / length)
    return jnp.concatenate([jnp.cos(angle), -jnp.sin(angle)], axis=0)


def whiten(spectrum, keep, half_len):
    power = jnp.sum(spectrum * spectrum, axis=-1, keepdims=True) / half_len
    return (spectrum * lax.rsqrt(power + 1e-06) * keep[:, None, None]).astype(jnp.bfloat16)


def cross_spectrum(local, partner, half_len):
    first = local.astype(jnp.float32)
    second = partner.astype(jnp.float32)
    real_a, imag_a = (first[..., :half_len], first[..., half_len:])
    real_b, imag_b = (second[..., :half_len], second[..., half_len:])
    real_sum = jnp.sum(real_a * real_b + imag_a * imag_b, axis=1)
    imag_sum = jnp.sum(imag_a * real_b - real_a * imag_b, axis=1)
    return jnp.concatenate([real_sum, imag_sum], axis=-1)


def on_device(samples, offsets, bad_mask):
    channels, segments, length = samples.shape
    half_len = length // 2
    stops = offsets.shape[0]
    spectrum = jnp.dot(
        samples.reshape(channels * segments, length),
        forward_table(length),
        preferred_element_type=jnp.float32,
    ).reshape(channels, segments, length)
    keep = (1 - bad_mask).astype(jnp.float32)
    white = whiten(spectrum, keep, half_len)
    pieces = []
    moving = white
    for stop in range(1, stops + 1):
        moving = shifted(moving, "blk", 1)
        partner = jnp.take(moving, offsets[stop - 1], axis=0)
        pieces.append(cross_spectrum(white, partner, half_len))
    cross = jnp.stack(pieces, axis=1)
    scale = 1.0 / math.sqrt(segments * lax.axis_size("rep") * half_len)
    back_table = inverse_table(length, LAGS)
    stacked = lax.psum(cross, "rep")
    correlations = (
        jnp.dot(
            stacked.reshape(channels * stops, length),
            back_table,
            precision=lax.Precision.HIGHEST,
            preferred_element_type=jnp.float32,
        ).reshape(channels, stops, -1)
        * scale
    )
    mirrored = []
    for stop in range(1, stops + 1):
        flipped = correlations[:, stop - 1, ::-1]
        mirrored.append(shifted(flipped, "blk", -stop))
    return (correlations, jnp.stack(mirrored, axis=1))


def solution(mesh):
    return jax.shard_map(
        on_device,
        mesh=mesh,
        in_specs=(P("blk", "rep", None), P(None, "blk"), P("blk")),
        out_specs=(P("blk", None, None), P("blk", None, None)),
        check_vma=False,
    )
```

profile of v0, /device:TPU:1, one launch (start us, length us, event | category | flops | bytes accessed | tf_op | source)
XLA Modules:
  0.0 241.3 jit_solution(5379508726055081933)
XLA Ops:
  7.2 33.8 %negate_convert_fusion = (bf16[2048,1024]{1,0:T(8,128)(2,1)S(1)}, bf16[2048,1024]{1,0:T(8,128)(2,1)S(1)}) fusion(), kind=kLoop, calls=%fused_computation.14 | loop fusion | flops 35651584 | bytes 8388608 | tf_op jit(solution)/shard_map/convert.1
  41.1 5.1 %fusion.15 = (f32[256]{0:T(256)S(1)}, f32[2048,256]{0,1:T(8,128)}) fusion(bf16[2048,1024]{1,0:T(8,128)(2,1)S(1)} %get-tuple-element.47, bf16[2048,1024]{1,0:T(8,128)(2,1)S(1)} %get-tuple-element.48, bf16[32,8,2048]{2,1,0:T(8,128)(2,1)S(1)} %copy-done), kind=kOutput, calls=%fused_computation.27 | convolution fusion | flops 2165309184 | bytes 11535360 | tf_op jit(solution)/shard_map/dot_general | solution.py:53
  46.3 1.9 fusion.28
  48.2 4.6 %collective-permute-start = (bf16[32,8,2048]{2,1,0:T(8,128)(2,1)S(1)}, bf16[32,8,2048]{2,1,0:T(8,128)(2,1)S(1)}, u32[]{:S(2)}, u32[]{:S(2)}) collective-permute-start(bf16[32,8,2048]{2,1,0:T(8,128)(2,1)S(1)} %get-tuple-element.26), channel_id=1, source_target_pairs={{0,2},{2,4},{4,6},{6,8},{8,10},{10,12},{12,14},{14,16},{16,18},{18... | collective-permute-start | bytes 3145736 | tf_op jit(solution)/shard_map/ppermute | solution.py:13
  52.8 11.7 %collective-permute-done = bf16[32,8,2048]{2,1,0:T(8,128)(2,1)S(1)} collective-permute-done((bf16[32,8,2048]{2,1,0:T(8,128)(2,1)S(1)}, bf16[32,8,2048]{2,1,0:T(8,128)(2,1)S(1)}, u32[]{:S(2)}, u32[]{:S(2)}) %collective-permute-start) | collective-permute-done | bytes 1048608 | tf_op jit(solution)/shard_map/ppermute | solution.py:13
  64.6 1.0 copy-done.2
  65.5 4.4 %collective-permute-start.1 = (bf16[32,8,2048]{2,1,0:T(8,128)(2,1)S(1)}, bf16[32,8,2048]{2,1,0:T(8,128)(2,1)}, u32[]{:S(2)}, u32[]{:S(2)}) collective-permute-start(bf16[32,8,2048]{2,1,0:T(8,128)(2,1)S(1)} %collective-permute-done), channel_id=1, source_target_pairs={{0,2},{2,4},{4,6},{6,8},{8,10},{10,12},{12,14},{14,16},{16,18},{18... | collective-permute-start | bytes 3145736 | tf_op jit(solution)/shard_map/ppermute | solution.py:13
  69.9 13.2 %collective-permute-done.1 = bf16[32,8,2048]{2,1,0:T(8,128)(2,1)} collective-permute-done((bf16[32,8,2048]{2,1,0:T(8,128)(2,1)S(1)}, bf16[32,8,2048]{2,1,0:T(8,128)(2,1)}, u32[]{:S(2)}, u32[]{:S(2)}) %collective-permute-start.1) | collective-permute-done | bytes 1048608 | tf_op jit(solution)/shard_map/ppermute | solution.py:13
  83.1 3.0 %collective-permute-start.2 = (bf16[32,8,2048]{2,1,0:T(8,128)(2,1)}, bf16[32,8,2048]{2,1,0:T(8,128)(2,1)}, u32[]{:S(2)}, u32[]{:S(2)}) collective-permute-start(bf16[32,8,2048]{2,1,0:T(8,128)(2,1)} %collective-permute-done.1), channel_id=1, source_target_pairs={{0,2},{2,4},{4,6},{6,8},{8,10},{10,12},{12,14},{14,16},{16,18},{18... | collective-permute-start | bytes 3145736 | tf_op jit(solution)/shard_map/ppermute | solution.py:13
  86.2 2.8 %gather_fusion = bf16[32,8,2048]{2,1,0:T(8,128)(2,1)} fusion(bf16[32,8,2048]{2,1,0:T(8,128)(2,1)} %copy-done.2, s32[1024]{0:T(1024)S(1)} %pad_clamp_fusion.3), kind=kCustom, calls=%fused_computation.clone | custom fusion | bytes 2097280 | tf_op jit(solution)/shard_map/jit(_take)/gather | solution.py:64
  89.0 2.8 %select_convert_fusion.3 = f32[32,8,2048]{2,1,0:T(8,128)} fusion(bf16[32,8,2048]{2,1,0:T(8,128)(2,1)} %gather_fusion, pred[32]{0:T(512)(128)(4,1)S(1)} %get-tuple-element.39), kind=kLoop, calls=%fused_computation.44 | loop fusion | flops 1048576 | bytes 3145760 | tf_op jit(solution)/shard_map/convert_element_type | solution.py:41
  91.8 2.8 %gather_fusion.1 = bf16[32,8,2048]{2,1,0:T(8,128)(2,1)} fusion(bf16[32,8,2048]{2,1,0:T(8,128)(2,1)} %collective-permute-done.1, s32[1024]{0:T(1024)S(1)} %pad_clamp_fusion.2), kind=kCustom, calls=%fused_computation.1.clone | custom fusion | bytes 2097280 | tf_op jit(solution)/shard_map/jit(_take)/gather | solution.py:64
  94.6 10.6 %collective-permute-done.2 = bf16[32,8,2048]{2,1,0:T(8,128)(2,1)} collective-permute-done((bf16[32,8,2048]{2,1,0:T(8,128)(2,1)}, bf16[32,8,2048]{2,1,0:T(8,128)(2,1)}, u32[]{:S(2)}, u32[]{:S(2)}) %collective-permute-start.2) | collective-permute-done | bytes 1048608 | tf_op jit(solution)/shard_map/ppermute | solution.py:13
  105.3 2.1 collective-permute-start.3
  107.4 2.7 %select_convert_fusion.2 = f32[32,8,2048]{2,1,0:T(8,128)} fusion(bf16[32,8,2048]{2,1,0:T(8,128)(2,1)} %gather_fusion.1, pred[32]{0:T(512)(128)(4,1)S(1)} %get-tuple-element.19), kind=kLoop, calls=%fused_computation.43 | loop fusion | flops 1048576 | bytes 3145760 | tf_op jit(solution)/shard_map/convert_element_type | solution.py:41
  110.1 2.9 %gather_fusion.2 = bf16[32,8,2048]{2,1,0:T(8,128)(2,1)} fusion(bf16[32,8,2048]{2,1,0:T(8,128)(2,1)} %collective-permute-done.2, s32[1024]{0:T(1024)S(1)} %pad_clamp_fusion.1), kind=kCustom, calls=%fused_computation.2.clone | custom fusion | bytes 2097280 | tf_op jit(solution)/shard_map/jit(_take)/gather | solution.py:64
  113.0 2.8 %select_convert_fusion.1 = f32[32,8,2048]{2,1,0:T(8,128)} fusion(bf16[32,8,2048]{2,1,0:T(8,128)(2,1)} %gather_fusion.2, pred[32]{0:T(512)(128)(4,1)S(1)} %get-tuple-element.43), kind=kLoop, calls=%fused_computation.42 | loop fusion | flops 1048576 | bytes 3145760 | tf_op jit(solution)/shard_map/convert_element_type | solution.py:41
  115.8 11.7 %collective-permute-done.3 = bf16[32,8,2048]{2,1,0:T(8,128)(2,1)} collective-permute-done((bf16[32,8,2048]{2,1,0:T(8,128)(2,1)}, bf16[32,8,2048]{2,1,0:T(8,128)(2,1)}, u32[]{:S(2)}, u32[]{:S(2)}) %collective-permute-start.3) | collective-permute-done | bytes 1048608 | tf_op jit(solution)/shard_map/ppermute | solution.py:13
  127.4 2.8 %gather_fusion.3 = bf16[32,8,2048]{2,1,0:T(8,128)(2,1)} fusion(bf16[32,8,2048]{2,1,0:T(8,128)(2,1)} %collective-permute-done.3, s32[1024]{0:T(1024)S(1)} %pad_clamp_fusion), kind=kCustom, calls=%fused_computation.3.clone | custom fusion | bytes 2097280 | tf_op jit(solution)/shard_map/jit(_take)/gather | solution.py:64
  130.3 1.6 select_convert_fusion
  132.2 5.4 %add_reduce_fusion.3 = (f32[32,1024]{1,0:T(8,128)S(1)}, f32[32,1024]{1,0:T(8,128)S(1)}, f32[32,1024]{1,0:T(8,128)S(1)}, f32[32,1024]{1,0:T(8,128)S(1)}, f32[32,1...) fusion(f32[32,8,2048]{2,1,0:T(8,128)S(1)} %copy-done.1, ...), kind=kLoop, calls=%fused_computation.52 | loop fusion | flops 8126464 | bytes 11534336 | tf_op jit(solution)/shard_map/reduce_sum | solution.py:44
  137.7 1.1 pad_maximum_fusion
  138.9 4.3 %fusion.24 = (f32[1024,257]{0,1:T(8,128)S(1)}, f32[1024,257]{0,1:T(8,128)S(1)}) fusion(s32[257]{0:T(512)S(1)} %add_select_fusion.2), kind=kLoop, calls=%fused_computation.53 | loop fusion | flops 3947520 | bytes 2106372 | tf_op jit(solution)/shard_map/cos | solution.py:31
  143.2 61.7 %all-reduce.2.cloned.1.call-done = f32[32,4,2048]{2,0,1:T(8,128)} async-done(((f32[32,4,2048]{2,0,1:T(8,128)}), f32[32,4,2048]{2,0,1:T(8,128)}) %all-reduce.2.cloned.1.call-update) | async-done | bytes 1048592 | tf_op jit(solution)/shard_map/psum | solution.py:69
  204.9 4.1 %fusion.16 = f32[32,4,257]{2,0,1:T(8,128)S(1)} fusion(f32[32,4,2048]{2,0,1:T(8,128)} %all-reduce.2.cloned.1.call-done, f32[1024,257]{0,1:T(8,128)S(1)} %get-tuple-element.38, f32[1024,257]{0,1:T(8,128)S(1)} %get-tuple-element.37), kind=kOutput, calls=%fused_computation.31 | convolution fusion | flops 809011328 | bytes 3285504 | tf_op jit(solution)/shard_map/dot_general | solution.py:71
  209.4 10.9 %collective-permute-start.7 = (f32[32,257]{1,0:T(8,128)S(1)}, f32[32,257]{1,0:T(8,128)S(1)}, u32[]{:S(2)}, u32[]{:S(2)}) collective-permute-start(f32[32,257]{1,0:T(8,128)S(1)} %slice_bitcast_fusion.3), channel_id=1, source_target_pairs={{0,504},{2,506},{4,508},{6,510},{8,0},{10,2},{12,4},{14,6},{16,8},... | collective-permute-start | bytes 98696 | tf_op jit(solution)/shard_map/ppermute | solution.py:13
  220.6 3.9 %collective-permute-start.6 = (f32[32,257]{1,0:T(8,128)S(1)}, f32[32,257]{1,0:T(8,128)S(1)}, u32[]{:S(2)}, u32[]{:S(2)}) collective-permute-start(f32[32,257]{1,0:T(8,128)S(1)} %slice_bitcast_fusion.2), channel_id=1, source_target_pairs={{0,506},{2,508},{4,510},{6,0},{8,2},{10,4},{12,6},{14,8},{16,10},{... | collective-permute-start | bytes 98696 | tf_op jit(solution)/shard_map/ppermute | solution.py:13
  224.8 3.1 %collective-permute-start.5 = (f32[32,257]{1,0:T(8,128)S(1)}, f32[32,257]{1,0:T(8,128)S(1)}, u32[]{:S(2)}, u32[]{:S(2)}) collective-permute-start(f32[32,257]{1,0:T(8,128)S(1)} %slice_bitcast_fusion.1), channel_id=1, source_target_pairs={{0,508},{2,510},{4,0},{6,2},{8,4},{10,6},{12,8},{14,10},{16,12},{1... | collective-permute-start | bytes 98696 | tf_op jit(solution)/shard_map/ppermute | solution.py:13
  228.2 1.9 collective-permute-start.4
  230.1 0.8 copy.7
  230.9 2.7 %collective-permute-done.4 = f32[32,257]{1,0:T(8,128)S(1)} collective-permute-done((f32[32,257]{1,0:T(8,128)S(1)}, f32[32,257]{1,0:T(8,128)S(1)}, u32[]{:S(2)}, u32[]{:S(2)}) %collective-permute-start.4) | collective-permute-done | bytes 32928 | tf_op jit(solution)/shard_map/ppermute | solution.py:13
  233.6 0.8 copy.8
  (37 shorter events, 1.9 us)
Async XLA Ops:
  7.2 33.9 %copy-start = (bf16[32,8,2048]{2,1,0:T(8,128)(2,1)S(1)}, bf16[32,8,2048]{2,1,0:T(8,128)(2,1)}, u32[]{:S(2)}) copy-start(bf16[32,8,2048]{2,1,0:T(8,128)(2,1)} %param.5) | copy-start | bytes 3145732
  7.2 33.9 %copy-start.4 = (s32[32]{0:T(128)S(1)}, s32[32]{0:T(128)}, u32[]{:S(2)}) copy-start(s32[32]{0:T(128)} %param.7) | copy-start | bytes 388
  7.2 197.7 %all-reduce.2.cloned.1.call-start = ((), (), s32[]{:S(2)}) async-start(), calls=%async_computation | async-start | bytes 2097152 | tf_op jit(solution)/shard_map/psum | solution.py:69
  46.3 39.9 %copy-start.3 = (s32[4,32]{1,0:T(4,128)S(1)}, s32[4,32]{1,0:T(4,128)}, u32[]{:S(2)}) copy-start(s32[4,32]{1,0:T(4,128)} %param.6) | copy-start | bytes 1540
  48.2 16.3 %collective-permute-start = (bf16[32,8,2048]{2,1,0:T(8,128)(2,1)S(1)}, bf16[32,8,2048]{2,1,0:T(8,128)(2,1)S(1)}, u32[]{:S(2)}, u32[]{:S(2)}) collective-permute-start(bf16[32,8,2048]{2,1,0:T(8,128)(2,1)S(1)} %get-tuple-element.26), channel_id=1, source_target_pairs={{0,2},{2,4},{4,6},{6,8},{8,10},{10,12},{12,14},{14,16},{16,18},{18... | collective-permute-start | bytes 3145736 | tf_op jit(solution)/shard_map/ppermute | solution.py:13
  64.6 1.0 copy-start.2
  65.5 17.6 %collective-permute-start.1 = (bf16[32,8,2048]{2,1,0:T(8,128)(2,1)S(1)}, bf16[32,8,2048]{2,1,0:T(8,128)(2,1)}, u32[]{:S(2)}, u32[]{:S(2)}) collective-permute-start(bf16[32,8,2048]{2,1,0:T(8,128)(2,1)S(1)} %collective-permute-done), channel_id=1, source_target_pairs={{0,2},{2,4},{4,6},{6,8},{8,10},{10,12},{12,14},{14,16},{16,18},{18... | collective-permute-start | bytes 3145736 | tf_op jit(solution)/shard_map/ppermute | solution.py:13
  83.1 22.1 %collective-permute-start.2 = (bf16[32,8,2048]{2,1,0:T(8,128)(2,1)}, bf16[32,8,2048]{2,1,0:T(8,128)(2,1)}, u32[]{:S(2)}, u32[]{:S(2)}) collective-permute-start(bf16[32,8,2048]{2,1,0:T(8,128)(2,1)} %collective-permute-done.1), channel_id=1, source_target_pairs={{0,2},{2,4},{4,6},{6,8},{8,10},{10,12},{12,14},{14,16},{16,18},{18... | collective-permute-start | bytes 3145736 | tf_op jit(solution)/shard_map/ppermute | solution.py:13
  105.3 22.1 %collective-permute-start.3 = (bf16[32,8,2048]{2,1,0:T(8,128)(2,1)}, bf16[32,8,2048]{2,1,0:T(8,128)(2,1)}, u32[]{:S(2)}, u32[]{:S(2)}) collective-permute-start(bf16[32,8,2048]{2,1,0:T(8,128)(2,1)} %collective-permute-done.2), channel_id=1, source_target_pairs={{0,2},{2,4},{4,6},{6,8},{8,10},{10,12},{12,14},{14,16},{16,18},{18... | collective-permute-start | bytes 3145736 | tf_op jit(solution)/shard_map/ppermute | solution.py:13
  130.3 1.9 copy-start.1
  209.4 21.5 %collective-permute-start.7 = (f32[32,257]{1,0:T(8,128)S(1)}, f32[32,257]{1,0:T(8,128)S(1)}, u32[]{:S(2)}, u32[]{:S(2)}) collective-permute-start(f32[32,257]{1,0:T(8,128)S(1)} %slice_bitcast_fusion.3), channel_id=1, source_target_pairs={{0,504},{2,506},{4,508},{6,510},{8,0},{10,2},{12,4},{14,6},{16,8},... | collective-permute-start | bytes 98696 | tf_op jit(solution)/shard_map/ppermute | solution.py:13
  220.6 10.4 %collective-permute-start.6 = (f32[32,257]{1,0:T(8,128)S(1)}, f32[32,257]{1,0:T(8,128)S(1)}, u32[]{:S(2)}, u32[]{:S(2)}) collective-permute-start(f32[32,257]{1,0:T(8,128)S(1)} %slice_bitcast_fusion.2), channel_id=1, source_target_pairs={{0,506},{2,508},{4,510},{6,0},{8,2},{10,4},{12,6},{14,8},{16,10},{... | collective-permute-start | bytes 98696 | tf_op jit(solution)/shard_map/ppermute | solution.py:13
  224.8 6.1 %collective-permute-start.5 = (f32[32,257]{1,0:T(8,128)S(1)}, f32[32,257]{1,0:T(8,128)S(1)}, u32[]{:S(2)}, u32[]{:S(2)}) collective-permute-start(f32[32,257]{1,0:T(8,128)S(1)} %slice_bitcast_fusion.1), channel_id=1, source_target_pairs={{0,508},{2,510},{4,0},{6,2},{8,4},{10,6},{12,8},{14,10},{16,12},{1... | collective-permute-start | bytes 98696 | tf_op jit(solution)/shard_map/ppermute | solution.py:13
  228.2 5.4 %collective-permute-start.4 = (f32[32,257]{1,0:T(8,128)S(1)}, f32[32,257]{1,0:T(8,128)S(1)}, u32[]{:S(2)}, u32[]{:S(2)}) collective-permute-start(f32[32,257]{1,0:T(8,128)S(1)} %slice_bitcast_fusion), channel_id=1, source_target_pairs={{0,510},{2,0},{4,2},{6,4},{8,6},{10,8},{12,10},{14,12},{16,14},{18... | collective-permute-start | bytes 98696 | tf_op jit(solution)/shard_map/ppermute | solution.py:13
Sparse Core Ops, SparseCore 0:
  139.0 65.8 all-reduce.1
where the time goes:
time: 242 us; the launch traced here: 241 us
  waiting for transfers between devices  112 us (46%)
  other arithmetic  56.7 us (23%)
  starting transfers between devices  33.9 us (14%)
  local copies, waits for them, and re-layouts  15.7 us (6%)
  between operations  14.3 us (6%)
  matrix products  9.17 us (4%)
    psum x1, waiting for transfers between devices, on_device(): stacked = lax.psum(cross, 'rep')  61.7 us
    ppermute x8, waiting for transfers between devices, shifted(): lax.ppermute(x, axis, [(i, (i + by) % length) for i in range(length)])  49.9 us
    another operation x1, other arithmetic  33.8 us
    ppermute x8, starting transfers between devices, shifted(): lax.ppermute(x, axis, [(i, (i + by) % length) for i in range(length)])  33.8 us
    gather x4, local copies, waits for them, and re-layouts, on_device(): partner = jnp.take(moving, offsets[stop - 1], axis=0)  11.4 us
    convert_element_type x4, other arithmetic, cross_spectrum(): second = partner.astype(jnp.float32)  9.85 us
    reduce_sum x1, other arithmetic, cross_spectrum(): real_sum = jnp.sum(real_a * real_b + imag_a * imag_b, axis=1)  5.42 us
    dot_general x1, matrix products, on_device(): jnp.dot(samples.reshape(channels * segments, length), forward_table(lengt...  5.06 us
  transfers between devices with their start and end apart: 9, of which 6 were waited for; matrix products, arithmetic and copies ran while one was open for 10% of the time, Pallas kernels for 0%

commit v1 on v0

v1 whole, which is shorter than its diff:
```python
import math

import jax
import jax.numpy as jnp
from jax import lax
from jax.sharding import PartitionSpec as P

LAGS = 128


def shifted(x, axis, by):
    length = lax.axis_size(axis)
    return lax.ppermute(x, axis, [(i, (i + by) % length) for i in range(length)])


def swapped(x, axis):
    length = lax.axis_size(axis)
    return lax.ppermute(x, axis, [(i, i ^ 1) for i in range(length)])


def cos_sin(phase, length):
    angle = phase.astype(jnp.float32) * (2.0 * math.pi / length)
    return jnp.cos(angle), jnp.sin(angle)


def forward_table(length):
    half_len = length // 2
    lo_len = 64
    hi_len = length // lo_len
    bin_idx = lax.iota(jnp.int32, half_len)
    hi_idx = lax.iota(jnp.int32, hi_len) * lo_len
    lo_idx = lax.iota(jnp.int32, lo_len)
    cos_hi, sin_hi = cos_sin(hi_idx[:, None] * bin_idx[None, :] % length, length)
    cos_lo, sin_lo = cos_sin(lo_idx[:, None] * bin_idx[None, :] % length, length)
    cos_hi, sin_hi = cos_hi[:, None, :], sin_hi[:, None, :]
    cos_lo, sin_lo = cos_lo[None, :, :], sin_lo[None, :, :]
    cos_t = cos_hi * cos_lo - sin_hi * sin_lo
    sin_t = sin_hi * cos_lo + cos_hi * sin_lo
    table = jnp.concatenate([cos_t, -sin_t], axis=-1)
    return table.reshape(length, length).astype(jnp.bfloat16)


def inverse_table(length, lag_half):
    half_len = length // 2
    lo_len = 32
    hi_len = half_len // lo_len
    lag_idx = (lax.iota(jnp.int32, 2 * lag_half + 1) - lag_half) % length
    hi_idx = lax.iota(jnp.int32, hi_len) * lo_len
    lo_idx = lax.iota(jnp.int32, lo_len)
    cos_hi, sin_hi = cos_sin(hi_idx[:, None] * lag_idx[None, :] % length, length)
    cos_lo, sin_lo = cos_sin(lo_idx[:, None] * lag_idx[None, :] % length, length)
    cos_hi, sin_hi = cos_hi[:, None, :], sin_hi[:, None, :]
    cos_lo, sin_lo = cos_lo[None, :, :], sin_lo[None, :, :]
    cos_t = (cos_hi * cos_lo - sin_hi * sin_lo).reshape(half_len, -1)
    sin_t = (sin_hi * cos_lo + cos_hi * sin_lo).reshape(half_len, -1)
    return jnp.concatenate([cos_t, -sin_t], axis=0)


def whiten(spectrum, keep, half_len):
    power = jnp.sum(spectrum * spectrum, axis=-1, keepdims=True) / half_len
    return (spectrum * lax.rsqrt(power + 1e-06) * keep[:, None, None]).astype(jnp.bfloat16)


def cross_spectrum(local, partner, half_len):
    first = local.astype(jnp.float32)
    second = partner.astype(jnp.float32)
    real_a, imag_a = (first[..., :half_len], first[..., half_len:])
    real_b, imag_b = (second[..., :half_len], second[..., half_len:])
    real_sum = jnp.sum(real_a * real_b + imag_a * imag_b, axis=1)
    imag_sum = jnp.sum(imag_a * real_b - real_a * imag_b, axis=1)
    return jnp.concatenate([real_sum, imag_sum], axis=-1)


def on_device(samples, offsets, bad_mask):
    channels, segments, length = samples.shape
    half_len = length // 2
    stops = offsets.shape[0]
    spectrum = jnp.dot(
        samples.reshape(channels * segments, length),
        forward_table(length),
        preferred_element_type=jnp.float32,
    ).reshape(channels, segments, length)
    keep = (1 - bad_mask).astype(jnp.float32)
    white = whiten(spectrum, keep, half_len)
    split = segments // 2
    ahead = white[:, :split]
    behind = white[:, split:]
    moving_ahead = ahead
    moving_behind = behind
    moving_offsets = offsets
    own_pieces = []
    later_pieces = []
    for stop in range(1, stops + 1):
        moving_ahead = shifted(moving_ahead, "blk", 1)
        moving_behind = shifted(moving_behind, "blk", -1)
        moving_offsets = shifted(moving_offsets, "blk", -1)
        partner = jnp.take(moving_ahead, offsets[stop - 1], axis=0)
        own_pieces.append(cross_spectrum(ahead, partner, half_len))
        local_partner = jnp.take(behind, moving_offsets[stop - 1], axis=0)
        later_pieces.append(cross_spectrum(moving_behind, local_partner, half_len))
    back_table = inverse_table(length, LAGS)
    pieces = jnp.stack([jnp.stack(own_pieces, axis=1), jnp.stack(later_pieces, axis=1)], axis=0)
    partial = jnp.dot(
        pieces.reshape(2 * channels * stops, length),
        back_table,
        precision=lax.Precision.HIGHEST,
        preferred_element_type=jnp.float32,
    ).reshape(2, channels, stops, -1)
    summed = partial + swapped(partial, "rep")
    own_part, later_part = summed[0], summed[1]
    scale = 1.0 / math.sqrt(segments * lax.axis_size("rep") * half_len)
    correlations = []
    mirrored = []
    for stop in range(1, stops + 1):
        from_earlier = shifted(later_part[:, stop - 1], "blk", stop)
        from_later = shifted(own_part[:, stop - 1], "blk", -stop)
        correlations.append((own_part[:, stop - 1] + from_earlier) * scale)
        mirrored.append(((from_later + later_part[:, stop - 1]) * scale)[:, ::-1])
    return (jnp.stack(correlations, axis=1), jnp.stack(mirrored, axis=1))


def solution(mesh):
    return jax.shard_map(
        on_device,
        mesh=mesh,
        in_specs=(P("blk", "rep", None), P(None, "blk"), P("blk")),
        out_specs=(P("blk", None, None), P("blk", None, None)),
        check_vma=False,
    )
```

time: 242 us -> 197 us (0.81)
  waiting for transfers between devices: 112 us -> 18.1 us
  starting transfers between devices: 33.9 us -> 110 us
  other arithmetic: 56.7 us -> 35.8 us
  between operations: 14.3 us -> 1.37 us
  local copies, waits for them, and re-layouts: 15.7 us -> 22.9 us
  matrix products: 9.17 us -> 6.07 us
    ppermute x8 -> x20, starting transfers between devices: 33.8 us -> 108 us  [shifted(): lax.ppermute(x, axis, [(i, (i + by) % length) for i in range(length)])]
    psum x1 -> x0, waiting for transfers between devices: 61.7 us -> none  [on_device(): stacked = lax.psum(cross, 'rep')]
    ppermute x8 -> x20, waiting for transfers between devices: 49.9 us -> 11.8 us  [shifted(): lax.ppermute(x, axis, [(i, (i + by) % length) for i in range(length)])]
    another operation x7 -> x18, other arithmetic: 35.1 us -> 5.02 us
    ppermute x0 -> x1, waiting for transfers between devices: none -> 6.29 us  [swapped(): return lax.ppermute(x, axis, [(i, i ^ 1) for i in range(length)])]
    convert_element_type x1 -> x5, other arithmetic: 1.94 us -> 6.4 us  [cross_spectrum(): first = local.astype(jnp.float32)]
    cos x1 -> x2, other arithmetic: 4.33 us -> 1.02 us  [cos_sin(): return (jnp.cos(angle), jnp.sin(angle))]
    reduce_sum x1 -> x5, other arithmetic: 5.42 us -> 8.72 us  [cross_spectrum(): real_sum = jnp.sum(real_a * real_b + imag_a * imag_b, axis=1)]
  transfers between devices with their start and end apart: 9 -> 21, of which waited for: 6 -> 6; matrix products, arithmetic and copies ran while one was open for 10% -> 24% of each run, Pallas kernels for 0% -> 0%
where the time goes in v1:
time: 197 us; the launch traced here: 194 us
  starting transfers between devices  110 us (56%)
  other arithmetic  35.8 us (18%)
  local copies, waits for them, and re-layouts  22.9 us (12%)
  waiting for transfers between devices  18.1 us (9%)
  matrix products  6.07 us (3%)
    ppermute x20, starting transfers between devices, shifted(): lax.ppermute(x, axis, [(i, (i + by) % length) for i in range(length)])  108 us
    ppermute x20, waiting for transfers between devices, shifted(): lax.ppermute(x, axis, [(i, (i + by) % length) for i in range(length)])  11.8 us
    convert_element_type x8, other arithmetic, cross_spectrum(): second = partner.astype(jnp.float32)  11.4 us
    gather x4, local copies, waits for them, and re-layouts, on_device(): partner = jnp.take(moving_ahead, offsets[stop - 1], axis=0)  10.5 us
    reduce_sum x5, other arithmetic, cross_spectrum(): real_sum = jnp.sum(real_a * real_b + imag_a * imag_b, axis=1)  8.72 us
    convert_element_type x5, other arithmetic, cross_spectrum(): first = local.astype(jnp.float32)  6.4 us
    ppermute x1, waiting for transfers between devices, swapped(): return lax.ppermute(x, axis, [(i, i ^ 1) for i in range(length)])  6.29 us
    unnamed x30, local copies, waits for them, and re-layouts  3.99 us
  transfers between devices with their start and end apart: 21, of which 6 were waited for; matrix products, arithmetic and copies ran while one was open for 24% of the time, Pallas kernels for 0%

profile of v1, /device:TPU:1, one launch (start us, length us, event | category | flops | bytes accessed | tf_op | source)
XLA Modules:
  0.0 194.3 jit_solution(8129745536400494761)
XLA Ops:
  2.3 3.0 %subtract_convert_fusion = (bf16[32,64,1024]{2,1,0:T(8,128)(2,1)S(1)}, bf16[32,64,1024]{2,1,0:T(8,128)(2,1)S(1)}) fusion(f32[64,1024]{1,0:T(8,128)S(1)} %get-tuple-element.86, f32[32,1024]{1,0:T(8,128)S(1)} %get-tuple-element.83, f32[64,1024]{1,0:T(8,128)S(1)} %get-tuple-element.87, f32[32,1024]{1,0:T(8,128)S(1)} %get-tuple-element.82), kind=kLoop, calls=%fused_computation.13 | loop fusion | flops 18874368 | bytes 9175040 | tf_op jit(solution)/shard_map/convert.3
  5.3 2.5 %fusion.12 = (f32[256]{0:T(256)S(1)}, f32[2048,256]{0,1:T(8,128)S(1)}) fusion(bf16[2048,1024]{1,0:T(8,128)(2,1)S(1)} %bitcast.128, bf16[2048,1024]{1,0:T(8,128)(2,1)S(1)} %bitcast.127, bf16[32,8,2048]{2,1,0:T(8,128)(2,1)S(1)} %copy-done), kind=kOutput, calls=%fused_computation.25 | convolution fusion | flops 2165309184 | bytes 11535360 | tf_op jit(solution)/shard_map/dot_general | solution.py:78
  10.0 4.6 %collective-permute-start = (bf16[32,4,2048]{2,1,0:T(4,128)(2,1)}, bf16[32,4,2048]{2,1,0:T(4,128)(2,1)}, u32[]{:S(2)}, u32[]{:S(2)}) collective-permute-start(bf16[32,4,2048]{2,1,0:T(4,128)(2,1)} %get-tuple-element.49), channel_id=1, source_target_pairs={{0,2},{2,4},{4,6},{6,8},{8,10},{10,12},{12,14},{14,16},{16,18},{18... | collective-permute-start | bytes 1572872 | tf_op jit(solution)/shard_map/ppermute | solution.py:13
  14.6 6.1 %collective-permute-start.5 = (s32[4,32]{1,0:T(4,128)S(1)}, s32[4,32]{1,0:T(4,128)S(1)}, u32[]{:S(2)}, u32[]{:S(2)}) collective-permute-start(s32[4,32]{1,0:T(4,128)S(1)} %copy-done.10), channel_id=1, source_target_pairs={{0,510},{2,0},{4,2},{6,4},{8,6},{10,8},{12,10},{14,12},{16,14},{18... | collective-permute-start | bytes 1544 | tf_op jit(solution)/shard_map/ppermute | solution.py:13
  20.7 10.4 %collective-permute-start.4 = (bf16[32,4,2048]{2,1,0:T(4,128)(2,1)S(1)}, bf16[32,4,2048]{2,1,0:T(4,128)(2,1)}, u32[]{:S(2)}, u32[]{:S(2)}) collective-permute-start(bf16[32,4,2048]{2,1,0:T(4,128)(2,1)S(1)} %get-tuple-element.48), channel_id=1, source_target_pairs={{0,510},{2,0},{4,2},{6,4},{8,6},{10,8},{12,10},{14,12},{16,14},{18... | collective-permute-start | bytes 1572872 | tf_op jit(solution)/shard_map/ppermute | solution.py:13
  33.3 2.8 %copy.7 = f32[1024,257]{0,1:T(8,128)} copy(f32[1024,257]{1,0:T(8,128)} %bitcast.126) | data formatting | bytes 2105344 | tf_op jit(solution)/shard_map/sub | solution.py:54
  38.6 2.6 %collective-permute-start.7 = (s32[4,32]{1,0:T(4,128)S(1)}, s32[4,32]{1,0:T(4,128)S(1)}, u32[]{:S(2)}, u32[]{:S(2)}) collective-permute-start(s32[4,32]{1,0:T(4,128)S(1)} %collective-permute-done.5), channel_id=1, source_target_pairs={{0,510},{2,0},{4,2},{6,4},{8,6},{10,8},{12,10},{14,12},{16,14},{18... | collective-permute-start | bytes 1544 | tf_op jit(solution)/shard_map/ppermute | solution.py:13
  44.5 2.6 %collective-permute-start.9 = (s32[4,32]{1,0:T(4,128)S(1)}, s32[4,32]{1,0:T(4,128)S(1)}, u32[]{:S(2)}, u32[]{:S(2)}) collective-permute-start(s32[4,32]{1,0:T(4,128)S(1)} %collective-permute-done.7), channel_id=1, source_target_pairs={{0,510},{2,0},{4,2},{6,4},{8,6},{10,8},{12,10},{14,12},{16,14},{18... | collective-permute-start | bytes 1544 | tf_op jit(solution)/shard_map/ppermute | solution.py:13
  50.4 8.3 %collective-permute-start.11 = (s32[4,32]{1,0:T(4,128)S(1)}, s32[4,32]{1,0:T(4,128)S(1)}, u32[]{:S(2)}, u32[]{:S(2)}) collective-permute-start(s32[4,32]{1,0:T(4,128)S(1)} %collective-permute-done.9), channel_id=1, source_target_pairs={{0,510},{2,0},{4,2},{6,4},{8,6},{10,8},{12,10},{14,12},{16,14},{18... | collective-permute-start | bytes 1544 | tf_op jit(solution)/shard_map/ppermute | solution.py:13
  61.4 9.7 %collective-permute-start.6 = (bf16[32,4,2048]{2,1,0:T(4,128)(2,1)}, bf16[32,4,2048]{2,1,0:T(4,128)(2,1)}, u32[]{:S(2)}, u32[]{:S(2)}) collective-permute-start(bf16[32,4,2048]{2,1,0:T(4,128)(2,1)} %collective-permute-done.4), channel_id=1, source_target_pairs={{0,510},{2,0},{4,2},{6,4},{8,6},{10,8},{12,10},{14,12},{16,14},{18... | collective-permute-start | bytes 1572872 | tf_op jit(solution)/shard_map/ppermute | solution.py:13
  73.2 1.9 collective-permute-start.1
  75.1 2.1 %gather_fusion = bf16[32,4,2048]{2,1,0:T(4,128)(2,1)S(1)} fusion(bf16[32,4,2048]{2,1,0:T(4,128)(2,1)} %collective-permute-done, s32[1024]{0:T(1024)S(1)} %pad_clamp_fusion.7), kind=kCustom, calls=%fused_computation.clone | custom fusion | bytes 1048704 | tf_op jit(solution)/shard_map/jit(_take)/gather | solution.py:97
  78.5 9.4 %collective-permute-start.8 = (bf16[32,4,2048]{2,1,0:T(4,128)(2,1)}, bf16[32,4,2048]{2,1,0:T(4,128)(2,1)}, u32[]{:S(2)}, u32[]{:S(2)}) collective-permute-start(bf16[32,4,2048]{2,1,0:T(4,128)(2,1)} %collective-permute-done.6), channel_id=1, source_target_pairs={{0,510},{2,0},{4,2},{6,4},{8,6},{10,8},{12,10},{14,12},{16,14},{18... | collective-permute-start | bytes 1572872 | tf_op jit(solution)/shard_map/ppermute | solution.py:13
  87.9 2.8 %gather_fusion.1 = bf16[32,4,2048]{2,1,0:T(4,128)(2,1)} fusion(bf16[32,4,2048]{2,1,0:T(4,128)(2,1)} %collective-permute-done.1, s32[1024]{0:T(1024)S(1)} %pad_clamp_fusion.6), kind=kCustom, calls=%fused_computation.1.clone | custom fusion | bytes 1048704 | tf_op jit(solution)/shard_map/jit(_take)/gather | solution.py:97
  90.7 2.3 %select_convert_fusion.6 = f32[32,4,2048]{2,1,0:T(4,128)} fusion(bf16[32,4,2048]{2,1,0:T(4,128)(2,1)} %gather_fusion.1, pred[32]{0:T(512)(128)(4,1)S(1)} %get-tuple-element.27), kind=kLoop, calls=%fused_computation.37 | loop fusion | flops 524288 | bytes 1572896 | tf_op jit(solution)/shard_map/convert_element_type | solution.py:66
  100.0 5.9 %collective-permute-done.2 = bf16[32,4,2048]{2,1,0:T(4,128)(2,1)} collective-permute-done((bf16[32,4,2048]{2,1,0:T(4,128)(2,1)}, bf16[32,4,2048]{2,1,0:T(4,128)(2,1)}, u32[]{:S(2)}, u32[]{:S(2)}) %collective-permute-start.2) | collective-permute-done | bytes 524320 | tf_op jit(solution)/shard_map/ppermute | solution.py:13
  108.5 14.8 %collective-permute-start.10 = (bf16[32,4,2048]{2,1,0:T(4,128)(2,1)}, bf16[32,4,2048]{2,1,0:T(4,128)(2,1)}, u32[]{:S(2)}, u32[]{:S(2)}) collective-permute-start(bf16[32,4,2048]{2,1,0:T(4,128)(2,1)} %collective-permute-done.8), channel_id=1, source_target_pairs={{0,510},{2,0},{4,2},{6,4},{8,6},{10,8},{12,10},{14,12},{16,14},{18... | collective-permute-start | bytes 1572872 | tf_op jit(solution)/shard_map/ppermute | solution.py:13
  123.3 2.8 %gather_fusion.2 = bf16[32,4,2048]{2,1,0:T(4,128)(2,1)} fusion(bf16[32,4,2048]{2,1,0:T(4,128)(2,1)} %collective-permute-done.2, s32[1024]{0:T(1024)S(1)} %pad_clamp_fusion.5), kind=kCustom, calls=%fused_computation.2.clone | custom fusion | bytes 1048704 | tf_op jit(solution)/shard_map/jit(_take)/gather | solution.py:97
  126.2 2.4 %select_convert_fusion.5 = f32[32,4,2048]{2,1,0:T(4,128)} fusion(bf16[32,4,2048]{2,1,0:T(4,128)(2,1)} %gather_fusion.2, pred[32]{0:T(512)(128)(4,1)S(1)} %get-tuple-element.74), kind=kLoop, calls=%fused_computation.36 | loop fusion | flops 524288 | bytes 1572896 | tf_op jit(solution)/shard_map/convert_element_type | solution.py:66
  128.6 2.8 %gather_fusion.3 = bf16[32,4,2048]{2,1,0:T(4,128)(2,1)} fusion(bf16[32,4,2048]{2,1,0:T(4,128)(2,1)} %collective-permute-done.3, s32[1024]{0:T(1024)S(1)} %pad_clamp_fusion.4), kind=kCustom, calls=%fused_computation.3.clone | custom fusion | bytes 1048704 | tf_op jit(solution)/shard_map/jit(_take)/gather | solution.py:97
  132.8 4.8 %add_reduce_fusion.7 = (f32[32,1024]{1,0:T(8,128)S(1)}, f32[32,1024]{1,0:T(8,128)S(1)}, f32[32,1024]{1,0:T(8,128)S(1)}, f32[32,1024]{1,0:T(8,128)S(1)}, f32[32,1...) fusion(f32[32,4,2048]{2,1,0:T(4,128)S(1)} %copy-done.7, ...), kind=kLoop, calls=%fused_computation.54 | loop fusion | flops 3932160 | bytes 6291456 | tf_op jit(solution)/shard_map/reduce_sum | solution.py:69
  141.5 3.6 %fusion.4 = f32[2,32,4,257]{3,1,2,0:T(8,128)S(1)} fusion(f32[1024,257]{0,1:T(8,128)S(1)} %copy-done.2, f32[1024,257]{0,1:T(8,128)S(1)} %copy-done.1, f32[1,32,4,2048]{3,1,2,0:T(8,128)S(1)} %maximum_bitcast_fusion.3, f32[1,32,4,2048]{3,1,2,0:T(8,128)S(1)} %maximum_bitcast_fusion.2), kind=kOutput, calls=%fused_computation.15 | convolution fusion | flops 1617954816 | bytes 4465664 | tf_op jit(solution)/shard_map/dot_general | solution.py:103
  145.1 2.2 %collective-permute-start.12 = (f32[2,32,4,257]{3,1,2,0:T(8,128)S(1)}, f32[2,32,4,257]{3,1,2,0:T(8,128)S(1)}, u32[]{:S(2)}, u32[]{:S(2)}) collective-permute-start(f32[2,32,4,257]{3,1,2,0:T(8,128)S(1)} %fusion.4), channel_id=1, source_target_pairs={{0,1},{1,0},{2,3},{3,2},{4,5},{5,4},{6,7},{7,6},{8,9},{9,8},{10,11... | collective-permute-start | bytes 789512 | tf_op jit(solution)/shard_map/ppermute | solution.py:18
  147.3 6.3 %collective-permute-done.12 = f32[2,32,4,257]{3,1,2,0:T(8,128)S(1)} collective-permute-done((f32[2,32,4,257]{3,1,2,0:T(8,128)S(1)}, f32[2,32,4,257]{3,1,2,0:T(8,128)S(1)}, u32[]{:S(2)}, u32[]{:S(2)}) %collective-permute-start.12) | collective-permute-done | bytes 263200 | tf_op jit(solution)/shard_map/ppermute | solution.py:18
  153.7 12.0 %collective-permute-start.17 = (f32[32,257]{1,0:T(8,128)S(1)}, f32[32,257]{1,0:T(8,128)S(1)}, u32[]{:S(2)}, u32[]{:S(2)}) collective-permute-start(f32[32,257]{1,0:T(8,128)S(1)} %get-tuple-element.58), channel_id=1, source_target_pairs={{0,510},{2,0},{4,2},{6,4},{8,6},{10,8},{12,10},{14,12},{16,14},{18... | collective-permute-start | bytes 98696 | tf_op jit(solution)/shard_map/ppermute | solution.py:13
  165.7 1.9 collective-permute-start.18
  167.6 1.9 collective-permute-start.19
  171.5 3.5 %collective-permute-start.13 = (f32[32,257]{1,0:T(8,128)S(1)}, f32[32,257]{1,0:T(8,128)S(1)}, u32[]{:S(2)}, u32[]{:S(2)}) collective-permute-start(f32[32,257]{1,0:T(8,128)S(1)} %get-tuple-element.66), channel_id=1, source_target_pairs={{0,2},{2,4},{4,6},{6,8},{8,10},{10,12},{12,14},{14,16},{16,18},{18... | collective-permute-start | bytes 98696 | tf_op jit(solution)/shard_map/ppermute | solution.py:13
  175.1 3.2 %collective-permute-start.14 = (f32[32,257]{1,0:T(8,128)S(1)}, f32[32,257]{1,0:T(8,128)S(1)}, u32[]{:S(2)}, u32[]{:S(2)}) collective-permute-start(f32[32,257]{1,0:T(8,128)S(1)} %get-tuple-element.69), channel_id=1, source_target_pairs={{0,4},{2,6},{4,8},{6,10},{8,12},{10,14},{12,16},{14,18},{16,20},{1... | collective-permute-start | bytes 98696 | tf_op jit(solution)/shard_map/ppermute | solution.py:13
  178.3 3.5 %collective-permute-start.15 = (f32[32,257]{1,0:T(8,128)S(1)}, f32[32,257]{1,0:T(8,128)S(1)}, u32[]{:S(2)}, u32[]{:S(2)}) collective-permute-start(f32[32,257]{1,0:T(8,128)S(1)} %get-tuple-element.68), channel_id=1, source_target_pairs={{0,6},{2,8},{4,10},{6,12},{8,14},{10,16},{12,18},{14,20},{16,22},{... | collective-permute-start | bytes 98696 | tf_op jit(solution)/shard_map/ppermute | solution.py:13
  181.9 5.6 %collective-permute-start.16 = (f32[32,257]{1,0:T(8,128)S(1)}, f32[32,257]{1,0:T(8,128)S(1)}, u32[]{:S(2)}, u32[]{:S(2)}) collective-permute-start(f32[32,257]{1,0:T(8,128)S(1)} %get-tuple-element.67), channel_id=1, source_target_pairs={{0,8},{2,10},{4,12},{6,14},{8,16},{10,18},{12,20},{14,22},{16,24},... | collective-permute-start | bytes 98696 | tf_op jit(solution)/shard_map/ppermute | solution.py:13
  190.3 3.2 %collective-permute-done.16 = f32[32,257]{1,0:T(8,128)S(1)} collective-permute-done((f32[32,257]{1,0:T(8,128)S(1)}, f32[32,257]{1,0:T(8,128)S(1)}, u32[]{:S(2)}, u32[]{:S(2)}) %collective-permute-start.16) | collective-permute-done | bytes 32928 | tf_op jit(solution)/shard_map/ppermute | solution.py:13
  (117 shorter events, 41.3 us)
Async XLA Ops:
  0.6 4.6 %copy-start = (bf16[32,8,2048]{2,1,0:T(8,128)(2,1)S(1)}, bf16[32,8,2048]{2,1,0:T(8,128)(2,1)}, u32[]{:S(2)}) copy-start(bf16[32,8,2048]{2,1,0:T(8,128)(2,1)} %param.5) | copy-start | bytes 3145732
  5.3 2.6 %copy-start.11 = (s32[32]{0:T(128)S(1)}, s32[32]{0:T(128)}, u32[]{:S(2)}) copy-start(s32[32]{0:T(128)} %param.7) | copy-start | bytes 388
  8.2 6.4 %copy-start.10 = (s32[4,32]{1,0:T(4,128)S(1)}, s32[4,32]{1,0:T(4,128)}, u32[]{:S(2)}) copy-start(s32[4,32]{1,0:T(4,128)} %param.6) | copy-start | bytes 1540
  10.0 63.2 %collective-permute-start = (bf16[32,4,2048]{2,1,0:T(4,128)(2,1)}, bf16[32,4,2048]{2,1,0:T(4,128)(2,1)}, u32[]{:S(2)}, u32[]{:S(2)}) collective-permute-start(bf16[32,4,2048]{2,1,0:T(4,128)(2,1)} %get-tuple-element.49), channel_id=1, source_target_pairs={{0,2},{2,4},{4,6},{6,8},{8,10},{10,12},{12,14},{14,16},{16,18},{18... | collective-permute-start | bytes 1572872 | tf_op jit(solution)/shard_map/ppermute | solution.py:13
  14.6 23.0 %collective-permute-start.5 = (s32[4,32]{1,0:T(4,128)S(1)}, s32[4,32]{1,0:T(4,128)S(1)}, u32[]{:S(2)}, u32[]{:S(2)}) collective-permute-start(s32[4,32]{1,0:T(4,128)S(1)} %copy-done.10), channel_id=1, source_target_pairs={{0,510},{2,0},{4,2},{6,4},{8,6},{10,8},{12,10},{14,12},{16,14},{18... | collective-permute-start | bytes 1544 | tf_op jit(solution)/shard_map/ppermute | solution.py:13
  20.7 40.6 %collective-permute-start.4 = (bf16[32,4,2048]{2,1,0:T(4,128)(2,1)S(1)}, bf16[32,4,2048]{2,1,0:T(4,128)(2,1)}, u32[]{:S(2)}, u32[]{:S(2)}) collective-permute-start(bf16[32,4,2048]{2,1,0:T(4,128)(2,1)S(1)} %get-tuple-element.48), channel_id=1, source_target_pairs={{0,510},{2,0},{4,2},{6,4},{8,6},{10,8},{12,10},{14,12},{16,14},{18... | collective-permute-start | bytes 1572872 | tf_op jit(solution)/shard_map/ppermute | solution.py:13
  38.6 4.9 %collective-permute-start.7 = (s32[4,32]{1,0:T(4,128)S(1)}, s32[4,32]{1,0:T(4,128)S(1)}, u32[]{:S(2)}, u32[]{:S(2)}) collective-permute-start(s32[4,32]{1,0:T(4,128)S(1)} %collective-permute-done.5), channel_id=1, source_target_pairs={{0,510},{2,0},{4,2},{6,4},{8,6},{10,8},{12,10},{14,12},{16,14},{18... | collective-permute-start | bytes 1544 | tf_op jit(solution)/shard_map/ppermute | solution.py:13
  44.5 4.9 %collective-permute-start.9 = (s32[4,32]{1,0:T(4,128)S(1)}, s32[4,32]{1,0:T(4,128)S(1)}, u32[]{:S(2)}, u32[]{:S(2)}) collective-permute-start(s32[4,32]{1,0:T(4,128)S(1)} %collective-permute-done.7), channel_id=1, source_target_pairs={{0,510},{2,0},{4,2},{6,4},{8,6},{10,8},{12,10},{14,12},{16,14},{18... | collective-permute-start | bytes 1544 | tf_op jit(solution)/shard_map/ppermute | solution.py:13
  50.4 9.6 %collective-permute-start.11 = (s32[4,32]{1,0:T(4,128)S(1)}, s32[4,32]{1,0:T(4,128)S(1)}, u32[]{:S(2)}, u32[]{:S(2)}) collective-permute-start(s32[4,32]{1,0:T(4,128)S(1)} %collective-permute-done.9), channel_id=1, source_target_pairs={{0,510},{2,0},{4,2},{6,4},{8,6},{10,8},{12,10},{14,12},{16,14},{18... | collective-permute-start | bytes 1544 | tf_op jit(solution)/shard_map/ppermute | solution.py:13
  61.1 11.1 %copy-start.6 = (f32[32,4,2048]{2,1,0:T(4,128)S(1)}, f32[32,4,2048]{2,1,0:T(4,128)}, u32[]{:S(2)}) copy-start(f32[32,4,2048]{2,1,0:T(4,128)} %select_convert_fusion.3) | copy-start | bytes 3145732
  61.4 17.1 %collective-permute-start.6 = (bf16[32,4,2048]{2,1,0:T(4,128)(2,1)}, bf16[32,4,2048]{2,1,0:T(4,128)(2,1)}, u32[]{:S(2)}, u32[]{:S(2)}) collective-permute-start(bf16[32,4,2048]{2,1,0:T(4,128)(2,1)} %collective-permute-done.4), channel_id=1, source_target_pairs={{0,510},{2,0},{4,2},{6,4},{8,6},{10,8},{12,10},{14,12},{16,14},{18... | collective-permute-start | bytes 1572872 | tf_op jit(solution)/shard_map/ppermute | solution.py:13
  73.2 14.8 %collective-permute-start.1 = (bf16[32,4,2048]{2,1,0:T(4,128)(2,1)}, bf16[32,4,2048]{2,1,0:T(4,128)(2,1)}, u32[]{:S(2)}, u32[]{:S(2)}) collective-permute-start(bf16[32,4,2048]{2,1,0:T(4,128)(2,1)} %collective-permute-done), channel_id=1, source_target_pairs={{0,2},{2,4},{4,6},{6,8},{8,10},{10,12},{12,14},{14,16},{16,18},{18... | collective-permute-start | bytes 1572872 | tf_op jit(solution)/shard_map/ppermute | solution.py:13
  78.5 17.7 %copy-start.4 = (f32[32,4,2048]{2,1,0:T(4,128)S(1)}, f32[32,4,2048]{2,1,0:T(4,128)}, u32[]{:S(2)}) copy-start(f32[32,4,2048]{2,1,0:T(4,128)} %select_convert_fusion.2) | copy-start | bytes 3145732
  78.5 19.4 %collective-permute-start.8 = (bf16[32,4,2048]{2,1,0:T(4,128)(2,1)}, bf16[32,4,2048]{2,1,0:T(4,128)(2,1)}, u32[]{:S(2)}, u32[]{:S(2)}) collective-permute-start(bf16[32,4,2048]{2,1,0:T(4,128)(2,1)} %collective-permute-done.6), channel_id=1, source_target_pairs={{0,510},{2,0},{4,2},{6,4},{8,6},{10,8},{12,10},{14,12},{16,14},{18... | collective-permute-start | bytes 1572872 | tf_op jit(solution)/shard_map/ppermute | solution.py:13
  93.1 12.8 %collective-permute-start.2 = (bf16[32,4,2048]{2,1,0:T(4,128)(2,1)}, bf16[32,4,2048]{2,1,0:T(4,128)(2,1)}, u32[]{:S(2)}, u32[]{:S(2)}) collective-permute-start(bf16[32,4,2048]{2,1,0:T(4,128)(2,1)} %collective-permute-done.1), channel_id=1, source_target_pairs={{0,2},{2,4},{4,6},{6,8},{8,10},{10,12},{12,14},{14,16},{16,18},{18... | collective-permute-start | bytes 1572872 | tf_op jit(solution)/shard_map/ppermute | solution.py:13
  96.1 2.9 %copy-start.5 = (f32[32,4,2048]{2,1,0:T(4,128)S(1)}, f32[32,4,2048]{2,1,0:T(4,128)}, u32[]{:S(2)}) copy-start(f32[32,4,2048]{2,1,0:T(4,128)} %select_convert_fusion.1) | copy-start | bytes 3145732
  105.9 22.6 %collective-permute-start.3 = (bf16[32,4,2048]{2,1,0:T(4,128)(2,1)}, bf16[32,4,2048]{2,1,0:T(4,128)(2,1)}, u32[]{:S(2)}, u32[]{:S(2)}) collective-permute-start(bf16[32,4,2048]{2,1,0:T(4,128)(2,1)} %collective-permute-done.2), channel_id=1, source_target_pairs={{0,2},{2,4},{4,6},{6,8},{8,10},{10,12},{12,14},{14,16},{16,18},{18... | collective-permute-start | bytes 1572872 | tf_op jit(solution)/shard_map/ppermute | solution.py:13
  108.5 29.2 %collective-permute-start.10 = (bf16[32,4,2048]{2,1,0:T(4,128)(2,1)}, bf16[32,4,2048]{2,1,0:T(4,128)(2,1)}, u32[]{:S(2)}, u32[]{:S(2)}) collective-permute-start(bf16[32,4,2048]{2,1,0:T(4,128)(2,1)} %collective-permute-done.8), channel_id=1, source_target_pairs={{0,510},{2,0},{4,2},{6,4},{8,6},{10,8},{12,10},{14,12},{16,14},{18... | collective-permute-start | bytes 1572872 | tf_op jit(solution)/shard_map/ppermute | solution.py:13
  126.2 6.6 %copy-start.3 = (f32[32,4,2048]{2,1,0:T(4,128)S(1)}, f32[32,4,2048]{2,1,0:T(4,128)}, u32[]{:S(2)}) copy-start(f32[32,4,2048]{2,1,0:T(4,128)} %get-tuple-element.47) | copy-start | bytes 3145732
  131.4 1.4 copy-start.7
  138.9 1.1 copy-start.8
  139.9 1.2 copy-start.1
  140.0 1.6 copy-start.2
  145.1 8.5 %collective-permute-start.12 = (f32[2,32,4,257]{3,1,2,0:T(8,128)S(1)}, f32[2,32,4,257]{3,1,2,0:T(8,128)S(1)}, u32[]{:S(2)}, u32[]{:S(2)}) collective-permute-start(f32[2,32,4,257]{3,1,2,0:T(8,128)S(1)} %fusion.4), channel_id=1, source_target_pairs={{0,1},{1,0},{2,3},{3,2},{4,5},{5,4},{6,7},{7,6},{8,9},{9,8},{10,11... | collective-permute-start | bytes 789512 | tf_op jit(solution)/shard_map/ppermute | solution.py:18
  153.7 21.4 %collective-permute-start.17 = (f32[32,257]{1,0:T(8,128)S(1)}, f32[32,257]{1,0:T(8,128)S(1)}, u32[]{:S(2)}, u32[]{:S(2)}) collective-permute-start(f32[32,257]{1,0:T(8,128)S(1)} %get-tuple-element.58), channel_id=1, source_target_pairs={{0,510},{2,0},{4,2},{6,4},{8,6},{10,8},{12,10},{14,12},{16,14},{18... | collective-permute-start | bytes 98696 | tf_op jit(solution)/shard_map/ppermute | solution.py:13
  165.7 12.6 %collective-permute-start.18 = (f32[32,257]{1,0:T(8,128)S(1)}, f32[32,257]{1,0:T(8,128)S(1)}, u32[]{:S(2)}, u32[]{:S(2)}) collective-permute-start(f32[32,257]{1,0:T(8,128)S(1)} %get-tuple-element.61), channel_id=1, source_target_pairs={{0,508},{2,510},{4,0},{6,2},{8,4},{10,6},{12,8},{14,10},{16,12},{1... | collective-permute-start | bytes 98696 | tf_op jit(solution)/shard_map/ppermute | solution.py:13
  167.6 14.2 %collective-permute-start.19 = (f32[32,257]{1,0:T(8,128)S(1)}, f32[32,257]{1,0:T(8,128)S(1)}, u32[]{:S(2)}, u32[]{:S(2)}) collective-permute-start(f32[32,257]{1,0:T(8,128)S(1)} %get-tuple-element.60), channel_id=1, source_target_pairs={{0,506},{2,508},{4,510},{6,0},{8,2},{10,4},{12,6},{14,8},{16,10},{... | collective-permute-start | bytes 98696 | tf_op jit(solution)/shard_map/ppermute | solution.py:13
  169.6 17.9 %collective-permute-start.20 = (f32[32,257]{1,0:T(8,128)S(1)}, f32[32,257]{1,0:T(8,128)S(1)}, u32[]{:S(2)}, u32[]{:S(2)}) collective-permute-start(f32[32,257]{1,0:T(8,128)S(1)} %get-tuple-element.59), channel_id=1, source_target_pairs={{0,504},{2,506},{4,508},{6,510},{8,0},{10,2},{12,4},{14,6},{16,8},... | collective-permute-start | bytes 98696 | tf_op jit(solution)/shard_map/ppermute | solution.py:13
  171.5 18.1 %collective-permute-start.13 = (f32[32,257]{1,0:T(8,128)S(1)}, f32[32,257]{1,0:T(8,128)S(1)}, u32[]{:S(2)}, u32[]{:S(2)}) collective-permute-start(f32[32,257]{1,0:T(8,128)S(1)} %get-tuple-element.66), channel_id=1, source_target_pairs={{0,2},{2,4},{4,6},{6,8},{8,10},{10,12},{12,14},{14,16},{16,18},{18... | collective-permute-start | bytes 98696 | tf_op jit(solution)/shard_map/ppermute | solution.py:13
  175.1 14.5 %collective-permute-start.14 = (f32[32,257]{1,0:T(8,128)S(1)}, f32[32,257]{1,0:T(8,128)S(1)}, u32[]{:S(2)}, u32[]{:S(2)}) collective-permute-start(f32[32,257]{1,0:T(8,128)S(1)} %get-tuple-element.69), channel_id=1, source_target_pairs={{0,4},{2,6},{4,8},{6,10},{8,12},{10,14},{12,16},{14,18},{16,20},{1... | collective-permute-start | bytes 98696 | tf_op jit(solution)/shard_map/ppermute | solution.py:13
  178.3 12.0 %collective-permute-start.15 = (f32[32,257]{1,0:T(8,128)S(1)}, f32[32,257]{1,0:T(8,128)S(1)}, u32[]{:S(2)}, u32[]{:S(2)}) collective-permute-start(f32[32,257]{1,0:T(8,128)S(1)} %get-tuple-element.68), channel_id=1, source_target_pairs={{0,6},{2,8},{4,10},{6,12},{8,14},{10,16},{12,18},{14,20},{16,22},{... | collective-permute-start | bytes 98696 | tf_op jit(solution)/shard_map/ppermute | solution.py:13
  181.9 11.6 %collective-permute-start.16 = (f32[32,257]{1,0:T(8,128)S(1)}, f32[32,257]{1,0:T(8,128)S(1)}, u32[]{:S(2)}, u32[]{:S(2)}) collective-permute-start(f32[32,257]{1,0:T(8,128)S(1)} %get-tuple-element.67), channel_id=1, source_target_pairs={{0,8},{2,10},{4,12},{6,14},{8,16},{10,18},{12,20},{14,22},{16,24},... | collective-permute-start | bytes 98696 | tf_op jit(solution)/shard_map/ppermute | solution.py:13
  (1 other events, 1.1 us)

commit v2 on v1

--- a/solution.py
+++ b/solution.py
@@ -85,19 +85,21 @@
     split = segments // 2
     ahead = white[:, :split]
     behind = white[:, split:]
+    dc_imag = lax.broadcasted_iota(jnp.int32, behind.shape, 2) == half_len
     moving_ahead = ahead
-    moving_behind = behind
-    moving_offsets = offsets
+    moving_behind = behind.at[:, :stops, half_len].set(offsets.T.astype(jnp.bfloat16))
     own_pieces = []
     later_pieces = []
     for stop in range(1, stops + 1):
-        moving_ahead = shifted(moving_ahead, "blk", 1)
-        moving_behind = shifted(moving_behind, "blk", -1)
-        moving_offsets = shifted(moving_offsets, "blk", -1)
+        moving_ahead, moving_behind = lax.optimization_barrier(
+            (shifted(moving_ahead, "blk", 1), shifted(moving_behind, "blk", -1))
+        )
         partner = jnp.take(moving_ahead, offsets[stop - 1], axis=0)
         own_pieces.append(cross_spectrum(ahead, partner, half_len))
-        local_partner = jnp.take(behind, moving_offsets[stop - 1], axis=0)
-        later_pieces.append(cross_spectrum(moving_behind, local_partner, half_len))
+        later_offsets = moving_behind[:, stop - 1, half_len].astype(jnp.int32)
+        local_partner = jnp.take(behind, later_offsets, axis=0)
+        later = jnp.where(dc_imag, jnp.zeros_like(moving_behind), moving_behind)
+        later_pieces.append(cross_spectrum(later, local_partner, half_len))
     back_table = inverse_table(length, LAGS)
     pieces = jnp.stack([jnp.stack(own_pieces, axis=1), jnp.stack(later_pieces, axis=1)], axis=0)
     partial = jnp.dot(

time: 197 us -> 172 us (0.87)
  starting transfers between devices: 110 us -> 87.3 us
  waiting for transfers between devices: 18.1 us -> 14.8 us
  local copies, waits for them, and re-layouts: 22.9 us -> 25.8 us
    ppermute x20 -> x16, starting transfers between devices: 108 us -> 85 us  [shifted(): lax.ppermute(x, axis, [(i, (i + by) % length) for i in range(length)])]
    convert_element_type x0 -> x4, other arithmetic: none -> 4.18 us  [on_device(): later_offsets = moving_behind[:, stop - 1, half_len].astype(jnp.int32)]
    unnamed x30 -> x35, local copies, waits for them, and re-layouts: 3.99 us -> 7.58 us
    ppermute x20 -> x16, waiting for transfers between devices: 11.8 us -> 8.53 us  [shifted(): lax.ppermute(x, axis, [(i, (i + by) % length) for i in range(length)])]
    convert_element_type x8, other arithmetic: 11.4 us -> 8.23 us  [cross_spectrum(): second = partner.astype(jnp.float32)]
    gather x4, local copies, waits for them, and re-layouts: 10.5 us -> 8.15 us  [on_device(): partner = jnp.take(moving_ahead, offsets[stop - 1], axis=0)]
    convert_element_type x5 -> x2, other arithmetic: 6.4 us -> 5.34 us  [cross_spectrum(): first = local.astype(jnp.float32)]
  transfers between devices with their start and end apart: 21 -> 17, of which waited for: 6 -> 6; matrix products, arithmetic and copies ran while one was open for 24% -> 17% of each run, Pallas kernels for 0% -> 0%
where the time goes in v2:
time: 172 us; the launch traced here: 170 us
  starting transfers between devices  87.3 us (51%)
  other arithmetic  34.5 us (20%)
  local copies, waits for them, and re-layouts  25.8 us (15%)
  waiting for transfers between devices  14.8 us (9%)
  matrix products  6.07 us (4%)
    ppermute x16, starting transfers between devices, shifted(): lax.ppermute(x, axis, [(i, (i + by) % length) for i in range(length)])  85 us
    reduce_sum x5, other arithmetic, cross_spectrum(): real_sum = jnp.sum(real_a * real_b + imag_a * imag_b, axis=1)  8.92 us
    ppermute x16, waiting for transfers between devices, shifted(): lax.ppermute(x, axis, [(i, (i + by) % length) for i in range(length)])  8.53 us
    convert_element_type x8, other arithmetic, cross_spectrum(): second = partner.astype(jnp.float32)  8.23 us
    gather x4, local copies, waits for them, and re-layouts, on_device(): partner = jnp.take(moving_ahead, offsets[stop - 1], axis=0)  8.15 us
    unnamed x35, local copies, waits for them, and re-layouts  7.58 us
    ppermute x1, waiting for transfers between devices, swapped(): return lax.ppermute(x, axis, [(i, i ^ 1) for i in range(length)])  6.29 us
    convert_element_type x2, other arithmetic, cross_spectrum(): first = local.astype(jnp.float32)  5.34 us
  transfers between devices with their start and end apart: 17, of which 6 were waited for; matrix products, arithmetic and copies ran while one was open for 17% of the time, Pallas kernels for 0%

profile of v2, /device:TPU:1, one launch (start us, length us, event | category | flops | bytes accessed | tf_op | source)
XLA Modules:
  0.0 169.8 jit_solution(17307176843754253596)
XLA Ops:
  2.3 3.0 %subtract_convert_fusion = (bf16[32,64,1024]{2,1,0:T(8,128)(2,1)S(1)}, bf16[32,64,1024]{2,1,0:T(8,128)(2,1)S(1)}) fusion(f32[64,1024]{1,0:T(8,128)S(1)} %get-tuple-element.112, f32[32,1024]{1,0:T(8,128)S(1)} %get-tuple-element.109, f32[64,1024]{1,0:T(8,128)S(1)} %get-tuple-element.113, f32[32,1024]{1,0:T(8,128)S(1)} %get-tuple-element.108), kind=kLoop, calls=%fused_computation.13 | loop fusion | flops 18874368 | bytes 9175040 | tf_op jit(solution)/shard_map/convert.7
  5.3 2.5 %fusion.12 = (f32[256]{0:T(256)S(1)}, f32[2048,256]{0,1:T(8,128)S(1)}) fusion(bf16[2048,1024]{1,0:T(8,128)(2,1)S(1)} %bitcast.120, bf16[2048,1024]{1,0:T(8,128)(2,1)S(1)} %bitcast.119, bf16[32,8,2048]{2,1,0:T(8,128)(2,1)S(1)} %copy-done), kind=kOutput, calls=%fused_computation.25 | convolution fusion | flops 2165309184 | bytes 11535360 | tf_op jit(solution)/shard_map/dot_general | solution.py:78
  8.2 1.8 %slice_convert_fusion = (f32[32,4,2048]{2,1,0:T(4,128)}, bf16[32,4,2048]{2,1,0:T(4,128)(2,1)S(1)}, bf16[32,4,2048]{2,1,0:T(4,128)(2,1)}) fusion(bf16[32,8,2048]{2,1,0:T(8,128)(2,1)S(1)} %fusion.11), kind=kLoop, calls=%fused_computation.174 | loop fusion | flops 262144 | bytes 3145728 | tf_op jit(solution)/shard_map/convert_element_type | solution.py:65
  12.4 8.8 %collective-permute-start.1 = (bf16[32,4,2048]{2,1,0:T(4,128)(2,1)}, bf16[32,4,2048]{2,1,0:T(4,128)(2,1)}, u32[]{:S(2)}, u32[]{:S(2)}) collective-permute-start(bf16[32,4,2048]{2,1,0:T(4,128)(2,1)} %scatter.4), channel_id=1, source_target_pairs={{0,510},{2,0},{4,2},{6,4},{8,6},{10,8},{12,10},{14,12},{16,14},{18... | collective-permute-start | bytes 1572872 | tf_op jit(solution)/shard_map/ppermute | solution.py:13
  21.2 1.9 %collective-permute-start = (bf16[32,4,2048]{2,1,0:T(4,128)(2,1)}, bf16[32,4,2048]{2,1,0:T(4,128)(2,1)}, u32[]{:S(2)}, u32[]{:S(2)}) collective-permute-start(bf16[32,4,2048]{2,1,0:T(4,128)(2,1)} %get-tuple-element.71), channel_id=1, source_target_pairs={{0,2},{2,4},{4,6},{6,8},{8,10},{10,12},{12,14},{14,16},{16,18},{18... | collective-permute-start | bytes 1572872 | tf_op jit(solution)/shard_map/ppermute | solution.py:13
  23.6 1.7 multiply_subtract_fusion
  25.3 2.8 %copy.15 = f32[1024,257]{0,1:T(8,128)} copy(f32[1024,257]{1,0:T(8,128)} %bitcast.118) | data formatting | bytes 2105344 | tf_op jit(solution)/shard_map/sub | solution.py:54
  29.6 3.7 %collective-permute-done = bf16[32,4,2048]{2,1,0:T(4,128)(2,1)} collective-permute-done((bf16[32,4,2048]{2,1,0:T(4,128)(2,1)}, bf16[32,4,2048]{2,1,0:T(4,128)(2,1)}, u32[]{:S(2)}, u32[]{:S(2)}) %collective-permute-start) | collective-permute-done | bytes 524320 | tf_op jit(solution)/shard_map/ppermute | solution.py:13
  33.3 14.8 %collective-permute-start.3 = (bf16[32,4,2048]{2,1,0:T(4,128)(2,1)}, bf16[32,4,2048]{2,1,0:T(4,128)(2,1)S(1)}, u32[]{:S(2)}, u32[]{:S(2)}) collective-permute-start(bf16[32,4,2048]{2,1,0:T(4,128)(2,1)} %collective-permute-done.1), channel_id=1, source_target_pairs={{0,510},{2,0},{4,2},{6,4},{8,6},{10,8},{12,10},{14,12},{16,14},{18... | collective-permute-start | bytes 1572872 | tf_op jit(solution)/shard_map/ppermute | solution.py:13
  49.6 1.9 %collective-permute-start.2 = (bf16[32,4,2048]{2,1,0:T(4,128)(2,1)}, bf16[32,4,2048]{2,1,0:T(4,128)(2,1)}, u32[]{:S(2)}, u32[]{:S(2)}) collective-permute-start(bf16[32,4,2048]{2,1,0:T(4,128)(2,1)} %collective-permute-done), channel_id=1, source_target_pairs={{0,2},{2,4},{4,6},{6,8},{8,10},{10,12},{12,14},{14,16},{16,18},{18... | collective-permute-start | bytes 1572872 | tf_op jit(solution)/shard_map/ppermute | solution.py:13
  51.5 2.0 %gather_fusion = bf16[32,4,2048]{2,1,0:T(4,128)(2,1)S(1)} fusion(bf16[32,4,2048]{2,1,0:T(4,128)(2,1)} %collective-permute-done, s32[1024]{0:T(1024)S(1)} %get-tuple-element.117), kind=kCustom, calls=%fused_computation.clone | custom fusion | bytes 1048704 | tf_op jit(solution)/shard_map/jit(_take)/gather | solution.py:97
  57.9 10.1 %collective-permute-start.5 = (bf16[32,4,2048]{2,1,0:T(4,128)(2,1)S(1)}, bf16[32,4,2048]{2,1,0:T(4,128)(2,1)S(1)}, u32[]{:S(2)}, u32[]{:S(2)}) collective-permute-start(bf16[32,4,2048]{2,1,0:T(4,128)(2,1)S(1)} %collective-permute-done.3), channel_id=1, source_target_pairs={{0,510},{2,0},{4,2},{6,4},{8,6},{10,8},{12,10},{14,12},{16,14},{18... | collective-permute-start | bytes 1572872 | tf_op jit(solution)/shard_map/ppermute | solution.py:13
  68.7 1.9 %collective-permute-start.4 = (bf16[32,4,2048]{2,1,0:T(4,128)(2,1)}, bf16[32,4,2048]{2,1,0:T(4,128)(2,1)}, u32[]{:S(2)}, u32[]{:S(2)}) collective-permute-start(bf16[32,4,2048]{2,1,0:T(4,128)(2,1)} %collective-permute-done.2), channel_id=1, source_target_pairs={{0,2},{2,4},{4,6},{6,8},{8,10},{10,12},{12,14},{14,16},{16,18},{18... | collective-permute-start | bytes 1572872 | tf_op jit(solution)/shard_map/ppermute | solution.py:13
  70.7 2.0 %gather_fusion.1 = bf16[32,4,2048]{2,1,0:T(4,128)(2,1)S(1)} fusion(bf16[32,4,2048]{2,1,0:T(4,128)(2,1)} %collective-permute-done.2, s32[1024]{0:T(1024)S(1)} %get-tuple-element.116), kind=kCustom, calls=%fused_computation.1.clone | custom fusion | bytes 1048704 | tf_op jit(solution)/shard_map/jit(_take)/gather | solution.py:97
  77.1 10.1 %collective-permute-start.7 = (bf16[32,4,2048]{2,1,0:T(4,128)(2,1)S(1)}, bf16[32,4,2048]{2,1,0:T(4,128)(2,1)}, u32[]{:S(2)}, u32[]{:S(2)}) collective-permute-start(bf16[32,4,2048]{2,1,0:T(4,128)(2,1)S(1)} %collective-permute-done.5), channel_id=1, source_target_pairs={{0,510},{2,0},{4,2},{6,4},{8,6},{10,8},{12,10},{14,12},{16,14},{18... | collective-permute-start | bytes 1572872 | tf_op jit(solution)/shard_map/ppermute | solution.py:13
  87.9 2.1 %collective-permute-start.6 = (bf16[32,4,2048]{2,1,0:T(4,128)(2,1)}, bf16[32,4,2048]{2,1,0:T(4,128)(2,1)}, u32[]{:S(2)}, u32[]{:S(2)}) collective-permute-start(bf16[32,4,2048]{2,1,0:T(4,128)(2,1)} %collective-permute-done.4), channel_id=1, source_target_pairs={{0,2},{2,4},{4,6},{6,8},{8,10},{10,12},{12,14},{14,16},{16,18},{18... | collective-permute-start | bytes 1572872 | tf_op jit(solution)/shard_map/ppermute | solution.py:13
  90.0 2.0 %gather_fusion.2 = bf16[32,4,2048]{2,1,0:T(4,128)(2,1)S(1)} fusion(bf16[32,4,2048]{2,1,0:T(4,128)(2,1)} %collective-permute-done.4, s32[1024]{0:T(1024)S(1)} %get-tuple-element.115), kind=kCustom, calls=%fused_computation.2.clone | custom fusion | bytes 1048704 | tf_op jit(solution)/shard_map/jit(_take)/gather | solution.py:97
  97.7 3.6 %select_convert_fusion.11 = (f32[32,4,2048]{2,1,0:T(4,128)}, f32[32,4,2048]{2,1,0:T(4,128)}, f32[32,4,2048]{2,1,0:T(4,128)}, f32[32,4,2048]{2,1,0:T(4,128)}) fusion(bf16[32,4,2048]{2,1,0:T(4,128)(2,1)} %collective-permute-done.1, pred[2048]{0:T(1024)(128)(4,1)S(1)} %iota_compare_fusion, bf16[32,4,2048]{2,1,0:T(4,128)(2,1)S(1)} %collective-permute-done.3, ...), kind=kLoop, calls=%fused_computation.50 | loop fusion | flops 2097152 | bytes 6293504 | tf_op jit(solution)/shard_map/convert_element_type | solution.py:65
  102.3 2.0 %gather_fusion.3 = bf16[32,4,2048]{2,1,0:T(4,128)(2,1)S(1)} fusion(bf16[32,4,2048]{2,1,0:T(4,128)(2,1)} %collective-permute-done.6, s32[1024]{0:T(1024)S(1)} %get-tuple-element.114), kind=kCustom, calls=%fused_computation.3.clone | custom fusion | bytes 1048704 | tf_op jit(solution)/shard_map/jit(_take)/gather | solution.py:97
  105.5 4.8 %add_reduce_fusion.7 = (f32[32,1024]{1,0:T(8,128)S(1)}, f32[32,1024]{1,0:T(8,128)S(1)}, f32[32,1024]{1,0:T(8,128)S(1)}, f32[32,1024]{1,0:T(8,128)S(1)}, f32[32,1...) fusion(f32[32,4,2048]{2,1,0:T(4,128)S(1)} %copy-done.7, ...), kind=kLoop, calls=%fused_computation.58 | loop fusion | flops 3932160 | bytes 6291456 | tf_op jit(solution)/shard_map/reduce_sum | solution.py:69
  118.5 3.6 %fusion.4 = f32[2,32,4,257]{3,1,2,0:T(8,128)S(1)} fusion(f32[1024,257]{0,1:T(8,128)S(1)} %copy-done.2, f32[1024,257]{0,1:T(8,128)S(1)} %copy-done.1, f32[1,32,4,2048]{3,1,2,0:T(8,128)S(1)} %maximum_bitcast_fusion.3, f32[1,32,4,2048]{3,1,2,0:T(8,128)S(1)} %maximum_bitcast_fusion.2), kind=kOutput, calls=%fused_computation.15 | convolution fusion | flops 1617954816 | bytes 4465664 | tf_op jit(solution)/shard_map/dot_general | solution.py:105
  122.1 2.2 %collective-permute-start.8 = (f32[2,32,4,257]{3,1,2,0:T(8,128)S(1)}, f32[2,32,4,257]{3,1,2,0:T(8,128)S(1)}, u32[]{:S(2)}, u32[]{:S(2)}) collective-permute-start(f32[2,32,4,257]{3,1,2,0:T(8,128)S(1)} %fusion.4), channel_id=1, source_target_pairs={{0,1},{1,0},{2,3},{3,2},{4,5},{5,4},{6,7},{7,6},{8,9},{9,8},{10,11... | collective-permute-start | bytes 789512 | tf_op jit(solution)/shard_map/ppermute | solution.py:18
  124.3 6.3 %collective-permute-done.8 = f32[2,32,4,257]{3,1,2,0:T(8,128)S(1)} collective-permute-done((f32[2,32,4,257]{3,1,2,0:T(8,128)S(1)}, f32[2,32,4,257]{3,1,2,0:T(8,128)S(1)}, u32[]{:S(2)}, u32[]{:S(2)}) %collective-permute-start.8) | collective-permute-done | bytes 263200 | tf_op jit(solution)/shard_map/ppermute | solution.py:18
  130.7 11.8 %collective-permute-start.13 = (f32[32,257]{1,0:T(8,128)S(1)}, f32[32,257]{1,0:T(8,128)S(1)}, u32[]{:S(2)}, u32[]{:S(2)}) collective-permute-start(f32[32,257]{1,0:T(8,128)S(1)} %get-tuple-element.80), channel_id=1, source_target_pairs={{0,510},{2,0},{4,2},{6,4},{8,6},{10,8},{12,10},{14,12},{16,14},{18... | collective-permute-start | bytes 98696 | tf_op jit(solution)/shard_map/ppermute | solution.py:13
  142.5 1.9 %collective-permute-start.14 = (f32[32,257]{1,0:T(8,128)S(1)}, f32[32,257]{1,0:T(8,128)S(1)}, u32[]{:S(2)}, u32[]{:S(2)}) collective-permute-start(f32[32,257]{1,0:T(8,128)S(1)} %get-tuple-element.83), channel_id=1, source_target_pairs={{0,508},{2,510},{4,0},{6,2},{8,4},{10,6},{12,8},{14,10},{16,12},{1... | collective-permute-start | bytes 98696 | tf_op jit(solution)/shard_map/ppermute | solution.py:13
  144.4 1.9 %collective-permute-start.15 = (f32[32,257]{1,0:T(8,128)S(1)}, f32[32,257]{1,0:T(8,128)S(1)}, u32[]{:S(2)}, u32[]{:S(2)}) collective-permute-start(f32[32,257]{1,0:T(8,128)S(1)} %get-tuple-element.82), channel_id=1, source_target_pairs={{0,506},{2,508},{4,510},{6,0},{8,2},{10,4},{12,6},{14,8},{16,10},{... | collective-permute-start | bytes 98696 | tf_op jit(solution)/shard_map/ppermute | solution.py:13
  146.4 1.9 %collective-permute-start.16 = (f32[32,257]{1,0:T(8,128)S(1)}, f32[32,257]{1,0:T(8,128)S(1)}, u32[]{:S(2)}, u32[]{:S(2)}) collective-permute-start(f32[32,257]{1,0:T(8,128)S(1)} %get-tuple-element.81), channel_id=1, source_target_pairs={{0,504},{2,506},{4,508},{6,510},{8,0},{10,2},{12,4},{14,6},{16,8},... | collective-permute-start | bytes 98696 | tf_op jit(solution)/shard_map/ppermute | solution.py:13
  148.3 3.4 %collective-permute-start.10 = (f32[32,257]{1,0:T(8,128)S(1)}, f32[32,257]{1,0:T(8,128)S(1)}, u32[]{:S(2)}, u32[]{:S(2)}) collective-permute-start(f32[32,257]{1,0:T(8,128)S(1)} %get-tuple-element.91), channel_id=1, source_target_pairs={{0,4},{2,6},{4,8},{6,10},{8,12},{10,14},{12,16},{14,18},{16,20},{1... | collective-permute-start | bytes 98696 | tf_op jit(solution)/shard_map/ppermute | solution.py:13
  151.7 5.0 %collective-permute-start.11 = (f32[32,257]{1,0:T(8,128)S(1)}, f32[32,257]{1,0:T(8,128)S(1)}, u32[]{:S(2)}, u32[]{:S(2)}) collective-permute-start(f32[32,257]{1,0:T(8,128)S(1)} %get-tuple-element.90), channel_id=1, source_target_pairs={{0,6},{2,8},{4,10},{6,12},{8,14},{10,16},{12,18},{14,20},{16,22},{... | collective-permute-start | bytes 98696 | tf_op jit(solution)/shard_map/ppermute | solution.py:13
  156.7 5.6 %collective-permute-start.12 = (f32[32,257]{1,0:T(8,128)S(1)}, f32[32,257]{1,0:T(8,128)S(1)}, u32[]{:S(2)}, u32[]{:S(2)}) collective-permute-start(f32[32,257]{1,0:T(8,128)S(1)} %get-tuple-element.89), channel_id=1, source_target_pairs={{0,8},{2,10},{4,12},{6,14},{8,16},{10,18},{12,20},{14,22},{16,24},... | collective-permute-start | bytes 98696 | tf_op jit(solution)/shard_map/ppermute | solution.py:13
  162.3 1.9 %collective-permute-start.9 = (f32[32,257]{1,0:T(8,128)S(1)}, f32[32,257]{1,0:T(8,128)S(1)}, u32[]{:S(2)}, u32[]{:S(2)}) collective-permute-start(f32[32,257]{1,0:T(8,128)S(1)} %get-tuple-element.88), channel_id=1, source_target_pairs={{0,2},{2,4},{4,6},{6,8},{8,10},{10,12},{12,14},{14,16},{16,18},{18... | collective-permute-start | bytes 98696 | tf_op jit(solution)/shard_map/ppermute | solution.py:13
  166.4 2.5 %collective-permute-done.12 = f32[32,257]{1,0:T(8,128)S(1)} collective-permute-done((f32[32,257]{1,0:T(8,128)S(1)}, f32[32,257]{1,0:T(8,128)S(1)}, u32[]{:S(2)}, u32[]{:S(2)}) %collective-permute-start.12) | collective-permute-done | bytes 32928 | tf_op jit(solution)/shard_map/ppermute | solution.py:13
  (121 shorter events, 36.8 us)
Async XLA Ops:
  0.6 4.6 %copy-start = (bf16[32,8,2048]{2,1,0:T(8,128)(2,1)S(1)}, bf16[32,8,2048]{2,1,0:T(8,128)(2,1)}, u32[]{:S(2)}) copy-start(bf16[32,8,2048]{2,1,0:T(8,128)(2,1)} %param.7) | copy-start | bytes 3145732
  5.3 2.6 %copy-start.13 = (s32[32]{0:T(128)S(1)}, s32[32]{0:T(128)}, u32[]{:S(2)}) copy-start(s32[32]{0:T(128)} %param.9) | copy-start | bytes 388
  8.2 2.6 %copy-start.12 = (s32[4,32]{1,0:T(4,128)S(1)}, s32[4,32]{1,0:T(4,128)}, u32[]{:S(2)}) copy-start(s32[4,32]{1,0:T(4,128)} %param.8) | copy-start | bytes 1540
  12.4 17.2 %collective-permute-start.1 = (bf16[32,4,2048]{2,1,0:T(4,128)(2,1)}, bf16[32,4,2048]{2,1,0:T(4,128)(2,1)}, u32[]{:S(2)}, u32[]{:S(2)}) collective-permute-start(bf16[32,4,2048]{2,1,0:T(4,128)(2,1)} %scatter.4), channel_id=1, source_target_pairs={{0,510},{2,0},{4,2},{6,4},{8,6},{10,8},{12,10},{14,12},{16,14},{18... | collective-permute-start | bytes 1572872 | tf_op jit(solution)/shard_map/ppermute | solution.py:13
  21.2 12.1 %collective-permute-start = (bf16[32,4,2048]{2,1,0:T(4,128)(2,1)}, bf16[32,4,2048]{2,1,0:T(4,128)(2,1)}, u32[]{:S(2)}, u32[]{:S(2)}) collective-permute-start(bf16[32,4,2048]{2,1,0:T(4,128)(2,1)} %get-tuple-element.71), channel_id=1, source_target_pairs={{0,2},{2,4},{4,6},{6,8},{8,10},{10,12},{12,14},{14,16},{16,18},{18... | collective-permute-start | bytes 1572872 | tf_op jit(solution)/shard_map/ppermute | solution.py:13
  33.3 23.7 %collective-permute-start.3 = (bf16[32,4,2048]{2,1,0:T(4,128)(2,1)}, bf16[32,4,2048]{2,1,0:T(4,128)(2,1)S(1)}, u32[]{:S(2)}, u32[]{:S(2)}) collective-permute-start(bf16[32,4,2048]{2,1,0:T(4,128)(2,1)} %collective-permute-done.1), channel_id=1, source_target_pairs={{0,510},{2,0},{4,2},{6,4},{8,6},{10,8},{12,10},{14,12},{16,14},{18... | collective-permute-start | bytes 1572872 | tf_op jit(solution)/shard_map/ppermute | solution.py:13
  49.6 8.3 %collective-permute-start.2 = (bf16[32,4,2048]{2,1,0:T(4,128)(2,1)}, bf16[32,4,2048]{2,1,0:T(4,128)(2,1)}, u32[]{:S(2)}, u32[]{:S(2)}) collective-permute-start(bf16[32,4,2048]{2,1,0:T(4,128)(2,1)} %collective-permute-done), channel_id=1, source_target_pairs={{0,2},{2,4},{4,6},{6,8},{8,10},{10,12},{12,14},{14,16},{16,18},{18... | collective-permute-start | bytes 1572872 | tf_op jit(solution)/shard_map/ppermute | solution.py:13
  57.9 18.4 %collective-permute-start.5 = (bf16[32,4,2048]{2,1,0:T(4,128)(2,1)S(1)}, bf16[32,4,2048]{2,1,0:T(4,128)(2,1)S(1)}, u32[]{:S(2)}, u32[]{:S(2)}) collective-permute-start(bf16[32,4,2048]{2,1,0:T(4,128)(2,1)S(1)} %collective-permute-done.3), channel_id=1, source_target_pairs={{0,510},{2,0},{4,2},{6,4},{8,6},{10,8},{12,10},{14,12},{16,14},{18... | collective-permute-start | bytes 1572872 | tf_op jit(solution)/shard_map/ppermute | solution.py:13
  68.7 8.3 %collective-permute-start.4 = (bf16[32,4,2048]{2,1,0:T(4,128)(2,1)}, bf16[32,4,2048]{2,1,0:T(4,128)(2,1)}, u32[]{:S(2)}, u32[]{:S(2)}) collective-permute-start(bf16[32,4,2048]{2,1,0:T(4,128)(2,1)} %collective-permute-done.2), channel_id=1, source_target_pairs={{0,2},{2,4},{4,6},{6,8},{8,10},{10,12},{12,14},{14,16},{16,18},{18... | collective-permute-start | bytes 1572872 | tf_op jit(solution)/shard_map/ppermute | solution.py:13
  77.1 19.2 %collective-permute-start.7 = (bf16[32,4,2048]{2,1,0:T(4,128)(2,1)S(1)}, bf16[32,4,2048]{2,1,0:T(4,128)(2,1)}, u32[]{:S(2)}, u32[]{:S(2)}) collective-permute-start(bf16[32,4,2048]{2,1,0:T(4,128)(2,1)S(1)} %collective-permute-done.5), channel_id=1, source_target_pairs={{0,510},{2,0},{4,2},{6,4},{8,6},{10,8},{12,10},{14,12},{16,14},{18... | collective-permute-start | bytes 1572872 | tf_op jit(solution)/shard_map/ppermute | solution.py:13
  87.9 8.3 %collective-permute-start.6 = (bf16[32,4,2048]{2,1,0:T(4,128)(2,1)}, bf16[32,4,2048]{2,1,0:T(4,128)(2,1)}, u32[]{:S(2)}, u32[]{:S(2)}) collective-permute-start(bf16[32,4,2048]{2,1,0:T(4,128)(2,1)} %collective-permute-done.4), channel_id=1, source_target_pairs={{0,2},{2,4},{4,6},{6,8},{8,10},{10,12},{12,14},{14,16},{16,18},{18... | collective-permute-start | bytes 1572872 | tf_op jit(solution)/shard_map/ppermute | solution.py:13
  101.3 3.3 %copy-start.3 = (f32[32,4,2048]{2,1,0:T(4,128)S(1)}, f32[32,4,2048]{2,1,0:T(4,128)}, u32[]{:S(2)}) copy-start(f32[32,4,2048]{2,1,0:T(4,128)} %get-tuple-element.69) | copy-start | bytes 3145732
  104.3 1.2 copy-start.7
  110.4 1.2 copy-start.4
  110.4 1.5 copy-start.11
  110.4 2.5 %copy-start.5 = (f32[32,4,2048]{2,1,0:T(4,128)S(1)}, f32[32,4,2048]{2,1,0:T(4,128)}, u32[]{:S(2)}) copy-start(f32[32,4,2048]{2,1,0:T(4,128)} %select_convert_fusion.2) | copy-start | bytes 3145732
  110.4 2.5 %copy-start.10 = (f32[32,4,2048]{2,1,0:T(4,128)S(1)}, f32[32,4,2048]{2,1,0:T(4,128)}, u32[]{:S(2)}) copy-start(f32[32,4,2048]{2,1,0:T(4,128)} %get-tuple-element.103) | copy-start | bytes 3145732
  112.9 1.2 copy-start.6
  112.9 1.5 copy-start.9
  114.4 1.3 copy-start.8
  116.9 1.2 copy-start.1
  116.9 1.6 copy-start.2
  122.1 8.5 %collective-permute-start.8 = (f32[2,32,4,257]{3,1,2,0:T(8,128)S(1)}, f32[2,32,4,257]{3,1,2,0:T(8,128)S(1)}, u32[]{:S(2)}, u32[]{:S(2)}) collective-permute-start(f32[2,32,4,257]{3,1,2,0:T(8,128)S(1)} %fusion.4), channel_id=1, source_target_pairs={{0,1},{1,0},{2,3},{3,2},{4,5},{5,4},{6,7},{7,6},{8,9},{9,8},{10,11... | collective-permute-start | bytes 789512 | tf_op jit(solution)/shard_map/ppermute | solution.py:18
  130.7 21.0 %collective-permute-start.13 = (f32[32,257]{1,0:T(8,128)S(1)}, f32[32,257]{1,0:T(8,128)S(1)}, u32[]{:S(2)}, u32[]{:S(2)}) collective-permute-start(f32[32,257]{1,0:T(8,128)S(1)} %get-tuple-element.80), channel_id=1, source_target_pairs={{0,510},{2,0},{4,2},{6,4},{8,6},{10,8},{12,10},{14,12},{16,14},{18... | collective-permute-start | bytes 98696 | tf_op jit(solution)/shard_map/ppermute | solution.py:13
  142.5 14.2 %collective-permute-start.14 = (f32[32,257]{1,0:T(8,128)S(1)}, f32[32,257]{1,0:T(8,128)S(1)}, u32[]{:S(2)}, u32[]{:S(2)}) collective-permute-start(f32[32,257]{1,0:T(8,128)S(1)} %get-tuple-element.83), channel_id=1, source_target_pairs={{0,508},{2,510},{4,0},{6,2},{8,4},{10,6},{12,8},{14,10},{16,12},{1... | collective-permute-start | bytes 98696 | tf_op jit(solution)/shard_map/ppermute | solution.py:13
  144.4 17.9 %collective-permute-start.15 = (f32[32,257]{1,0:T(8,128)S(1)}, f32[32,257]{1,0:T(8,128)S(1)}, u32[]{:S(2)}, u32[]{:S(2)}) collective-permute-start(f32[32,257]{1,0:T(8,128)S(1)} %get-tuple-element.82), channel_id=1, source_target_pairs={{0,506},{2,508},{4,510},{6,0},{8,2},{10,4},{12,6},{14,8},{16,10},{... | collective-permute-start | bytes 98696 | tf_op jit(solution)/shard_map/ppermute | solution.py:13
  146.4 17.9 %collective-permute-start.16 = (f32[32,257]{1,0:T(8,128)S(1)}, f32[32,257]{1,0:T(8,128)S(1)}, u32[]{:S(2)}, u32[]{:S(2)}) collective-permute-start(f32[32,257]{1,0:T(8,128)S(1)} %get-tuple-element.81), channel_id=1, source_target_pairs={{0,504},{2,506},{4,508},{6,510},{8,0},{10,2},{12,4},{14,6},{16,8},... | collective-permute-start | bytes 98696 | tf_op jit(solution)/shard_map/ppermute | solution.py:13
  148.3 18.1 %collective-permute-start.10 = (f32[32,257]{1,0:T(8,128)S(1)}, f32[32,257]{1,0:T(8,128)S(1)}, u32[]{:S(2)}, u32[]{:S(2)}) collective-permute-start(f32[32,257]{1,0:T(8,128)S(1)} %get-tuple-element.91), channel_id=1, source_target_pairs={{0,4},{2,6},{4,8},{6,10},{8,12},{10,14},{12,16},{14,18},{16,20},{1... | collective-permute-start | bytes 98696 | tf_op jit(solution)/shard_map/ppermute | solution.py:13
  151.7 14.7 %collective-permute-start.11 = (f32[32,257]{1,0:T(8,128)S(1)}, f32[32,257]{1,0:T(8,128)S(1)}, u32[]{:S(2)}, u32[]{:S(2)}) collective-permute-start(f32[32,257]{1,0:T(8,128)S(1)} %get-tuple-element.90), channel_id=1, source_target_pairs={{0,6},{2,8},{4,10},{6,12},{8,14},{10,16},{12,18},{14,20},{16,22},{... | collective-permute-start | bytes 98696 | tf_op jit(solution)/shard_map/ppermute | solution.py:13
  156.7 12.2 %collective-permute-start.12 = (f32[32,257]{1,0:T(8,128)S(1)}, f32[32,257]{1,0:T(8,128)S(1)}, u32[]{:S(2)}, u32[]{:S(2)}) collective-permute-start(f32[32,257]{1,0:T(8,128)S(1)} %get-tuple-element.89), channel_id=1, source_target_pairs={{0,8},{2,10},{4,12},{6,14},{8,16},{10,18},{12,20},{14,22},{16,24},... | collective-permute-start | bytes 98696 | tf_op jit(solution)/shard_map/ppermute | solution.py:13
  162.3 6.7 %collective-permute-start.9 = (f32[32,257]{1,0:T(8,128)S(1)}, f32[32,257]{1,0:T(8,128)S(1)}, u32[]{:S(2)}, u32[]{:S(2)}) collective-permute-start(f32[32,257]{1,0:T(8,128)S(1)} %get-tuple-element.88), channel_id=1, source_target_pairs={{0,2},{2,4},{4,6},{6,8},{8,10},{10,12},{12,14},{14,16},{16,18},{18... | collective-permute-start | bytes 98696 | tf_op jit(solution)/shard_map/ppermute | solution.py:13

commit v3 on v2

--- a/solution.py
+++ b/solution.py
@@ -88,37 +88,42 @@
     dc_imag = lax.broadcasted_iota(jnp.int32, behind.shape, 2) == half_len
     moving_ahead = ahead
     moving_behind = behind.at[:, :stops, half_len].set(offsets.T.astype(jnp.bfloat16))
-    own_pieces = []
-    later_pieces = []
+    back_table = inverse_table(length, LAGS)
+    own_parts, later_parts, from_earlier, from_later = [], [], [], []
+    lags = jnp.zeros((2 * channels, back_table.shape[1]), jnp.float32)
     for stop in range(1, stops + 1):
-        moving_ahead, moving_behind = lax.optimization_barrier(
-            (shifted(moving_ahead, "blk", 1), shifted(moving_behind, "blk", -1))
+        moving_ahead, moving_behind, lags = lax.optimization_barrier(
+            (shifted(moving_ahead, "blk", 1), shifted(moving_behind, "blk", -1), lags)
         )
+        if stop > 1:
+            own_parts.append(lags[:channels])
+            later_parts.append(lags[channels:])
+            from_earlier.append(shifted(lags[channels:], "blk", stop - 1))
+            from_later.append(shifted(lags[:channels], "blk", 1 - stop))
         partner = jnp.take(moving_ahead, offsets[stop - 1], axis=0)
-        own_pieces.append(cross_spectrum(ahead, partner, half_len))
+        own = cross_spectrum(ahead, partner, half_len)
         later_offsets = moving_behind[:, stop - 1, half_len].astype(jnp.int32)
         local_partner = jnp.take(behind, later_offsets, axis=0)
         later = jnp.where(dc_imag, jnp.zeros_like(moving_behind), moving_behind)
-        later_pieces.append(cross_spectrum(later, local_partner, half_len))
-    back_table = inverse_table(length, LAGS)
-    pieces = jnp.stack([jnp.stack(own_pieces, axis=1), jnp.stack(later_pieces, axis=1)], axis=0)
-    partial = jnp.dot(
-        pieces.reshape(2 * channels * stops, length),
-        back_table,
-        precision=lax.Precision.HIGHEST,
-        preferred_element_type=jnp.float32,
-    ).reshape(2, channels, stops, -1)
-    summed = partial + swapped(partial, "rep")
-    own_part, later_part = summed[0], summed[1]
+        later = cross_spectrum(later, local_partner, half_len)
+        lags = jnp.dot(
+            jnp.concatenate([own, later], axis=0),
+            back_table,
+            precision=lax.Precision.HIGHEST,
+            preferred_element_type=jnp.float32,
+        )
+    own_parts.append(lags[:channels])
+    later_parts.append(lags[channels:])
+    from_earlier.append(shifted(lags[channels:], "blk", stops))
+    from_later.append(shifted(lags[:channels], "blk", -stops))
+    corr_part = jnp.stack(own_parts, axis=1) + jnp.stack(from_earlier, axis=1)
+    mirror_part = jnp.stack(from_later, axis=1) + jnp.stack(later_parts, axis=1)
+    parts = jnp.stack([corr_part, mirror_part], axis=0)
+    summed = parts + swapped(parts, "rep")
     scale = 1.0 / math.sqrt(segments * lax.axis_size("rep") * half_len)
-    correlations = []
-    mirrored = []
-    for stop in range(1, stops + 1):
-        from_earlier = shifted(later_part[:, stop - 1], "blk", stop)
-        from_later = shifted(own_part[:, stop - 1], "blk", -stop)
-        correlations.append((own_part[:, stop - 1] + from_earlier) * scale)
-        mirrored.append(((from_later + later_part[:, stop - 1]) * scale)[:, ::-1])
-    return (jnp.stack(correlations, axis=1), jnp.stack(mirrored, axis=1))
+    correlations = summed[0] * scale
+    mirrored = (summed[1] * scale)[:, :, ::-1]
+    return (correlations, mirrored)
 
 
 def solution(mesh):

time: 172 us -> 187 us (1.087)
  other arithmetic: 34.5 us -> 48.1 us
  starting transfers between devices: 87.3 us -> 82.7 us
  matrix products: 6.07 us -> 10.3 us
  waiting for transfers between devices: 14.8 us -> 18.3 us
    convert_element_type x2 -> x5, other arithmetic: 5.34 us -> 10.6 us  [cross_spectrum(): first = local.astype(jnp.float32)]
    unnamed x35 -> x40, local copies, waits for them, and re-layouts: 7.58 us -> 2.79 us
    ppermute x16, starting transfers between devices: 85 us -> 80.5 us  [shifted(): lax.ppermute(x, axis, [(i, (i + by) % length) for i in range(length)])]
    dot_general x1 -> x4, matrix products: 3.57 us -> 7.77 us  [on_device(): jnp.dot(jnp.concatenate([own, later], axis=0), back_table, precision=lax....]
    ppermute x1, waiting for transfers between devices: 6.29 us -> 9.96 us  [swapped(): return lax.ppermute(x, axis, [(i, i ^ 1) for i in range(length)])]
    gather x4, local copies, waits for them, and re-layouts: 3.96 us -> 7.19 us  [on_device(): local_partner = jnp.take(behind, later_offsets, axis=0)]
    gather x4, local copies, waits for them, and re-layouts: 8.15 us -> 11.3 us  [on_device(): partner = jnp.take(moving_ahead, offsets[stop - 1], axis=0)]
    convert_element_type x8, other arithmetic: 8.23 us -> 11.1 us  [cross_spectrum(): second = partner.astype(jnp.float32)]
  transfers between devices with their start and end apart: 17 -> 17, of which waited for: 6 -> 3; matrix products, arithmetic and copies ran while one was open for 17% -> 34% of each run, Pallas kernels for 0% -> 0%
where the time goes in v3:
time: 187 us; the launch traced here: 185 us
  starting transfers between devices  82.7 us (44%)
  other arithmetic  48.1 us (26%)
  local copies, waits for them, and re-layouts  24.4 us (13%)
  waiting for transfers between devices  18.3 us (10%)
  matrix products  10.3 us (6%)
    ppermute x16, starting transfers between devices, shifted(): lax.ppermute(x, axis, [(i, (i + by) % length) for i in range(length)])  80.5 us
    gather x4, local copies, waits for them, and re-layouts, on_device(): partner = jnp.take(moving_ahead, offsets[stop - 1], axis=0)  11.3 us
    convert_element_type x8, other arithmetic, cross_spectrum(): second = partner.astype(jnp.float32)  11.1 us
    convert_element_type x5, other arithmetic, cross_spectrum(): first = local.astype(jnp.float32)  10.6 us
    reduce_sum x8, other arithmetic, cross_spectrum(): real_sum = jnp.sum(real_a * real_b + imag_a * imag_b, axis=1)  10.2 us
    ppermute x1, waiting for transfers between devices, swapped(): return lax.ppermute(x, axis, [(i, i ^ 1) for i in range(length)])  9.96 us
    ppermute x16, waiting for transfers between devices, shifted(): lax.ppermute(x, axis, [(i, (i + by) % length) for i in range(length)])  8.33 us
    dot_general x4, matrix products, on_device(): jnp.dot(jnp.concatenate([own, later], axis=0), back_table, precision=lax....  7.77 us
  transfers between devices with their start and end apart: 17, of which 3 were waited for; matrix products, arithmetic and copies ran while one was open for 34% of the time, Pallas kernels for 0%

profile of v3, /device:TPU:1, one launch (start us, length us, event | category | flops | bytes accessed | tf_op | source)
XLA Modules:
  0.0 185.1 jit_solution(15282251546074255791)
XLA Ops:
  2.3 3.0 %subtract_convert_fusion = (bf16[32,64,1024]{2,1,0:T(8,128)(2,1)S(1)}, bf16[32,64,1024]{2,1,0:T(8,128)(2,1)S(1)}) fusion(f32[64,1024]{1,0:T(8,128)S(1)} %get-tuple-element.106, f32[32,1024]{1,0:T(8,128)S(1)} %get-tuple-element.103, f32[64,1024]{1,0:T(8,128)S(1)} %get-tuple-element.107, f32[32,1024]{1,0:T(8,128)S(1)} %get-tuple-element.102), kind=kLoop, calls=%fused_computation.13 | loop fusion | flops 18874368 | bytes 9175040 | tf_op jit(solution)/shard_map/convert.7
  5.3 2.5 %fusion.6 = (f32[256]{0:T(256)S(1)}, f32[2048,256]{0,1:T(8,128)S(1)}) fusion(bf16[2048,1024]{1,0:T(8,128)(2,1)S(1)} %bitcast.74, bf16[2048,1024]{1,0:T(8,128)(2,1)S(1)} %bitcast.73, bf16[32,8,2048]{2,1,0:T(8,128)(2,1)S(1)} %copy-done), kind=kOutput, calls=%fused_computation.19 | convolution fusion | flops 2165309184 | bytes 11535360 | tf_op jit(solution)/shard_map/dot_general | solution.py:78
  12.4 8.8 %collective-permute-start.1 = (bf16[32,4,2048]{2,1,0:T(4,128)(2,1)}, bf16[32,4,2048]{2,1,0:T(4,128)(2,1)}, u32[]{:S(2)}, u32[]{:S(2)}) collective-permute-start(bf16[32,4,2048]{2,1,0:T(4,128)(2,1)} %scatter.4), channel_id=1, source_target_pairs={{0,510},{2,0},{4,2},{6,4},{8,6},{10,8},{12,10},{14,12},{16,14},{18... | collective-permute-start | bytes 1572872 | tf_op jit(solution)/shard_map/ppermute | solution.py:13
  21.2 1.9 %collective-permute-start = (bf16[32,4,2048]{2,1,0:T(4,128)(2,1)}, bf16[32,4,2048]{2,1,0:T(4,128)(2,1)}, u32[]{:S(2)}, u32[]{:S(2)}) collective-permute-start(bf16[32,4,2048]{2,1,0:T(4,128)(2,1)} %get-tuple-element.69), channel_id=1, source_target_pairs={{0,2},{2,4},{4,6},{6,8},{8,10},{10,12},{12,14},{14,16},{16,18},{18... | collective-permute-start | bytes 1572872 | tf_op jit(solution)/shard_map/ppermute | solution.py:13
  25.3 8.1 %collective-permute-done = bf16[32,4,2048]{2,1,0:T(4,128)(2,1)} collective-permute-done((bf16[32,4,2048]{2,1,0:T(4,128)(2,1)}, bf16[32,4,2048]{2,1,0:T(4,128)(2,1)}, u32[]{:S(2)}, u32[]{:S(2)}) %collective-permute-start) | collective-permute-done | bytes 524320 | tf_op jit(solution)/shard_map/ppermute | solution.py:13
  34.8 14.8 %collective-permute-start.3 = (bf16[32,4,2048]{2,1,0:T(4,128)(2,1)}, bf16[32,4,2048]{2,1,0:T(4,128)(2,1)}, u32[]{:S(2)}, u32[]{:S(2)}) collective-permute-start(bf16[32,4,2048]{2,1,0:T(4,128)(2,1)} %collective-permute-done.1), channel_id=1, source_target_pairs={{0,510},{2,0},{4,2},{6,4},{8,6},{10,8},{12,10},{14,12},{16,14},{18... | collective-permute-start | bytes 1572872 | tf_op jit(solution)/shard_map/ppermute | solution.py:13
  51.4 2.2 %select_convert_fusion.11 = f32[32,4,2048]{2,1,0:T(4,128)} fusion(bf16[32,4,2048]{2,1,0:T(4,128)(2,1)} %collective-permute-done.1, pred[2048]{0:T(1024)(128)(4,1)S(1)} %iota_compare_fusion), kind=kLoop, calls=%fused_computation.80 | loop fusion | flops 524288 | bytes 1574912 | tf_op jit(solution)/shard_map/convert_element_type | solution.py:65
  53.6 2.1 %collective-permute-start.2 = (bf16[32,4,2048]{2,1,0:T(4,128)(2,1)}, bf16[32,4,2048]{2,1,0:T(4,128)(2,1)}, u32[]{:S(2)}, u32[]{:S(2)}) collective-permute-start(bf16[32,4,2048]{2,1,0:T(4,128)(2,1)} %collective-permute-done), channel_id=1, source_target_pairs={{0,2},{2,4},{4,6},{6,8},{8,10},{10,12},{12,14},{14,16},{16,18},{18... | collective-permute-start | bytes 1572872 | tf_op jit(solution)/shard_map/ppermute | solution.py:13
  55.7 2.8 %gather_fusion = bf16[32,4,2048]{2,1,0:T(4,128)(2,1)} fusion(bf16[32,4,2048]{2,1,0:T(4,128)(2,1)} %collective-permute-done, s32[1024]{0:T(1024)S(1)} %get-tuple-element.111), kind=kCustom, calls=%fused_computation.clone | custom fusion | bytes 1048704 | tf_op jit(solution)/shard_map/jit(_take)/gather | solution.py:103
  63.4 1.9 %fusion.10 = f32[64,257]{1,0:T(8,128)S(1)} fusion(f32[1024,257]{1,0:T(8,128)S(1)} %bitcast.69, f32[1024,257]{1,0:T(8,128)S(1)} %bitcast.65, f32[32,1024]{1,0:T(8,128)S(1)} %get-tuple-element.58, f32[32,1024]{1,0:T(8,128)S(1)} %get-tuple-element.57, f32[32,1024]{1,0:T(8,128)S(1)} %get-tuple-element.56, f32[32,1024]{1,0:T(8,128)S(1)} %get-tuple-element.55), kind=kOutput, calls=%fused_computation.25 | convolution fusion | flops 405145600 | bytes 2695424 | tf_op jit(solution)/shard_map/dot_general | solution.py:109
  66.8 2.2 %select_convert_fusion.10 = f32[32,4,2048]{2,1,0:T(4,128)} fusion(bf16[32,4,2048]{2,1,0:T(4,128)(2,1)} %collective-permute-done.3, pred[2048]{0:T(1024)(128)(4,1)S(1)} %iota_compare_fusion), kind=kLoop, calls=%fused_computation.75 | loop fusion | flops 524288 | bytes 1574912 | tf_op jit(solution)/shard_map/convert_element_type | solution.py:65
  69.0 6.7 %collective-permute-start.5 = (bf16[32,4,2048]{2,1,0:T(4,128)(2,1)}, bf16[32,4,2048]{2,1,0:T(4,128)(2,1)}, u32[]{:S(2)}, u32[]{:S(2)}) collective-permute-start(bf16[32,4,2048]{2,1,0:T(4,128)(2,1)} %collective-permute-done.3), channel_id=1, source_target_pairs={{0,510},{2,0},{4,2},{6,4},{8,6},{10,8},{12,10},{14,12},{16,14},{18... | collective-permute-start | bytes 1572872 | tf_op jit(solution)/shard_map/ppermute | solution.py:13
  75.7 1.9 %collective-permute-start.4 = (bf16[32,4,2048]{2,1,0:T(4,128)(2,1)}, bf16[32,4,2048]{2,1,0:T(4,128)(2,1)}, u32[]{:S(2)}, u32[]{:S(2)}) collective-permute-start(bf16[32,4,2048]{2,1,0:T(4,128)(2,1)} %collective-permute-done.2), channel_id=1, source_target_pairs={{0,2},{2,4},{4,6},{6,8},{8,10},{10,12},{12,14},{14,16},{16,18},{18... | collective-permute-start | bytes 1572872 | tf_op jit(solution)/shard_map/ppermute | solution.py:13
  77.6 2.8 %gather_fusion.2 = bf16[32,4,2048]{2,1,0:T(4,128)(2,1)} fusion(bf16[32,4,2048]{2,1,0:T(4,128)(2,1)} %collective-permute-done.2, s32[1024]{0:T(1024)S(1)} %get-tuple-element.110), kind=kCustom, calls=%fused_computation.2.clone | custom fusion | bytes 1048704 | tf_op jit(solution)/shard_map/jit(_take)/gather | solution.py:103
  89.6 1.9 %fusion.9 = f32[64,257]{1,0:T(8,128)S(1)} fusion(f32[1024,257]{1,0:T(8,128)S(1)} %bitcast.70, f32[1024,257]{1,0:T(8,128)S(1)} %bitcast.66, f32[32,1024]{1,0:T(8,128)S(1)} %get-tuple-element.54, f32[32,1024]{1,0:T(8,128)S(1)} %get-tuple-element.53, f32[32,1024]{1,0:T(8,128)S(1)} %get-tuple-element.52, f32[32,1024]{1,0:T(8,128)S(1)} %get-tuple-element.51), kind=kOutput, calls=%fused_computation.24 | convolution fusion | flops 405145600 | bytes 2695424 | tf_op jit(solution)/shard_map/dot_general | solution.py:109
  93.0 2.2 %select_convert_fusion.9 = f32[32,4,2048]{2,1,0:T(4,128)} fusion(bf16[32,4,2048]{2,1,0:T(4,128)(2,1)} %collective-permute-done.5, pred[2048]{0:T(1024)(128)(4,1)S(1)} %iota_compare_fusion), kind=kLoop, calls=%fused_computation.70 | loop fusion | flops 524288 | bytes 1574912 | tf_op jit(solution)/shard_map/convert_element_type | solution.py:65
  95.2 5.3 %collective-permute-start.7 = (bf16[32,4,2048]{2,1,0:T(4,128)(2,1)}, bf16[32,4,2048]{2,1,0:T(4,128)(2,1)}, u32[]{:S(2)}, u32[]{:S(2)}) collective-permute-start(bf16[32,4,2048]{2,1,0:T(4,128)(2,1)} %collective-permute-done.5), channel_id=1, source_target_pairs={{0,510},{2,0},{4,2},{6,4},{8,6},{10,8},{12,10},{14,12},{16,14},{18... | collective-permute-start | bytes 1572872 | tf_op jit(solution)/shard_map/ppermute | solution.py:13
  100.5 1.9 %collective-permute-start.6 = (bf16[32,4,2048]{2,1,0:T(4,128)(2,1)}, bf16[32,4,2048]{2,1,0:T(4,128)(2,1)}, u32[]{:S(2)}, u32[]{:S(2)}) collective-permute-start(bf16[32,4,2048]{2,1,0:T(4,128)(2,1)} %collective-permute-done.4), channel_id=1, source_target_pairs={{0,2},{2,4},{4,6},{6,8},{8,10},{10,12},{12,14},{14,16},{16,18},{18... | collective-permute-start | bytes 1572872 | tf_op jit(solution)/shard_map/ppermute | solution.py:13
  102.4 2.8 %gather_fusion.4 = bf16[32,4,2048]{2,1,0:T(4,128)(2,1)} fusion(bf16[32,4,2048]{2,1,0:T(4,128)(2,1)} %collective-permute-done.4, s32[1024]{0:T(1024)S(1)} %get-tuple-element.109), kind=kCustom, calls=%fused_computation.4.clone | custom fusion | bytes 1048704 | tf_op jit(solution)/shard_map/jit(_take)/gather | solution.py:103
  107.7 2.3 %collective-permute-start.9 = (f32[32,257]{1,0:T(8,128)}, f32[32,257]{1,0:T(8,128)}, u32[]{:S(2)}, u32[]{:S(2)}) collective-permute-start(f32[32,257]{1,0:T(8,128)} %get-tuple-element.80), channel_id=1, source_target_pairs={{0,4},{2,6},{4,8},{6,10},{8,12},{10,14},{12,16},{14,18},{16,20},{1... | collective-permute-start | bytes 98696 | tf_op jit(solution)/shard_map/ppermute | solution.py:13
  114.7 1.9 %fusion.8 = f32[64,257]{1,0:T(8,128)S(1)} fusion(f32[1024,257]{1,0:T(8,128)S(1)} %bitcast.71, f32[1024,257]{1,0:T(8,128)S(1)} %bitcast.67, f32[32,1024]{1,0:T(8,128)S(1)} %get-tuple-element.50, f32[32,1024]{1,0:T(8,128)S(1)} %get-tuple-element.49, f32[32,1024]{1,0:T(8,128)S(1)} %get-tuple-element.48, f32[32,1024]{1,0:T(8,128)S(1)} %get-tuple-element.47), kind=kOutput, calls=%fused_computation.23 | convolution fusion | flops 405145600 | bytes 2695424 | tf_op jit(solution)/shard_map/dot_general | solution.py:109
  119.2 2.2 %select_convert_fusion.8 = f32[32,4,2048]{2,1,0:T(4,128)} fusion(bf16[32,4,2048]{2,1,0:T(4,128)(2,1)} %collective-permute-done.7, pred[2048]{0:T(1024)(128)(4,1)S(1)} %iota_compare_fusion), kind=kLoop, calls=%fused_computation.65 | loop fusion | flops 524288 | bytes 1574912 | tf_op jit(solution)/shard_map/convert_element_type | solution.py:65
  121.4 2.8 %gather_fusion.6 = bf16[32,4,2048]{2,1,0:T(4,128)(2,1)} fusion(bf16[32,4,2048]{2,1,0:T(4,128)(2,1)} %collective-permute-done.6, s32[1024]{0:T(1024)S(1)} %get-tuple-element.108), kind=kCustom, calls=%fused_computation.6.clone | custom fusion | bytes 1048704 | tf_op jit(solution)/shard_map/jit(_take)/gather | solution.py:103
  125.5 2.2 %add_reduce_fusion.1 = (f32[32,1024]{1,0:T(8,128)S(1)}, f32[32,1024]{1,0:T(8,128)S(1)}) fusion(f32[32,4,2048]{2,1,0:T(4,128)S(1)} %select_convert_fusion.1, f32[32,4,2048]{2,1,0:T(4,128)} %get-tuple-element.67), kind=kLoop, calls=%fused_computation.67 | loop fusion | flops 983040 | bytes 2359296 | tf_op jit(solution)/shard_map/reduce_sum | solution.py:69
  132.3 2.2 %add_reduce_fusion = (f32[32,1024]{1,0:T(8,128)S(1)}, f32[32,1024]{1,0:T(8,128)S(1)}) fusion(f32[32,4,2048]{2,1,0:T(4,128)S(1)} %select_convert_fusion, f32[32,4,2048]{2,1,0:T(4,128)} %select_convert_fusion.8), kind=kLoop, calls=%fused_computation.64 | loop fusion | flops 983040 | bytes 2359296 | tf_op jit(solution)/shard_map/reduce_sum | solution.py:69
  134.6 1.9 %fusion.7 = f32[64,257]{1,0:T(8,128)S(1)} fusion(f32[1024,257]{1,0:T(8,128)S(1)} %bitcast.72, f32[1024,257]{1,0:T(8,128)S(1)} %bitcast.68, f32[32,1024]{1,0:T(8,128)S(1)} %get-tuple-element.46, f32[32,1024]{1,0:T(8,128)S(1)} %get-tuple-element.45, f32[32,1024]{1,0:T(8,128)S(1)} %get-tuple-element.44, f32[32,1024]{1,0:T(8,128)S(1)} %get-tuple-element.43), kind=kOutput, calls=%fused_computation.22 | convolution fusion | flops 405145600 | bytes 2695424 | tf_op jit(solution)/shard_map/dot_general | solution.py:109
  140.5 9.0 %collective-permute-start.12 = (f32[32,257]{1,0:T(8,128)S(1)}, f32[32,257]{1,0:T(8,128)S(1)}, u32[]{:S(2)}, u32[]{:S(2)}) collective-permute-start(f32[32,257]{1,0:T(8,128)S(1)} %copy-done.14), channel_id=1, source_target_pairs={{0,510},{2,0},{4,2},{6,4},{8,6},{10,8},{12,10},{14,12},{16,14},{18... | collective-permute-start | bytes 98696 | tf_op jit(solution)/shard_map/ppermute | solution.py:13
  149.5 9.0 %collective-permute-start.13 = (f32[32,257]{1,0:T(8,128)S(1)}, f32[32,257]{1,0:T(8,128)S(1)}, u32[]{:S(2)}, u32[]{:S(2)}) collective-permute-start(f32[32,257]{1,0:T(8,128)S(1)} %copy-done.15), channel_id=1, source_target_pairs={{0,508},{2,510},{4,0},{6,2},{8,4},{10,6},{12,8},{14,10},{16,12},{1... | collective-permute-start | bytes 98696 | tf_op jit(solution)/shard_map/ppermute | solution.py:13
  158.5 4.5 %collective-permute-start.15 = (f32[32,257]{1,0:T(8,128)S(1)}, f32[32,257]{1,0:T(8,128)S(1)}, u32[]{:S(2)}, u32[]{:S(2)}) collective-permute-start(f32[32,257]{1,0:T(8,128)S(1)} %get-tuple-element.91), channel_id=1, source_target_pairs={{0,504},{2,506},{4,508},{6,510},{8,0},{10,2},{12,4},{14,6},{16,8},... | collective-permute-start | bytes 98696 | tf_op jit(solution)/shard_map/ppermute | solution.py:13
  163.1 6.5 %collective-permute-start.14 = (f32[32,257]{1,0:T(8,128)S(1)}, f32[32,257]{1,0:T(8,128)S(1)}, u32[]{:S(2)}, u32[]{:S(2)}) collective-permute-start(f32[32,257]{1,0:T(8,128)S(1)} %get-tuple-element.87), channel_id=1, source_target_pairs={{0,506},{2,508},{4,510},{6,0},{8,2},{10,4},{12,6},{14,8},{16,10},{... | collective-permute-start | bytes 98696 | tf_op jit(solution)/shard_map/ppermute | solution.py:13
  170.8 2.2 %collective-permute-start.16 = (f32[2,32,4,257]{3,1,2,0:T(8,128)S(1)}, f32[2,32,4,257]{3,1,2,0:T(8,128)S(1)}, u32[]{:S(2)}, u32[]{:S(2)}) collective-permute-start(f32[2,32,4,257]{3,1,2,0:T(8,128)S(1)} %pad_maximum_fusion.5), channel_id=1, source_target_pairs={{0,1},{1,0},{2,3},{3,2},{4,5},{5,4},{6,7},{7,6},{8,9},{9,8},{10,11... | collective-permute-start | bytes 789512 | tf_op jit(solution)/shard_map/ppermute | solution.py:18
  173.0 10.0 %collective-permute-done.16 = f32[2,32,4,257]{3,1,2,0:T(8,128)S(1)} collective-permute-done((f32[2,32,4,257]{3,1,2,0:T(8,128)S(1)}, f32[2,32,4,257]{3,1,2,0:T(8,128)S(1)}, u32[]{:S(2)}, u32[]{:S(2)}) %collective-permute-start.16) | collective-permute-done | bytes 263200 | tf_op jit(solution)/shard_map/ppermute | solution.py:18
  (121 shorter events, 51.1 us)
Async XLA Ops:
  0.6 4.6 %copy-start = (bf16[32,8,2048]{2,1,0:T(8,128)(2,1)S(1)}, bf16[32,8,2048]{2,1,0:T(8,128)(2,1)}, u32[]{:S(2)}) copy-start(bf16[32,8,2048]{2,1,0:T(8,128)(2,1)} %param.7) | copy-start | bytes 3145732
  12.4 12.8 %collective-permute-start.1 = (bf16[32,4,2048]{2,1,0:T(4,128)(2,1)}, bf16[32,4,2048]{2,1,0:T(4,128)(2,1)}, u32[]{:S(2)}, u32[]{:S(2)}) collective-permute-start(bf16[32,4,2048]{2,1,0:T(4,128)(2,1)} %scatter.4), channel_id=1, source_target_pairs={{0,510},{2,0},{4,2},{6,4},{8,6},{10,8},{12,10},{14,12},{16,14},{18... | collective-permute-start | bytes 1572872 | tf_op jit(solution)/shard_map/ppermute | solution.py:13
  21.2 12.1 %collective-permute-start = (bf16[32,4,2048]{2,1,0:T(4,128)(2,1)}, bf16[32,4,2048]{2,1,0:T(4,128)(2,1)}, u32[]{:S(2)}, u32[]{:S(2)}) collective-permute-start(bf16[32,4,2048]{2,1,0:T(4,128)(2,1)} %get-tuple-element.69), channel_id=1, source_target_pairs={{0,2},{2,4},{4,6},{6,8},{8,10},{10,12},{12,14},{14,16},{16,18},{18... | collective-permute-start | bytes 1572872 | tf_op jit(solution)/shard_map/ppermute | solution.py:13
  34.8 30.6 %collective-permute-start.3 = (bf16[32,4,2048]{2,1,0:T(4,128)(2,1)}, bf16[32,4,2048]{2,1,0:T(4,128)(2,1)}, u32[]{:S(2)}, u32[]{:S(2)}) collective-permute-start(bf16[32,4,2048]{2,1,0:T(4,128)(2,1)} %collective-permute-done.1), channel_id=1, source_target_pairs={{0,510},{2,0},{4,2},{6,4},{8,6},{10,8},{12,10},{14,12},{16,14},{18... | collective-permute-start | bytes 1572872 | tf_op jit(solution)/shard_map/ppermute | solution.py:13
  53.6 11.8 %collective-permute-start.2 = (bf16[32,4,2048]{2,1,0:T(4,128)(2,1)}, bf16[32,4,2048]{2,1,0:T(4,128)(2,1)}, u32[]{:S(2)}, u32[]{:S(2)}) collective-permute-start(bf16[32,4,2048]{2,1,0:T(4,128)(2,1)} %collective-permute-done), channel_id=1, source_target_pairs={{0,2},{2,4},{4,6},{6,8},{8,10},{10,12},{12,14},{14,16},{16,18},{18... | collective-permute-start | bytes 1572872 | tf_op jit(solution)/shard_map/ppermute | solution.py:13
  58.5 3.9 %copy-start.5 = (f32[32,4,2048]{2,1,0:T(4,128)S(1)}, f32[32,4,2048]{2,1,0:T(4,128)}, u32[]{:S(2)}) copy-start(f32[32,4,2048]{2,1,0:T(4,128)} %get-tuple-element.67) | copy-start | bytes 3145732
  59.9 3.4 %copy-start.1 = (f32[32,32,257]{2,1,0:T(8,128)S(1)}, f32[32,32,257]{2,1,0:T(8,128)}, u32[]{:S(2)}) copy-start(f32[32,32,257]{2,1,0:T(8,128)} %get-tuple-element.75) | copy-start | bytes 3158020
  69.0 22.5 %collective-permute-start.5 = (bf16[32,4,2048]{2,1,0:T(4,128)(2,1)}, bf16[32,4,2048]{2,1,0:T(4,128)(2,1)}, u32[]{:S(2)}, u32[]{:S(2)}) collective-permute-start(bf16[32,4,2048]{2,1,0:T(4,128)(2,1)} %collective-permute-done.3), channel_id=1, source_target_pairs={{0,510},{2,0},{4,2},{6,4},{8,6},{10,8},{12,10},{14,12},{16,14},{18... | collective-permute-start | bytes 1572872 | tf_op jit(solution)/shard_map/ppermute | solution.py:13
  75.7 15.8 %collective-permute-start.4 = (bf16[32,4,2048]{2,1,0:T(4,128)(2,1)}, bf16[32,4,2048]{2,1,0:T(4,128)(2,1)}, u32[]{:S(2)}, u32[]{:S(2)}) collective-permute-start(bf16[32,4,2048]{2,1,0:T(4,128)(2,1)} %collective-permute-done.2), channel_id=1, source_target_pairs={{0,2},{2,4},{4,6},{6,8},{8,10},{10,12},{12,14},{14,16},{16,18},{18... | collective-permute-start | bytes 1572872 | tf_op jit(solution)/shard_map/ppermute | solution.py:13
  82.2 5.4 %copy-start.6 = (f32[32,4,2048]{2,1,0:T(4,128)S(1)}, f32[32,4,2048]{2,1,0:T(4,128)}, u32[]{:S(2)}) copy-start(f32[32,4,2048]{2,1,0:T(4,128)} %get-tuple-element.67) | copy-start | bytes 3145732
  82.2 6.4 %copy-start.8 = (f32[32,4,2048]{2,1,0:T(4,128)S(1)}, f32[32,4,2048]{2,1,0:T(4,128)}, u32[]{:S(2)}) copy-start(f32[32,4,2048]{2,1,0:T(4,128)} %select_convert_fusion.10) | copy-start | bytes 3145732
  82.9 66.6 %collective-permute-start.8 = (f32[32,257]{1,0:T(8,128)}, f32[32,257]{1,0:T(8,128)}, u32[]{:S(2)}, u32[]{:S(2)}) collective-permute-start(f32[32,257]{1,0:T(8,128)} %get-tuple-element.76), channel_id=1, source_target_pairs={{0,2},{2,4},{4,6},{6,8},{8,10},{10,12},{12,14},{14,16},{16,18},{18... | collective-permute-start | bytes 98696 | tf_op jit(solution)/shard_map/ppermute | solution.py:13
  86.1 3.4 %copy-start.2 = (f32[32,32,257]{2,1,0:T(8,128)S(1)}, f32[32,32,257]{2,1,0:T(8,128)}, u32[]{:S(2)}) copy-start(f32[32,32,257]{2,1,0:T(8,128)} %get-tuple-element.75) | copy-start | bytes 3158020
  95.2 21.5 %collective-permute-start.7 = (bf16[32,4,2048]{2,1,0:T(4,128)(2,1)}, bf16[32,4,2048]{2,1,0:T(4,128)(2,1)}, u32[]{:S(2)}, u32[]{:S(2)}) collective-permute-start(bf16[32,4,2048]{2,1,0:T(4,128)(2,1)} %collective-permute-done.5), channel_id=1, source_target_pairs={{0,510},{2,0},{4,2},{6,4},{8,6},{10,8},{12,10},{14,12},{16,14},{18... | collective-permute-start | bytes 1572872 | tf_op jit(solution)/shard_map/ppermute | solution.py:13
  100.5 16.2 %collective-permute-start.6 = (bf16[32,4,2048]{2,1,0:T(4,128)(2,1)}, bf16[32,4,2048]{2,1,0:T(4,128)(2,1)}, u32[]{:S(2)}, u32[]{:S(2)}) collective-permute-start(bf16[32,4,2048]{2,1,0:T(4,128)(2,1)} %collective-permute-done.4), channel_id=1, source_target_pairs={{0,2},{2,4},{4,6},{6,8},{8,10},{10,12},{12,14},{14,16},{16,18},{18... | collective-permute-start | bytes 1572872 | tf_op jit(solution)/shard_map/ppermute | solution.py:13
  107.0 5.7 %copy-start.7 = (f32[32,4,2048]{2,1,0:T(4,128)S(1)}, f32[32,4,2048]{2,1,0:T(4,128)}, u32[]{:S(2)}) copy-start(f32[32,4,2048]{2,1,0:T(4,128)} %get-tuple-element.67) | copy-start | bytes 3145732
  107.0 6.7 %copy-start.9 = (f32[32,4,2048]{2,1,0:T(4,128)S(1)}, f32[32,4,2048]{2,1,0:T(4,128)}, u32[]{:S(2)}) copy-start(f32[32,4,2048]{2,1,0:T(4,128)} %select_convert_fusion.9) | copy-start | bytes 3145732
  107.7 50.8 %collective-permute-start.9 = (f32[32,257]{1,0:T(8,128)}, f32[32,257]{1,0:T(8,128)}, u32[]{:S(2)}, u32[]{:S(2)}) collective-permute-start(f32[32,257]{1,0:T(8,128)} %get-tuple-element.80), channel_id=1, source_target_pairs={{0,4},{2,6},{4,8},{6,10},{8,12},{10,14},{12,16},{14,18},{16,20},{1... | collective-permute-start | bytes 98696 | tf_op jit(solution)/shard_map/ppermute | solution.py:13
  111.3 3.4 %copy-start.3 = (f32[32,32,257]{2,1,0:T(8,128)S(1)}, f32[32,32,257]{2,1,0:T(8,128)}, u32[]{:S(2)}) copy-start(f32[32,32,257]{2,1,0:T(8,128)} %get-tuple-element.75) | copy-start | bytes 3158020
  130.8 3.7 %copy-start.4 = (f32[32,32,257]{2,1,0:T(8,128)S(1)}, f32[32,32,257]{2,1,0:T(8,128)}, u32[]{:S(2)}) copy-start(f32[32,32,257]{2,1,0:T(8,128)} %get-tuple-element.75) | copy-start | bytes 3158020
  132.3 8.2 %copy-start.14 = (f32[32,257]{1,0:T(8,128)S(1)}, f32[32,257]{1,0:T(8,128)}, u32[]{:S(2)}) copy-start(f32[32,257]{1,0:T(8,128)} %get-tuple-element.79) | copy-start | bytes 98692
  132.3 17.2 %copy-start.15 = (f32[32,257]{1,0:T(8,128)S(1)}, f32[32,257]{1,0:T(8,128)}, u32[]{:S(2)}) copy-start(f32[32,257]{1,0:T(8,128)} %get-tuple-element.83) | copy-start | bytes 98692
  132.3 37.3 %copy-start.11 = (f32[1,32,1,257]{3,1,2,0:T(8,128)S(1)}, f32[1,32,1,257]{3,1,2,0:T(8,128)}, u32[]{:S(2)}) copy-start(f32[1,32,1,257]{3,1,2,0:T(8,128)} %get-tuple-element.77) | copy-start | bytes 98692
  132.3 37.3 %copy-start.13 = (f32[1,32,1,257]{3,1,2,0:T(8,128)S(1)}, f32[1,32,1,257]{3,1,2,0:T(8,128)}, u32[]{:S(2)}) copy-start(f32[1,32,1,257]{3,1,2,0:T(8,128)} %get-tuple-element.81) | copy-start | bytes 98692
  132.3 38.4 %copy-start.12 = (f32[1,32,1,257]{3,1,2,0:T(8,128)S(1)}, f32[1,32,1,257]{3,1,2,0:T(8,128)}, u32[]{:S(2)}) copy-start(f32[1,32,1,257]{3,1,2,0:T(8,128)} %get-tuple-element.82) | copy-start | bytes 98692
  136.6 26.5 %collective-permute-start.11 = (f32[32,257]{1,0:T(8,128)S(1)}, f32[32,257]{1,0:T(8,128)S(1)}, u32[]{:S(2)}, u32[]{:S(2)}) collective-permute-start(f32[32,257]{1,0:T(8,128)S(1)} %get-tuple-element.88), channel_id=1, source_target_pairs={{0,8},{2,10},{4,12},{6,14},{8,16},{10,18},{12,20},{14,22},{16,24},... | collective-permute-start | bytes 98696 | tf_op jit(solution)/shard_map/ppermute | solution.py:13
  138.5 31.1 %collective-permute-start.10 = (f32[32,257]{1,0:T(8,128)S(1)}, f32[32,257]{1,0:T(8,128)S(1)}, u32[]{:S(2)}, u32[]{:S(2)}) collective-permute-start(f32[32,257]{1,0:T(8,128)S(1)} %get-tuple-element.84), channel_id=1, source_target_pairs={{0,6},{2,8},{4,10},{6,12},{8,14},{10,16},{12,18},{14,20},{16,22},{... | collective-permute-start | bytes 98696 | tf_op jit(solution)/shard_map/ppermute | solution.py:13
  140.5 30.0 %collective-permute-start.12 = (f32[32,257]{1,0:T(8,128)S(1)}, f32[32,257]{1,0:T(8,128)S(1)}, u32[]{:S(2)}, u32[]{:S(2)}) collective-permute-start(f32[32,257]{1,0:T(8,128)S(1)} %copy-done.14), channel_id=1, source_target_pairs={{0,510},{2,0},{4,2},{6,4},{8,6},{10,8},{12,10},{14,12},{16,14},{18... | collective-permute-start | bytes 98696 | tf_op jit(solution)/shard_map/ppermute | solution.py:13
  149.5 21.0 %collective-permute-start.13 = (f32[32,257]{1,0:T(8,128)S(1)}, f32[32,257]{1,0:T(8,128)S(1)}, u32[]{:S(2)}, u32[]{:S(2)}) collective-permute-start(f32[32,257]{1,0:T(8,128)S(1)} %copy-done.15), channel_id=1, source_target_pairs={{0,508},{2,510},{4,0},{6,2},{8,4},{10,6},{12,8},{14,10},{16,12},{1... | collective-permute-start | bytes 98696 | tf_op jit(solution)/shard_map/ppermute | solution.py:13
  158.5 12.0 %collective-permute-start.15 = (f32[32,257]{1,0:T(8,128)S(1)}, f32[32,257]{1,0:T(8,128)S(1)}, u32[]{:S(2)}, u32[]{:S(2)}) collective-permute-start(f32[32,257]{1,0:T(8,128)S(1)} %get-tuple-element.91), channel_id=1, source_target_pairs={{0,504},{2,506},{4,508},{6,510},{8,0},{10,2},{12,4},{14,6},{16,8},... | collective-permute-start | bytes 98696 | tf_op jit(solution)/shard_map/ppermute | solution.py:13
  163.1 7.6 %collective-permute-start.14 = (f32[32,257]{1,0:T(8,128)S(1)}, f32[32,257]{1,0:T(8,128)S(1)}, u32[]{:S(2)}, u32[]{:S(2)}) collective-permute-start(f32[32,257]{1,0:T(8,128)S(1)} %get-tuple-element.87), channel_id=1, source_target_pairs={{0,506},{2,508},{4,510},{6,0},{8,2},{10,4},{12,6},{14,8},{16,10},{... | collective-permute-start | bytes 98696 | tf_op jit(solution)/shard_map/ppermute | solution.py:13
  170.8 12.2 %collective-permute-start.16 = (f32[2,32,4,257]{3,1,2,0:T(8,128)S(1)}, f32[2,32,4,257]{3,1,2,0:T(8,128)S(1)}, u32[]{:S(2)}, u32[]{:S(2)}) collective-permute-start(f32[2,32,4,257]{3,1,2,0:T(8,128)S(1)} %pad_maximum_fusion.5), channel_id=1, source_target_pairs={{0,1},{1,0},{2,3},{3,2},{4,5},{5,4},{6,7},{7,6},{8,9},{9,8},{10,11... | collective-permute-start | bytes 789512 | tf_op jit(solution)/shard_map/ppermute | solution.py:18
  (3 other events, 8.4 us)

commit v4 on v3

--- a/solution.py
+++ b/solution.py
@@ -58,17 +58,20 @@
 
 def whiten(spectrum, keep, half_len):
     power = jnp.sum(spectrum * spectrum, axis=-1, keepdims=True) / half_len
-    return (spectrum * lax.rsqrt(power + 1e-06) * keep[:, None, None]).astype(jnp.bfloat16)
+    return (spectrum * lax.rsqrt(power + 1e-06) * keep).astype(jnp.bfloat16)
 
 
 def cross_spectrum(local, partner, half_len):
-    first = local.astype(jnp.float32)
-    second = partner.astype(jnp.float32)
-    real_a, imag_a = (first[..., :half_len], first[..., half_len:])
-    real_b, imag_b = (second[..., :half_len], second[..., half_len:])
-    real_sum = jnp.sum(real_a * real_b + imag_a * imag_b, axis=1)
-    imag_sum = jnp.sum(imag_a * real_b - real_a * imag_b, axis=1)
+    real_a, imag_a = (local[..., :half_len], local[..., half_len:])
+    real_b, imag_b = (partner[..., :half_len], partner[..., half_len:])
+    real_sum = jnp.sum(real_a * real_b + imag_a * imag_b, axis=0)
+    imag_sum = jnp.sum(imag_a * real_b - real_a * imag_b, axis=0)
     return jnp.concatenate([real_sum, imag_sum], axis=-1)
+
+
+def pick_rows(rows, block):
+    picks = (rows[:, None] == lax.iota(jnp.int32, block.shape[1])[None, :]).astype(block.dtype)
+    return jnp.einsum("gp,spk->sgk", picks, block, preferred_element_type=jnp.float32)
 
 
 def on_device(samples, offsets, bad_mask):
@@ -76,18 +79,19 @@
     half_len = length // 2
     stops = offsets.shape[0]
     spectrum = jnp.dot(
-        samples.reshape(channels * segments, length),
+        jnp.swapaxes(samples, 0, 1).reshape(segments * channels, length),
         forward_table(length),
         preferred_element_type=jnp.float32,
-    ).reshape(channels, segments, length)
+    ).reshape(segments, channels, length)
     keep = (1 - bad_mask).astype(jnp.float32)
-    white = whiten(spectrum, keep, half_len)
+    white = whiten(spectrum, keep[None, :, None], half_len)
     split = segments // 2
-    ahead = white[:, :split]
-    behind = white[:, split:]
+    ahead = white[:split]
+    behind = white[split:]
+    ahead_f32 = ahead.astype(jnp.float32)
     dc_imag = lax.broadcasted_iota(jnp.int32, behind.shape, 2) == half_len
     moving_ahead = ahead
-    moving_behind = behind.at[:, :stops, half_len].set(offsets.T.astype(jnp.bfloat16))
+    moving_behind = behind.at[:stops, :, half_len].set(offsets.astype(jnp.bfloat16))
     back_table = inverse_table(length, LAGS)
     own_parts, later_parts, from_earlier, from_later = [], [], [], []
     lags = jnp.zeros((2 * channels, back_table.shape[1]), jnp.float32)
@@ -100,12 +104,10 @@
             later_parts.append(lags[channels:])
             from_earlier.append(shifted(lags[channels:], "blk", stop - 1))
             from_later.append(shifted(lags[:channels], "blk", 1 - stop))
-        partner = jnp.take(moving_ahead, offsets[stop - 1], axis=0)
-        own = cross_spectrum(ahead, partner, half_len)
-        later_offsets = moving_behind[:, stop - 1, half_len].astype(jnp.int32)
-        local_partner = jnp.take(behind, later_offsets, axis=0)
-        later = jnp.where(dc_imag, jnp.zeros_like(moving_behind), moving_behind)
-        later = cross_spectrum(later, local_partner, half_len)
+        own = cross_spectrum(ahead_f32, pick_rows(offsets[stop - 1], moving_ahead), half_len)
+        later_offsets = moving_behind[stop - 1, :, half_len].astype(jnp.int32)
+        later = jnp.where(dc_imag, jnp.zeros_like(moving_behind), moving_behind).astype(jnp.float32)
+        later = cross_spectrum(later, pick_rows(later_offsets, behind), half_len)
         lags = jnp.dot(
             jnp.concatenate([own, later], axis=0),
             back_table,

time: 187 us -> 143 us (0.76)
  other arithmetic: 48.1 us -> 9.05 us
  local copies, waits for them, and re-layouts: 24.4 us -> 4.06 us
  waiting for transfers between devices: 18.3 us -> 26 us
  starting transfers between devices: 82.7 us -> 87.8 us
  matrix products: 10.3 us -> 13 us
    convert_element_type x18 -> x10, other arithmetic: 27.7 us -> 1.41 us  [the longest x1 0.47 us: whiten(): return (spectrum * lax.rsqrt(power + 1e-06) * keep).astype(jnp.bfloat16)]
    gather x8 -> x0, local copies, waits for them, and re-layouts: 18.4 us -> none  [the longest x4 11.3 us: on_device(): partner = jnp.take(moving_ahead, offsets[stop - 1], axis=0)]
    ppermute x16, waiting for transfers between devices: 8.33 us -> 17.6 us  [shifted(): lax.ppermute(x, axis, [(i, (i + by) % length) for i in range(length)])]
    reduce_sum x8, other arithmetic: 10.2 us -> 1.91 us  [cross_spectrum(): real_sum = jnp.sum(real_a * real_b + imag_a * imag_b, axis=0)]
    ppermute x16, starting transfers between devices: 80.5 us -> 85.6 us  [shifted(): lax.ppermute(x, axis, [(i, (i + by) % length) for i in range(length)])]
    dot_general x1 -> x9, matrix products: 2.5 us -> 5.21 us  [the longest x8 2.72 us: pick_rows(): jnp.einsum('gp,spk->sgk', picks, block, preferred_element_type=jnp.float32)]
  transfers between devices with their start and end apart: 17 -> 17, of which waited for: 3 -> 6; matrix products, arithmetic and copies ran while one was open for 34% -> 10% of each run, Pallas kernels for 0% -> 0%
where the time goes in v4:
time: 143 us; the launch traced here: 141 us
  starting transfers between devices  87.8 us (61%)
  waiting for transfers between devices  26 us (18%)
  matrix products  13 us (9%)
  other arithmetic  9.05 us (6%)
  local copies, waits for them, and re-layouts  4.06 us (3%)
    ppermute x16, starting transfers between devices, shifted(): lax.ppermute(x, axis, [(i, (i + by) % length) for i in range(length)])  85.6 us
    ppermute x16, waiting for transfers between devices, shifted(): lax.ppermute(x, axis, [(i, (i + by) % length) for i in range(length)])  17.6 us
    ppermute x1, waiting for transfers between devices, swapped(): return lax.ppermute(x, axis, [(i, i ^ 1) for i in range(length)])  8.45 us
    dot_general x4, matrix products, on_device(): jnp.dot(jnp.concatenate([own, later], axis=0), back_table, precision=lax....  7.79 us
    unnamed x8, local copies, waits for them, and re-layouts  3.72 us
    another operation x2, other arithmetic  2.89 us
  transfers between devices with their start and end apart: 17, of which 6 were waited for; matrix products, arithmetic and copies ran while one was open for 10% of the time, Pallas kernels for 0%

profile of v4, /device:TPU:1, one launch (start us, length us, event | category | flops | bytes accessed | tf_op | source)
XLA Modules:
  0.0 141.1 jit_solution(3506089023232728208)
XLA Ops:
  0.6 1.0 fusion.47
  2.3 1.8 %copy.8 = bf16[32,8,2048]{2,0,1:T(8,128)(2,1)S(1)} copy(bf16[32,8,2048]{2,1,0:T(8,128)(2,1)} %param.5) | data formatting | bytes 2097152 | tf_op args[0]
  4.1 2.9 %subtract_convert_fusion = (bf16[32,64,1024]{2,1,0:T(8,128)(2,1)S(1)}, bf16[32,64,1024]{2,1,0:T(8,128)(2,1)S(1)}) fusion(f32[64,1024]{1,0:T(8,128)S(1)} %get-tuple-element.93, f32[32,1024]{1,0:T(8,128)S(1)} %get-tuple-element.90, f32[64,1024]{1,0:T(8,128)S(1)} %get-tuple-element.94, f32[32,1024]{1,0:T(8,128)S(1)} %get-tuple-element.89), kind=kLoop, calls=%fused_computation.5 | loop fusion | flops 18874368 | bytes 9175040 | tf_op jit(solution)/shard_map/convert.7
  7.0 2.5 %fusion.4 = (f32[256]{0:T(256)S(1)}, f32[2048,256]{0,1:T(8,128)S(1)}) fusion(bf16[256,2048]{1,0:T(8,128)(2,1)S(1)} %bitcast.112, bf16[2048,1024]{1,0:T(8,128)(2,1)S(1)} %bitcast.110, bf16[2048,1024]{1,0:T(8,128)(2,1)S(1)} %bitcast.109), kind=kOutput, calls=%fused_computation.16 | convolution fusion | flops 2165309184 | bytes 11535360 | tf_op jit(solution)/shard_map/dot_general | solution.py:81
  10.5 8.8 %collective-permute-start.1 = (bf16[4,32,2048]{2,1,0:T(8,128)(2,1)S(1)}, bf16[4,32,2048]{2,1,0:T(8,128)(2,1)S(1)}, u32[]{:S(2)}, u32[]{:S(2)}) collective-permute-start(bf16[4,32,2048]{2,1,0:T(8,128)(2,1)S(1)} %scatter.4), channel_id=1, source_target_pairs={{0,510},{2,0},{4,2},{6,4},{8,6},{10,8},{12,10},{14,12},{16,14},{18... | collective-permute-start | bytes 1572872 | tf_op jit(solution)/shard_map/ppermute | solution.py:13
  19.3 1.9 %collective-permute-start = (bf16[4,32,2048]{2,1,0:T(8,128)(2,1)S(1)}, bf16[4,32,2048]{2,1,0:T(8,128)(2,1)S(1)}, u32[]{:S(2)}, u32[]{:S(2)}) collective-permute-start(bf16[4,32,2048]{2,1,0:T(8,128)(2,1)S(1)} %get-tuple-element.58), channel_id=1, source_target_pairs={{0,2},{2,4},{4,6},{6,8},{8,10},{10,12},{12,14},{14,16},{16,18},{18... | collective-permute-start | bytes 1572872 | tf_op jit(solution)/shard_map/ppermute | solution.py:13
  22.1 8.9 %collective-permute-done = bf16[4,32,2048]{2,1,0:T(8,128)(2,1)S(1)} collective-permute-done((bf16[4,32,2048]{2,1,0:T(8,128)(2,1)S(1)}, bf16[4,32,2048]{2,1,0:T(8,128)(2,1)S(1)}, u32[]{:S(2)}, u32[]{:S(2)}) %collective-permute-start) | collective-permute-done | bytes 524320 | tf_op jit(solution)/shard_map/ppermute | solution.py:13
  31.2 14.8 %collective-permute-start.3 = (bf16[4,32,2048]{2,1,0:T(8,128)(2,1)S(1)}, bf16[4,32,2048]{2,1,0:T(8,128)(2,1)S(1)}, u32[]{:S(2)}, u32[]{:S(2)}) collective-permute-start(bf16[4,32,2048]{2,1,0:T(8,128)(2,1)S(1)} %collective-permute-done.1), channel_id=1, source_target_pairs={{0,510},{2,0},{4,2},{6,4},{8,6},{10,8},{12,10},{14,12},{16,14},{18... | collective-permute-start | bytes 1572872 | tf_op jit(solution)/shard_map/ppermute | solution.py:13
  46.4 1.9 %collective-permute-start.2 = (bf16[4,32,2048]{2,1,0:T(8,128)(2,1)S(1)}, bf16[4,32,2048]{2,1,0:T(8,128)(2,1)S(1)}, u32[]{:S(2)}, u32[]{:S(2)}) collective-permute-start(bf16[4,32,2048]{2,1,0:T(8,128)(2,1)S(1)} %collective-permute-done), channel_id=1, source_target_pairs={{0,2},{2,4},{4,6},{6,8},{8,10},{10,12},{12,14},{14,16},{16,18},{18... | collective-permute-start | bytes 1572872 | tf_op jit(solution)/shard_map/ppermute | solution.py:13
  49.2 1.9 %fusion.8 = f32[64,257]{1,0:T(8,128)S(1)} fusion(f32[1024,257]{1,0:T(8,128)S(1)} %bitcast.105, f32[1024,257]{1,0:T(8,128)S(1)} %bitcast.101, f32[32,1024]{1,0:T(8,128)S(1)} %get-tuple-element.55, f32[32,1024]{1,0:T(8,128)S(1)} %get-tuple-element.54, f32[32,1024]{1,0:T(8,128)S(1)} %get-tuple-element.53, f32[32,1024]{1,0:T(8,128)S(1)} %get-tuple-element.52), kind=kOutput, calls=%fused_computation.23 | convolution fusion | flops 405145600 | bytes 2695424 | tf_op jit(solution)/shard_map/dot_general | solution.py:111
  51.2 3.3 %collective-permute-done.2 = bf16[4,32,2048]{2,1,0:T(8,128)(2,1)S(1)} collective-permute-done((bf16[4,32,2048]{2,1,0:T(8,128)(2,1)S(1)}, bf16[4,32,2048]{2,1,0:T(8,128)(2,1)S(1)}, u32[]{:S(2)}, u32[]{:S(2)}) %collective-permute-start.2) | collective-permute-done | bytes 524320 | tf_op jit(solution)/shard_map/ppermute | solution.py:13
  54.6 10.1 %collective-permute-start.5 = (bf16[4,32,2048]{2,1,0:T(8,128)(2,1)S(1)}, bf16[4,32,2048]{2,1,0:T(8,128)(2,1)S(1)}, u32[]{:S(2)}, u32[]{:S(2)}) collective-permute-start(bf16[4,32,2048]{2,1,0:T(8,128)(2,1)S(1)} %collective-permute-done.3), channel_id=1, source_target_pairs={{0,510},{2,0},{4,2},{6,4},{8,6},{10,8},{12,10},{14,12},{16,14},{18... | collective-permute-start | bytes 1572872 | tf_op jit(solution)/shard_map/ppermute | solution.py:13
  64.8 1.9 %collective-permute-start.4 = (bf16[4,32,2048]{2,1,0:T(8,128)(2,1)S(1)}, bf16[4,32,2048]{2,1,0:T(8,128)(2,1)S(1)}, u32[]{:S(2)}, u32[]{:S(2)}) collective-permute-start(bf16[4,32,2048]{2,1,0:T(8,128)(2,1)S(1)} %collective-permute-done.2), channel_id=1, source_target_pairs={{0,2},{2,4},{4,6},{6,8},{8,10},{10,12},{12,14},{14,16},{16,18},{18... | collective-permute-start | bytes 1572872 | tf_op jit(solution)/shard_map/ppermute | solution.py:13
  67.3 2.1 %collective-permute-start.8 = (f32[32,257]{1,0:T(8,128)S(1)}, f32[32,257]{1,0:T(8,128)S(1)}, u32[]{:S(2)}, u32[]{:S(2)}) collective-permute-start(f32[32,257]{1,0:T(8,128)S(1)} %get-tuple-element.65), channel_id=1, source_target_pairs={{0,2},{2,4},{4,6},{6,8},{8,10},{10,12},{12,14},{14,16},{16,18},{18... | collective-permute-start | bytes 98696 | tf_op jit(solution)/shard_map/ppermute | solution.py:13
  70.0 1.9 %fusion.7 = f32[64,257]{1,0:T(8,128)S(1)} fusion(f32[1024,257]{1,0:T(8,128)S(1)} %bitcast.106, f32[1024,257]{1,0:T(8,128)S(1)} %bitcast.102, f32[32,1024]{1,0:T(8,128)S(1)} %get-tuple-element.51, f32[32,1024]{1,0:T(8,128)S(1)} %get-tuple-element.50, f32[32,1024]{1,0:T(8,128)S(1)} %get-tuple-element.49, f32[32,1024]{1,0:T(8,128)S(1)} %get-tuple-element.48), kind=kOutput, calls=%fused_computation.22 | convolution fusion | flops 405145600 | bytes 2695424 | tf_op jit(solution)/shard_map/dot_general | solution.py:111
  72.0 0.8 collective-permute-done.4
  73.0 10.1 %collective-permute-start.7 = (bf16[4,32,2048]{2,1,0:T(8,128)(2,1)S(1)}, bf16[4,32,2048]{2,1,0:T(8,128)(2,1)S(1)}, u32[]{:S(2)}, u32[]{:S(2)}) collective-permute-start(bf16[4,32,2048]{2,1,0:T(8,128)(2,1)S(1)} %collective-permute-done.5), channel_id=1, source_target_pairs={{0,510},{2,0},{4,2},{6,4},{8,6},{10,8},{12,10},{14,12},{16,14},{18... | collective-permute-start | bytes 1572872 | tf_op jit(solution)/shard_map/ppermute | solution.py:13
  83.1 1.9 %collective-permute-start.6 = (bf16[4,32,2048]{2,1,0:T(8,128)(2,1)S(1)}, bf16[4,32,2048]{2,1,0:T(8,128)(2,1)S(1)}, u32[]{:S(2)}, u32[]{:S(2)}) collective-permute-start(bf16[4,32,2048]{2,1,0:T(8,128)(2,1)S(1)} %collective-permute-done.4), channel_id=1, source_target_pairs={{0,2},{2,4},{4,6},{6,8},{8,10},{10,12},{12,14},{14,16},{16,18},{18... | collective-permute-start | bytes 1572872 | tf_op jit(solution)/shard_map/ppermute | solution.py:13
  85.7 1.9 %collective-permute-start.9 = (f32[32,257]{1,0:T(8,128)S(1)}, f32[32,257]{1,0:T(8,128)S(1)}, u32[]{:S(2)}, u32[]{:S(2)}) collective-permute-start(f32[32,257]{1,0:T(8,128)S(1)} %get-tuple-element.69), channel_id=1, source_target_pairs={{0,4},{2,6},{4,8},{6,10},{8,12},{10,14},{12,16},{14,18},{16,20},{1... | collective-permute-start | bytes 98696 | tf_op jit(solution)/shard_map/ppermute | solution.py:13
  88.2 1.9 %fusion.6 = f32[64,257]{1,0:T(8,128)S(1)} fusion(f32[1024,257]{1,0:T(8,128)S(1)} %bitcast.107, f32[1024,257]{1,0:T(8,128)S(1)} %bitcast.103, f32[32,1024]{1,0:T(8,128)S(1)} %get-tuple-element.47, f32[32,1024]{1,0:T(8,128)S(1)} %get-tuple-element.46, f32[32,1024]{1,0:T(8,128)S(1)} %get-tuple-element.45, f32[32,1024]{1,0:T(8,128)S(1)} %get-tuple-element.44), kind=kOutput, calls=%fused_computation.21 | convolution fusion | flops 405145600 | bytes 2695424 | tf_op jit(solution)/shard_map/dot_general | solution.py:111
  90.1 2.6 %collective-permute-done.6 = bf16[4,32,2048]{2,1,0:T(8,128)(2,1)S(1)} collective-permute-done((bf16[4,32,2048]{2,1,0:T(8,128)(2,1)S(1)}, bf16[4,32,2048]{2,1,0:T(8,128)(2,1)S(1)}, u32[]{:S(2)}, u32[]{:S(2)}) %collective-permute-start.6) | collective-permute-done | bytes 524320 | tf_op jit(solution)/shard_map/ppermute | solution.py:13
  94.1 2.0 %fusion.5 = f32[64,257]{1,0:T(8,128)S(1)} fusion(f32[1024,257]{1,0:T(8,128)S(1)} %bitcast.108, f32[1024,257]{1,0:T(8,128)S(1)} %bitcast.104, f32[32,1024]{1,0:T(8,128)S(1)} %get-tuple-element.43, f32[32,1024]{1,0:T(8,128)S(1)} %get-tuple-element.42, f32[32,1024]{1,0:T(8,128)S(1)} %get-tuple-element.41, f32[32,1024]{1,0:T(8,128)S(1)} %get-tuple-element.40), kind=kOutput, calls=%fused_computation.20 | convolution fusion | flops 405145600 | bytes 2695424 | tf_op jit(solution)/shard_map/dot_general | solution.py:111
  96.1 1.9 %collective-permute-start.11 = (f32[32,257]{1,0:T(8,128)S(1)}, f32[32,257]{1,0:T(8,128)S(1)}, u32[]{:S(2)}, u32[]{:S(2)}) collective-permute-start(f32[32,257]{1,0:T(8,128)S(1)} %get-tuple-element.77), channel_id=1, source_target_pairs={{0,8},{2,10},{4,12},{6,14},{8,16},{10,18},{12,20},{14,22},{16,24},... | collective-permute-start | bytes 98696 | tf_op jit(solution)/shard_map/ppermute | solution.py:13
  98.1 1.9 %collective-permute-start.10 = (f32[32,257]{1,0:T(8,128)S(1)}, f32[32,257]{1,0:T(8,128)S(1)}, u32[]{:S(2)}, u32[]{:S(2)}) collective-permute-start(f32[32,257]{1,0:T(8,128)S(1)} %get-tuple-element.73), channel_id=1, source_target_pairs={{0,6},{2,8},{4,10},{6,12},{8,14},{10,16},{12,18},{14,20},{16,22},{... | collective-permute-start | bytes 98696 | tf_op jit(solution)/shard_map/ppermute | solution.py:13
  100.0 9.1 %collective-permute-start.12 = (f32[32,257]{1,0:T(8,128)S(1)}, f32[32,257]{1,0:T(8,128)S(1)}, u32[]{:S(2)}, u32[]{:S(2)}) collective-permute-start(f32[32,257]{1,0:T(8,128)S(1)} %get-tuple-element.68), channel_id=1, source_target_pairs={{0,510},{2,0},{4,2},{6,4},{8,6},{10,8},{12,10},{14,12},{16,14},{18... | collective-permute-start | bytes 98696 | tf_op jit(solution)/shard_map/ppermute | solution.py:13
  109.1 4.5 %collective-permute-start.13 = (f32[32,257]{1,0:T(8,128)S(1)}, f32[32,257]{1,0:T(8,128)S(1)}, u32[]{:S(2)}, u32[]{:S(2)}) collective-permute-start(f32[32,257]{1,0:T(8,128)S(1)} %get-tuple-element.72), channel_id=1, source_target_pairs={{0,508},{2,510},{4,0},{6,2},{8,4},{10,6},{12,8},{14,10},{16,12},{1... | collective-permute-start | bytes 98696 | tf_op jit(solution)/shard_map/ppermute | solution.py:13
  113.6 7.7 %collective-permute-start.15 = (f32[32,257]{1,0:T(8,128)S(1)}, f32[32,257]{1,0:T(8,128)S(1)}, u32[]{:S(2)}, u32[]{:S(2)}) collective-permute-start(f32[32,257]{1,0:T(8,128)S(1)} %get-tuple-element.80), channel_id=1, source_target_pairs={{0,504},{2,506},{4,508},{6,510},{8,0},{10,2},{12,4},{14,6},{16,8},... | collective-permute-start | bytes 98696 | tf_op jit(solution)/shard_map/ppermute | solution.py:13
  121.3 5.0 %collective-permute-start.14 = (f32[32,257]{1,0:T(8,128)S(1)}, f32[32,257]{1,0:T(8,128)S(1)}, u32[]{:S(2)}, u32[]{:S(2)}) collective-permute-start(f32[32,257]{1,0:T(8,128)S(1)} %get-tuple-element.76), channel_id=1, source_target_pairs={{0,506},{2,508},{4,510},{6,0},{8,2},{10,4},{12,6},{14,8},{16,10},{... | collective-permute-start | bytes 98696 | tf_op jit(solution)/shard_map/ppermute | solution.py:13
  126.4 1.9 %collective-permute-done.14 = f32[32,257]{1,0:T(8,128)S(1)} collective-permute-done((f32[32,257]{1,0:T(8,128)S(1)}, f32[32,257]{1,0:T(8,128)S(1)}, u32[]{:S(2)}, u32[]{:S(2)}) %collective-permute-start.14) | collective-permute-done | bytes 32928 | tf_op jit(solution)/shard_map/ppermute | solution.py:13
  128.4 2.2 %collective-permute-start.16 = (f32[2,32,4,257]{3,1,2,0:T(8,128)S(1)}, f32[2,32,4,257]{3,1,2,0:T(8,128)S(1)}, u32[]{:S(2)}, u32[]{:S(2)}) collective-permute-start(f32[2,32,4,257]{3,1,2,0:T(8,128)S(1)} %pad_maximum_fusion.5), channel_id=1, source_target_pairs={{0,1},{1,0},{2,3},{3,2},{4,5},{5,4},{6,7},{7,6},{8,9},{9,8},{10,11... | collective-permute-start | bytes 789512 | tf_op jit(solution)/shard_map/ppermute | solution.py:18
  130.6 8.4 %collective-permute-done.16 = f32[2,32,4,257]{3,1,2,0:T(8,128)S(1)} collective-permute-done((f32[2,32,4,257]{3,1,2,0:T(8,128)S(1)}, f32[2,32,4,257]{3,1,2,0:T(8,128)S(1)}, u32[]{:S(2)}, u32[]{:S(2)}) %collective-permute-start.16) | collective-permute-done | bytes 263200 | tf_op jit(solution)/shard_map/ppermute | solution.py:18
  139.5 0.8 copy.11
  (67 shorter events, 9.3 us)
Async XLA Ops:
  7.0 2.6 %copy-start.1 = (s32[32]{0:T(128)S(1)}, s32[32]{0:T(128)}, u32[]{:S(2)}) copy-start(s32[32]{0:T(128)} %param.7) | copy-start | bytes 388
  9.6 0.7 copy-start
  10.5 11.7 %collective-permute-start.1 = (bf16[4,32,2048]{2,1,0:T(8,128)(2,1)S(1)}, bf16[4,32,2048]{2,1,0:T(8,128)(2,1)S(1)}, u32[]{:S(2)}, u32[]{:S(2)}) collective-permute-start(bf16[4,32,2048]{2,1,0:T(8,128)(2,1)S(1)} %scatter.4), channel_id=1, source_target_pairs={{0,510},{2,0},{4,2},{6,4},{8,6},{10,8},{12,10},{14,12},{16,14},{18... | collective-permute-start | bytes 1572872 | tf_op jit(solution)/shard_map/ppermute | solution.py:13
  19.3 11.8 %collective-permute-start = (bf16[4,32,2048]{2,1,0:T(8,128)(2,1)S(1)}, bf16[4,32,2048]{2,1,0:T(8,128)(2,1)S(1)}, u32[]{:S(2)}, u32[]{:S(2)}) collective-permute-start(bf16[4,32,2048]{2,1,0:T(8,128)(2,1)S(1)} %get-tuple-element.58), channel_id=1, source_target_pairs={{0,2},{2,4},{4,6},{6,8},{8,10},{10,12},{12,14},{14,16},{16,18},{18... | collective-permute-start | bytes 1572872 | tf_op jit(solution)/shard_map/ppermute | solution.py:13
  31.2 20.0 %collective-permute-start.3 = (bf16[4,32,2048]{2,1,0:T(8,128)(2,1)S(1)}, bf16[4,32,2048]{2,1,0:T(8,128)(2,1)S(1)}, u32[]{:S(2)}, u32[]{:S(2)}) collective-permute-start(bf16[4,32,2048]{2,1,0:T(8,128)(2,1)S(1)} %collective-permute-done.1), channel_id=1, source_target_pairs={{0,510},{2,0},{4,2},{6,4},{8,6},{10,8},{12,10},{14,12},{16,14},{18... | collective-permute-start | bytes 1572872 | tf_op jit(solution)/shard_map/ppermute | solution.py:13
  46.4 8.0 %collective-permute-start.2 = (bf16[4,32,2048]{2,1,0:T(8,128)(2,1)S(1)}, bf16[4,32,2048]{2,1,0:T(8,128)(2,1)S(1)}, u32[]{:S(2)}, u32[]{:S(2)}) collective-permute-start(bf16[4,32,2048]{2,1,0:T(8,128)(2,1)S(1)} %collective-permute-done), channel_id=1, source_target_pairs={{0,2},{2,4},{4,6},{6,8},{8,10},{10,12},{12,14},{14,16},{16,18},{18... | collective-permute-start | bytes 1572872 | tf_op jit(solution)/shard_map/ppermute | solution.py:13
  54.6 18.2 %collective-permute-start.5 = (bf16[4,32,2048]{2,1,0:T(8,128)(2,1)S(1)}, bf16[4,32,2048]{2,1,0:T(8,128)(2,1)S(1)}, u32[]{:S(2)}, u32[]{:S(2)}) collective-permute-start(bf16[4,32,2048]{2,1,0:T(8,128)(2,1)S(1)} %collective-permute-done.3), channel_id=1, source_target_pairs={{0,510},{2,0},{4,2},{6,4},{8,6},{10,8},{12,10},{14,12},{16,14},{18... | collective-permute-start | bytes 1572872 | tf_op jit(solution)/shard_map/ppermute | solution.py:13
  64.8 8.0 %collective-permute-start.4 = (bf16[4,32,2048]{2,1,0:T(8,128)(2,1)S(1)}, bf16[4,32,2048]{2,1,0:T(8,128)(2,1)S(1)}, u32[]{:S(2)}, u32[]{:S(2)}) collective-permute-start(bf16[4,32,2048]{2,1,0:T(8,128)(2,1)S(1)} %collective-permute-done.2), channel_id=1, source_target_pairs={{0,2},{2,4},{4,6},{6,8},{8,10},{10,12},{12,14},{14,16},{16,18},{18... | collective-permute-start | bytes 1572872 | tf_op jit(solution)/shard_map/ppermute | solution.py:13
  67.3 41.7 %collective-permute-start.8 = (f32[32,257]{1,0:T(8,128)S(1)}, f32[32,257]{1,0:T(8,128)S(1)}, u32[]{:S(2)}, u32[]{:S(2)}) collective-permute-start(f32[32,257]{1,0:T(8,128)S(1)} %get-tuple-element.65), channel_id=1, source_target_pairs={{0,2},{2,4},{4,6},{6,8},{8,10},{10,12},{12,14},{14,16},{16,18},{18... | collective-permute-start | bytes 98696 | tf_op jit(solution)/shard_map/ppermute | solution.py:13
  73.0 19.7 %collective-permute-start.7 = (bf16[4,32,2048]{2,1,0:T(8,128)(2,1)S(1)}, bf16[4,32,2048]{2,1,0:T(8,128)(2,1)S(1)}, u32[]{:S(2)}, u32[]{:S(2)}) collective-permute-start(bf16[4,32,2048]{2,1,0:T(8,128)(2,1)S(1)} %collective-permute-done.5), channel_id=1, source_target_pairs={{0,510},{2,0},{4,2},{6,4},{8,6},{10,8},{12,10},{14,12},{16,14},{18... | collective-permute-start | bytes 1572872 | tf_op jit(solution)/shard_map/ppermute | solution.py:13
  83.1 9.6 %collective-permute-start.6 = (bf16[4,32,2048]{2,1,0:T(8,128)(2,1)S(1)}, bf16[4,32,2048]{2,1,0:T(8,128)(2,1)S(1)}, u32[]{:S(2)}, u32[]{:S(2)}) collective-permute-start(bf16[4,32,2048]{2,1,0:T(8,128)(2,1)S(1)} %collective-permute-done.4), channel_id=1, source_target_pairs={{0,2},{2,4},{4,6},{6,8},{8,10},{10,12},{12,14},{14,16},{16,18},{18... | collective-permute-start | bytes 1572872 | tf_op jit(solution)/shard_map/ppermute | solution.py:13
  85.7 28.0 %collective-permute-start.9 = (f32[32,257]{1,0:T(8,128)S(1)}, f32[32,257]{1,0:T(8,128)S(1)}, u32[]{:S(2)}, u32[]{:S(2)}) collective-permute-start(f32[32,257]{1,0:T(8,128)S(1)} %get-tuple-element.69), channel_id=1, source_target_pairs={{0,4},{2,6},{4,8},{6,10},{8,12},{10,14},{12,16},{14,18},{16,20},{1... | collective-permute-start | bytes 98696 | tf_op jit(solution)/shard_map/ppermute | solution.py:13
  96.1 25.2 %collective-permute-start.11 = (f32[32,257]{1,0:T(8,128)S(1)}, f32[32,257]{1,0:T(8,128)S(1)}, u32[]{:S(2)}, u32[]{:S(2)}) collective-permute-start(f32[32,257]{1,0:T(8,128)S(1)} %get-tuple-element.77), channel_id=1, source_target_pairs={{0,8},{2,10},{4,12},{6,14},{8,16},{10,18},{12,20},{14,22},{16,24},... | collective-permute-start | bytes 98696 | tf_op jit(solution)/shard_map/ppermute | solution.py:13
  98.1 28.2 %collective-permute-start.10 = (f32[32,257]{1,0:T(8,128)S(1)}, f32[32,257]{1,0:T(8,128)S(1)}, u32[]{:S(2)}, u32[]{:S(2)}) collective-permute-start(f32[32,257]{1,0:T(8,128)S(1)} %get-tuple-element.73), channel_id=1, source_target_pairs={{0,6},{2,8},{4,10},{6,12},{8,14},{10,16},{12,18},{14,20},{16,22},{... | collective-permute-start | bytes 98696 | tf_op jit(solution)/shard_map/ppermute | solution.py:13
  100.0 26.3 %collective-permute-start.12 = (f32[32,257]{1,0:T(8,128)S(1)}, f32[32,257]{1,0:T(8,128)S(1)}, u32[]{:S(2)}, u32[]{:S(2)}) collective-permute-start(f32[32,257]{1,0:T(8,128)S(1)} %get-tuple-element.68), channel_id=1, source_target_pairs={{0,510},{2,0},{4,2},{6,4},{8,6},{10,8},{12,10},{14,12},{16,14},{18... | collective-permute-start | bytes 98696 | tf_op jit(solution)/shard_map/ppermute | solution.py:13
  109.1 17.3 %collective-permute-start.13 = (f32[32,257]{1,0:T(8,128)S(1)}, f32[32,257]{1,0:T(8,128)S(1)}, u32[]{:S(2)}, u32[]{:S(2)}) collective-permute-start(f32[32,257]{1,0:T(8,128)S(1)} %get-tuple-element.72), channel_id=1, source_target_pairs={{0,508},{2,510},{4,0},{6,2},{8,4},{10,6},{12,8},{14,10},{16,12},{1... | collective-permute-start | bytes 98696 | tf_op jit(solution)/shard_map/ppermute | solution.py:13
  113.6 12.7 %collective-permute-start.15 = (f32[32,257]{1,0:T(8,128)S(1)}, f32[32,257]{1,0:T(8,128)S(1)}, u32[]{:S(2)}, u32[]{:S(2)}) collective-permute-start(f32[32,257]{1,0:T(8,128)S(1)} %get-tuple-element.80), channel_id=1, source_target_pairs={{0,504},{2,506},{4,508},{6,510},{8,0},{10,2},{12,4},{14,6},{16,8},... | collective-permute-start | bytes 98696 | tf_op jit(solution)/shard_map/ppermute | solution.py:13
  121.3 7.0 %collective-permute-start.14 = (f32[32,257]{1,0:T(8,128)S(1)}, f32[32,257]{1,0:T(8,128)S(1)}, u32[]{:S(2)}, u32[]{:S(2)}) collective-permute-start(f32[32,257]{1,0:T(8,128)S(1)} %get-tuple-element.76), channel_id=1, source_target_pairs={{0,506},{2,508},{4,510},{6,0},{8,2},{10,4},{12,6},{14,8},{16,10},{... | collective-permute-start | bytes 98696 | tf_op jit(solution)/shard_map/ppermute | solution.py:13
  128.4 10.6 %collective-permute-start.16 = (f32[2,32,4,257]{3,1,2,0:T(8,128)S(1)}, f32[2,32,4,257]{3,1,2,0:T(8,128)S(1)}, u32[]{:S(2)}, u32[]{:S(2)}) collective-permute-start(f32[2,32,4,257]{3,1,2,0:T(8,128)S(1)} %pad_maximum_fusion.5), channel_id=1, source_target_pairs={{0,1},{1,0},{2,3},{3,2},{4,5},{5,4},{6,7},{7,6},{8,9},{9,8},{10,11... | collective-permute-start | bytes 789512 | tf_op jit(solution)/shard_map/ppermute | solution.py:18

commit v5 on v4

--- a/solution.py
+++ b/solution.py
@@ -93,17 +93,19 @@
     moving_ahead = ahead
     moving_behind = behind.at[:stops, :, half_len].set(offsets.astype(jnp.bfloat16))
     back_table = inverse_table(length, LAGS)
-    own_parts, later_parts, from_earlier, from_later = [], [], [], []
+    own_parts, later_parts, arrived = [], [], []
     lags = jnp.zeros((2 * channels, back_table.shape[1]), jnp.float32)
+    in_flight = ()
     for stop in range(1, stops + 1):
-        moving_ahead, moving_behind, lags = lax.optimization_barrier(
-            (shifted(moving_ahead, "blk", 1), shifted(moving_behind, "blk", -1), lags)
+        moving_ahead, moving_behind, lags, landed = lax.optimization_barrier(
+            (shifted(moving_ahead, "blk", 1), shifted(moving_behind, "blk", -1), lags, in_flight)
         )
+        arrived.extend(landed)
+        in_flight = ()
         if stop > 1:
             own_parts.append(lags[:channels])
             later_parts.append(lags[channels:])
-            from_earlier.append(shifted(lags[channels:], "blk", stop - 1))
-            from_later.append(shifted(lags[:channels], "blk", 1 - stop))
+            in_flight = ((shifted(lags[channels:], "blk", stop - 1), shifted(lags[:channels], "blk", 1 - stop)),)
         own = cross_spectrum(ahead_f32, pick_rows(offsets[stop - 1], moving_ahead), half_len)
         later_offsets = moving_behind[stop - 1, :, half_len].astype(jnp.int32)
         later = jnp.where(dc_imag, jnp.zeros_like(moving_behind), moving_behind).astype(jnp.float32)
@@ -114,10 +116,12 @@
             precision=lax.Precision.HIGHEST,
             preferred_element_type=jnp.float32,
         )
+    arrived.extend(in_flight)
     own_parts.append(lags[:channels])
     later_parts.append(lags[channels:])
-    from_earlier.append(shifted(lags[channels:], "blk", stops))
-    from_later.append(shifted(lags[:channels], "blk", -stops))
+    arrived.append((shifted(lags[channels:], "blk", stops), shifted(lags[:channels], "blk", -stops)))
+    from_earlier = [pair[0] for pair in arrived]
+    from_later = [pair[1] for pair in arrived]
     corr_part = jnp.stack(own_parts, axis=1) + jnp.stack(from_earlier, axis=1)
     mirror_part = jnp.stack(from_later, axis=1) + jnp.stack(later_parts, axis=1)
     parts = jnp.stack([corr_part, mirror_part], axis=0)

time: 143 us -> 150 us (1.049)
  starting transfers between devices: 87.8 us -> 92.4 us
  matrix products: 13 us -> 15.6 us
  other arithmetic: 9.05 us -> 10.7 us
    ppermute x16, starting transfers between devices: 85.6 us -> 90.1 us  [shifted(): lax.ppermute(x, axis, [(i, (i + by) % length) for i in range(length)])]
    dot_general x1, matrix products: 2.49 us -> 5.05 us  [on_device(): jnp.dot(jnp.swapaxes(samples, 0, 1).reshape(segments * channels, length),...]
    ppermute x16, waiting for transfers between devices: 17.6 us -> 15.4 us  [shifted(): lax.ppermute(x, axis, [(i, (i + by) % length) for i in range(length)])]
    convert_element_type x1, other arithmetic: 0.47 us -> 2.08 us  [whiten(): return (spectrum * lax.rsqrt(power + 1e-06) * keep).astype(jnp.bfloat16)]
  transfers between devices with their start and end apart: 17 -> 17, of which waited for: 6 -> 6; matrix products, arithmetic and copies ran while one was open for 10% -> 7% of each run, Pallas kernels for 0% -> 0%
where the time goes in v5:
time: 150 us; the launch traced here: 149 us
  starting transfers between devices  92.4 us (62%)
  waiting for transfers between devices  25 us (17%)
  matrix products  15.6 us (10%)
  other arithmetic  10.7 us (7%)
  local copies, waits for them, and re-layouts  4.05 us (3%)
    ppermute x16, starting transfers between devices, shifted(): lax.ppermute(x, axis, [(i, (i + by) % length) for i in range(length)])  90.1 us
    ppermute x16, waiting for transfers between devices, shifted(): lax.ppermute(x, axis, [(i, (i + by) % length) for i in range(length)])  15.4 us
    ppermute x1, waiting for transfers between devices, swapped(): return lax.ppermute(x, axis, [(i, i ^ 1) for i in range(length)])  9.56 us
    dot_general x4, matrix products, on_device(): jnp.dot(jnp.concatenate([own, later], axis=0), back_table, precision=lax....  7.78 us
    dot_general x1, matrix products, on_device(): jnp.dot(jnp.swapaxes(samples, 0, 1).reshape(segments * channels, length),...  5.05 us
    unnamed x8, local copies, waits for them, and re-layouts  3.7 us
  transfers between devices with their start and end apart: 17, of which 6 were waited for; matrix products, arithmetic and copies ran while one was open for 7% of the time, Pallas kernels for 0%

profile of v5, /device:TPU:1, one launch (start us, length us, event | category | flops | bytes accessed | tf_op | source)
XLA Modules:
  0.0 148.9 jit_solution(10840381469484670354)
XLA Ops:
  0.6 1.0 fusion.47
  2.3 1.8 %copy.8 = bf16[32,8,2048]{2,0,1:T(8,128)(2,1)S(1)} copy(bf16[32,8,2048]{2,1,0:T(8,128)(2,1)} %param.5) | data formatting | bytes 2097152 | tf_op args[0]
  4.1 3.0 %subtract_convert_fusion = (bf16[32,64,1024]{2,1,0:T(8,128)(2,1)S(1)}, bf16[32,64,1024]{2,1,0:T(8,128)(2,1)S(1)}) fusion(f32[64,1024]{1,0:T(8,128)S(1)} %get-tuple-element.101, f32[32,1024]{1,0:T(8,128)S(1)} %get-tuple-element.98, f32[64,1024]{1,0:T(8,128)S(1)} %get-tuple-element.102, f32[32,1024]{1,0:T(8,128)S(1)} %get-tuple-element.97), kind=kLoop, calls=%fused_computation.5 | loop fusion | flops 18874368 | bytes 9175040 | tf_op jit(solution)/shard_map/convert.7
  7.1 5.0 %fusion.4 = (f32[256]{0:T(256)S(1)}, f32[2048,256]{0,1:T(8,128)}) fusion(bf16[256,2048]{1,0:T(8,128)(2,1)S(1)} %bitcast.112, bf16[2048,1024]{1,0:T(8,128)(2,1)S(1)} %bitcast.110, bf16[2048,1024]{1,0:T(8,128)(2,1)S(1)} %bitcast.109), kind=kOutput, calls=%fused_computation.16 | convolution fusion | flops 2165309184 | bytes 11535360 | tf_op jit(solution)/shard_map/dot_general | solution.py:81
  12.2 2.1 %multiply_convert_fusion = bf16[8,32,2048]{2,1,0:T(8,128)(2,1)S(1)} fusion(f32[8,32,2048]{2,1,0:T(8,128)} %bitcast.111, f32[32]{0:T(128)S(1)} %subtract_convert_fusion.1, f32[8,32]{1,0:T(8,128)S(1)} %rsqrt.12), kind=kLoop, calls=%fused_computation.17 | loop fusion | flops 1572864 | bytes 3146880 | tf_op jit(solution)/shard_map/convert_element_type | solution.py:61
  14.7 8.8 %collective-permute-start.1 = (bf16[4,32,2048]{2,1,0:T(8,128)(2,1)S(1)}, bf16[4,32,2048]{2,1,0:T(8,128)(2,1)S(1)}, u32[]{:S(2)}, u32[]{:S(2)}) collective-permute-start(bf16[4,32,2048]{2,1,0:T(8,128)(2,1)S(1)} %scatter.4), channel_id=1, source_target_pairs={{0,510},{2,0},{4,2},{6,4},{8,6},{10,8},{12,10},{14,12},{16,14},{18... | collective-permute-start | bytes 1572872 | tf_op jit(solution)/shard_map/ppermute | solution.py:13
  23.5 1.9 %collective-permute-start = (bf16[4,32,2048]{2,1,0:T(8,128)(2,1)S(1)}, bf16[4,32,2048]{2,1,0:T(8,128)(2,1)S(1)}, u32[]{:S(2)}, u32[]{:S(2)}) collective-permute-start(bf16[4,32,2048]{2,1,0:T(8,128)(2,1)S(1)} %get-tuple-element.66), channel_id=1, source_target_pairs={{0,2},{2,4},{4,6},{6,8},{8,10},{10,12},{12,14},{14,16},{16,18},{18... | collective-permute-start | bytes 1572872 | tf_op jit(solution)/shard_map/ppermute | solution.py:13
  26.4 8.9 %collective-permute-done = bf16[4,32,2048]{2,1,0:T(8,128)(2,1)S(1)} collective-permute-done((bf16[4,32,2048]{2,1,0:T(8,128)(2,1)S(1)}, bf16[4,32,2048]{2,1,0:T(8,128)(2,1)S(1)}, u32[]{:S(2)}, u32[]{:S(2)}) %collective-permute-start) | collective-permute-done | bytes 524320 | tf_op jit(solution)/shard_map/ppermute | solution.py:13
  35.4 14.8 %collective-permute-start.3 = (bf16[4,32,2048]{2,1,0:T(8,128)(2,1)S(1)}, bf16[4,32,2048]{2,1,0:T(8,128)(2,1)S(1)}, u32[]{:S(2)}, u32[]{:S(2)}) collective-permute-start(bf16[4,32,2048]{2,1,0:T(8,128)(2,1)S(1)} %collective-permute-done.1), channel_id=1, source_target_pairs={{0,510},{2,0},{4,2},{6,4},{8,6},{10,8},{12,10},{14,12},{16,14},{18... | collective-permute-start | bytes 1572872 | tf_op jit(solution)/shard_map/ppermute | solution.py:13
  50.7 1.9 %collective-permute-start.2 = (bf16[4,32,2048]{2,1,0:T(8,128)(2,1)S(1)}, bf16[4,32,2048]{2,1,0:T(8,128)(2,1)S(1)}, u32[]{:S(2)}, u32[]{:S(2)}) collective-permute-start(bf16[4,32,2048]{2,1,0:T(8,128)(2,1)S(1)} %collective-permute-done), channel_id=1, source_target_pairs={{0,2},{2,4},{4,6},{6,8},{8,10},{10,12},{12,14},{14,16},{16,18},{18... | collective-permute-start | bytes 1572872 | tf_op jit(solution)/shard_map/ppermute | solution.py:13
  53.4 1.9 %fusion.8 = f32[64,257]{1,0:T(8,128)S(1)} fusion(f32[1024,257]{1,0:T(8,128)S(1)} %bitcast.105, f32[1024,257]{1,0:T(8,128)S(1)} %bitcast.101, f32[32,1024]{1,0:T(8,128)S(1)} %get-tuple-element.63, f32[32,1024]{1,0:T(8,128)S(1)} %get-tuple-element.62, f32[32,1024]{1,0:T(8,128)S(1)} %get-tuple-element.61, f32[32,1024]{1,0:T(8,128)S(1)} %get-tuple-element.60), kind=kOutput, calls=%fused_computation.23 | convolution fusion | flops 405145600 | bytes 2695424 | tf_op jit(solution)/shard_map/dot_general | solution.py:113
  55.4 3.3 %collective-permute-done.2 = bf16[4,32,2048]{2,1,0:T(8,128)(2,1)S(1)} collective-permute-done((bf16[4,32,2048]{2,1,0:T(8,128)(2,1)S(1)}, bf16[4,32,2048]{2,1,0:T(8,128)(2,1)S(1)}, u32[]{:S(2)}, u32[]{:S(2)}) %collective-permute-start.2) | collective-permute-done | bytes 524320 | tf_op jit(solution)/shard_map/ppermute | solution.py:13
  58.9 10.1 %collective-permute-start.5 = (bf16[4,32,2048]{2,1,0:T(8,128)(2,1)S(1)}, bf16[4,32,2048]{2,1,0:T(8,128)(2,1)S(1)}, u32[]{:S(2)}, u32[]{:S(2)}) collective-permute-start(bf16[4,32,2048]{2,1,0:T(8,128)(2,1)S(1)} %collective-permute-done.3), channel_id=1, source_target_pairs={{0,510},{2,0},{4,2},{6,4},{8,6},{10,8},{12,10},{14,12},{16,14},{18... | collective-permute-start | bytes 1572872 | tf_op jit(solution)/shard_map/ppermute | solution.py:13
  69.0 1.9 %collective-permute-start.4 = (bf16[4,32,2048]{2,1,0:T(8,128)(2,1)S(1)}, bf16[4,32,2048]{2,1,0:T(8,128)(2,1)S(1)}, u32[]{:S(2)}, u32[]{:S(2)}) collective-permute-start(bf16[4,32,2048]{2,1,0:T(8,128)(2,1)S(1)} %collective-permute-done.2), channel_id=1, source_target_pairs={{0,2},{2,4},{4,6},{6,8},{8,10},{10,12},{12,14},{14,16},{16,18},{18... | collective-permute-start | bytes 1572872 | tf_op jit(solution)/shard_map/ppermute | solution.py:13
  71.5 1.9 %collective-permute-start.6 = (f32[32,257]{1,0:T(8,128)S(1)}, f32[32,257]{1,0:T(8,128)S(1)}, u32[]{:S(2)}, u32[]{:S(2)}) collective-permute-start(f32[32,257]{1,0:T(8,128)S(1)} %get-tuple-element.83), channel_id=1, source_target_pairs={{0,2},{2,4},{4,6},{6,8},{8,10},{10,12},{12,14},{14,16},{16,18},{18... | collective-permute-start | bytes 98696 | tf_op jit(solution)/shard_map/ppermute | solution.py:13
  73.5 2.6 %collective-permute-start.7 = (f32[32,257]{1,0:T(8,128)S(1)}, f32[32,257]{1,0:T(8,128)S(1)}, u32[]{:S(2)}, u32[]{:S(2)}) collective-permute-start(f32[32,257]{1,0:T(8,128)S(1)} %get-tuple-element.84), channel_id=1, source_target_pairs={{0,510},{2,0},{4,2},{6,4},{8,6},{10,8},{12,10},{14,12},{16,14},{18... | collective-permute-start | bytes 98696 | tf_op jit(solution)/shard_map/ppermute | solution.py:13
  76.7 1.9 %fusion.7 = f32[64,257]{1,0:T(8,128)S(1)} fusion(f32[1024,257]{1,0:T(8,128)S(1)} %bitcast.106, f32[1024,257]{1,0:T(8,128)S(1)} %bitcast.102, f32[32,1024]{1,0:T(8,128)S(1)} %get-tuple-element.59, f32[32,1024]{1,0:T(8,128)S(1)} %get-tuple-element.58, f32[32,1024]{1,0:T(8,128)S(1)} %get-tuple-element.57, f32[32,1024]{1,0:T(8,128)S(1)} %get-tuple-element.56), kind=kOutput, calls=%fused_computation.22 | convolution fusion | flops 405145600 | bytes 2695424 | tf_op jit(solution)/shard_map/dot_general | solution.py:113
  79.1 9.1 %collective-permute-start.9 = (bf16[4,32,2048]{2,1,0:T(8,128)(2,1)S(1)}, bf16[4,32,2048]{2,1,0:T(8,128)(2,1)S(1)}, u32[]{:S(2)}, u32[]{:S(2)}) collective-permute-start(bf16[4,32,2048]{2,1,0:T(8,128)(2,1)S(1)} %collective-permute-done.5), channel_id=1, source_target_pairs={{0,510},{2,0},{4,2},{6,4},{8,6},{10,8},{12,10},{14,12},{16,14},{18... | collective-permute-start | bytes 1572872 | tf_op jit(solution)/shard_map/ppermute | solution.py:13
  88.2 1.9 %collective-permute-start.8 = (bf16[4,32,2048]{2,1,0:T(8,128)(2,1)S(1)}, bf16[4,32,2048]{2,1,0:T(8,128)(2,1)S(1)}, u32[]{:S(2)}, u32[]{:S(2)}) collective-permute-start(bf16[4,32,2048]{2,1,0:T(8,128)(2,1)S(1)} %collective-permute-done.4), channel_id=1, source_target_pairs={{0,2},{2,4},{4,6},{6,8},{8,10},{10,12},{12,14},{14,16},{16,18},{18... | collective-permute-start | bytes 1572872 | tf_op jit(solution)/shard_map/ppermute | solution.py:13
  90.8 1.9 %collective-permute-start.10 = (f32[32,257]{1,0:T(8,128)S(1)}, f32[32,257]{1,0:T(8,128)S(1)}, u32[]{:S(2)}, u32[]{:S(2)}) collective-permute-start(f32[32,257]{1,0:T(8,128)S(1)} %get-tuple-element.87), channel_id=1, source_target_pairs={{0,4},{2,6},{4,8},{6,10},{8,12},{10,14},{12,16},{14,18},{16,20},{1... | collective-permute-start | bytes 98696 | tf_op jit(solution)/shard_map/ppermute | solution.py:13
  92.7 15.4 %collective-permute-start.11 = (f32[32,257]{1,0:T(8,128)S(1)}, f32[32,257]{1,0:T(8,128)S(1)}, u32[]{:S(2)}, u32[]{:S(2)}) collective-permute-start(f32[32,257]{1,0:T(8,128)S(1)} %get-tuple-element.88), channel_id=1, source_target_pairs={{0,508},{2,510},{4,0},{6,2},{8,4},{10,6},{12,8},{14,10},{16,12},{1... | collective-permute-start | bytes 98696 | tf_op jit(solution)/shard_map/ppermute | solution.py:13
  108.7 1.9 %fusion.6 = f32[64,257]{1,0:T(8,128)S(1)} fusion(f32[1024,257]{1,0:T(8,128)S(1)} %bitcast.107, f32[1024,257]{1,0:T(8,128)S(1)} %bitcast.103, f32[32,1024]{1,0:T(8,128)S(1)} %get-tuple-element.55, f32[32,1024]{1,0:T(8,128)S(1)} %get-tuple-element.54, f32[32,1024]{1,0:T(8,128)S(1)} %get-tuple-element.53, f32[32,1024]{1,0:T(8,128)S(1)} %get-tuple-element.52), kind=kOutput, calls=%fused_computation.21 | convolution fusion | flops 405145600 | bytes 2695424 | tf_op jit(solution)/shard_map/dot_general | solution.py:113
  112.7 1.9 %fusion.5 = f32[64,257]{1,0:T(8,128)S(1)} fusion(f32[1024,257]{1,0:T(8,128)S(1)} %bitcast.108, f32[1024,257]{1,0:T(8,128)S(1)} %bitcast.104, f32[32,1024]{1,0:T(8,128)S(1)} %get-tuple-element.51, f32[32,1024]{1,0:T(8,128)S(1)} %get-tuple-element.50, f32[32,1024]{1,0:T(8,128)S(1)} %get-tuple-element.49, f32[32,1024]{1,0:T(8,128)S(1)} %get-tuple-element.48), kind=kOutput, calls=%fused_computation.20 | convolution fusion | flops 405145600 | bytes 2695424 | tf_op jit(solution)/shard_map/dot_general | solution.py:113
  114.7 1.9 %collective-permute-start.13 = (f32[32,257]{1,0:T(8,128)S(1)}, f32[32,257]{1,0:T(8,128)S(1)}, u32[]{:S(2)}, u32[]{:S(2)}) collective-permute-start(f32[32,257]{1,0:T(8,128)S(1)} %get-tuple-element.77), channel_id=1, source_target_pairs={{0,8},{2,10},{4,12},{6,14},{8,16},{10,18},{12,20},{14,22},{16,24},... | collective-permute-start | bytes 98696 | tf_op jit(solution)/shard_map/ppermute | solution.py:13
  116.6 1.9 %collective-permute-start.12 = (f32[32,257]{1,0:T(8,128)S(1)}, f32[32,257]{1,0:T(8,128)S(1)}, u32[]{:S(2)}, u32[]{:S(2)}) collective-permute-start(f32[32,257]{1,0:T(8,128)S(1)} %get-tuple-element.73), channel_id=1, source_target_pairs={{0,6},{2,8},{4,10},{6,12},{8,14},{10,16},{12,18},{14,20},{16,22},{... | collective-permute-start | bytes 98696 | tf_op jit(solution)/shard_map/ppermute | solution.py:13
  118.6 10.0 %collective-permute-start.15 = (f32[32,257]{1,0:T(8,128)S(1)}, f32[32,257]{1,0:T(8,128)S(1)}, u32[]{:S(2)}, u32[]{:S(2)}) collective-permute-start(f32[32,257]{1,0:T(8,128)S(1)} %get-tuple-element.80), channel_id=1, source_target_pairs={{0,504},{2,506},{4,508},{6,510},{8,0},{10,2},{12,4},{14,6},{16,8},... | collective-permute-start | bytes 98696 | tf_op jit(solution)/shard_map/ppermute | solution.py:13
  128.5 3.9 %collective-permute-start.14 = (f32[32,257]{1,0:T(8,128)S(1)}, f32[32,257]{1,0:T(8,128)S(1)}, u32[]{:S(2)}, u32[]{:S(2)}) collective-permute-start(f32[32,257]{1,0:T(8,128)S(1)} %get-tuple-element.76), channel_id=1, source_target_pairs={{0,506},{2,508},{4,510},{6,0},{8,2},{10,4},{12,6},{14,8},{16,10},{... | collective-permute-start | bytes 98696 | tf_op jit(solution)/shard_map/ppermute | solution.py:13
  132.5 2.4 %collective-permute-done.14 = f32[32,257]{1,0:T(8,128)S(1)} collective-permute-done((f32[32,257]{1,0:T(8,128)S(1)}, f32[32,257]{1,0:T(8,128)S(1)}, u32[]{:S(2)}, u32[]{:S(2)}) %collective-permute-start.14) | collective-permute-done | bytes 32928 | tf_op jit(solution)/shard_map/ppermute | solution.py:13
  135.0 2.3 %collective-permute-start.16 = (f32[2,32,4,257]{3,1,2,0:T(8,128)S(1)}, f32[2,32,4,257]{3,1,2,0:T(8,128)S(1)}, u32[]{:S(2)}, u32[]{:S(2)}) collective-permute-start(f32[2,32,4,257]{3,1,2,0:T(8,128)S(1)} %pad_maximum_fusion.5), channel_id=1, source_target_pairs={{0,1},{1,0},{2,3},{3,2},{4,5},{5,4},{6,7},{7,6},{8,9},{9,8},{10,11... | collective-permute-start | bytes 789512 | tf_op jit(solution)/shard_map/ppermute | solution.py:18
  137.3 9.6 %collective-permute-done.16 = f32[2,32,4,257]{3,1,2,0:T(8,128)S(1)} collective-permute-done((f32[2,32,4,257]{3,1,2,0:T(8,128)S(1)}, f32[2,32,4,257]{3,1,2,0:T(8,128)S(1)}, u32[]{:S(2)}, u32[]{:S(2)}) %collective-permute-start.16) | collective-permute-done | bytes 263200 | tf_op jit(solution)/shard_map/ppermute | solution.py:18
  147.3 0.8 copy.11
  148.1 0.8 copy.10
  (67 shorter events, 8.9 us)
Async XLA Ops:
  7.0 5.2 %copy-start.1 = (s32[32]{0:T(128)S(1)}, s32[32]{0:T(128)}, u32[]{:S(2)}) copy-start(s32[32]{0:T(128)} %param.7) | copy-start | bytes 388
  12.2 2.3 %copy-start = (s32[4,32]{1,0:T(4,128)S(1)}, s32[4,32]{1,0:T(4,128)}, u32[]{:S(2)}) copy-start(s32[4,32]{1,0:T(4,128)} %param.6) | copy-start | bytes 1540
  14.7 11.7 %collective-permute-start.1 = (bf16[4,32,2048]{2,1,0:T(8,128)(2,1)S(1)}, bf16[4,32,2048]{2,1,0:T(8,128)(2,1)S(1)}, u32[]{:S(2)}, u32[]{:S(2)}) collective-permute-start(bf16[4,32,2048]{2,1,0:T(8,128)(2,1)S(1)} %scatter.4), channel_id=1, source_target_pairs={{0,510},{2,0},{4,2},{6,4},{8,6},{10,8},{12,10},{14,12},{16,14},{18... | collective-permute-start | bytes 1572872 | tf_op jit(solution)/shard_map/ppermute | solution.py:13
  23.5 11.8 %collective-permute-start = (bf16[4,32,2048]{2,1,0:T(8,128)(2,1)S(1)}, bf16[4,32,2048]{2,1,0:T(8,128)(2,1)S(1)}, u32[]{:S(2)}, u32[]{:S(2)}) collective-permute-start(bf16[4,32,2048]{2,1,0:T(8,128)(2,1)S(1)} %get-tuple-element.66), channel_id=1, source_target_pairs={{0,2},{2,4},{4,6},{6,8},{8,10},{10,12},{12,14},{14,16},{16,18},{18... | collective-permute-start | bytes 1572872 | tf_op jit(solution)/shard_map/ppermute | solution.py:13
  35.4 20.0 %collective-permute-start.3 = (bf16[4,32,2048]{2,1,0:T(8,128)(2,1)S(1)}, bf16[4,32,2048]{2,1,0:T(8,128)(2,1)S(1)}, u32[]{:S(2)}, u32[]{:S(2)}) collective-permute-start(bf16[4,32,2048]{2,1,0:T(8,128)(2,1)S(1)} %collective-permute-done.1), channel_id=1, source_target_pairs={{0,510},{2,0},{4,2},{6,4},{8,6},{10,8},{12,10},{14,12},{16,14},{18... | collective-permute-start | bytes 1572872 | tf_op jit(solution)/shard_map/ppermute | solution.py:13
  50.7 8.0 %collective-permute-start.2 = (bf16[4,32,2048]{2,1,0:T(8,128)(2,1)S(1)}, bf16[4,32,2048]{2,1,0:T(8,128)(2,1)S(1)}, u32[]{:S(2)}, u32[]{:S(2)}) collective-permute-start(bf16[4,32,2048]{2,1,0:T(8,128)(2,1)S(1)} %collective-permute-done), channel_id=1, source_target_pairs={{0,2},{2,4},{4,6},{6,8},{8,10},{10,12},{12,14},{14,16},{16,18},{18... | collective-permute-start | bytes 1572872 | tf_op jit(solution)/shard_map/ppermute | solution.py:13
  58.9 20.0 %collective-permute-start.5 = (bf16[4,32,2048]{2,1,0:T(8,128)(2,1)S(1)}, bf16[4,32,2048]{2,1,0:T(8,128)(2,1)S(1)}, u32[]{:S(2)}, u32[]{:S(2)}) collective-permute-start(bf16[4,32,2048]{2,1,0:T(8,128)(2,1)S(1)} %collective-permute-done.3), channel_id=1, source_target_pairs={{0,510},{2,0},{4,2},{6,4},{8,6},{10,8},{12,10},{14,12},{16,14},{18... | collective-permute-start | bytes 1572872 | tf_op jit(solution)/shard_map/ppermute | solution.py:13
  69.0 9.9 %collective-permute-start.4 = (bf16[4,32,2048]{2,1,0:T(8,128)(2,1)S(1)}, bf16[4,32,2048]{2,1,0:T(8,128)(2,1)S(1)}, u32[]{:S(2)}, u32[]{:S(2)}) collective-permute-start(bf16[4,32,2048]{2,1,0:T(8,128)(2,1)S(1)} %collective-permute-done.2), channel_id=1, source_target_pairs={{0,2},{2,4},{4,6},{6,8},{8,10},{10,12},{12,14},{14,16},{16,18},{18... | collective-permute-start | bytes 1572872 | tf_op jit(solution)/shard_map/ppermute | solution.py:13
  71.5 7.1 %collective-permute-start.6 = (f32[32,257]{1,0:T(8,128)S(1)}, f32[32,257]{1,0:T(8,128)S(1)}, u32[]{:S(2)}, u32[]{:S(2)}) collective-permute-start(f32[32,257]{1,0:T(8,128)S(1)} %get-tuple-element.83), channel_id=1, source_target_pairs={{0,2},{2,4},{4,6},{6,8},{8,10},{10,12},{12,14},{14,16},{16,18},{18... | collective-permute-start | bytes 98696 | tf_op jit(solution)/shard_map/ppermute | solution.py:13
  73.5 5.4 %collective-permute-start.7 = (f32[32,257]{1,0:T(8,128)S(1)}, f32[32,257]{1,0:T(8,128)S(1)}, u32[]{:S(2)}, u32[]{:S(2)}) collective-permute-start(f32[32,257]{1,0:T(8,128)S(1)} %get-tuple-element.84), channel_id=1, source_target_pairs={{0,510},{2,0},{4,2},{6,4},{8,6},{10,8},{12,10},{14,12},{16,14},{18... | collective-permute-start | bytes 98696 | tf_op jit(solution)/shard_map/ppermute | solution.py:13
  79.1 32.2 %collective-permute-start.9 = (bf16[4,32,2048]{2,1,0:T(8,128)(2,1)S(1)}, bf16[4,32,2048]{2,1,0:T(8,128)(2,1)S(1)}, u32[]{:S(2)}, u32[]{:S(2)}) collective-permute-start(bf16[4,32,2048]{2,1,0:T(8,128)(2,1)S(1)} %collective-permute-done.5), channel_id=1, source_target_pairs={{0,510},{2,0},{4,2},{6,4},{8,6},{10,8},{12,10},{14,12},{16,14},{18... | collective-permute-start | bytes 1572872 | tf_op jit(solution)/shard_map/ppermute | solution.py:13
  88.2 23.1 %collective-permute-start.8 = (bf16[4,32,2048]{2,1,0:T(8,128)(2,1)S(1)}, bf16[4,32,2048]{2,1,0:T(8,128)(2,1)S(1)}, u32[]{:S(2)}, u32[]{:S(2)}) collective-permute-start(bf16[4,32,2048]{2,1,0:T(8,128)(2,1)S(1)} %collective-permute-done.4), channel_id=1, source_target_pairs={{0,2},{2,4},{4,6},{6,8},{8,10},{10,12},{12,14},{14,16},{16,18},{18... | collective-permute-start | bytes 1572872 | tf_op jit(solution)/shard_map/ppermute | solution.py:13
  90.8 20.5 %collective-permute-start.10 = (f32[32,257]{1,0:T(8,128)S(1)}, f32[32,257]{1,0:T(8,128)S(1)}, u32[]{:S(2)}, u32[]{:S(2)}) collective-permute-start(f32[32,257]{1,0:T(8,128)S(1)} %get-tuple-element.87), channel_id=1, source_target_pairs={{0,4},{2,6},{4,8},{6,10},{8,12},{10,14},{12,16},{14,18},{16,20},{1... | collective-permute-start | bytes 98696 | tf_op jit(solution)/shard_map/ppermute | solution.py:13
  92.7 18.6 %collective-permute-start.11 = (f32[32,257]{1,0:T(8,128)S(1)}, f32[32,257]{1,0:T(8,128)S(1)}, u32[]{:S(2)}, u32[]{:S(2)}) collective-permute-start(f32[32,257]{1,0:T(8,128)S(1)} %get-tuple-element.88), channel_id=1, source_target_pairs={{0,508},{2,510},{4,0},{6,2},{8,4},{10,6},{12,8},{14,10},{16,12},{1... | collective-permute-start | bytes 98696 | tf_op jit(solution)/shard_map/ppermute | solution.py:13
  114.7 17.8 %collective-permute-start.13 = (f32[32,257]{1,0:T(8,128)S(1)}, f32[32,257]{1,0:T(8,128)S(1)}, u32[]{:S(2)}, u32[]{:S(2)}) collective-permute-start(f32[32,257]{1,0:T(8,128)S(1)} %get-tuple-element.77), channel_id=1, source_target_pairs={{0,8},{2,10},{4,12},{6,14},{8,16},{10,18},{12,20},{14,22},{16,24},... | collective-permute-start | bytes 98696 | tf_op jit(solution)/shard_map/ppermute | solution.py:13
  116.6 15.9 %collective-permute-start.12 = (f32[32,257]{1,0:T(8,128)S(1)}, f32[32,257]{1,0:T(8,128)S(1)}, u32[]{:S(2)}, u32[]{:S(2)}) collective-permute-start(f32[32,257]{1,0:T(8,128)S(1)} %get-tuple-element.73), channel_id=1, source_target_pairs={{0,6},{2,8},{4,10},{6,12},{8,14},{10,16},{12,18},{14,20},{16,22},{... | collective-permute-start | bytes 98696 | tf_op jit(solution)/shard_map/ppermute | solution.py:13
  118.6 14.0 %collective-permute-start.15 = (f32[32,257]{1,0:T(8,128)S(1)}, f32[32,257]{1,0:T(8,128)S(1)}, u32[]{:S(2)}, u32[]{:S(2)}) collective-permute-start(f32[32,257]{1,0:T(8,128)S(1)} %get-tuple-element.80), channel_id=1, source_target_pairs={{0,504},{2,506},{4,508},{6,510},{8,0},{10,2},{12,4},{14,6},{16,8},... | collective-permute-start | bytes 98696 | tf_op jit(solution)/shard_map/ppermute | solution.py:13
  128.5 6.4 %collective-permute-start.14 = (f32[32,257]{1,0:T(8,128)S(1)}, f32[32,257]{1,0:T(8,128)S(1)}, u32[]{:S(2)}, u32[]{:S(2)}) collective-permute-start(f32[32,257]{1,0:T(8,128)S(1)} %get-tuple-element.76), channel_id=1, source_target_pairs={{0,506},{2,508},{4,510},{6,0},{8,2},{10,4},{12,6},{14,8},{16,10},{... | collective-permute-start | bytes 98696 | tf_op jit(solution)/shard_map/ppermute | solution.py:13
  135.0 11.8 %collective-permute-start.16 = (f32[2,32,4,257]{3,1,2,0:T(8,128)S(1)}, f32[2,32,4,257]{3,1,2,0:T(8,128)S(1)}, u32[]{:S(2)}, u32[]{:S(2)}) collective-permute-start(f32[2,32,4,257]{3,1,2,0:T(8,128)S(1)} %pad_maximum_fusion.5), channel_id=1, source_target_pairs={{0,1},{1,0},{2,3},{3,2},{4,5},{5,4},{6,7},{7,6},{8,9},{9,8},{10,11... | collective-permute-start | bytes 789512 | tf_op jit(solution)/shard_map/ppermute | solution.py:18

commit v6 on v4

--- a/solution.py
+++ b/solution.py
@@ -93,31 +93,39 @@
     moving_ahead = ahead
     moving_behind = behind.at[:stops, :, half_len].set(offsets.astype(jnp.bfloat16))
     back_table = inverse_table(length, LAGS)
-    own_parts, later_parts, from_earlier, from_later = [], [], [], []
-    lags = jnp.zeros((2 * channels, back_table.shape[1]), jnp.float32)
-    for stop in range(1, stops + 1):
-        moving_ahead, moving_behind, lags = lax.optimization_barrier(
-            (shifted(moving_ahead, "blk", 1), shifted(moving_behind, "blk", -1), lags)
-        )
-        if stop > 1:
-            own_parts.append(lags[:channels])
-            later_parts.append(lags[channels:])
-            from_earlier.append(shifted(lags[channels:], "blk", stop - 1))
-            from_later.append(shifted(lags[:channels], "blk", 1 - stop))
-        own = cross_spectrum(ahead_f32, pick_rows(offsets[stop - 1], moving_ahead), half_len)
-        later_offsets = moving_behind[stop - 1, :, half_len].astype(jnp.int32)
-        later = jnp.where(dc_imag, jnp.zeros_like(moving_behind), moving_behind).astype(jnp.float32)
+
+    def lags_of(stop, earlier, later):
+        own = cross_spectrum(ahead_f32, pick_rows(offsets[stop - 1], earlier), half_len)
+        later_offsets = later[stop - 1, :, half_len].astype(jnp.int32)
+        later = jnp.where(dc_imag, jnp.zeros_like(later), later).astype(jnp.float32)
         later = cross_spectrum(later, pick_rows(later_offsets, behind), half_len)
-        lags = jnp.dot(
+        return jnp.dot(
             jnp.concatenate([own, later], axis=0),
             back_table,
             precision=lax.Precision.HIGHEST,
             preferred_element_type=jnp.float32,
         )
-    own_parts.append(lags[:channels])
-    later_parts.append(lags[channels:])
-    from_earlier.append(shifted(lags[channels:], "blk", stops))
-    from_later.append(shifted(lags[:channels], "blk", -stops))
+
+    near = stops // 2
+    first = lax.optimization_barrier(
+        tuple(shifted(moving_ahead, "blk", d) for d in range(1, near + 1))
+        + tuple(shifted(moving_behind, "blk", -d) for d in range(1, near + 1))
+    )
+    lags = [lags_of(d, first[d - 1], first[near + d - 1]) for d in range(1, near + 1)]
+    far_ahead, far_behind, lags = lax.optimization_barrier(
+        (
+            shifted(jnp.concatenate(first[:near], axis=0), "blk", near),
+            shifted(jnp.concatenate(first[near:], axis=0), "blk", -near),
+            lags,
+        )
+    )
+    for d in range(near + 1, stops + 1):
+        at = (d - near - 1) * split
+        lags.append(lags_of(d, far_ahead[at:at + split], far_behind[at:at + split]))
+    own_parts = [piece[:channels] for piece in lags]
+    later_parts = [piece[channels:] for piece in lags]
+    from_earlier = [shifted(piece[channels:], "blk", d) for d, piece in enumerate(lags, 1)]
+    from_later = [shifted(piece[:channels], "blk", -d) for d, piece in enumerate(lags, 1)]
     corr_part = jnp.stack(own_parts, axis=1) + jnp.stack(from_earlier, axis=1)
     mirror_part = jnp.stack(from_later, axis=1) + jnp.stack(later_parts, axis=1)
     parts = jnp.stack([corr_part, mirror_part], axis=0)

time: 143 us -> 144 us (level); the launches traced: 141 us -> 144 us
  waiting for transfers between devices: 26 us -> 54.1 us
  starting transfers between devices: 87.8 us -> 62.2 us
    ppermute x16 -> x14, waiting for transfers between devices: 17.6 us -> 44.7 us  [shifted(): lax.ppermute(x, axis, [(i, (i + by) % length) for i in range(length)])]
    ppermute x16 -> x14, starting transfers between devices: 85.6 us -> 60 us  [shifted(): lax.ppermute(x, axis, [(i, (i + by) % length) for i in range(length)])]
  transfers between devices with their start and end apart: 17 -> 15, of which waited for: 6 -> 7; matrix products, arithmetic and copies ran while one was open for 10% -> 6% of each run, Pallas kernels for 0% -> 0%
where the time goes in v6:
time: 144 us
  starting transfers between devices  62.2 us (43%)
  waiting for transfers between devices  54.1 us (38%)
  matrix products  13 us (9%)
  other arithmetic  9.11 us (6%)
  local copies, waits for them, and re-layouts  4.05 us (3%)
    ppermute x14, starting transfers between devices, shifted(): lax.ppermute(x, axis, [(i, (i + by) % length) for i in range(length)])  60 us
    ppermute x14, waiting for transfers between devices, shifted(): lax.ppermute(x, axis, [(i, (i + by) % length) for i in range(length)])  44.7 us
    ppermute x1, waiting for transfers between devices, swapped(): return lax.ppermute(x, axis, [(i, i ^ 1) for i in range(length)])  9.47 us
    dot_general x4, matrix products, lags_of(): jnp.dot(jnp.concatenate([own, later], axis=0), back_table, precision=lax....  7.79 us
    unnamed x8, local copies, waits for them, and re-layouts  3.71 us
    another operation x2, other arithmetic  2.96 us
  transfers between devices with their start and end apart: 15, of which 7 were waited for; matrix products, arithmetic and copies ran while one was open for 6% of the time, Pallas kernels for 0%

profile of v6, /device:TPU:1, one launch (start us, length us, event | category | flops | bytes accessed | tf_op | source)
XLA Modules:
  0.0 143.6 jit_solution(9787951787320755644)
XLA Ops:
  0.6 1.0 fusion.47
  2.3 1.8 %copy.8 = bf16[32,8,2048]{2,0,1:T(8,128)(2,1)S(1)} copy(bf16[32,8,2048]{2,1,0:T(8,128)(2,1)} %param.5) | data formatting | bytes 2097152 | tf_op args[0]
  4.1 3.0 %subtract_convert_fusion = (bf16[32,64,1024]{2,1,0:T(8,128)(2,1)S(1)}, bf16[32,64,1024]{2,1,0:T(8,128)(2,1)S(1)}) fusion(f32[64,1024]{1,0:T(8,128)S(1)} %get-tuple-element.97, f32[32,1024]{1,0:T(8,128)S(1)} %get-tuple-element.94, f32[64,1024]{1,0:T(8,128)S(1)} %get-tuple-element.98, f32[32,1024]{1,0:T(8,128)S(1)} %get-tuple-element.93), kind=kLoop, calls=%fused_computation.5 | loop fusion | flops 18874368 | bytes 9175040 | tf_op jit(solution)/shard_map/convert.7
  7.1 2.5 %fusion.4 = (f32[256]{0:T(256)S(1)}, f32[2048,256]{0,1:T(8,128)S(1)}) fusion(bf16[256,2048]{1,0:T(8,128)(2,1)S(1)} %bitcast.112, bf16[2048,1024]{1,0:T(8,128)(2,1)S(1)} %bitcast.110, bf16[2048,1024]{1,0:T(8,128)(2,1)S(1)} %bitcast.109), kind=kOutput, calls=%fused_computation.16 | convolution fusion | flops 2165309184 | bytes 11535360 | tf_op jit(solution)/shard_map/dot_general | solution.py:81
  10.6 8.8 %collective-permute-start.2 = (bf16[4,32,2048]{2,1,0:T(8,128)(2,1)S(1)}, bf16[4,32,2048]{2,1,0:T(8,128)(2,1)S(1)}, u32[]{:S(2)}, u32[]{:S(2)}) collective-permute-start(bf16[4,32,2048]{2,1,0:T(8,128)(2,1)S(1)} %scatter.4), channel_id=1, source_target_pairs={{0,510},{2,0},{4,2},{6,4},{8,6},{10,8},{12,10},{14,12},{16,14},{18... | collective-permute-start | bytes 1572872 | tf_op jit(solution)/shard_map/ppermute | solution.py:13
  19.4 10.7 %collective-permute-start.3 = (bf16[4,32,2048]{2,1,0:T(8,128)(2,1)S(1)}, bf16[4,32,2048]{2,1,0:T(8,128)(2,1)S(1)}, u32[]{:S(2)}, u32[]{:S(2)}) collective-permute-start(bf16[4,32,2048]{2,1,0:T(8,128)(2,1)S(1)} %scatter.4), channel_id=1, source_target_pairs={{0,508},{2,510},{4,0},{6,2},{8,4},{10,6},{12,8},{14,10},{16,12},{1... | collective-permute-start | bytes 1572872 | tf_op jit(solution)/shard_map/ppermute | solution.py:13
  30.0 3.3 %collective-permute-start = (bf16[4,32,2048]{2,1,0:T(8,128)(2,1)S(1)}, bf16[4,32,2048]{2,1,0:T(8,128)(2,1)S(1)}, u32[]{:S(2)}, u32[]{:S(2)}) collective-permute-start(bf16[4,32,2048]{2,1,0:T(8,128)(2,1)S(1)} %get-tuple-element.60), channel_id=1, source_target_pairs={{0,2},{2,4},{4,6},{6,8},{8,10},{10,12},{12,14},{14,16},{16,18},{18... | collective-permute-start | bytes 1572872 | tf_op jit(solution)/shard_map/ppermute | solution.py:13
  33.3 1.9 %collective-permute-start.1 = (bf16[4,32,2048]{2,1,0:T(8,128)(2,1)S(1)}, bf16[4,32,2048]{2,1,0:T(8,128)(2,1)S(1)}, u32[]{:S(2)}, u32[]{:S(2)}) collective-permute-start(bf16[4,32,2048]{2,1,0:T(8,128)(2,1)S(1)} %get-tuple-element.60), channel_id=1, source_target_pairs={{0,4},{2,6},{4,8},{6,10},{8,12},{10,14},{12,16},{14,18},{16,20},{1... | collective-permute-start | bytes 1572872 | tf_op jit(solution)/shard_map/ppermute | solution.py:13
  36.2 5.6 %collective-permute-done.3 = bf16[4,32,2048]{2,1,0:T(8,128)(2,1)S(1)} collective-permute-done((bf16[4,32,2048]{2,1,0:T(8,128)(2,1)S(1)}, bf16[4,32,2048]{2,1,0:T(8,128)(2,1)S(1)}, u32[]{:S(2)}, u32[]{:S(2)}) %collective-permute-start.3) | collective-permute-done | bytes 524320 | tf_op jit(solution)/shard_map/ppermute | solution.py:13
  41.8 0.6 collective-permute-done
  42.4 15.4 %collective-permute-done.1 = bf16[4,32,2048]{2,1,0:T(8,128)(2,1)S(1)} collective-permute-done((bf16[4,32,2048]{2,1,0:T(8,128)(2,1)S(1)}, bf16[4,32,2048]{2,1,0:T(8,128)(2,1)S(1)}, u32[]{:S(2)}, u32[]{:S(2)}) %collective-permute-start.1) | collective-permute-done | bytes 524320 | tf_op jit(solution)/shard_map/ppermute | solution.py:13
  59.5 1.9 %collective-permute-start.5 = (bf16[8,32,2048]{2,1,0:T(8,128)(2,1)S(1)}, bf16[8,32,2048]{2,1,0:T(8,128)(2,1)S(1)}, u32[]{:S(2)}, u32[]{:S(2)}) collective-permute-start(bf16[8,32,2048]{2,1,0:T(8,128)(2,1)S(1)} %pad_maximum_fusion.6), channel_id=1, source_target_pairs={{0,508},{2,510},{4,0},{6,2},{8,4},{10,6},{12,8},{14,10},{16,12},{1... | collective-permute-start | bytes 3145736 | tf_op jit(solution)/shard_map/ppermute | solution.py:13
  61.4 3.5 %collective-permute-start.4 = (bf16[8,32,2048]{2,1,0:T(8,128)(2,1)S(1)}, bf16[8,32,2048]{2,1,0:T(8,128)(2,1)S(1)}, u32[]{:S(2)}, u32[]{:S(2)}) collective-permute-start(bf16[8,32,2048]{2,1,0:T(8,128)(2,1)S(1)} %pad_maximum_fusion.5), channel_id=1, source_target_pairs={{0,4},{2,6},{4,8},{6,10},{8,12},{10,14},{12,16},{14,18},{16,20},{1... | collective-permute-start | bytes 3145736 | tf_op jit(solution)/shard_map/ppermute | solution.py:13
  65.7 1.9 %fusion.7 = f32[64,257]{1,0:T(8,128)S(1)} fusion(f32[1024,257]{1,0:T(8,128)S(1)} %bitcast.105, f32[1024,257]{1,0:T(8,128)S(1)} %bitcast.101, f32[32,1024]{1,0:T(8,128)S(1)} %get-tuple-element.45, f32[32,1024]{1,0:T(8,128)S(1)} %get-tuple-element.44, f32[32,1024]{1,0:T(8,128)S(1)} %get-tuple-element.43, f32[32,1024]{1,0:T(8,128)S(1)} %get-tuple-element.42), kind=kOutput, calls=%fused_computation.22 | convolution fusion | flops 405145600 | bytes 2695424 | tf_op jit(solution)/shard_map/dot_general | solution.py:102
  68.2 1.9 %fusion.8 = f32[64,257]{1,0:T(8,128)S(1)} fusion(f32[1024,257]{1,0:T(8,128)S(1)} %bitcast.106, f32[1024,257]{1,0:T(8,128)S(1)} %bitcast.102, f32[32,1024]{1,0:T(8,128)S(1)} %get-tuple-element.49, f32[32,1024]{1,0:T(8,128)S(1)} %get-tuple-element.48, f32[32,1024]{1,0:T(8,128)S(1)} %get-tuple-element.54, f32[32,1024]{1,0:T(8,128)S(1)} %get-tuple-element.55), kind=kOutput, calls=%fused_computation.23 | convolution fusion | flops 405145600 | bytes 2695424 | tf_op jit(solution)/shard_map/dot_general | solution.py:102
  70.2 14.5 %collective-permute-done.5 = bf16[8,32,2048]{2,1,0:T(8,128)(2,1)S(1)} collective-permute-done((bf16[8,32,2048]{2,1,0:T(8,128)(2,1)S(1)}, bf16[8,32,2048]{2,1,0:T(8,128)(2,1)S(1)}, u32[]{:S(2)}, u32[]{:S(2)}) %collective-permute-start.5) | collective-permute-done | bytes 1048608 | tf_op jit(solution)/shard_map/ppermute | solution.py:13
  84.7 7.4 %collective-permute-done.4 = bf16[8,32,2048]{2,1,0:T(8,128)(2,1)S(1)} collective-permute-done((bf16[8,32,2048]{2,1,0:T(8,128)(2,1)S(1)}, bf16[8,32,2048]{2,1,0:T(8,128)(2,1)S(1)}, u32[]{:S(2)}, u32[]{:S(2)}) %collective-permute-start.4) | collective-permute-done | bytes 1048608 | tf_op jit(solution)/shard_map/ppermute | solution.py:13
  94.0 1.9 %fusion.6 = f32[64,257]{1,0:T(8,128)S(1)} fusion(f32[1024,257]{1,0:T(8,128)S(1)} %bitcast.107, f32[1024,257]{1,0:T(8,128)S(1)} %bitcast.103, f32[32,1024]{1,0:T(8,128)S(1)} %get-tuple-element.37, f32[32,1024]{1,0:T(8,128)S(1)} %get-tuple-element.36, f32[32,1024]{1,0:T(8,128)S(1)} %get-tuple-element.35, f32[32,1024]{1,0:T(8,128)S(1)} %get-tuple-element.34), kind=kOutput, calls=%fused_computation.21 | convolution fusion | flops 405145600 | bytes 2695424 | tf_op jit(solution)/shard_map/dot_general | solution.py:102
  96.0 1.9 %collective-permute-start.8 = (f32[32,257]{1,0:T(8,128)S(1)}, f32[32,257]{1,0:T(8,128)S(1)}, u32[]{:S(2)}, u32[]{:S(2)}) collective-permute-start(f32[32,257]{1,0:T(8,128)S(1)} %get-tuple-element.75), channel_id=1, source_target_pairs={{0,6},{2,8},{4,10},{6,12},{8,14},{10,16},{12,18},{14,20},{16,22},{... | collective-permute-start | bytes 98696 | tf_op jit(solution)/shard_map/ppermute | solution.py:13
  98.5 1.9 %fusion.5 = f32[64,257]{1,0:T(8,128)S(1)} fusion(f32[1024,257]{1,0:T(8,128)S(1)} %bitcast.108, f32[1024,257]{1,0:T(8,128)S(1)} %bitcast.104, f32[32,1024]{1,0:T(8,128)S(1)} %get-tuple-element.41, f32[32,1024]{1,0:T(8,128)S(1)} %get-tuple-element.40, f32[32,1024]{1,0:T(8,128)S(1)} %get-tuple-element.50, f32[32,1024]{1,0:T(8,128)S(1)} %get-tuple-element.51), kind=kOutput, calls=%fused_computation.20 | convolution fusion | flops 405145600 | bytes 2695424 | tf_op jit(solution)/shard_map/dot_general | solution.py:102
  100.5 1.9 %collective-permute-start.9 = (f32[32,257]{1,0:T(8,128)S(1)}, f32[32,257]{1,0:T(8,128)S(1)}, u32[]{:S(2)}, u32[]{:S(2)}) collective-permute-start(f32[32,257]{1,0:T(8,128)S(1)} %get-tuple-element.79), channel_id=1, source_target_pairs={{0,8},{2,10},{4,12},{6,14},{8,16},{10,18},{12,20},{14,22},{16,24},... | collective-permute-start | bytes 98696 | tf_op jit(solution)/shard_map/ppermute | solution.py:13
  102.5 1.9 %collective-permute-start.6 = (f32[32,257]{1,0:T(8,128)S(1)}, f32[32,257]{1,0:T(8,128)S(1)}, u32[]{:S(2)}, u32[]{:S(2)}) collective-permute-start(f32[32,257]{1,0:T(8,128)S(1)} %get-tuple-element.67), channel_id=1, source_target_pairs={{0,2},{2,4},{4,6},{6,8},{8,10},{10,12},{12,14},{14,16},{16,18},{18... | collective-permute-start | bytes 98696 | tf_op jit(solution)/shard_map/ppermute | solution.py:13
  104.4 1.9 %collective-permute-start.7 = (f32[32,257]{1,0:T(8,128)S(1)}, f32[32,257]{1,0:T(8,128)S(1)}, u32[]{:S(2)}, u32[]{:S(2)}) collective-permute-start(f32[32,257]{1,0:T(8,128)S(1)} %get-tuple-element.71), channel_id=1, source_target_pairs={{0,4},{2,6},{4,8},{6,10},{8,12},{10,14},{12,16},{14,18},{16,20},{1... | collective-permute-start | bytes 98696 | tf_op jit(solution)/shard_map/ppermute | solution.py:13
  106.4 9.7 %collective-permute-start.12 = (f32[32,257]{1,0:T(8,128)S(1)}, f32[32,257]{1,0:T(8,128)S(1)}, u32[]{:S(2)}, u32[]{:S(2)}) collective-permute-start(f32[32,257]{1,0:T(8,128)S(1)} %get-tuple-element.78), channel_id=1, source_target_pairs={{0,506},{2,508},{4,510},{6,0},{8,2},{10,4},{12,6},{14,8},{16,10},{... | collective-permute-start | bytes 98696 | tf_op jit(solution)/shard_map/ppermute | solution.py:13
  116.1 4.3 %collective-permute-start.13 = (f32[32,257]{1,0:T(8,128)S(1)}, f32[32,257]{1,0:T(8,128)S(1)}, u32[]{:S(2)}, u32[]{:S(2)}) collective-permute-start(f32[32,257]{1,0:T(8,128)S(1)} %get-tuple-element.82), channel_id=1, source_target_pairs={{0,504},{2,506},{4,508},{6,510},{8,0},{10,2},{12,4},{14,6},{16,8},... | collective-permute-start | bytes 98696 | tf_op jit(solution)/shard_map/ppermute | solution.py:13
  120.4 3.6 %collective-permute-start.10 = (f32[32,257]{1,0:T(8,128)S(1)}, f32[32,257]{1,0:T(8,128)S(1)}, u32[]{:S(2)}, u32[]{:S(2)}) collective-permute-start(f32[32,257]{1,0:T(8,128)S(1)} %get-tuple-element.70), channel_id=1, source_target_pairs={{0,510},{2,0},{4,2},{6,4},{8,6},{10,8},{12,10},{14,12},{16,14},{18... | collective-permute-start | bytes 98696 | tf_op jit(solution)/shard_map/ppermute | solution.py:13
  124.1 4.6 %collective-permute-start.11 = (f32[32,257]{1,0:T(8,128)S(1)}, f32[32,257]{1,0:T(8,128)S(1)}, u32[]{:S(2)}, u32[]{:S(2)}) collective-permute-start(f32[32,257]{1,0:T(8,128)S(1)} %get-tuple-element.74), channel_id=1, source_target_pairs={{0,508},{2,510},{4,0},{6,2},{8,4},{10,6},{12,8},{14,10},{16,12},{1... | collective-permute-start | bytes 98696 | tf_op jit(solution)/shard_map/ppermute | solution.py:13
  128.7 1.1 collective-permute-done.11
  129.9 2.2 %collective-permute-start.14 = (f32[2,32,4,257]{3,1,2,0:T(8,128)S(1)}, f32[2,32,4,257]{3,1,2,0:T(8,128)S(1)}, u32[]{:S(2)}, u32[]{:S(2)}) collective-permute-start(f32[2,32,4,257]{3,1,2,0:T(8,128)S(1)} %pad_maximum_fusion.7), channel_id=1, source_target_pairs={{0,1},{1,0},{2,3},{3,2},{4,5},{5,4},{6,7},{7,6},{8,9},{9,8},{10,11... | collective-permute-start | bytes 789512 | tf_op jit(solution)/shard_map/ppermute | solution.py:18
  132.1 9.5 %collective-permute-done.14 = f32[2,32,4,257]{3,1,2,0:T(8,128)S(1)} collective-permute-done((f32[2,32,4,257]{3,1,2,0:T(8,128)S(1)}, f32[2,32,4,257]{3,1,2,0:T(8,128)S(1)}, u32[]{:S(2)}, u32[]{:S(2)}) %collective-permute-start.14) | collective-permute-done | bytes 263200 | tf_op jit(solution)/shard_map/ppermute | solution.py:18
  142.0 0.8 copy.11
  142.8 0.8 copy.10
  (60 shorter events, 8.5 us)
Async XLA Ops:
  7.0 2.6 %copy-start.1 = (s32[32]{0:T(128)S(1)}, s32[32]{0:T(128)}, u32[]{:S(2)}) copy-start(s32[32]{0:T(128)} %param.7) | copy-start | bytes 388
  9.6 0.7 copy-start
  10.6 25.6 %collective-permute-start.2 = (bf16[4,32,2048]{2,1,0:T(8,128)(2,1)S(1)}, bf16[4,32,2048]{2,1,0:T(8,128)(2,1)S(1)}, u32[]{:S(2)}, u32[]{:S(2)}) collective-permute-start(bf16[4,32,2048]{2,1,0:T(8,128)(2,1)S(1)} %scatter.4), channel_id=1, source_target_pairs={{0,510},{2,0},{4,2},{6,4},{8,6},{10,8},{12,10},{14,12},{16,14},{18... | collective-permute-start | bytes 1572872 | tf_op jit(solution)/shard_map/ppermute | solution.py:13
  19.4 22.5 %collective-permute-start.3 = (bf16[4,32,2048]{2,1,0:T(8,128)(2,1)S(1)}, bf16[4,32,2048]{2,1,0:T(8,128)(2,1)S(1)}, u32[]{:S(2)}, u32[]{:S(2)}) collective-permute-start(bf16[4,32,2048]{2,1,0:T(8,128)(2,1)S(1)} %scatter.4), channel_id=1, source_target_pairs={{0,508},{2,510},{4,0},{6,2},{8,4},{10,6},{12,8},{14,10},{16,12},{1... | collective-permute-start | bytes 1572872 | tf_op jit(solution)/shard_map/ppermute | solution.py:13
  30.0 12.4 %collective-permute-start = (bf16[4,32,2048]{2,1,0:T(8,128)(2,1)S(1)}, bf16[4,32,2048]{2,1,0:T(8,128)(2,1)S(1)}, u32[]{:S(2)}, u32[]{:S(2)}) collective-permute-start(bf16[4,32,2048]{2,1,0:T(8,128)(2,1)S(1)} %get-tuple-element.60), channel_id=1, source_target_pairs={{0,2},{2,4},{4,6},{6,8},{8,10},{10,12},{12,14},{14,16},{16,18},{18... | collective-permute-start | bytes 1572872 | tf_op jit(solution)/shard_map/ppermute | solution.py:13
  33.3 24.6 %collective-permute-start.1 = (bf16[4,32,2048]{2,1,0:T(8,128)(2,1)S(1)}, bf16[4,32,2048]{2,1,0:T(8,128)(2,1)S(1)}, u32[]{:S(2)}, u32[]{:S(2)}) collective-permute-start(bf16[4,32,2048]{2,1,0:T(8,128)(2,1)S(1)} %get-tuple-element.60), channel_id=1, source_target_pairs={{0,4},{2,6},{4,8},{6,10},{8,12},{10,14},{12,16},{14,18},{16,20},{1... | collective-permute-start | bytes 1572872 | tf_op jit(solution)/shard_map/ppermute | solution.py:13
  59.5 25.2 %collective-permute-start.5 = (bf16[8,32,2048]{2,1,0:T(8,128)(2,1)S(1)}, bf16[8,32,2048]{2,1,0:T(8,128)(2,1)S(1)}, u32[]{:S(2)}, u32[]{:S(2)}) collective-permute-start(bf16[8,32,2048]{2,1,0:T(8,128)(2,1)S(1)} %pad_maximum_fusion.6), channel_id=1, source_target_pairs={{0,508},{2,510},{4,0},{6,2},{8,4},{10,6},{12,8},{14,10},{16,12},{1... | collective-permute-start | bytes 3145736 | tf_op jit(solution)/shard_map/ppermute | solution.py:13
  61.4 30.6 %collective-permute-start.4 = (bf16[8,32,2048]{2,1,0:T(8,128)(2,1)S(1)}, bf16[8,32,2048]{2,1,0:T(8,128)(2,1)S(1)}, u32[]{:S(2)}, u32[]{:S(2)}) collective-permute-start(bf16[8,32,2048]{2,1,0:T(8,128)(2,1)S(1)} %pad_maximum_fusion.5), channel_id=1, source_target_pairs={{0,4},{2,6},{4,8},{6,10},{8,12},{10,14},{12,16},{14,18},{16,20},{1... | collective-permute-start | bytes 3145736 | tf_op jit(solution)/shard_map/ppermute | solution.py:13
  96.0 20.1 %collective-permute-start.8 = (f32[32,257]{1,0:T(8,128)S(1)}, f32[32,257]{1,0:T(8,128)S(1)}, u32[]{:S(2)}, u32[]{:S(2)}) collective-permute-start(f32[32,257]{1,0:T(8,128)S(1)} %get-tuple-element.75), channel_id=1, source_target_pairs={{0,6},{2,8},{4,10},{6,12},{8,14},{10,16},{12,18},{14,20},{16,22},{... | collective-permute-start | bytes 98696 | tf_op jit(solution)/shard_map/ppermute | solution.py:13
  100.5 19.9 %collective-permute-start.9 = (f32[32,257]{1,0:T(8,128)S(1)}, f32[32,257]{1,0:T(8,128)S(1)}, u32[]{:S(2)}, u32[]{:S(2)}) collective-permute-start(f32[32,257]{1,0:T(8,128)S(1)} %get-tuple-element.79), channel_id=1, source_target_pairs={{0,8},{2,10},{4,12},{6,14},{8,16},{10,18},{12,20},{14,22},{16,24},... | collective-permute-start | bytes 98696 | tf_op jit(solution)/shard_map/ppermute | solution.py:13
  102.5 21.6 %collective-permute-start.6 = (f32[32,257]{1,0:T(8,128)S(1)}, f32[32,257]{1,0:T(8,128)S(1)}, u32[]{:S(2)}, u32[]{:S(2)}) collective-permute-start(f32[32,257]{1,0:T(8,128)S(1)} %get-tuple-element.67), channel_id=1, source_target_pairs={{0,2},{2,4},{4,6},{6,8},{8,10},{10,12},{12,14},{14,16},{16,18},{18... | collective-permute-start | bytes 98696 | tf_op jit(solution)/shard_map/ppermute | solution.py:13
  104.4 24.2 %collective-permute-start.7 = (f32[32,257]{1,0:T(8,128)S(1)}, f32[32,257]{1,0:T(8,128)S(1)}, u32[]{:S(2)}, u32[]{:S(2)}) collective-permute-start(f32[32,257]{1,0:T(8,128)S(1)} %get-tuple-element.71), channel_id=1, source_target_pairs={{0,4},{2,6},{4,8},{6,10},{8,12},{10,14},{12,16},{14,18},{16,20},{1... | collective-permute-start | bytes 98696 | tf_op jit(solution)/shard_map/ppermute | solution.py:13
  106.4 22.3 %collective-permute-start.12 = (f32[32,257]{1,0:T(8,128)S(1)}, f32[32,257]{1,0:T(8,128)S(1)}, u32[]{:S(2)}, u32[]{:S(2)}) collective-permute-start(f32[32,257]{1,0:T(8,128)S(1)} %get-tuple-element.78), channel_id=1, source_target_pairs={{0,506},{2,508},{4,510},{6,0},{8,2},{10,4},{12,6},{14,8},{16,10},{... | collective-permute-start | bytes 98696 | tf_op jit(solution)/shard_map/ppermute | solution.py:13
  116.1 12.6 %collective-permute-start.13 = (f32[32,257]{1,0:T(8,128)S(1)}, f32[32,257]{1,0:T(8,128)S(1)}, u32[]{:S(2)}, u32[]{:S(2)}) collective-permute-start(f32[32,257]{1,0:T(8,128)S(1)} %get-tuple-element.82), channel_id=1, source_target_pairs={{0,504},{2,506},{4,508},{6,510},{8,0},{10,2},{12,4},{14,6},{16,8},... | collective-permute-start | bytes 98696 | tf_op jit(solution)/shard_map/ppermute | solution.py:13
  120.4 8.3 %collective-permute-start.10 = (f32[32,257]{1,0:T(8,128)S(1)}, f32[32,257]{1,0:T(8,128)S(1)}, u32[]{:S(2)}, u32[]{:S(2)}) collective-permute-start(f32[32,257]{1,0:T(8,128)S(1)} %get-tuple-element.70), channel_id=1, source_target_pairs={{0,510},{2,0},{4,2},{6,4},{8,6},{10,8},{12,10},{14,12},{16,14},{18... | collective-permute-start | bytes 98696 | tf_op jit(solution)/shard_map/ppermute | solution.py:13
  124.1 5.7 %collective-permute-start.11 = (f32[32,257]{1,0:T(8,128)S(1)}, f32[32,257]{1,0:T(8,128)S(1)}, u32[]{:S(2)}, u32[]{:S(2)}) collective-permute-start(f32[32,257]{1,0:T(8,128)S(1)} %get-tuple-element.74), channel_id=1, source_target_pairs={{0,508},{2,510},{4,0},{6,2},{8,4},{10,6},{12,8},{14,10},{16,12},{1... | collective-permute-start | bytes 98696 | tf_op jit(solution)/shard_map/ppermute | solution.py:13
  129.9 11.7 %collective-permute-start.14 = (f32[2,32,4,257]{3,1,2,0:T(8,128)S(1)}, f32[2,32,4,257]{3,1,2,0:T(8,128)S(1)}, u32[]{:S(2)}, u32[]{:S(2)}) collective-permute-start(f32[2,32,4,257]{3,1,2,0:T(8,128)S(1)} %pad_maximum_fusion.7), channel_id=1, source_target_pairs={{0,1},{1,0},{2,3},{3,2},{4,5},{5,4},{6,7},{7,6},{8,9},{9,8},{10,11... | collective-permute-start | bytes 789512 | tf_op jit(solution)/shard_map/ppermute | solution.py:18

commit v7 on v6

--- a/solution.py
+++ b/solution.py
@@ -112,20 +112,25 @@
         + tuple(shifted(moving_behind, "blk", -d) for d in range(1, near + 1))
     )
     lags = [lags_of(d, first[d - 1], first[near + d - 1]) for d in range(1, near + 1)]
-    far_ahead, far_behind, lags = lax.optimization_barrier(
+    early = [
+        (shifted(piece[channels:], "blk", d), shifted(piece[:channels], "blk", -d)) for d, piece in enumerate(lags, 1)
+    ]
+    far_ahead, far_behind, early = lax.optimization_barrier(
         (
             shifted(jnp.concatenate(first[:near], axis=0), "blk", near),
             shifted(jnp.concatenate(first[near:], axis=0), "blk", -near),
-            lags,
+            early,
         )
     )
     for d in range(near + 1, stops + 1):
         at = (d - near - 1) * split
         lags.append(lags_of(d, far_ahead[at:at + split], far_behind[at:at + split]))
+    late = [(shifted(lags[d - 1][channels:], "blk", d), shifted(lags[d - 1][:channels], "blk", -d)) for d in
+            range(near + 1, stops + 1)]
     own_parts = [piece[:channels] for piece in lags]
     later_parts = [piece[channels:] for piece in lags]
-    from_earlier = [shifted(piece[channels:], "blk", d) for d, piece in enumerate(lags, 1)]
-    from_later = [shifted(piece[:channels], "blk", -d) for d, piece in enumerate(lags, 1)]
+    from_earlier = [pair[0] for pair in early + late]
+    from_later = [pair[1] for pair in early + late]
     corr_part = jnp.stack(own_parts, axis=1) + jnp.stack(from_earlier, axis=1)
     mirror_part = jnp.stack(from_later, axis=1) + jnp.stack(later_parts, axis=1)
     parts = jnp.stack([corr_part, mirror_part], axis=0)

time: 144 us -> 138 us (0.958); the launches traced: 144 us -> 136 us
  waiting for transfers between devices: 54.1 us -> 43.9 us
  starting transfers between devices: 62.2 us -> 64.9 us
    ppermute x14, waiting for transfers between devices: 44.7 us -> 36.1 us  [shifted(): lax.ppermute(x, axis, [(i, (i + by) % length) for i in range(length)])]
    ppermute x14, starting transfers between devices: 60 us -> 62.7 us  [shifted(): lax.ppermute(x, axis, [(i, (i + by) % length) for i in range(length)])]
    ppermute x1, waiting for transfers between devices: 9.47 us -> 7.74 us  [swapped(): return lax.ppermute(x, axis, [(i, i ^ 1) for i in range(length)])]
where the time goes in v7:
time: 138 us; the launch traced here: 136 us
  starting transfers between devices  64.9 us (47%)
  waiting for transfers between devices  43.9 us (32%)
  matrix products  13 us (9%)
  other arithmetic  9.1 us (7%)
  local copies, waits for them, and re-layouts  4.05 us (3%)
    ppermute x14, starting transfers between devices, shifted(): lax.ppermute(x, axis, [(i, (i + by) % length) for i in range(length)])  62.7 us
    ppermute x14, waiting for transfers between devices, shifted(): lax.ppermute(x, axis, [(i, (i + by) % length) for i in range(length)])  36.1 us
    dot_general x4, matrix products, lags_of(): jnp.dot(jnp.concatenate([own, later], axis=0), back_table, precision=lax....  7.78 us
    ppermute x1, waiting for transfers between devices, swapped(): return lax.ppermute(x, axis, [(i, i ^ 1) for i in range(length)])  7.74 us
    unnamed x8, local copies, waits for them, and re-layouts  3.71 us
    another operation x2, other arithmetic  2.96 us
  transfers between devices with their start and end apart: 15, of which 7 were waited for; matrix products, arithmetic and copies ran while one was open for 6% of the time, Pallas kernels for 0%

profile of v7, /device:TPU:1, one launch (start us, length us, event | category | flops | bytes accessed | tf_op | source)
XLA Modules:
  0.0 136.0 jit_solution(10219010334163071326)
XLA Ops:
  0.6 1.0 fusion.47
  2.3 1.8 %copy.8 = bf16[32,8,2048]{2,0,1:T(8,128)(2,1)S(1)} copy(bf16[32,8,2048]{2,1,0:T(8,128)(2,1)} %param.5) | data formatting | bytes 2097152 | tf_op args[0]
  4.1 3.0 %subtract_convert_fusion = (bf16[32,64,1024]{2,1,0:T(8,128)(2,1)S(1)}, bf16[32,64,1024]{2,1,0:T(8,128)(2,1)S(1)}) fusion(f32[64,1024]{1,0:T(8,128)S(1)} %get-tuple-element.101, f32[32,1024]{1,0:T(8,128)S(1)} %get-tuple-element.98, f32[64,1024]{1,0:T(8,128)S(1)} %get-tuple-element.102, f32[32,1024]{1,0:T(8,128)S(1)} %get-tuple-element.97), kind=kLoop, calls=%fused_computation.5 | loop fusion | flops 18874368 | bytes 9175040 | tf_op jit(solution)/shard_map/convert.7
  7.1 2.5 %fusion.4 = (f32[256]{0:T(256)S(1)}, f32[2048,256]{0,1:T(8,128)S(1)}) fusion(bf16[256,2048]{1,0:T(8,128)(2,1)S(1)} %bitcast.112, bf16[2048,1024]{1,0:T(8,128)(2,1)S(1)} %bitcast.110, bf16[2048,1024]{1,0:T(8,128)(2,1)S(1)} %bitcast.109), kind=kOutput, calls=%fused_computation.16 | convolution fusion | flops 2165309184 | bytes 11535360 | tf_op jit(solution)/shard_map/dot_general | solution.py:81
  10.6 8.8 %collective-permute-start.2 = (bf16[4,32,2048]{2,1,0:T(8,128)(2,1)S(1)}, bf16[4,32,2048]{2,1,0:T(8,128)(2,1)S(1)}, u32[]{:S(2)}, u32[]{:S(2)}) collective-permute-start(bf16[4,32,2048]{2,1,0:T(8,128)(2,1)S(1)} %scatter.4), channel_id=1, source_target_pairs={{0,510},{2,0},{4,2},{6,4},{8,6},{10,8},{12,10},{14,12},{16,14},{18... | collective-permute-start | bytes 1572872 | tf_op jit(solution)/shard_map/ppermute | solution.py:13
  19.4 10.7 %collective-permute-start.3 = (bf16[4,32,2048]{2,1,0:T(8,128)(2,1)S(1)}, bf16[4,32,2048]{2,1,0:T(8,128)(2,1)S(1)}, u32[]{:S(2)}, u32[]{:S(2)}) collective-permute-start(bf16[4,32,2048]{2,1,0:T(8,128)(2,1)S(1)} %scatter.4), channel_id=1, source_target_pairs={{0,508},{2,510},{4,0},{6,2},{8,4},{10,6},{12,8},{14,10},{16,12},{1... | collective-permute-start | bytes 1572872 | tf_op jit(solution)/shard_map/ppermute | solution.py:13
  30.0 3.3 %collective-permute-start = (bf16[4,32,2048]{2,1,0:T(8,128)(2,1)S(1)}, bf16[4,32,2048]{2,1,0:T(8,128)(2,1)S(1)}, u32[]{:S(2)}, u32[]{:S(2)}) collective-permute-start(bf16[4,32,2048]{2,1,0:T(8,128)(2,1)S(1)} %get-tuple-element.64), channel_id=1, source_target_pairs={{0,2},{2,4},{4,6},{6,8},{8,10},{10,12},{12,14},{14,16},{16,18},{18... | collective-permute-start | bytes 1572872 | tf_op jit(solution)/shard_map/ppermute | solution.py:13
  33.3 1.9 %collective-permute-start.1 = (bf16[4,32,2048]{2,1,0:T(8,128)(2,1)S(1)}, bf16[4,32,2048]{2,1,0:T(8,128)(2,1)S(1)}, u32[]{:S(2)}, u32[]{:S(2)}) collective-permute-start(bf16[4,32,2048]{2,1,0:T(8,128)(2,1)S(1)} %get-tuple-element.64), channel_id=1, source_target_pairs={{0,4},{2,6},{4,8},{6,10},{8,12},{10,14},{12,16},{14,18},{16,20},{1... | collective-permute-start | bytes 1572872 | tf_op jit(solution)/shard_map/ppermute | solution.py:13
  36.2 5.6 %collective-permute-done.3 = bf16[4,32,2048]{2,1,0:T(8,128)(2,1)S(1)} collective-permute-done((bf16[4,32,2048]{2,1,0:T(8,128)(2,1)S(1)}, bf16[4,32,2048]{2,1,0:T(8,128)(2,1)S(1)}, u32[]{:S(2)}, u32[]{:S(2)}) %collective-permute-start.3) | collective-permute-done | bytes 524320 | tf_op jit(solution)/shard_map/ppermute | solution.py:13
  41.8 0.6 collective-permute-done
  42.4 15.4 %collective-permute-done.1 = bf16[4,32,2048]{2,1,0:T(8,128)(2,1)S(1)} collective-permute-done((bf16[4,32,2048]{2,1,0:T(8,128)(2,1)S(1)}, bf16[4,32,2048]{2,1,0:T(8,128)(2,1)S(1)}, u32[]{:S(2)}, u32[]{:S(2)}) %collective-permute-start.1) | collective-permute-done | bytes 524320 | tf_op jit(solution)/shard_map/ppermute | solution.py:13
  59.4 1.9 %collective-permute-start.5 = (bf16[8,32,2048]{2,1,0:T(8,128)(2,1)S(1)}, bf16[8,32,2048]{2,1,0:T(8,128)(2,1)S(1)}, u32[]{:S(2)}, u32[]{:S(2)}) collective-permute-start(bf16[8,32,2048]{2,1,0:T(8,128)(2,1)S(1)} %pad_maximum_fusion.6), channel_id=1, source_target_pairs={{0,508},{2,510},{4,0},{6,2},{8,4},{10,6},{12,8},{14,10},{16,12},{1... | collective-permute-start | bytes 3145736 | tf_op jit(solution)/shard_map/ppermute | solution.py:13
  61.3 3.4 %collective-permute-start.4 = (bf16[8,32,2048]{2,1,0:T(8,128)(2,1)S(1)}, bf16[8,32,2048]{2,1,0:T(8,128)(2,1)S(1)}, u32[]{:S(2)}, u32[]{:S(2)}) collective-permute-start(bf16[8,32,2048]{2,1,0:T(8,128)(2,1)S(1)} %pad_maximum_fusion.5), channel_id=1, source_target_pairs={{0,4},{2,6},{4,8},{6,10},{8,12},{10,14},{12,16},{14,18},{16,20},{1... | collective-permute-start | bytes 3145736 | tf_op jit(solution)/shard_map/ppermute | solution.py:13
  65.4 1.9 %fusion.7 = f32[64,257]{1,0:T(8,128)S(1)} fusion(f32[1024,257]{1,0:T(8,128)S(1)} %bitcast.105, f32[1024,257]{1,0:T(8,128)S(1)} %bitcast.101, f32[32,1024]{1,0:T(8,128)S(1)} %get-tuple-element.49, f32[32,1024]{1,0:T(8,128)S(1)} %get-tuple-element.48, f32[32,1024]{1,0:T(8,128)S(1)} %get-tuple-element.47, f32[32,1024]{1,0:T(8,128)S(1)} %get-tuple-element.46), kind=kOutput, calls=%fused_computation.22 | convolution fusion | flops 405145600 | bytes 2695424 | tf_op jit(solution)/shard_map/dot_general | solution.py:102
  67.3 2.1 %collective-permute-start.8 = (f32[32,257]{1,0:T(8,128)S(1)}, f32[32,257]{1,0:T(8,128)S(1)}, u32[]{:S(2)}, u32[]{:S(2)}) collective-permute-start(f32[32,257]{1,0:T(8,128)S(1)} %get-tuple-element.85), channel_id=1, source_target_pairs={{0,4},{2,6},{4,8},{6,10},{8,12},{10,14},{12,16},{14,18},{16,20},{1... | collective-permute-start | bytes 98696 | tf_op jit(solution)/shard_map/ppermute | solution.py:13
  69.4 9.1 %collective-permute-start.9 = (f32[32,257]{1,0:T(8,128)S(1)}, f32[32,257]{1,0:T(8,128)S(1)}, u32[]{:S(2)}, u32[]{:S(2)}) collective-permute-start(f32[32,257]{1,0:T(8,128)S(1)} %get-tuple-element.86), channel_id=1, source_target_pairs={{0,508},{2,510},{4,0},{6,2},{8,4},{10,6},{12,8},{14,10},{16,12},{1... | collective-permute-start | bytes 98696 | tf_op jit(solution)/shard_map/ppermute | solution.py:13
  79.2 1.9 %fusion.8 = f32[64,257]{1,0:T(8,128)S(1)} fusion(f32[1024,257]{1,0:T(8,128)S(1)} %bitcast.106, f32[1024,257]{1,0:T(8,128)S(1)} %bitcast.102, f32[32,1024]{1,0:T(8,128)S(1)} %get-tuple-element.53, f32[32,1024]{1,0:T(8,128)S(1)} %get-tuple-element.52, f32[32,1024]{1,0:T(8,128)S(1)} %get-tuple-element.58, f32[32,1024]{1,0:T(8,128)S(1)} %get-tuple-element.59), kind=kOutput, calls=%fused_computation.23 | convolution fusion | flops 405145600 | bytes 2695424 | tf_op jit(solution)/shard_map/dot_general | solution.py:102
  81.2 1.9 %collective-permute-start.6 = (f32[32,257]{1,0:T(8,128)S(1)}, f32[32,257]{1,0:T(8,128)S(1)}, u32[]{:S(2)}, u32[]{:S(2)}) collective-permute-start(f32[32,257]{1,0:T(8,128)S(1)} %get-tuple-element.81), channel_id=1, source_target_pairs={{0,2},{2,4},{4,6},{6,8},{8,10},{10,12},{12,14},{14,16},{16,18},{18... | collective-permute-start | bytes 98696 | tf_op jit(solution)/shard_map/ppermute | solution.py:13
  83.1 9.8 %collective-permute-done.8 = f32[32,257]{1,0:T(8,128)S(1)} collective-permute-done((f32[32,257]{1,0:T(8,128)S(1)}, f32[32,257]{1,0:T(8,128)S(1)}, u32[]{:S(2)}, u32[]{:S(2)}) %collective-permute-start.8) | collective-permute-done | bytes 32928 | tf_op jit(solution)/shard_map/ppermute | solution.py:13
  93.0 1.9 %collective-permute-start.7 = (f32[32,257]{1,0:T(8,128)S(1)}, f32[32,257]{1,0:T(8,128)S(1)}, u32[]{:S(2)}, u32[]{:S(2)}) collective-permute-start(f32[32,257]{1,0:T(8,128)S(1)} %get-tuple-element.82), channel_id=1, source_target_pairs={{0,510},{2,0},{4,2},{6,4},{8,6},{10,8},{12,10},{14,12},{16,14},{18... | collective-permute-start | bytes 98696 | tf_op jit(solution)/shard_map/ppermute | solution.py:13
  94.9 3.5 %collective-permute-done.7 = f32[32,257]{1,0:T(8,128)S(1)} collective-permute-done((f32[32,257]{1,0:T(8,128)S(1)}, f32[32,257]{1,0:T(8,128)S(1)}, u32[]{:S(2)}, u32[]{:S(2)}) %collective-permute-start.7) | collective-permute-done | bytes 32928 | tf_op jit(solution)/shard_map/ppermute | solution.py:13
  100.4 1.9 %fusion.6 = f32[64,257]{1,0:T(8,128)S(1)} fusion(f32[1024,257]{1,0:T(8,128)S(1)} %bitcast.107, f32[1024,257]{1,0:T(8,128)S(1)} %bitcast.103, f32[32,1024]{1,0:T(8,128)S(1)} %get-tuple-element.41, f32[32,1024]{1,0:T(8,128)S(1)} %get-tuple-element.40, f32[32,1024]{1,0:T(8,128)S(1)} %get-tuple-element.39, f32[32,1024]{1,0:T(8,128)S(1)} %get-tuple-element.38), kind=kOutput, calls=%fused_computation.21 | convolution fusion | flops 405145600 | bytes 2695424 | tf_op jit(solution)/shard_map/dot_general | solution.py:102
  102.4 1.9 %collective-permute-start.10 = (f32[32,257]{1,0:T(8,128)S(1)}, f32[32,257]{1,0:T(8,128)S(1)}, u32[]{:S(2)}, u32[]{:S(2)}) collective-permute-start(f32[32,257]{1,0:T(8,128)S(1)} %get-tuple-element.71), channel_id=1, source_target_pairs={{0,6},{2,8},{4,10},{6,12},{8,14},{10,16},{12,18},{14,20},{16,22},{... | collective-permute-start | bytes 98696 | tf_op jit(solution)/shard_map/ppermute | solution.py:13
  104.9 1.9 %fusion.5 = f32[64,257]{1,0:T(8,128)S(1)} fusion(f32[1024,257]{1,0:T(8,128)S(1)} %bitcast.108, f32[1024,257]{1,0:T(8,128)S(1)} %bitcast.104, f32[32,1024]{1,0:T(8,128)S(1)} %get-tuple-element.45, f32[32,1024]{1,0:T(8,128)S(1)} %get-tuple-element.44, f32[32,1024]{1,0:T(8,128)S(1)} %get-tuple-element.54, f32[32,1024]{1,0:T(8,128)S(1)} %get-tuple-element.55), kind=kOutput, calls=%fused_computation.20 | convolution fusion | flops 405145600 | bytes 2695424 | tf_op jit(solution)/shard_map/dot_general | solution.py:102
  106.9 1.9 %collective-permute-start.11 = (f32[32,257]{1,0:T(8,128)S(1)}, f32[32,257]{1,0:T(8,128)S(1)}, u32[]{:S(2)}, u32[]{:S(2)}) collective-permute-start(f32[32,257]{1,0:T(8,128)S(1)} %get-tuple-element.75), channel_id=1, source_target_pairs={{0,8},{2,10},{4,12},{6,14},{8,16},{10,18},{12,20},{14,22},{16,24},... | collective-permute-start | bytes 98696 | tf_op jit(solution)/shard_map/ppermute | solution.py:13
  108.8 9.4 %collective-permute-start.12 = (f32[32,257]{1,0:T(8,128)S(1)}, f32[32,257]{1,0:T(8,128)S(1)}, u32[]{:S(2)}, u32[]{:S(2)}) collective-permute-start(f32[32,257]{1,0:T(8,128)S(1)} %get-tuple-element.74), channel_id=1, source_target_pairs={{0,506},{2,508},{4,510},{6,0},{8,2},{10,4},{12,6},{14,8},{16,10},{... | collective-permute-start | bytes 98696 | tf_op jit(solution)/shard_map/ppermute | solution.py:13
  118.2 4.5 %collective-permute-start.13 = (f32[32,257]{1,0:T(8,128)S(1)}, f32[32,257]{1,0:T(8,128)S(1)}, u32[]{:S(2)}, u32[]{:S(2)}) collective-permute-start(f32[32,257]{1,0:T(8,128)S(1)} %get-tuple-element.78), channel_id=1, source_target_pairs={{0,504},{2,506},{4,508},{6,510},{8,0},{10,2},{12,4},{14,6},{16,8},... | collective-permute-start | bytes 98696 | tf_op jit(solution)/shard_map/ppermute | solution.py:13
  122.8 1.1 collective-permute-done.13
  124.0 2.2 %collective-permute-start.14 = (f32[2,32,4,257]{3,1,2,0:T(8,128)S(1)}, f32[2,32,4,257]{3,1,2,0:T(8,128)S(1)}, u32[]{:S(2)}, u32[]{:S(2)}) collective-permute-start(f32[2,32,4,257]{3,1,2,0:T(8,128)S(1)} %pad_maximum_fusion.7), channel_id=1, source_target_pairs={{0,1},{1,0},{2,3},{3,2},{4,5},{5,4},{6,7},{7,6},{8,9},{9,8},{10,11... | collective-permute-start | bytes 789512 | tf_op jit(solution)/shard_map/ppermute | solution.py:18
  126.2 7.7 %collective-permute-done.14 = f32[2,32,4,257]{3,1,2,0:T(8,128)S(1)} collective-permute-done((f32[2,32,4,257]{3,1,2,0:T(8,128)S(1)}, f32[2,32,4,257]{3,1,2,0:T(8,128)S(1)}, u32[]{:S(2)}, u32[]{:S(2)}) %collective-permute-start.14) | collective-permute-done | bytes 263200 | tf_op jit(solution)/shard_map/ppermute | solution.py:18
  134.4 0.8 copy.11
  135.2 0.8 copy.10
  (60 shorter events, 8.5 us)
Async XLA Ops:
  7.0 2.6 %copy-start.1 = (s32[32]{0:T(128)S(1)}, s32[32]{0:T(128)}, u32[]{:S(2)}) copy-start(s32[32]{0:T(128)} %param.7) | copy-start | bytes 388
  9.6 0.7 copy-start
  10.6 25.6 %collective-permute-start.2 = (bf16[4,32,2048]{2,1,0:T(8,128)(2,1)S(1)}, bf16[4,32,2048]{2,1,0:T(8,128)(2,1)S(1)}, u32[]{:S(2)}, u32[]{:S(2)}) collective-permute-start(bf16[4,32,2048]{2,1,0:T(8,128)(2,1)S(1)} %scatter.4), channel_id=1, source_target_pairs={{0,510},{2,0},{4,2},{6,4},{8,6},{10,8},{12,10},{14,12},{16,14},{18... | collective-permute-start | bytes 1572872 | tf_op jit(solution)/shard_map/ppermute | solution.py:13
  19.4 22.5 %collective-permute-start.3 = (bf16[4,32,2048]{2,1,0:T(8,128)(2,1)S(1)}, bf16[4,32,2048]{2,1,0:T(8,128)(2,1)S(1)}, u32[]{:S(2)}, u32[]{:S(2)}) collective-permute-start(bf16[4,32,2048]{2,1,0:T(8,128)(2,1)S(1)} %scatter.4), channel_id=1, source_target_pairs={{0,508},{2,510},{4,0},{6,2},{8,4},{10,6},{12,8},{14,10},{16,12},{1... | collective-permute-start | bytes 1572872 | tf_op jit(solution)/shard_map/ppermute | solution.py:13
  30.0 12.4 %collective-permute-start = (bf16[4,32,2048]{2,1,0:T(8,128)(2,1)S(1)}, bf16[4,32,2048]{2,1,0:T(8,128)(2,1)S(1)}, u32[]{:S(2)}, u32[]{:S(2)}) collective-permute-start(bf16[4,32,2048]{2,1,0:T(8,128)(2,1)S(1)} %get-tuple-element.64), channel_id=1, source_target_pairs={{0,2},{2,4},{4,6},{6,8},{8,10},{10,12},{12,14},{14,16},{16,18},{18... | collective-permute-start | bytes 1572872 | tf_op jit(solution)/shard_map/ppermute | solution.py:13
  33.3 24.6 %collective-permute-start.1 = (bf16[4,32,2048]{2,1,0:T(8,128)(2,1)S(1)}, bf16[4,32,2048]{2,1,0:T(8,128)(2,1)S(1)}, u32[]{:S(2)}, u32[]{:S(2)}) collective-permute-start(bf16[4,32,2048]{2,1,0:T(8,128)(2,1)S(1)} %get-tuple-element.64), channel_id=1, source_target_pairs={{0,4},{2,6},{4,8},{6,10},{8,12},{10,14},{12,16},{14,18},{16,20},{1... | collective-permute-start | bytes 1572872 | tf_op jit(solution)/shard_map/ppermute | solution.py:13
  59.4 39.0 %collective-permute-start.5 = (bf16[8,32,2048]{2,1,0:T(8,128)(2,1)S(1)}, bf16[8,32,2048]{2,1,0:T(8,128)(2,1)S(1)}, u32[]{:S(2)}, u32[]{:S(2)}) collective-permute-start(bf16[8,32,2048]{2,1,0:T(8,128)(2,1)S(1)} %pad_maximum_fusion.6), channel_id=1, source_target_pairs={{0,508},{2,510},{4,0},{6,2},{8,4},{10,6},{12,8},{14,10},{16,12},{1... | collective-permute-start | bytes 3145736 | tf_op jit(solution)/shard_map/ppermute | solution.py:13
  61.3 37.1 %collective-permute-start.4 = (bf16[8,32,2048]{2,1,0:T(8,128)(2,1)S(1)}, bf16[8,32,2048]{2,1,0:T(8,128)(2,1)S(1)}, u32[]{:S(2)}, u32[]{:S(2)}) collective-permute-start(bf16[8,32,2048]{2,1,0:T(8,128)(2,1)S(1)} %pad_maximum_fusion.5), channel_id=1, source_target_pairs={{0,4},{2,6},{4,8},{6,10},{8,12},{10,14},{12,16},{14,18},{16,20},{1... | collective-permute-start | bytes 3145736 | tf_op jit(solution)/shard_map/ppermute | solution.py:13
  67.3 25.7 %collective-permute-start.8 = (f32[32,257]{1,0:T(8,128)S(1)}, f32[32,257]{1,0:T(8,128)S(1)}, u32[]{:S(2)}, u32[]{:S(2)}) collective-permute-start(f32[32,257]{1,0:T(8,128)S(1)} %get-tuple-element.85), channel_id=1, source_target_pairs={{0,4},{2,6},{4,8},{6,10},{8,12},{10,14},{12,16},{14,18},{16,20},{1... | collective-permute-start | bytes 98696 | tf_op jit(solution)/shard_map/ppermute | solution.py:13
  69.4 25.5 %collective-permute-start.9 = (f32[32,257]{1,0:T(8,128)S(1)}, f32[32,257]{1,0:T(8,128)S(1)}, u32[]{:S(2)}, u32[]{:S(2)}) collective-permute-start(f32[32,257]{1,0:T(8,128)S(1)} %get-tuple-element.86), channel_id=1, source_target_pairs={{0,508},{2,510},{4,0},{6,2},{8,4},{10,6},{12,8},{14,10},{16,12},{1... | collective-permute-start | bytes 98696 | tf_op jit(solution)/shard_map/ppermute | solution.py:13
  81.2 13.7 %collective-permute-start.6 = (f32[32,257]{1,0:T(8,128)S(1)}, f32[32,257]{1,0:T(8,128)S(1)}, u32[]{:S(2)}, u32[]{:S(2)}) collective-permute-start(f32[32,257]{1,0:T(8,128)S(1)} %get-tuple-element.81), channel_id=1, source_target_pairs={{0,2},{2,4},{4,6},{6,8},{8,10},{10,12},{12,14},{14,16},{16,18},{18... | collective-permute-start | bytes 98696 | tf_op jit(solution)/shard_map/ppermute | solution.py:13
  93.0 5.4 %collective-permute-start.7 = (f32[32,257]{1,0:T(8,128)S(1)}, f32[32,257]{1,0:T(8,128)S(1)}, u32[]{:S(2)}, u32[]{:S(2)}) collective-permute-start(f32[32,257]{1,0:T(8,128)S(1)} %get-tuple-element.82), channel_id=1, source_target_pairs={{0,510},{2,0},{4,2},{6,4},{8,6},{10,8},{12,10},{14,12},{16,14},{18... | collective-permute-start | bytes 98696 | tf_op jit(solution)/shard_map/ppermute | solution.py:13
  102.4 20.4 %collective-permute-start.10 = (f32[32,257]{1,0:T(8,128)S(1)}, f32[32,257]{1,0:T(8,128)S(1)}, u32[]{:S(2)}, u32[]{:S(2)}) collective-permute-start(f32[32,257]{1,0:T(8,128)S(1)} %get-tuple-element.71), channel_id=1, source_target_pairs={{0,6},{2,8},{4,10},{6,12},{8,14},{10,16},{12,18},{14,20},{16,22},{... | collective-permute-start | bytes 98696 | tf_op jit(solution)/shard_map/ppermute | solution.py:13
  106.9 15.9 %collective-permute-start.11 = (f32[32,257]{1,0:T(8,128)S(1)}, f32[32,257]{1,0:T(8,128)S(1)}, u32[]{:S(2)}, u32[]{:S(2)}) collective-permute-start(f32[32,257]{1,0:T(8,128)S(1)} %get-tuple-element.75), channel_id=1, source_target_pairs={{0,8},{2,10},{4,12},{6,14},{8,16},{10,18},{12,20},{14,22},{16,24},... | collective-permute-start | bytes 98696 | tf_op jit(solution)/shard_map/ppermute | solution.py:13
  108.8 14.0 %collective-permute-start.12 = (f32[32,257]{1,0:T(8,128)S(1)}, f32[32,257]{1,0:T(8,128)S(1)}, u32[]{:S(2)}, u32[]{:S(2)}) collective-permute-start(f32[32,257]{1,0:T(8,128)S(1)} %get-tuple-element.74), channel_id=1, source_target_pairs={{0,506},{2,508},{4,510},{6,0},{8,2},{10,4},{12,6},{14,8},{16,10},{... | collective-permute-start | bytes 98696 | tf_op jit(solution)/shard_map/ppermute | solution.py:13
  118.2 5.7 %collective-permute-start.13 = (f32[32,257]{1,0:T(8,128)S(1)}, f32[32,257]{1,0:T(8,128)S(1)}, u32[]{:S(2)}, u32[]{:S(2)}) collective-permute-start(f32[32,257]{1,0:T(8,128)S(1)} %get-tuple-element.78), channel_id=1, source_target_pairs={{0,504},{2,506},{4,508},{6,510},{8,0},{10,2},{12,4},{14,6},{16,8},... | collective-permute-start | bytes 98696 | tf_op jit(solution)/shard_map/ppermute | solution.py:13
  124.0 10.0 %collective-permute-start.14 = (f32[2,32,4,257]{3,1,2,0:T(8,128)S(1)}, f32[2,32,4,257]{3,1,2,0:T(8,128)S(1)}, u32[]{:S(2)}, u32[]{:S(2)}) collective-permute-start(f32[2,32,4,257]{3,1,2,0:T(8,128)S(1)} %pad_maximum_fusion.7), channel_id=1, source_target_pairs={{0,1},{1,0},{2,3},{3,2},{4,5},{5,4},{6,7},{7,6},{8,9},{9,8},{10,11... | collective-permute-start | bytes 789512 | tf_op jit(solution)/shard_map/ppermute | solution.py:18

commit v8 on v7

--- a/solution.py
+++ b/solution.py
@@ -115,18 +115,13 @@
     early = [
         (shifted(piece[channels:], "blk", d), shifted(piece[:channels], "blk", -d)) for d, piece in enumerate(lags, 1)
     ]
-    far_ahead, far_behind, early = lax.optimization_barrier(
-        (
-            shifted(jnp.concatenate(first[:near], axis=0), "blk", near),
-            shifted(jnp.concatenate(first[near:], axis=0), "blk", -near),
-            early,
+    late = []
+    for d in range(near + 1, stops + 1):
+        far_ahead, far_behind, early = lax.optimization_barrier(
+            (shifted(first[d - near - 1], "blk", near), shifted(first[d - 1], "blk", -near), early)
         )
-    )
-    for d in range(near + 1, stops + 1):
-        at = (d - near - 1) * split
-        lags.append(lags_of(d, far_ahead[at:at + split], far_behind[at:at + split]))
-    late = [(shifted(lags[d - 1][channels:], "blk", d), shifted(lags[d - 1][:channels], "blk", -d)) for d in
-            range(near + 1, stops + 1)]
+        lags.append(lags_of(d, far_ahead, far_behind))
+        late.append((shifted(lags[d - 1][channels:], "blk", d), shifted(lags[d - 1][:channels], "blk", -d)))
     own_parts = [piece[:channels] for piece in lags]
     later_parts = [piece[channels:] for piece in lags]
     from_earlier = [pair[0] for pair in early + late]

time: 138 us -> 152 us (1.10)
  the two profiles are of different devices: /device:TPU:1 before, /device:TPU:8 now
where the time goes in v8:
time: 152 us
  starting transfers between devices  79.9 us (53%)
  waiting for transfers between devices  44.8 us (29%)
  matrix products  13 us (9%)
  other arithmetic  9.02 us (6%)
  local copies, waits for them, and re-layouts  4.05 us (3%)
    ppermute x16, starting transfers between devices, shifted(): lax.ppermute(x, axis, [(i, (i + by) % length) for i in range(length)])  77.3 us
    ppermute x16, waiting for transfers between devices, shifted(): lax.ppermute(x, axis, [(i, (i + by) % length) for i in range(length)])  36.5 us
    ppermute x1, waiting for transfers between devices, swapped(): return lax.ppermute(x, axis, [(i, i ^ 1) for i in range(length)])  8.28 us
    dot_general x4, matrix products, lags_of(): jnp.dot(jnp.concatenate([own, later], axis=0), back_table, precision=lax....  7.78 us
    unnamed x8, local copies, waits for them, and re-layouts  3.71 us
  transfers between devices with their start and end apart: 17, of which 9 were waited for; matrix products, arithmetic and copies ran while one was open for 7% of the time, Pallas kernels for 0%

profile of v8, /device:TPU:8, one launch (start us, length us, event | category | flops | bytes accessed | tf_op | source)
XLA Modules:
  0.0 151.9 jit_solution(12507777198507384846)
XLA Ops:
  2.3 1.8 %copy.8 = bf16[32,8,2048]{2,0,1:T(8,128)(2,1)S(1)} copy(bf16[32,8,2048]{2,1,0:T(8,128)(2,1)} %param.5) | data formatting | bytes 2097152 | tf_op args[0]
  4.1 3.0 %subtract_convert_fusion = (bf16[32,64,1024]{2,1,0:T(8,128)(2,1)S(1)}, bf16[32,64,1024]{2,1,0:T(8,128)(2,1)S(1)}) fusion(f32[64,1024]{1,0:T(8,128)S(1)} %get-tuple-element.111, f32[32,1024]{1,0:T(8,128)S(1)} %get-tuple-element.108, f32[64,1024]{1,0:T(8,128)S(1)} %get-tuple-element.112, f32[32,1024]{1,0:T(8,128)S(1)} %get-tuple-element.107), kind=kLoop, calls=%fused_computation.5 | loop fusion | flops 18874368 | bytes 9175040 | tf_op jit(solution)/shard_map/convert.7
  7.1 2.5 %fusion.4 = (f32[256]{0:T(256)S(1)}, f32[2048,256]{0,1:T(8,128)S(1)}) fusion(bf16[256,2048]{1,0:T(8,128)(2,1)S(1)} %bitcast.112, bf16[2048,1024]{1,0:T(8,128)(2,1)S(1)} %bitcast.110, bf16[2048,1024]{1,0:T(8,128)(2,1)S(1)} %bitcast.109), kind=kOutput, calls=%fused_computation.16 | convolution fusion | flops 2165309184 | bytes 11535360 | tf_op jit(solution)/shard_map/dot_general | solution.py:81
  10.6 1.9 %collective-permute-start.2 = (bf16[4,32,2048]{2,1,0:T(8,128)(2,1)S(1)}, bf16[4,32,2048]{2,1,0:T(8,128)(2,1)S(1)}, u32[]{:S(2)}, u32[]{:S(2)}) collective-permute-start(bf16[4,32,2048]{2,1,0:T(8,128)(2,1)S(1)} %scatter.4), channel_id=1, source_target_pairs={{0,510},{2,0},{4,2},{6,4},{8,6},{10,8},{12,10},{14,12},{16,14},{18... | collective-permute-start | bytes 1572872 | tf_op jit(solution)/shard_map/ppermute | solution.py:13
  12.5 16.2 %collective-permute-start.3 = (bf16[4,32,2048]{2,1,0:T(8,128)(2,1)S(1)}, bf16[4,32,2048]{2,1,0:T(8,128)(2,1)S(1)}, u32[]{:S(2)}, u32[]{:S(2)}) collective-permute-start(bf16[4,32,2048]{2,1,0:T(8,128)(2,1)S(1)} %scatter.4), channel_id=1, source_target_pairs={{0,508},{2,510},{4,0},{6,2},{8,4},{10,6},{12,8},{14,10},{16,12},{1... | collective-permute-start | bytes 1572872 | tf_op jit(solution)/shard_map/ppermute | solution.py:13
  28.7 1.9 %collective-permute-start = (bf16[4,32,2048]{2,1,0:T(8,128)(2,1)S(1)}, bf16[4,32,2048]{2,1,0:T(8,128)(2,1)S(1)}, u32[]{:S(2)}, u32[]{:S(2)}) collective-permute-start(bf16[4,32,2048]{2,1,0:T(8,128)(2,1)S(1)} %get-tuple-element.72), channel_id=1, source_target_pairs={{0,2},{2,4},{4,6},{6,8},{8,10},{10,12},{12,14},{14,16},{16,18},{18... | collective-permute-start | bytes 1572872 | tf_op jit(solution)/shard_map/ppermute | solution.py:13
  30.6 1.9 %collective-permute-start.1 = (bf16[4,32,2048]{2,1,0:T(8,128)(2,1)S(1)}, bf16[4,32,2048]{2,1,0:T(8,128)(2,1)S(1)}, u32[]{:S(2)}, u32[]{:S(2)}) collective-permute-start(bf16[4,32,2048]{2,1,0:T(8,128)(2,1)S(1)} %get-tuple-element.72), channel_id=1, source_target_pairs={{0,4},{2,6},{4,8},{6,10},{8,12},{10,14},{12,16},{14,18},{16,20},{1... | collective-permute-start | bytes 1572872 | tf_op jit(solution)/shard_map/ppermute | solution.py:13
  33.5 1.9 %collective-permute-done.3 = bf16[4,32,2048]{2,1,0:T(8,128)(2,1)S(1)} collective-permute-done((bf16[4,32,2048]{2,1,0:T(8,128)(2,1)S(1)}, bf16[4,32,2048]{2,1,0:T(8,128)(2,1)S(1)}, u32[]{:S(2)}, u32[]{:S(2)}) %collective-permute-start.3) | collective-permute-done | bytes 524320 | tf_op jit(solution)/shard_map/ppermute | solution.py:13
  35.4 6.9 %collective-permute-done = bf16[4,32,2048]{2,1,0:T(8,128)(2,1)S(1)} collective-permute-done((bf16[4,32,2048]{2,1,0:T(8,128)(2,1)S(1)}, bf16[4,32,2048]{2,1,0:T(8,128)(2,1)S(1)}, u32[]{:S(2)}, u32[]{:S(2)}) %collective-permute-start) | collective-permute-done | bytes 524320 | tf_op jit(solution)/shard_map/ppermute | solution.py:13
  42.2 5.1 %collective-permute-done.1 = bf16[4,32,2048]{2,1,0:T(8,128)(2,1)S(1)} collective-permute-done((bf16[4,32,2048]{2,1,0:T(8,128)(2,1)S(1)}, bf16[4,32,2048]{2,1,0:T(8,128)(2,1)S(1)}, u32[]{:S(2)}, u32[]{:S(2)}) %collective-permute-start.1) | collective-permute-done | bytes 524320 | tf_op jit(solution)/shard_map/ppermute | solution.py:13
  47.5 9.0 %collective-permute-start.5 = (bf16[4,32,2048]{2,1,0:T(8,128)(2,1)S(1)}, bf16[4,32,2048]{2,1,0:T(8,128)(2,1)S(1)}, u32[]{:S(2)}, u32[]{:S(2)}) collective-permute-start(bf16[4,32,2048]{2,1,0:T(8,128)(2,1)S(1)} %collective-permute-done.2), channel_id=1, source_target_pairs={{0,508},{2,510},{4,0},{6,2},{8,4},{10,6},{12,8},{14,10},{16,12},{1... | collective-permute-start | bytes 1572872 | tf_op jit(solution)/shard_map/ppermute | solution.py:13
  56.6 1.9 %collective-permute-start.11 = (bf16[4,32,2048]{2,1,0:T(8,128)(2,1)S(1)}, bf16[4,32,2048]{2,1,0:T(8,128)(2,1)S(1)}, u32[]{:S(2)}, u32[]{:S(2)}) collective-permute-start(bf16[4,32,2048]{2,1,0:T(8,128)(2,1)S(1)} %collective-permute-done.3), channel_id=1, source_target_pairs={{0,508},{2,510},{4,0},{6,2},{8,4},{10,6},{12,8},{14,10},{16,12},{1... | collective-permute-start | bytes 1572872 | tf_op jit(solution)/shard_map/ppermute | solution.py:13
  59.0 3.9 %collective-permute-start.10 = (bf16[4,32,2048]{2,1,0:T(8,128)(2,1)S(1)}, bf16[4,32,2048]{2,1,0:T(8,128)(2,1)S(1)}, u32[]{:S(2)}, u32[]{:S(2)}) collective-permute-start(bf16[4,32,2048]{2,1,0:T(8,128)(2,1)S(1)} %collective-permute-done.1), channel_id=1, source_target_pairs={{0,4},{2,6},{4,8},{6,10},{8,12},{10,14},{12,16},{14,18},{16,20},{1... | collective-permute-start | bytes 1572872 | tf_op jit(solution)/shard_map/ppermute | solution.py:13
  63.3 1.9 %collective-permute-start.4 = (bf16[4,32,2048]{2,1,0:T(8,128)(2,1)S(1)}, bf16[4,32,2048]{2,1,0:T(8,128)(2,1)S(1)}, u32[]{:S(2)}, u32[]{:S(2)}) collective-permute-start(bf16[4,32,2048]{2,1,0:T(8,128)(2,1)S(1)} %collective-permute-done), channel_id=1, source_target_pairs={{0,4},{2,6},{4,8},{6,10},{8,12},{10,14},{12,16},{14,18},{16,20},{1... | collective-permute-start | bytes 1572872 | tf_op jit(solution)/shard_map/ppermute | solution.py:13
  66.3 1.9 %fusion.7 = f32[64,257]{1,0:T(8,128)S(1)} fusion(f32[1024,257]{1,0:T(8,128)S(1)} %bitcast.105, f32[1024,257]{1,0:T(8,128)S(1)} %bitcast.101, f32[32,1024]{1,0:T(8,128)S(1)} %get-tuple-element.61, f32[32,1024]{1,0:T(8,128)S(1)} %get-tuple-element.60, f32[32,1024]{1,0:T(8,128)S(1)} %get-tuple-element.59, f32[32,1024]{1,0:T(8,128)S(1)} %get-tuple-element.58), kind=kOutput, calls=%fused_computation.22 | convolution fusion | flops 405145600 | bytes 2695424 | tf_op jit(solution)/shard_map/dot_general | solution.py:102
  68.2 2.1 %collective-permute-start.8 = (f32[32,257]{1,0:T(8,128)S(1)}, f32[32,257]{1,0:T(8,128)S(1)}, u32[]{:S(2)}, u32[]{:S(2)}) collective-permute-start(f32[32,257]{1,0:T(8,128)S(1)} %get-tuple-element.93), channel_id=1, source_target_pairs={{0,4},{2,6},{4,8},{6,10},{8,12},{10,14},{12,16},{14,18},{16,20},{1... | collective-permute-start | bytes 98696 | tf_op jit(solution)/shard_map/ppermute | solution.py:13
  70.9 1.9 %fusion.8 = f32[64,257]{1,0:T(8,128)S(1)} fusion(f32[1024,257]{1,0:T(8,128)S(1)} %bitcast.106, f32[1024,257]{1,0:T(8,128)S(1)} %bitcast.102, f32[32,1024]{1,0:T(8,128)S(1)} %get-tuple-element.65, f32[32,1024]{1,0:T(8,128)S(1)} %get-tuple-element.64, f32[32,1024]{1,0:T(8,128)S(1)} %get-tuple-element.68, f32[32,1024]{1,0:T(8,128)S(1)} %get-tuple-element.69), kind=kOutput, calls=%fused_computation.23 | convolution fusion | flops 405145600 | bytes 2695424 | tf_op jit(solution)/shard_map/dot_general | solution.py:102
  72.9 13.4 %collective-permute-done.8 = f32[32,257]{1,0:T(8,128)S(1)} collective-permute-done((f32[32,257]{1,0:T(8,128)S(1)}, f32[32,257]{1,0:T(8,128)S(1)}, u32[]{:S(2)}, u32[]{:S(2)}) %collective-permute-start.8) | collective-permute-done | bytes 32928 | tf_op jit(solution)/shard_map/ppermute | solution.py:13
  86.3 7.3 %collective-permute-start.9 = (f32[32,257]{1,0:T(8,128)S(1)}, f32[32,257]{1,0:T(8,128)S(1)}, u32[]{:S(2)}, u32[]{:S(2)}) collective-permute-start(f32[32,257]{1,0:T(8,128)S(1)} %get-tuple-element.94), channel_id=1, source_target_pairs={{0,508},{2,510},{4,0},{6,2},{8,4},{10,6},{12,8},{14,10},{16,12},{1... | collective-permute-start | bytes 98696 | tf_op jit(solution)/shard_map/ppermute | solution.py:13
  95.4 2.8 %collective-permute-start.6 = (f32[32,257]{1,0:T(8,128)S(1)}, f32[32,257]{1,0:T(8,128)S(1)}, u32[]{:S(2)}, u32[]{:S(2)}) collective-permute-start(f32[32,257]{1,0:T(8,128)S(1)} %get-tuple-element.89), channel_id=1, source_target_pairs={{0,2},{2,4},{4,6},{6,8},{8,10},{10,12},{12,14},{14,16},{16,18},{18... | collective-permute-start | bytes 98696 | tf_op jit(solution)/shard_map/ppermute | solution.py:13
  98.2 3.4 %collective-permute-done.6 = f32[32,257]{1,0:T(8,128)S(1)} collective-permute-done((f32[32,257]{1,0:T(8,128)S(1)}, f32[32,257]{1,0:T(8,128)S(1)}, u32[]{:S(2)}, u32[]{:S(2)}) %collective-permute-start.6) | collective-permute-done | bytes 32928 | tf_op jit(solution)/shard_map/ppermute | solution.py:13
  101.6 1.9 %collective-permute-start.7 = (f32[32,257]{1,0:T(8,128)S(1)}, f32[32,257]{1,0:T(8,128)S(1)}, u32[]{:S(2)}, u32[]{:S(2)}) collective-permute-start(f32[32,257]{1,0:T(8,128)S(1)} %get-tuple-element.90), channel_id=1, source_target_pairs={{0,510},{2,0},{4,2},{6,4},{8,6},{10,8},{12,10},{14,12},{16,14},{18... | collective-permute-start | bytes 98696 | tf_op jit(solution)/shard_map/ppermute | solution.py:13
  103.6 1.7 %collective-permute-done.7 = f32[32,257]{1,0:T(8,128)S(1)} collective-permute-done((f32[32,257]{1,0:T(8,128)S(1)}, f32[32,257]{1,0:T(8,128)S(1)}, u32[]{:S(2)}, u32[]{:S(2)}) %collective-permute-start.7) | collective-permute-done | bytes 32928 | tf_op jit(solution)/shard_map/ppermute | solution.py:13
  107.4 1.9 %fusion.6 = f32[64,257]{1,0:T(8,128)S(1)} fusion(f32[1024,257]{1,0:T(8,128)S(1)} %bitcast.107, f32[1024,257]{1,0:T(8,128)S(1)} %bitcast.103, f32[32,1024]{1,0:T(8,128)S(1)} %get-tuple-element.53, f32[32,1024]{1,0:T(8,128)S(1)} %get-tuple-element.52, f32[32,1024]{1,0:T(8,128)S(1)} %get-tuple-element.51, f32[32,1024]{1,0:T(8,128)S(1)} %get-tuple-element.50), kind=kOutput, calls=%fused_computation.21 | convolution fusion | flops 405145600 | bytes 2695424 | tf_op jit(solution)/shard_map/dot_general | solution.py:102
  109.4 1.9 %collective-permute-start.12 = (f32[32,257]{1,0:T(8,128)S(1)}, f32[32,257]{1,0:T(8,128)S(1)}, u32[]{:S(2)}, u32[]{:S(2)}) collective-permute-start(f32[32,257]{1,0:T(8,128)S(1)} %get-tuple-element.79), channel_id=1, source_target_pairs={{0,6},{2,8},{4,10},{6,12},{8,14},{10,16},{12,18},{14,20},{16,22},{... | collective-permute-start | bytes 98696 | tf_op jit(solution)/shard_map/ppermute | solution.py:13
  111.9 1.9 %fusion.5 = f32[64,257]{1,0:T(8,128)S(1)} fusion(f32[1024,257]{1,0:T(8,128)S(1)} %bitcast.108, f32[1024,257]{1,0:T(8,128)S(1)} %bitcast.104, f32[32,1024]{1,0:T(8,128)S(1)} %get-tuple-element.57, f32[32,1024]{1,0:T(8,128)S(1)} %get-tuple-element.56, f32[32,1024]{1,0:T(8,128)S(1)} %get-tuple-element.66, f32[32,1024]{1,0:T(8,128)S(1)} %get-tuple-element.67), kind=kOutput, calls=%fused_computation.20 | convolution fusion | flops 405145600 | bytes 2695424 | tf_op jit(solution)/shard_map/dot_general | solution.py:102
  113.9 1.9 %collective-permute-start.13 = (f32[32,257]{1,0:T(8,128)S(1)}, f32[32,257]{1,0:T(8,128)S(1)}, u32[]{:S(2)}, u32[]{:S(2)}) collective-permute-start(f32[32,257]{1,0:T(8,128)S(1)} %get-tuple-element.83), channel_id=1, source_target_pairs={{0,8},{2,10},{4,12},{6,14},{8,16},{10,18},{12,20},{14,22},{16,24},... | collective-permute-start | bytes 98696 | tf_op jit(solution)/shard_map/ppermute | solution.py:13
  115.8 16.1 %collective-permute-start.14 = (f32[32,257]{1,0:T(8,128)S(1)}, f32[32,257]{1,0:T(8,128)S(1)}, u32[]{:S(2)}, u32[]{:S(2)}) collective-permute-start(f32[32,257]{1,0:T(8,128)S(1)} %get-tuple-element.82), channel_id=1, source_target_pairs={{0,506},{2,508},{4,510},{6,0},{8,2},{10,4},{12,6},{14,8},{16,10},{... | collective-permute-start | bytes 98696 | tf_op jit(solution)/shard_map/ppermute | solution.py:13
  131.9 4.5 %collective-permute-start.15 = (f32[32,257]{1,0:T(8,128)S(1)}, f32[32,257]{1,0:T(8,128)S(1)}, u32[]{:S(2)}, u32[]{:S(2)}) collective-permute-start(f32[32,257]{1,0:T(8,128)S(1)} %get-tuple-element.86), channel_id=1, source_target_pairs={{0,504},{2,506},{4,508},{6,510},{8,0},{10,2},{12,4},{14,6},{16,8},... | collective-permute-start | bytes 98696 | tf_op jit(solution)/shard_map/ppermute | solution.py:13
  136.5 2.4 %collective-permute-done.15 = f32[32,257]{1,0:T(8,128)S(1)} collective-permute-done((f32[32,257]{1,0:T(8,128)S(1)}, f32[32,257]{1,0:T(8,128)S(1)}, u32[]{:S(2)}, u32[]{:S(2)}) %collective-permute-start.15) | collective-permute-done | bytes 32928 | tf_op jit(solution)/shard_map/ppermute | solution.py:13
  138.9 2.5 %collective-permute-start.16 = (f32[2,32,4,257]{3,1,2,0:T(8,128)S(1)}, f32[2,32,4,257]{3,1,2,0:T(8,128)S(1)}, u32[]{:S(2)}, u32[]{:S(2)}) collective-permute-start(f32[2,32,4,257]{3,1,2,0:T(8,128)S(1)} %pad_maximum_fusion.5), channel_id=1, source_target_pairs={{0,1},{1,0},{2,3},{3,2},{4,5},{5,4},{6,7},{7,6},{8,9},{9,8},{10,11... | collective-permute-start | bytes 789512 | tf_op jit(solution)/shard_map/ppermute | solution.py:18
  141.5 8.3 %collective-permute-done.16 = f32[2,32,4,257]{3,1,2,0:T(8,128)S(1)} collective-permute-done((f32[2,32,4,257]{3,1,2,0:T(8,128)S(1)}, f32[2,32,4,257]{3,1,2,0:T(8,128)S(1)}, u32[]{:S(2)}, u32[]{:S(2)}) %collective-permute-start.16) | collective-permute-done | bytes 263200 | tf_op jit(solution)/shard_map/ppermute | solution.py:18
  (63 shorter events, 12.7 us)
Async XLA Ops:
  7.0 2.6 %copy-start.1 = (s32[32]{0:T(128)S(1)}, s32[32]{0:T(128)}, u32[]{:S(2)}) copy-start(s32[32]{0:T(128)} %param.7) | copy-start | bytes 388
  9.6 0.7 copy-start
  10.6 22.9 %collective-permute-start.2 = (bf16[4,32,2048]{2,1,0:T(8,128)(2,1)S(1)}, bf16[4,32,2048]{2,1,0:T(8,128)(2,1)S(1)}, u32[]{:S(2)}, u32[]{:S(2)}) collective-permute-start(bf16[4,32,2048]{2,1,0:T(8,128)(2,1)S(1)} %scatter.4), channel_id=1, source_target_pairs={{0,510},{2,0},{4,2},{6,4},{8,6},{10,8},{12,10},{14,12},{16,14},{18... | collective-permute-start | bytes 1572872 | tf_op jit(solution)/shard_map/ppermute | solution.py:13
  12.5 22.9 %collective-permute-start.3 = (bf16[4,32,2048]{2,1,0:T(8,128)(2,1)S(1)}, bf16[4,32,2048]{2,1,0:T(8,128)(2,1)S(1)}, u32[]{:S(2)}, u32[]{:S(2)}) collective-permute-start(bf16[4,32,2048]{2,1,0:T(8,128)(2,1)S(1)} %scatter.4), channel_id=1, source_target_pairs={{0,508},{2,510},{4,0},{6,2},{8,4},{10,6},{12,8},{14,10},{16,12},{1... | collective-permute-start | bytes 1572872 | tf_op jit(solution)/shard_map/ppermute | solution.py:13
  28.7 13.5 %collective-permute-start = (bf16[4,32,2048]{2,1,0:T(8,128)(2,1)S(1)}, bf16[4,32,2048]{2,1,0:T(8,128)(2,1)S(1)}, u32[]{:S(2)}, u32[]{:S(2)}) collective-permute-start(bf16[4,32,2048]{2,1,0:T(8,128)(2,1)S(1)} %get-tuple-element.72), channel_id=1, source_target_pairs={{0,2},{2,4},{4,6},{6,8},{8,10},{10,12},{12,14},{14,16},{16,18},{18... | collective-permute-start | bytes 1572872 | tf_op jit(solution)/shard_map/ppermute | solution.py:13
  30.6 16.8 %collective-permute-start.1 = (bf16[4,32,2048]{2,1,0:T(8,128)(2,1)S(1)}, bf16[4,32,2048]{2,1,0:T(8,128)(2,1)S(1)}, u32[]{:S(2)}, u32[]{:S(2)}) collective-permute-start(bf16[4,32,2048]{2,1,0:T(8,128)(2,1)S(1)} %get-tuple-element.72), channel_id=1, source_target_pairs={{0,4},{2,6},{4,8},{6,10},{8,12},{10,14},{12,16},{14,18},{16,20},{1... | collective-permute-start | bytes 1572872 | tf_op jit(solution)/shard_map/ppermute | solution.py:13
  47.5 57.8 %collective-permute-start.5 = (bf16[4,32,2048]{2,1,0:T(8,128)(2,1)S(1)}, bf16[4,32,2048]{2,1,0:T(8,128)(2,1)S(1)}, u32[]{:S(2)}, u32[]{:S(2)}) collective-permute-start(bf16[4,32,2048]{2,1,0:T(8,128)(2,1)S(1)} %collective-permute-done.2), channel_id=1, source_target_pairs={{0,508},{2,510},{4,0},{6,2},{8,4},{10,6},{12,8},{14,10},{16,12},{1... | collective-permute-start | bytes 1572872 | tf_op jit(solution)/shard_map/ppermute | solution.py:13
  56.6 48.8 %collective-permute-start.11 = (bf16[4,32,2048]{2,1,0:T(8,128)(2,1)S(1)}, bf16[4,32,2048]{2,1,0:T(8,128)(2,1)S(1)}, u32[]{:S(2)}, u32[]{:S(2)}) collective-permute-start(bf16[4,32,2048]{2,1,0:T(8,128)(2,1)S(1)} %collective-permute-done.3), channel_id=1, source_target_pairs={{0,508},{2,510},{4,0},{6,2},{8,4},{10,6},{12,8},{14,10},{16,12},{1... | collective-permute-start | bytes 1572872 | tf_op jit(solution)/shard_map/ppermute | solution.py:13
  59.0 46.4 %collective-permute-start.10 = (bf16[4,32,2048]{2,1,0:T(8,128)(2,1)S(1)}, bf16[4,32,2048]{2,1,0:T(8,128)(2,1)S(1)}, u32[]{:S(2)}, u32[]{:S(2)}) collective-permute-start(bf16[4,32,2048]{2,1,0:T(8,128)(2,1)S(1)} %collective-permute-done.1), channel_id=1, source_target_pairs={{0,4},{2,6},{4,8},{6,10},{8,12},{10,14},{12,16},{14,18},{16,20},{1... | collective-permute-start | bytes 1572872 | tf_op jit(solution)/shard_map/ppermute | solution.py:13
  63.3 42.0 %collective-permute-start.4 = (bf16[4,32,2048]{2,1,0:T(8,128)(2,1)S(1)}, bf16[4,32,2048]{2,1,0:T(8,128)(2,1)S(1)}, u32[]{:S(2)}, u32[]{:S(2)}) collective-permute-start(bf16[4,32,2048]{2,1,0:T(8,128)(2,1)S(1)} %collective-permute-done), channel_id=1, source_target_pairs={{0,4},{2,6},{4,8},{6,10},{8,12},{10,14},{12,16},{14,18},{16,20},{1... | collective-permute-start | bytes 1572872 | tf_op jit(solution)/shard_map/ppermute | solution.py:13
  68.2 18.1 %collective-permute-start.8 = (f32[32,257]{1,0:T(8,128)S(1)}, f32[32,257]{1,0:T(8,128)S(1)}, u32[]{:S(2)}, u32[]{:S(2)}) collective-permute-start(f32[32,257]{1,0:T(8,128)S(1)} %get-tuple-element.93), channel_id=1, source_target_pairs={{0,4},{2,6},{4,8},{6,10},{8,12},{10,14},{12,16},{14,18},{16,20},{1... | collective-permute-start | bytes 98696 | tf_op jit(solution)/shard_map/ppermute | solution.py:13
  86.3 9.1 %collective-permute-start.9 = (f32[32,257]{1,0:T(8,128)S(1)}, f32[32,257]{1,0:T(8,128)S(1)}, u32[]{:S(2)}, u32[]{:S(2)}) collective-permute-start(f32[32,257]{1,0:T(8,128)S(1)} %get-tuple-element.94), channel_id=1, source_target_pairs={{0,508},{2,510},{4,0},{6,2},{8,4},{10,6},{12,8},{14,10},{16,12},{1... | collective-permute-start | bytes 98696 | tf_op jit(solution)/shard_map/ppermute | solution.py:13
  95.4 6.3 %collective-permute-start.6 = (f32[32,257]{1,0:T(8,128)S(1)}, f32[32,257]{1,0:T(8,128)S(1)}, u32[]{:S(2)}, u32[]{:S(2)}) collective-permute-start(f32[32,257]{1,0:T(8,128)S(1)} %get-tuple-element.89), channel_id=1, source_target_pairs={{0,2},{2,4},{4,6},{6,8},{8,10},{10,12},{12,14},{14,16},{16,18},{18... | collective-permute-start | bytes 98696 | tf_op jit(solution)/shard_map/ppermute | solution.py:13
  101.6 3.6 %collective-permute-start.7 = (f32[32,257]{1,0:T(8,128)S(1)}, f32[32,257]{1,0:T(8,128)S(1)}, u32[]{:S(2)}, u32[]{:S(2)}) collective-permute-start(f32[32,257]{1,0:T(8,128)S(1)} %get-tuple-element.90), channel_id=1, source_target_pairs={{0,510},{2,0},{4,2},{6,4},{8,6},{10,8},{12,10},{14,12},{16,14},{18... | collective-permute-start | bytes 98696 | tf_op jit(solution)/shard_map/ppermute | solution.py:13
  109.4 27.0 %collective-permute-start.12 = (f32[32,257]{1,0:T(8,128)S(1)}, f32[32,257]{1,0:T(8,128)S(1)}, u32[]{:S(2)}, u32[]{:S(2)}) collective-permute-start(f32[32,257]{1,0:T(8,128)S(1)} %get-tuple-element.79), channel_id=1, source_target_pairs={{0,6},{2,8},{4,10},{6,12},{8,14},{10,16},{12,18},{14,20},{16,22},{... | collective-permute-start | bytes 98696 | tf_op jit(solution)/shard_map/ppermute | solution.py:13
  113.9 22.6 %collective-permute-start.13 = (f32[32,257]{1,0:T(8,128)S(1)}, f32[32,257]{1,0:T(8,128)S(1)}, u32[]{:S(2)}, u32[]{:S(2)}) collective-permute-start(f32[32,257]{1,0:T(8,128)S(1)} %get-tuple-element.83), channel_id=1, source_target_pairs={{0,8},{2,10},{4,12},{6,14},{8,16},{10,18},{12,20},{14,22},{16,24},... | collective-permute-start | bytes 98696 | tf_op jit(solution)/shard_map/ppermute | solution.py:13
  115.8 20.7 %collective-permute-start.14 = (f32[32,257]{1,0:T(8,128)S(1)}, f32[32,257]{1,0:T(8,128)S(1)}, u32[]{:S(2)}, u32[]{:S(2)}) collective-permute-start(f32[32,257]{1,0:T(8,128)S(1)} %get-tuple-element.82), channel_id=1, source_target_pairs={{0,506},{2,508},{4,510},{6,0},{8,2},{10,4},{12,6},{14,8},{16,10},{... | collective-permute-start | bytes 98696 | tf_op jit(solution)/shard_map/ppermute | solution.py:13
  131.9 7.0 %collective-permute-start.15 = (f32[32,257]{1,0:T(8,128)S(1)}, f32[32,257]{1,0:T(8,128)S(1)}, u32[]{:S(2)}, u32[]{:S(2)}) collective-permute-start(f32[32,257]{1,0:T(8,128)S(1)} %get-tuple-element.86), channel_id=1, source_target_pairs={{0,504},{2,506},{4,508},{6,510},{8,0},{10,2},{12,4},{14,6},{16,8},... | collective-permute-start | bytes 98696 | tf_op jit(solution)/shard_map/ppermute | solution.py:13
  138.9 10.8 %collective-permute-start.16 = (f32[2,32,4,257]{3,1,2,0:T(8,128)S(1)}, f32[2,32,4,257]{3,1,2,0:T(8,128)S(1)}, u32[]{:S(2)}, u32[]{:S(2)}) collective-permute-start(f32[2,32,4,257]{3,1,2,0:T(8,128)S(1)} %pad_maximum_fusion.5), channel_id=1, source_target_pairs={{0,1},{1,0},{2,3},{3,2},{4,5},{5,4},{6,7},{7,6},{8,9},{9,8},{10,11... | collective-permute-start | bytes 789512 | tf_op jit(solution)/shard_map/ppermute | solution.py:18

commit v9 on v7

--- a/solution.py
+++ b/solution.py
@@ -78,11 +78,7 @@
     channels, segments, length = samples.shape
     half_len = length // 2
     stops = offsets.shape[0]
-    spectrum = jnp.dot(
-        jnp.swapaxes(samples, 0, 1).reshape(segments * channels, length),
-        forward_table(length),
-        preferred_element_type=jnp.float32,
-    ).reshape(segments, channels, length)
+    spectrum = jnp.einsum("csn,nk->sck", samples, forward_table(length), preferred_element_type=jnp.float32)
     keep = (1 - bad_mask).astype(jnp.float32)
     white = whiten(spectrum, keep[None, :, None], half_len)
     split = segments // 2

time: 138 us -> 138 us (level)
    unnamed x8 -> x9, local copies, waits for them, and re-layouts: 3.71 us -> 1.91 us
where the time goes in v9:
time: 138 us; the launch traced here: 137 us
  starting transfers between devices  64.8 us (47%)
  waiting for transfers between devices  44.2 us (32%)
  matrix products  13.1 us (9%)
  other arithmetic  10.1 us (7%)
  local copies, waits for them, and re-layouts  3.52 us (3%)
    ppermute x14, starting transfers between devices, shifted(): lax.ppermute(x, axis, [(i, (i + by) % length) for i in range(length)])  62.7 us
    ppermute x14, waiting for transfers between devices, shifted(): lax.ppermute(x, axis, [(i, (i + by) % length) for i in range(length)])  36.3 us
    ppermute x1, waiting for transfers between devices, swapped(): return lax.ppermute(x, axis, [(i, i ^ 1) for i in range(length)])  7.84 us
    dot_general x4, matrix products, lags_of(): jnp.dot(jnp.concatenate([own, later], axis=0), back_table, precision=lax....  7.78 us
    another operation x2, other arithmetic  2.96 us
  transfers between devices with their start and end apart: 15, of which 7 were waited for; matrix products, arithmetic and copies ran while one was open for 6% of the time, Pallas kernels for 0%

profile of v9, /device:TPU:1, one launch (start us, length us, event | category | flops | bytes accessed | tf_op | source)
XLA Modules:
  0.0 136.9 jit_solution(176652588308700803)
XLA Ops:
  0.6 1.0 fusion.47
  2.3 3.0 %subtract_convert_fusion = (bf16[32,64,1024]{2,1,0:T(8,128)(2,1)S(1)}, bf16[32,64,1024]{2,1,0:T(8,128)(2,1)S(1)}) fusion(f32[64,1024]{1,0:T(8,128)S(1)} %get-tuple-element.101, f32[32,1024]{1,0:T(8,128)S(1)} %get-tuple-element.98, f32[64,1024]{1,0:T(8,128)S(1)} %get-tuple-element.102, f32[32,1024]{1,0:T(8,128)S(1)} %get-tuple-element.97), kind=kLoop, calls=%fused_computation.5 | loop fusion | flops 18874368 | bytes 9175040 | tf_op jit(solution)/shard_map/convert.7
  5.3 2.6 %multiply_reduce_fusion = (f32[8,32]{1,0:T(8,128)S(1)}, f32[8,32,2048]{2,1,0:T(8,128)S(1)}) fusion(bf16[32,8,2048]{2,1,0:T(8,128)(2,1)S(1)} %copy-done, bf16[2048,1024]{1,0:T(8,128)(2,1)S(1)} %bitcast.109, bf16[2048,1024]{1,0:T(8,128)(2,1)S(1)} %bitcast.108), kind=kOutput, calls=%fused_computation.17 | convolution fusion | flops 2165309184 | bytes 11535360 | tf_op jit(solution)/shard_map/csn,nk->sck/dot_general | solution.py:81
  8.4 1.2 slice_convert_fusion
  9.7 1.4 %scatter.4 = bf16[4,32,2048]{2,1,0:T(8,128)(2,1)} dynamic-update-slice(bf16[4,32,2048]{2,1,0:T(8,128)(2,1)} %get-tuple-element.63, bf16[4,32,1]{2,1,0:T(8,128)(2,1)S(1)} %copy.10, s32[]{:T(128)} %constant.84.clone.1, s32[]{:T(128)} %constant.84.clone.1, s32[]{:T(128)} %constant.92.clone.1) | dynamic-update-slice | bytes 516 | tf_op jit(solution)/shard_map/scatter | solution.py:90
  11.2 8.8 %collective-permute-start.2 = (bf16[4,32,2048]{2,1,0:T(8,128)(2,1)}, bf16[4,32,2048]{2,1,0:T(8,128)(2,1)S(1)}, u32[]{:S(2)}, u32[]{:S(2)}) collective-permute-start(bf16[4,32,2048]{2,1,0:T(8,128)(2,1)} %scatter.4), channel_id=1, source_target_pairs={{0,510},{2,0},{4,2},{6,4},{8,6},{10,8},{12,10},{14,12},{16,14},{18... | collective-permute-start | bytes 1572872 | tf_op jit(solution)/shard_map/ppermute | solution.py:13
  19.9 10.7 %collective-permute-start.3 = (bf16[4,32,2048]{2,1,0:T(8,128)(2,1)}, bf16[4,32,2048]{2,1,0:T(8,128)(2,1)S(1)}, u32[]{:S(2)}, u32[]{:S(2)}) collective-permute-start(bf16[4,32,2048]{2,1,0:T(8,128)(2,1)} %scatter.4), channel_id=1, source_target_pairs={{0,508},{2,510},{4,0},{6,2},{8,4},{10,6},{12,8},{14,10},{16,12},{1... | collective-permute-start | bytes 1572872 | tf_op jit(solution)/shard_map/ppermute | solution.py:13
  30.6 3.3 %collective-permute-start = (bf16[4,32,2048]{2,1,0:T(8,128)(2,1)}, bf16[4,32,2048]{2,1,0:T(8,128)(2,1)S(1)}, u32[]{:S(2)}, u32[]{:S(2)}) collective-permute-start(bf16[4,32,2048]{2,1,0:T(8,128)(2,1)} %get-tuple-element.64), channel_id=1, source_target_pairs={{0,2},{2,4},{4,6},{6,8},{8,10},{10,12},{12,14},{14,16},{16,18},{18... | collective-permute-start | bytes 1572872 | tf_op jit(solution)/shard_map/ppermute | solution.py:13
  33.9 1.9 %collective-permute-start.1 = (bf16[4,32,2048]{2,1,0:T(8,128)(2,1)}, bf16[4,32,2048]{2,1,0:T(8,128)(2,1)S(1)}, u32[]{:S(2)}, u32[]{:S(2)}) collective-permute-start(bf16[4,32,2048]{2,1,0:T(8,128)(2,1)} %get-tuple-element.64), channel_id=1, source_target_pairs={{0,4},{2,6},{4,8},{6,10},{8,12},{10,14},{12,16},{14,18},{16,20},{1... | collective-permute-start | bytes 1572872 | tf_op jit(solution)/shard_map/ppermute | solution.py:13
  36.7 6.0 %collective-permute-done.3 = bf16[4,32,2048]{2,1,0:T(8,128)(2,1)S(1)} collective-permute-done((bf16[4,32,2048]{2,1,0:T(8,128)(2,1)}, bf16[4,32,2048]{2,1,0:T(8,128)(2,1)S(1)}, u32[]{:S(2)}, u32[]{:S(2)}) %collective-permute-start.3) | collective-permute-done | bytes 524320 | tf_op jit(solution)/shard_map/ppermute | solution.py:13
  43.3 15.3 %collective-permute-done.1 = bf16[4,32,2048]{2,1,0:T(8,128)(2,1)S(1)} collective-permute-done((bf16[4,32,2048]{2,1,0:T(8,128)(2,1)}, bf16[4,32,2048]{2,1,0:T(8,128)(2,1)S(1)}, u32[]{:S(2)}, u32[]{:S(2)}) %collective-permute-start.1) | collective-permute-done | bytes 524320 | tf_op jit(solution)/shard_map/ppermute | solution.py:13
  60.2 1.9 %collective-permute-start.5 = (bf16[8,32,2048]{2,1,0:T(8,128)(2,1)S(1)}, bf16[8,32,2048]{2,1,0:T(8,128)(2,1)S(1)}, u32[]{:S(2)}, u32[]{:S(2)}) collective-permute-start(bf16[8,32,2048]{2,1,0:T(8,128)(2,1)S(1)} %pad_maximum_fusion.6), channel_id=1, source_target_pairs={{0,508},{2,510},{4,0},{6,2},{8,4},{10,6},{12,8},{14,10},{16,12},{1... | collective-permute-start | bytes 3145736 | tf_op jit(solution)/shard_map/ppermute | solution.py:13
  62.1 3.4 %collective-permute-start.4 = (bf16[8,32,2048]{2,1,0:T(8,128)(2,1)S(1)}, bf16[8,32,2048]{2,1,0:T(8,128)(2,1)S(1)}, u32[]{:S(2)}, u32[]{:S(2)}) collective-permute-start(bf16[8,32,2048]{2,1,0:T(8,128)(2,1)S(1)} %pad_maximum_fusion.5), channel_id=1, source_target_pairs={{0,4},{2,6},{4,8},{6,10},{8,12},{10,14},{12,16},{14,18},{16,20},{1... | collective-permute-start | bytes 3145736 | tf_op jit(solution)/shard_map/ppermute | solution.py:13
  66.1 1.9 %fusion.6 = f32[64,257]{1,0:T(8,128)S(1)} fusion(f32[1024,257]{1,0:T(8,128)S(1)} %bitcast.104, f32[1024,257]{1,0:T(8,128)S(1)} %bitcast.100, f32[32,1024]{1,0:T(8,128)S(1)} %get-tuple-element.49, f32[32,1024]{1,0:T(8,128)S(1)} %get-tuple-element.48, f32[32,1024]{1,0:T(8,128)S(1)} %get-tuple-element.47, f32[32,1024]{1,0:T(8,128)S(1)} %get-tuple-element.46), kind=kOutput, calls=%fused_computation.22 | convolution fusion | flops 405145600 | bytes 2695424 | tf_op jit(solution)/shard_map/dot_general | solution.py:98
  68.1 1.9 %collective-permute-start.8 = (f32[32,257]{1,0:T(8,128)S(1)}, f32[32,257]{1,0:T(8,128)S(1)}, u32[]{:S(2)}, u32[]{:S(2)}) collective-permute-start(f32[32,257]{1,0:T(8,128)S(1)} %get-tuple-element.85), channel_id=1, source_target_pairs={{0,4},{2,6},{4,8},{6,10},{8,12},{10,14},{12,16},{14,18},{16,20},{1... | collective-permute-start | bytes 98696 | tf_op jit(solution)/shard_map/ppermute | solution.py:13
  70.0 9.3 %collective-permute-start.9 = (f32[32,257]{1,0:T(8,128)S(1)}, f32[32,257]{1,0:T(8,128)S(1)}, u32[]{:S(2)}, u32[]{:S(2)}) collective-permute-start(f32[32,257]{1,0:T(8,128)S(1)} %get-tuple-element.86), channel_id=1, source_target_pairs={{0,508},{2,510},{4,0},{6,2},{8,4},{10,6},{12,8},{14,10},{16,12},{1... | collective-permute-start | bytes 98696 | tf_op jit(solution)/shard_map/ppermute | solution.py:13
  80.0 1.9 %fusion.7 = f32[64,257]{1,0:T(8,128)S(1)} fusion(f32[1024,257]{1,0:T(8,128)S(1)} %bitcast.105, f32[1024,257]{1,0:T(8,128)S(1)} %bitcast.101, f32[32,1024]{1,0:T(8,128)S(1)} %get-tuple-element.53, f32[32,1024]{1,0:T(8,128)S(1)} %get-tuple-element.52, f32[32,1024]{1,0:T(8,128)S(1)} %get-tuple-element.58, f32[32,1024]{1,0:T(8,128)S(1)} %get-tuple-element.59), kind=kOutput, calls=%fused_computation.23 | convolution fusion | flops 405145600 | bytes 2695424 | tf_op jit(solution)/shard_map/dot_general | solution.py:98
  82.0 1.9 %collective-permute-start.6 = (f32[32,257]{1,0:T(8,128)S(1)}, f32[32,257]{1,0:T(8,128)S(1)}, u32[]{:S(2)}, u32[]{:S(2)}) collective-permute-start(f32[32,257]{1,0:T(8,128)S(1)} %get-tuple-element.81), channel_id=1, source_target_pairs={{0,2},{2,4},{4,6},{6,8},{8,10},{10,12},{12,14},{14,16},{16,18},{18... | collective-permute-start | bytes 98696 | tf_op jit(solution)/shard_map/ppermute | solution.py:13
  83.9 9.8 %collective-permute-done.8 = f32[32,257]{1,0:T(8,128)S(1)} collective-permute-done((f32[32,257]{1,0:T(8,128)S(1)}, f32[32,257]{1,0:T(8,128)S(1)}, u32[]{:S(2)}, u32[]{:S(2)}) %collective-permute-start.8) | collective-permute-done | bytes 32928 | tf_op jit(solution)/shard_map/ppermute | solution.py:13
  93.8 1.9 %collective-permute-start.7 = (f32[32,257]{1,0:T(8,128)S(1)}, f32[32,257]{1,0:T(8,128)S(1)}, u32[]{:S(2)}, u32[]{:S(2)}) collective-permute-start(f32[32,257]{1,0:T(8,128)S(1)} %get-tuple-element.82), channel_id=1, source_target_pairs={{0,510},{2,0},{4,2},{6,4},{8,6},{10,8},{12,10},{14,12},{16,14},{18... | collective-permute-start | bytes 98696 | tf_op jit(solution)/shard_map/ppermute | solution.py:13
  95.7 3.5 %collective-permute-done.7 = f32[32,257]{1,0:T(8,128)S(1)} collective-permute-done((f32[32,257]{1,0:T(8,128)S(1)}, f32[32,257]{1,0:T(8,128)S(1)}, u32[]{:S(2)}, u32[]{:S(2)}) %collective-permute-start.7) | collective-permute-done | bytes 32928 | tf_op jit(solution)/shard_map/ppermute | solution.py:13
  101.2 1.9 %fusion.5 = f32[64,257]{1,0:T(8,128)S(1)} fusion(f32[1024,257]{1,0:T(8,128)S(1)} %bitcast.106, f32[1024,257]{1,0:T(8,128)S(1)} %bitcast.102, f32[32,1024]{1,0:T(8,128)S(1)} %get-tuple-element.41, f32[32,1024]{1,0:T(8,128)S(1)} %get-tuple-element.40, f32[32,1024]{1,0:T(8,128)S(1)} %get-tuple-element.39, f32[32,1024]{1,0:T(8,128)S(1)} %get-tuple-element.38), kind=kOutput, calls=%fused_computation.21 | convolution fusion | flops 405145600 | bytes 2695424 | tf_op jit(solution)/shard_map/dot_general | solution.py:98
  103.1 1.9 %collective-permute-start.10 = (f32[32,257]{1,0:T(8,128)S(1)}, f32[32,257]{1,0:T(8,128)S(1)}, u32[]{:S(2)}, u32[]{:S(2)}) collective-permute-start(f32[32,257]{1,0:T(8,128)S(1)} %get-tuple-element.71), channel_id=1, source_target_pairs={{0,6},{2,8},{4,10},{6,12},{8,14},{10,16},{12,18},{14,20},{16,22},{... | collective-permute-start | bytes 98696 | tf_op jit(solution)/shard_map/ppermute | solution.py:13
  105.7 1.9 %fusion.4 = f32[64,257]{1,0:T(8,128)S(1)} fusion(f32[1024,257]{1,0:T(8,128)S(1)} %bitcast.107, f32[1024,257]{1,0:T(8,128)S(1)} %bitcast.103, f32[32,1024]{1,0:T(8,128)S(1)} %get-tuple-element.45, f32[32,1024]{1,0:T(8,128)S(1)} %get-tuple-element.44, f32[32,1024]{1,0:T(8,128)S(1)} %get-tuple-element.54, f32[32,1024]{1,0:T(8,128)S(1)} %get-tuple-element.55), kind=kOutput, calls=%fused_computation.20 | convolution fusion | flops 405145600 | bytes 2695424 | tf_op jit(solution)/shard_map/dot_general | solution.py:98
  107.6 1.9 %collective-permute-start.11 = (f32[32,257]{1,0:T(8,128)S(1)}, f32[32,257]{1,0:T(8,128)S(1)}, u32[]{:S(2)}, u32[]{:S(2)}) collective-permute-start(f32[32,257]{1,0:T(8,128)S(1)} %get-tuple-element.75), channel_id=1, source_target_pairs={{0,8},{2,10},{4,12},{6,14},{8,16},{10,18},{12,20},{14,22},{16,24},... | collective-permute-start | bytes 98696 | tf_op jit(solution)/shard_map/ppermute | solution.py:13
  109.6 9.4 %collective-permute-start.12 = (f32[32,257]{1,0:T(8,128)S(1)}, f32[32,257]{1,0:T(8,128)S(1)}, u32[]{:S(2)}, u32[]{:S(2)}) collective-permute-start(f32[32,257]{1,0:T(8,128)S(1)} %get-tuple-element.74), channel_id=1, source_target_pairs={{0,506},{2,508},{4,510},{6,0},{8,2},{10,4},{12,6},{14,8},{16,10},{... | collective-permute-start | bytes 98696 | tf_op jit(solution)/shard_map/ppermute | solution.py:13
  118.9 4.5 %collective-permute-start.13 = (f32[32,257]{1,0:T(8,128)S(1)}, f32[32,257]{1,0:T(8,128)S(1)}, u32[]{:S(2)}, u32[]{:S(2)}) collective-permute-start(f32[32,257]{1,0:T(8,128)S(1)} %get-tuple-element.78), channel_id=1, source_target_pairs={{0,504},{2,506},{4,508},{6,510},{8,0},{10,2},{12,4},{14,6},{16,8},... | collective-permute-start | bytes 98696 | tf_op jit(solution)/shard_map/ppermute | solution.py:13
  123.6 1.1 collective-permute-done.13
  124.7 2.2 %collective-permute-start.14 = (f32[2,32,4,257]{3,1,2,0:T(8,128)S(1)}, f32[2,32,4,257]{3,1,2,0:T(8,128)S(1)}, u32[]{:S(2)}, u32[]{:S(2)}) collective-permute-start(f32[2,32,4,257]{3,1,2,0:T(8,128)S(1)} %pad_maximum_fusion.7), channel_id=1, source_target_pairs={{0,1},{1,0},{2,3},{3,2},{4,5},{5,4},{6,7},{7,6},{8,9},{9,8},{10,11... | collective-permute-start | bytes 789512 | tf_op jit(solution)/shard_map/ppermute | solution.py:18
  126.9 7.8 %collective-permute-done.14 = f32[2,32,4,257]{3,1,2,0:T(8,128)S(1)} collective-permute-done((f32[2,32,4,257]{3,1,2,0:T(8,128)S(1)}, f32[2,32,4,257]{3,1,2,0:T(8,128)S(1)}, u32[]{:S(2)}, u32[]{:S(2)}) %collective-permute-start.14) | collective-permute-done | bytes 263200 | tf_op jit(solution)/shard_map/ppermute | solution.py:18
  135.3 0.8 copy.12
  136.1 0.8 copy.11
  (60 shorter events, 8.8 us)
Async XLA Ops:
  0.6 4.6 %copy-start = (bf16[32,8,2048]{2,1,0:T(8,128)(2,1)S(1)}, bf16[32,8,2048]{2,1,0:T(8,128)(2,1)}, u32[]{:S(2)}) copy-start(bf16[32,8,2048]{2,1,0:T(8,128)(2,1)} %param.5) | copy-start | bytes 3145732
  5.3 2.6 %copy-start.2 = (s32[32]{0:T(128)S(1)}, s32[32]{0:T(128)}, u32[]{:S(2)}) copy-start(s32[32]{0:T(128)} %param.7) | copy-start | bytes 388
  7.9 1.7 %copy-start.1 = (s32[4,32]{1,0:T(4,128)S(1)}, s32[4,32]{1,0:T(4,128)}, u32[]{:S(2)}) copy-start(s32[4,32]{1,0:T(4,128)} %param.6) | copy-start | bytes 1540
  11.2 25.6 %collective-permute-start.2 = (bf16[4,32,2048]{2,1,0:T(8,128)(2,1)}, bf16[4,32,2048]{2,1,0:T(8,128)(2,1)S(1)}, u32[]{:S(2)}, u32[]{:S(2)}) collective-permute-start(bf16[4,32,2048]{2,1,0:T(8,128)(2,1)} %scatter.4), channel_id=1, source_target_pairs={{0,510},{2,0},{4,2},{6,4},{8,6},{10,8},{12,10},{14,12},{16,14},{18... | collective-permute-start | bytes 1572872 | tf_op jit(solution)/shard_map/ppermute | solution.py:13
  19.9 22.8 %collective-permute-start.3 = (bf16[4,32,2048]{2,1,0:T(8,128)(2,1)}, bf16[4,32,2048]{2,1,0:T(8,128)(2,1)S(1)}, u32[]{:S(2)}, u32[]{:S(2)}) collective-permute-start(bf16[4,32,2048]{2,1,0:T(8,128)(2,1)} %scatter.4), channel_id=1, source_target_pairs={{0,508},{2,510},{4,0},{6,2},{8,4},{10,6},{12,8},{14,10},{16,12},{1... | collective-permute-start | bytes 1572872 | tf_op jit(solution)/shard_map/ppermute | solution.py:13
  30.6 12.7 %collective-permute-start = (bf16[4,32,2048]{2,1,0:T(8,128)(2,1)}, bf16[4,32,2048]{2,1,0:T(8,128)(2,1)S(1)}, u32[]{:S(2)}, u32[]{:S(2)}) collective-permute-start(bf16[4,32,2048]{2,1,0:T(8,128)(2,1)} %get-tuple-element.64), channel_id=1, source_target_pairs={{0,2},{2,4},{4,6},{6,8},{8,10},{10,12},{12,14},{14,16},{16,18},{18... | collective-permute-start | bytes 1572872 | tf_op jit(solution)/shard_map/ppermute | solution.py:13
  33.9 24.8 %collective-permute-start.1 = (bf16[4,32,2048]{2,1,0:T(8,128)(2,1)}, bf16[4,32,2048]{2,1,0:T(8,128)(2,1)S(1)}, u32[]{:S(2)}, u32[]{:S(2)}) collective-permute-start(bf16[4,32,2048]{2,1,0:T(8,128)(2,1)} %get-tuple-element.64), channel_id=1, source_target_pairs={{0,4},{2,6},{4,8},{6,10},{8,12},{10,14},{12,16},{14,18},{16,20},{1... | collective-permute-start | bytes 1572872 | tf_op jit(solution)/shard_map/ppermute | solution.py:13
  60.2 39.0 %collective-permute-start.5 = (bf16[8,32,2048]{2,1,0:T(8,128)(2,1)S(1)}, bf16[8,32,2048]{2,1,0:T(8,128)(2,1)S(1)}, u32[]{:S(2)}, u32[]{:S(2)}) collective-permute-start(bf16[8,32,2048]{2,1,0:T(8,128)(2,1)S(1)} %pad_maximum_fusion.6), channel_id=1, source_target_pairs={{0,508},{2,510},{4,0},{6,2},{8,4},{10,6},{12,8},{14,10},{16,12},{1... | collective-permute-start | bytes 3145736 | tf_op jit(solution)/shard_map/ppermute | solution.py:13
  62.1 37.1 %collective-permute-start.4 = (bf16[8,32,2048]{2,1,0:T(8,128)(2,1)S(1)}, bf16[8,32,2048]{2,1,0:T(8,128)(2,1)S(1)}, u32[]{:S(2)}, u32[]{:S(2)}) collective-permute-start(bf16[8,32,2048]{2,1,0:T(8,128)(2,1)S(1)} %pad_maximum_fusion.5), channel_id=1, source_target_pairs={{0,4},{2,6},{4,8},{6,10},{8,12},{10,14},{12,16},{14,18},{16,20},{1... | collective-permute-start | bytes 3145736 | tf_op jit(solution)/shard_map/ppermute | solution.py:13
  68.1 25.7 %collective-permute-start.8 = (f32[32,257]{1,0:T(8,128)S(1)}, f32[32,257]{1,0:T(8,128)S(1)}, u32[]{:S(2)}, u32[]{:S(2)}) collective-permute-start(f32[32,257]{1,0:T(8,128)S(1)} %get-tuple-element.85), channel_id=1, source_target_pairs={{0,4},{2,6},{4,8},{6,10},{8,12},{10,14},{12,16},{14,18},{16,20},{1... | collective-permute-start | bytes 98696 | tf_op jit(solution)/shard_map/ppermute | solution.py:13
  70.0 25.6 %collective-permute-start.9 = (f32[32,257]{1,0:T(8,128)S(1)}, f32[32,257]{1,0:T(8,128)S(1)}, u32[]{:S(2)}, u32[]{:S(2)}) collective-permute-start(f32[32,257]{1,0:T(8,128)S(1)} %get-tuple-element.86), channel_id=1, source_target_pairs={{0,508},{2,510},{4,0},{6,2},{8,4},{10,6},{12,8},{14,10},{16,12},{1... | collective-permute-start | bytes 98696 | tf_op jit(solution)/shard_map/ppermute | solution.py:13
  82.0 13.7 %collective-permute-start.6 = (f32[32,257]{1,0:T(8,128)S(1)}, f32[32,257]{1,0:T(8,128)S(1)}, u32[]{:S(2)}, u32[]{:S(2)}) collective-permute-start(f32[32,257]{1,0:T(8,128)S(1)} %get-tuple-element.81), channel_id=1, source_target_pairs={{0,2},{2,4},{4,6},{6,8},{8,10},{10,12},{12,14},{14,16},{16,18},{18... | collective-permute-start | bytes 98696 | tf_op jit(solution)/shard_map/ppermute | solution.py:13
  93.8 5.4 %collective-permute-start.7 = (f32[32,257]{1,0:T(8,128)S(1)}, f32[32,257]{1,0:T(8,128)S(1)}, u32[]{:S(2)}, u32[]{:S(2)}) collective-permute-start(f32[32,257]{1,0:T(8,128)S(1)} %get-tuple-element.82), channel_id=1, source_target_pairs={{0,510},{2,0},{4,2},{6,4},{8,6},{10,8},{12,10},{14,12},{16,14},{18... | collective-permute-start | bytes 98696 | tf_op jit(solution)/shard_map/ppermute | solution.py:13
  103.1 20.4 %collective-permute-start.10 = (f32[32,257]{1,0:T(8,128)S(1)}, f32[32,257]{1,0:T(8,128)S(1)}, u32[]{:S(2)}, u32[]{:S(2)}) collective-permute-start(f32[32,257]{1,0:T(8,128)S(1)} %get-tuple-element.71), channel_id=1, source_target_pairs={{0,6},{2,8},{4,10},{6,12},{8,14},{10,16},{12,18},{14,20},{16,22},{... | collective-permute-start | bytes 98696 | tf_op jit(solution)/shard_map/ppermute | solution.py:13
  107.6 15.9 %collective-permute-start.11 = (f32[32,257]{1,0:T(8,128)S(1)}, f32[32,257]{1,0:T(8,128)S(1)}, u32[]{:S(2)}, u32[]{:S(2)}) collective-permute-start(f32[32,257]{1,0:T(8,128)S(1)} %get-tuple-element.75), channel_id=1, source_target_pairs={{0,8},{2,10},{4,12},{6,14},{8,16},{10,18},{12,20},{14,22},{16,24},... | collective-permute-start | bytes 98696 | tf_op jit(solution)/shard_map/ppermute | solution.py:13
  109.6 14.0 %collective-permute-start.12 = (f32[32,257]{1,0:T(8,128)S(1)}, f32[32,257]{1,0:T(8,128)S(1)}, u32[]{:S(2)}, u32[]{:S(2)}) collective-permute-start(f32[32,257]{1,0:T(8,128)S(1)} %get-tuple-element.74), channel_id=1, source_target_pairs={{0,506},{2,508},{4,510},{6,0},{8,2},{10,4},{12,6},{14,8},{16,10},{... | collective-permute-start | bytes 98696 | tf_op jit(solution)/shard_map/ppermute | solution.py:13
  118.9 5.7 %collective-permute-start.13 = (f32[32,257]{1,0:T(8,128)S(1)}, f32[32,257]{1,0:T(8,128)S(1)}, u32[]{:S(2)}, u32[]{:S(2)}) collective-permute-start(f32[32,257]{1,0:T(8,128)S(1)} %get-tuple-element.78), channel_id=1, source_target_pairs={{0,504},{2,506},{4,508},{6,510},{8,0},{10,2},{12,4},{14,6},{16,8},... | collective-permute-start | bytes 98696 | tf_op jit(solution)/shard_map/ppermute | solution.py:13
  124.7 10.0 %collective-permute-start.14 = (f32[2,32,4,257]{3,1,2,0:T(8,128)S(1)}, f32[2,32,4,257]{3,1,2,0:T(8,128)S(1)}, u32[]{:S(2)}, u32[]{:S(2)}) collective-permute-start(f32[2,32,4,257]{3,1,2,0:T(8,128)S(1)} %pad_maximum_fusion.7), channel_id=1, source_target_pairs={{0,1},{1,0},{2,3},{3,2},{4,5},{5,4},{6,7},{7,6},{8,9},{9,8},{10,11... | collective-permute-start | bytes 789512 | tf_op jit(solution)/shard_map/ppermute | solution.py:18

commit v10 on v4

--- a/solution.py
+++ b/solution.py
@@ -16,6 +16,14 @@
 def swapped(x, axis):
     length = lax.axis_size(axis)
     return lax.ppermute(x, axis, [(i, i ^ 1) for i in range(length)])
+
+
+def along(x, first_by, second_by, flip=False):
+    blocks = lax.axis_size("blk")
+    land = 1 if flip else 0
+    perm = [(b * 2, ((b + first_by) % blocks) * 2 + land) for b in range(blocks)]
+    perm += [(b * 2 + 1, ((b + second_by) % blocks) * 2 + 1 - land) for b in range(blocks)]
+    return lax.ppermute(x, ("blk", "rep"), perm)
 
 
 def cos_sin(phase, length):
@@ -85,48 +93,33 @@
     ).reshape(segments, channels, length)
     keep = (1 - bad_mask).astype(jnp.float32)
     white = whiten(spectrum, keep[None, :, None], half_len)
-    split = segments // 2
-    ahead = white[:split]
-    behind = white[split:]
-    ahead_f32 = ahead.astype(jnp.float32)
-    dc_imag = lax.broadcasted_iota(jnp.int32, behind.shape, 2) == half_len
-    moving_ahead = ahead
-    moving_behind = behind.at[:stops, :, half_len].set(offsets.astype(jnp.bfloat16))
+    first_rep = lax.axis_index("rep") == 0
+    dc_imag = lax.broadcasted_iota(jnp.int32, white.shape, 2) == half_len
+    moving = white.at[:stops, :, half_len].set(offsets.astype(jnp.bfloat16))
     back_table = inverse_table(length, LAGS)
-    own_parts, later_parts, from_earlier, from_later = [], [], [], []
-    lags = jnp.zeros((2 * channels, back_table.shape[1]), jnp.float32)
+    lags = []
     for stop in range(1, stops + 1):
-        moving_ahead, moving_behind, lags = lax.optimization_barrier(
-            (shifted(moving_ahead, "blk", 1), shifted(moving_behind, "blk", -1), lags)
+        moving, lags = lax.optimization_barrier((along(moving, 1, -1), lags))
+        arrived = jnp.where(dc_imag, jnp.zeros_like(moving), moving)
+        rows = jnp.where(first_rep, offsets[stop - 1], moving[stop - 1, :, half_len].astype(jnp.int32))
+        paired = jnp.where(first_rep, white, arrived).astype(jnp.float32)
+        partner = pick_rows(rows, jnp.where(first_rep, arrived, white))
+        lags.append(
+            jnp.dot(
+                cross_spectrum(paired, partner, half_len),
+                back_table,
+                precision=lax.Precision.HIGHEST,
+                preferred_element_type=jnp.float32,
+            )
         )
-        if stop > 1:
-            own_parts.append(lags[:channels])
-            later_parts.append(lags[channels:])
-            from_earlier.append(shifted(lags[channels:], "blk", stop - 1))
-            from_later.append(shifted(lags[:channels], "blk", 1 - stop))
-        own = cross_spectrum(ahead_f32, pick_rows(offsets[stop - 1], moving_ahead), half_len)
-        later_offsets = moving_behind[stop - 1, :, half_len].astype(jnp.int32)
-        later = jnp.where(dc_imag, jnp.zeros_like(moving_behind), moving_behind).astype(jnp.float32)
-        later = cross_spectrum(later, pick_rows(later_offsets, behind), half_len)
-        lags = jnp.dot(
-            jnp.concatenate([own, later], axis=0),
-            back_table,
-            precision=lax.Precision.HIGHEST,
-            preferred_element_type=jnp.float32,
-        )
-    own_parts.append(lags[:channels])
-    later_parts.append(lags[channels:])
-    from_earlier.append(shifted(lags[channels:], "blk", stops))
-    from_later.append(shifted(lags[:channels], "blk", -stops))
-    corr_part = jnp.stack(own_parts, axis=1) + jnp.stack(from_earlier, axis=1)
-    mirror_part = jnp.stack(from_later, axis=1) + jnp.stack(later_parts, axis=1)
-    parts = jnp.stack([corr_part, mirror_part], axis=0)
-    summed = parts + swapped(parts, "rep")
+    mine = jnp.stack(lags, axis=1)
+    across = jnp.stack([along(piece, -d, d, flip=True) for d, piece in enumerate(lags, 1)], axis=1)
+    beside = jnp.stack([along(piece, -d, d) for d, piece in enumerate(lags, 1)], axis=1)
+    other = swapped(mine, "rep")
     scale = 1.0 / math.sqrt(segments * lax.axis_size("rep") * half_len)
-    correlations = summed[0] * scale
-    mirrored = (summed[1] * scale)[:, :, ::-1]
+    correlations = jnp.where(first_rep, mine + across, other + beside) * scale
+    mirrored = (jnp.where(first_rep, beside + other, across + mine) * scale)[:, :, ::-1]
     return (correlations, mirrored)
-
 
 def solution(mesh):
     return jax.shard_map(

time: 143 us -> 164 us (1.15)
  the two profiles are of different devices: /device:TPU:1 before, /device:TPU:10 now
where the time goes in v10:
time: 164 us; the launch traced here: 163 us
  starting transfers between devices  77.6 us (47%)
  waiting for transfers between devices  45.2 us (28%)
  other arithmetic  18 us (11%)
  matrix products  13.1 us (8%)
  local copies, waits for them, and re-layouts  8.21 us (5%)
    ppermute x12, starting transfers between devices, along(): return lax.ppermute(x, ('blk', 'rep'), perm)  75.7 us
    ppermute x12, waiting for transfers between devices, along(): return lax.ppermute(x, ('blk', 'rep'), perm)  45.2 us
    dot_general x4, matrix products, on_device(): jnp.dot(cross_spectrum(paired, partner, half_len), back_table, precision=...  7.29 us
    another operation x5, other arithmetic  7.04 us
    unnamed x11, local copies, waits for them, and re-layouts  4.7 us
    convert_element_type x4, other arithmetic, on_device(): paired = jnp.where(first_rep, white, arrived).astype(jnp.float32)  4.46 us
    dot_general x4, matrix products, pick_rows(): jnp.einsum('gp,spk->sgk', picks, block, preferred_element_type=jnp.float32)  3.3 us
  transfers between devices with their start and end apart: 13, of which 5 were waited for; matrix products, arithmetic and copies ran while one was open for 9% of the time, Pallas kernels for 0%

profile of v10, /device:TPU:10, one launch (start us, length us, event | category | flops | bytes accessed | tf_op | source)
XLA Modules:
  0.0 163.1 jit_solution(4471428433160200842)
XLA Ops:
  0.6 1.0 fusion.42
  2.3 1.8 %copy.8 = bf16[32,8,2048]{2,0,1:T(8,128)(2,1)S(1)} copy(bf16[32,8,2048]{2,1,0:T(8,128)(2,1)} %param.5) | data formatting | bytes 2097152 | tf_op args[0]
  4.1 2.9 %subtract_convert_fusion = (bf16[32,64,1024]{2,1,0:T(8,128)(2,1)S(1)}, bf16[32,64,1024]{2,1,0:T(8,128)(2,1)S(1)}) fusion(f32[64,1024]{1,0:T(8,128)S(1)} %get-tuple-element.58, f32[32,1024]{1,0:T(8,128)S(1)} %get-tuple-element.55, f32[64,1024]{1,0:T(8,128)S(1)} %get-tuple-element.59, f32[32,1024]{1,0:T(8,128)S(1)} %get-tuple-element.54), kind=kLoop, calls=%fused_computation.5 | loop fusion | flops 18874368 | bytes 9175040 | tf_op jit(solution)/shard_map/convert.7
  7.0 2.5 %fusion.4 = (f32[256]{0:T(256)S(1)}, f32[2048,256]{0,1:T(8,128)S(1)}) fusion(bf16[256,2048]{1,0:T(8,128)(2,1)S(1)} %bitcast.74, bf16[2048,1024]{1,0:T(8,128)(2,1)S(1)} %bitcast.73, bf16[2048,1024]{1,0:T(8,128)(2,1)S(1)} %bitcast.72), kind=kOutput, calls=%fused_computation.12 | convolution fusion | flops 2165309184 | bytes 11535360 | tf_op jit(solution)/shard_map/dot_general | solution.py:89
  10.8 1.0 copy.12
  11.8 2.1 %and_reduce_fusion = pred[]{:T(512)} fusion(s32[3]{0:T(128)S(1)} %copy-done.1, s32[1]{0:T(128)} %get-tuple-element.52, s32[1]{0:T(128)} %constant.94.clone.1, s32[1]{0:T(128)} %get-tuple-element.53), kind=kLoop, calls=%fused_computation.131 | loop fusion | flops 17 | bytes 25 | tf_op jit(solution)/shard_map/reduce.1
  13.9 2.1 %dynamic-slice_select_fusion = bf16[4,32,1]{2,1,0:T(8,128)(2,1)S(1)} fusion(bf16[4,32,1]{2,1,0:T(8,128)(2,1)S(1)} %copy.9, bf16[8,32,2048]{2,1,0:T(8,128)(2,1)S(1)} %multiply_convert_fusion, s32[]{:T(128)} %bitcast.7, s32[]{:T(128)} %bitcast.8, pred[]{:T(512)} %and_reduce_fusion), kind=kLoop, calls=%fused_computation.105 | loop fusion | flops 128 | bytes 777 | tf_op jit(solution)/shard_map/select.1
  16.0 2.7 %scatter.4 = bf16[8,32,2048]{2,1,0:T(8,128)(2,1)} dynamic-update-slice(bf16[8,32,2048]{2,1,0:T(8,128)(2,1)} %copy.12, bf16[4,32,1]{2,1,0:T(8,128)(2,1)S(1)} %dynamic-slice_select_fusion, s32[]{:T(128)} %bitcast.7, s32[]{:T(128)} %constant.84.clone.1, s32[]{:T(128)} %bitcast.8) | dynamic-update-slice | bytes 516 | tf_op jit(solution)/shard_map/scatter | solution.py:98
  18.7 1.9 %collective-permute-start = (bf16[8,32,2048]{2,1,0:T(8,128)(2,1)}, bf16[8,32,2048]{2,1,0:T(8,128)(2,1)}, u32[]{:S(2)}, u32[]{:S(2)}) collective-permute-start(bf16[8,32,2048]{2,1,0:T(8,128)(2,1)} %scatter.4), channel_id=1, source_target_pairs={{0,2},{2,4},{4,6},{6,8},{8,10},{10,12},{12,14},{14,16},{16,18},{18... | collective-permute-start | bytes 3145736 | tf_op jit(solution)/shard_map/ppermute | solution.py:26
  21.5 11.7 %collective-permute-done = bf16[8,32,2048]{2,1,0:T(8,128)(2,1)} collective-permute-done((bf16[8,32,2048]{2,1,0:T(8,128)(2,1)}, bf16[8,32,2048]{2,1,0:T(8,128)(2,1)}, u32[]{:S(2)}, u32[]{:S(2)}) %collective-permute-start) | collective-permute-done | bytes 1048608 | tf_op jit(solution)/shard_map/ppermute | solution.py:26
  34.0 3.8 %collective-permute-start.1 = (bf16[8,32,2048]{2,1,0:T(8,128)(2,1)}, bf16[8,32,2048]{2,1,0:T(8,128)(2,1)S(1)}, u32[]{:S(2)}, u32[]{:S(2)}) collective-permute-start(bf16[8,32,2048]{2,1,0:T(8,128)(2,1)} %collective-permute-done), channel_id=1, source_target_pairs={{0,2},{2,4},{4,6},{6,8},{8,10},{10,12},{12,14},{14,16},{16,18},{18... | collective-permute-start | bytes 3145736 | tf_op jit(solution)/shard_map/ppermute | solution.py:26
  37.8 1.8 %convolution_bitcast_fusion.3 = f32[8,32,2048]{2,1,0:T(8,128)S(1)} fusion(bf16[8,32,2048]{2,1,0:T(8,128)(2,1)S(1)} %multiply_convert_fusion, pred[]{:T(512)S(6)} %eq.77, bf16[8,32,2048]{2,1,0:T(8,128)(2,1)} %collective-permute-done, pred[2048]{0:T(1024)(128)(4,1)S(1)} %iota_compare_fusion.4, s32[32]{0:T(128)S(1)} %broadcast_select_fusion.12), kind=kOutput, calls=%fused_computation.10 | convolution fusion | flops 34604032 | bytes 4196481 | tf_op jit(solution)/shard_map/gp,spk->sgk/dot_general | solution.py:82
  39.6 2.2 %select_convert_fusion.3 = f32[8,32,2048]{2,1,0:T(8,128)S(1)} fusion(pred[]{:T(512)S(6)} %eq.77, bf16[8,32,2048]{2,1,0:T(8,128)(2,1)} %collective-permute-done, pred[2048]{0:T(1024)(128)(4,1)S(1)} %iota_compare_fusion.4, f32[32]{0:T(128)S(1)} %subtract_convert_fusion.1, f32[8,32,2048]{2,1,0:T(8,128)S(1)} %bitcast.60, f32[8,32]{1,0:T(8,128)S(1)} %rsqrt.12), kind=kLoop, calls=%fused_computation.35 | loop fusion | flops 3145728 | bytes 5246081 | tf_op jit(solution)/shard_map/convert_element_type | solution.py:105
  42.3 1.8 %fusion.8 = f32[32,257]{1,0:T(8,128)S(1)} fusion(f32[1024,257]{1,0:T(8,128)S(1)} %bitcast.68, f32[1024,257]{1,0:T(8,128)S(1)} %bitcast.64, f32[32,1024]{1,0:T(8,128)S(1)} %get-tuple-element.43, f32[32,1024]{1,0:T(8,128)S(1)} %get-tuple-element.42), kind=kOutput, calls=%fused_computation.19 | convolution fusion | flops 202704896 | bytes 2400384 | tf_op jit(solution)/shard_map/dot_general | solution.py:108
  44.1 6.3 %collective-permute-done.1 = bf16[8,32,2048]{2,1,0:T(8,128)(2,1)S(1)} collective-permute-done((bf16[8,32,2048]{2,1,0:T(8,128)(2,1)}, bf16[8,32,2048]{2,1,0:T(8,128)(2,1)S(1)}, u32[]{:S(2)}, u32[]{:S(2)}) %collective-permute-start.1) | collective-permute-done | bytes 1048608 | tf_op jit(solution)/shard_map/ppermute | solution.py:26
  50.5 7.4 %collective-permute-start.2 = (bf16[8,32,2048]{2,1,0:T(8,128)(2,1)S(1)}, bf16[8,32,2048]{2,1,0:T(8,128)(2,1)S(1)}, u32[]{:S(2)}, u32[]{:S(2)}) collective-permute-start(bf16[8,32,2048]{2,1,0:T(8,128)(2,1)S(1)} %collective-permute-done.1), channel_id=1, source_target_pairs={{0,2},{2,4},{4,6},{6,8},{8,10},{10,12},{12,14},{14,16},{16,18},{18... | collective-permute-start | bytes 3145736 | tf_op jit(solution)/shard_map/ppermute | solution.py:26
  59.7 1.8 %fusion.7 = f32[32,257]{1,0:T(8,128)S(1)} fusion(f32[1024,257]{1,0:T(8,128)S(1)} %bitcast.69, f32[1024,257]{1,0:T(8,128)S(1)} %bitcast.65, f32[32,1024]{1,0:T(8,128)S(1)} %get-tuple-element.41, f32[32,1024]{1,0:T(8,128)S(1)} %get-tuple-element.40), kind=kOutput, calls=%fused_computation.18 | convolution fusion | flops 202704896 | bytes 2400384 | tf_op jit(solution)/shard_map/dot_general | solution.py:108
  61.6 8.5 %collective-permute-done.2 = bf16[8,32,2048]{2,1,0:T(8,128)(2,1)S(1)} collective-permute-done((bf16[8,32,2048]{2,1,0:T(8,128)(2,1)S(1)}, bf16[8,32,2048]{2,1,0:T(8,128)(2,1)S(1)}, u32[]{:S(2)}, u32[]{:S(2)}) %collective-permute-start.2) | collective-permute-done | bytes 1048608 | tf_op jit(solution)/shard_map/ppermute | solution.py:26
  70.1 7.4 %collective-permute-start.3 = (bf16[8,32,2048]{2,1,0:T(8,128)(2,1)S(1)}, bf16[8,32,2048]{2,1,0:T(8,128)(2,1)S(1)}, u32[]{:S(2)}, u32[]{:S(2)}) collective-permute-start(bf16[8,32,2048]{2,1,0:T(8,128)(2,1)S(1)} %collective-permute-done.2), channel_id=1, source_target_pairs={{0,2},{2,4},{4,6},{6,8},{8,10},{10,12},{12,14},{14,16},{16,18},{18... | collective-permute-start | bytes 3145736 | tf_op jit(solution)/shard_map/ppermute | solution.py:26
  79.4 1.8 %fusion.6 = f32[32,257]{1,0:T(8,128)S(1)} fusion(f32[1024,257]{1,0:T(8,128)S(1)} %bitcast.70, f32[1024,257]{1,0:T(8,128)S(1)} %bitcast.66, f32[32,1024]{1,0:T(8,128)S(1)} %get-tuple-element.39, f32[32,1024]{1,0:T(8,128)S(1)} %get-tuple-element.38), kind=kOutput, calls=%fused_computation.17 | convolution fusion | flops 202704896 | bytes 2400384 | tf_op jit(solution)/shard_map/dot_general | solution.py:108
  81.2 8.6 %collective-permute-done.3 = bf16[8,32,2048]{2,1,0:T(8,128)(2,1)S(1)} collective-permute-done((bf16[8,32,2048]{2,1,0:T(8,128)(2,1)S(1)}, bf16[8,32,2048]{2,1,0:T(8,128)(2,1)S(1)}, u32[]{:S(2)}, u32[]{:S(2)}) %collective-permute-start.3) | collective-permute-done | bytes 1048608 | tf_op jit(solution)/shard_map/ppermute | solution.py:26
  91.8 1.8 %fusion.5 = f32[32,257]{1,0:T(8,128)S(1)} fusion(f32[1024,257]{1,0:T(8,128)S(1)} %bitcast.71, f32[1024,257]{1,0:T(8,128)S(1)} %bitcast.67, f32[32,1024]{1,0:T(8,128)S(1)} %get-tuple-element.37, f32[32,1024]{1,0:T(8,128)S(1)} %get-tuple-element.36), kind=kOutput, calls=%fused_computation.16 | convolution fusion | flops 202704896 | bytes 2400384 | tf_op jit(solution)/shard_map/dot_general | solution.py:108
  93.6 1.9 %collective-permute-start.8 = (f32[32,4,257]{2,0,1:T(8,128)S(1)}, f32[32,4,257]{2,0,1:T(8,128)S(1)}, u32[]{:S(2)}, u32[]{:S(2)}) collective-permute-start(f32[32,4,257]{2,0,1:T(8,128)S(1)} %pad_maximum_fusion.5), channel_id=1, source_target_pairs={{0,1},{1,0},{2,3},{3,2},{4,5},{5,4},{6,7},{7,6},{8,9},{9,8},{10,11... | collective-permute-start | bytes 394760 | tf_op jit(solution)/shard_map/ppermute | solution.py:18
  95.6 1.9 %collective-permute-start.7 = (f32[32,257]{1,0:T(8,128)S(1)}, f32[32,257]{1,0:T(8,128)S(1)}, u32[]{:S(2)}, u32[]{:S(2)}) collective-permute-start(f32[32,257]{1,0:T(8,128)S(1)} %fusion.5), channel_id=1, source_target_pairs={{0,505},{2,507},{4,509},{6,511},{8,1},{10,3},{12,5},{14,7},{16,9},... | collective-permute-start | bytes 98696 | tf_op jit(solution)/shard_map/ppermute | solution.py:26
  97.5 2.6 %collective-permute-start.12 = (f32[32,257]{1,0:T(8,128)S(1)}, f32[32,257]{1,0:T(8,128)S(1)}, u32[]{:S(2)}, u32[]{:S(2)}) collective-permute-start(f32[32,257]{1,0:T(8,128)S(1)} %fusion.5), channel_id=1, source_target_pairs={{0,504},{2,506},{4,508},{6,510},{8,0},{10,2},{12,4},{14,6},{16,8},... | collective-permute-start | bytes 98696 | tf_op jit(solution)/shard_map/ppermute | solution.py:26
  100.1 35.5 %collective-permute-start.4 = (f32[32,257]{1,0:T(8,128)S(1)}, f32[32,257]{1,0:T(8,128)S(1)}, u32[]{:S(2)}, u32[]{:S(2)}) collective-permute-start(f32[32,257]{1,0:T(8,128)S(1)} %fusion.8), channel_id=1, source_target_pairs={{0,511},{2,1},{4,3},{6,5},{8,7},{10,9},{12,11},{14,13},{16,15},{18... | collective-permute-start | bytes 98696 | tf_op jit(solution)/shard_map/ppermute | solution.py:26
  135.5 1.9 %collective-permute-start.5 = (f32[32,257]{1,0:T(8,128)S(1)}, f32[32,257]{1,0:T(8,128)S(1)}, u32[]{:S(2)}, u32[]{:S(2)}) collective-permute-start(f32[32,257]{1,0:T(8,128)S(1)} %fusion.7), channel_id=1, source_target_pairs={{0,509},{2,511},{4,1},{6,3},{8,5},{10,7},{12,9},{14,11},{16,13},{1... | collective-permute-start | bytes 98696 | tf_op jit(solution)/shard_map/ppermute | solution.py:26
  137.5 1.9 %collective-permute-start.6 = (f32[32,257]{1,0:T(8,128)S(1)}, f32[32,257]{1,0:T(8,128)S(1)}, u32[]{:S(2)}, u32[]{:S(2)}) collective-permute-start(f32[32,257]{1,0:T(8,128)S(1)} %fusion.6), channel_id=1, source_target_pairs={{0,507},{2,509},{4,511},{6,1},{8,3},{10,5},{12,7},{14,9},{16,11},{... | collective-permute-start | bytes 98696 | tf_op jit(solution)/shard_map/ppermute | solution.py:26
  139.4 1.9 %collective-permute-start.9 = (f32[32,257]{1,0:T(8,128)S(1)}, f32[32,257]{1,0:T(8,128)S(1)}, u32[]{:S(2)}, u32[]{:S(2)}) collective-permute-start(f32[32,257]{1,0:T(8,128)S(1)} %fusion.8), channel_id=1, source_target_pairs={{0,510},{2,0},{4,2},{6,4},{8,6},{10,8},{12,10},{14,12},{16,14},{18... | collective-permute-start | bytes 98696 | tf_op jit(solution)/shard_map/ppermute | solution.py:26
  141.4 7.6 %collective-permute-start.10 = (f32[32,257]{1,0:T(8,128)S(1)}, f32[32,257]{1,0:T(8,128)S(1)}, u32[]{:S(2)}, u32[]{:S(2)}) collective-permute-start(f32[32,257]{1,0:T(8,128)S(1)} %fusion.7), channel_id=1, source_target_pairs={{0,508},{2,510},{4,0},{6,2},{8,4},{10,6},{12,8},{14,10},{16,12},{1... | collective-permute-start | bytes 98696 | tf_op jit(solution)/shard_map/ppermute | solution.py:26
  149.0 1.9 %collective-permute-start.11 = (f32[32,257]{1,0:T(8,128)S(1)}, f32[32,257]{1,0:T(8,128)S(1)}, u32[]{:S(2)}, u32[]{:S(2)}) collective-permute-start(f32[32,257]{1,0:T(8,128)S(1)} %fusion.6), channel_id=1, source_target_pairs={{0,506},{2,508},{4,510},{6,0},{8,2},{10,4},{12,6},{14,8},{16,10},{... | collective-permute-start | bytes 98696 | tf_op jit(solution)/shard_map/ppermute | solution.py:26
  150.9 10.1 %collective-permute-done.11 = f32[32,257]{1,0:T(8,128)S(1)} collective-permute-done((f32[32,257]{1,0:T(8,128)S(1)}, f32[32,257]{1,0:T(8,128)S(1)}, u32[]{:S(2)}, u32[]{:S(2)}) %collective-permute-start.11) | collective-permute-done | bytes 32928 | tf_op jit(solution)/shard_map/ppermute | solution.py:26
  (54 shorter events, 12.0 us)
Async XLA Ops:
  7.0 2.6 %copy-start.2 = (s32[32]{0:T(128)S(1)}, s32[32]{0:T(128)}, u32[]{:S(2)}) copy-start(s32[32]{0:T(128)} %param.7) | copy-start | bytes 388
  7.0 3.2 %copy-start = (s32[4,32]{1,0:T(4,128)S(1)}, s32[4,32]{1,0:T(4,128)}, u32[]{:S(2)}) copy-start(s32[4,32]{1,0:T(4,128)} %param.6) | copy-start | bytes 1540
  10.3 1.5 copy-start.1
  18.7 14.5 %collective-permute-start = (bf16[8,32,2048]{2,1,0:T(8,128)(2,1)}, bf16[8,32,2048]{2,1,0:T(8,128)(2,1)}, u32[]{:S(2)}, u32[]{:S(2)}) collective-permute-start(bf16[8,32,2048]{2,1,0:T(8,128)(2,1)} %scatter.4), channel_id=1, source_target_pairs={{0,2},{2,4},{4,6},{6,8},{8,10},{10,12},{12,14},{14,16},{16,18},{18... | collective-permute-start | bytes 3145736 | tf_op jit(solution)/shard_map/ppermute | solution.py:26
  34.0 16.4 %collective-permute-start.1 = (bf16[8,32,2048]{2,1,0:T(8,128)(2,1)}, bf16[8,32,2048]{2,1,0:T(8,128)(2,1)S(1)}, u32[]{:S(2)}, u32[]{:S(2)}) collective-permute-start(bf16[8,32,2048]{2,1,0:T(8,128)(2,1)} %collective-permute-done), channel_id=1, source_target_pairs={{0,2},{2,4},{4,6},{6,8},{8,10},{10,12},{12,14},{14,16},{16,18},{18... | collective-permute-start | bytes 3145736 | tf_op jit(solution)/shard_map/ppermute | solution.py:26
  50.5 19.5 %collective-permute-start.2 = (bf16[8,32,2048]{2,1,0:T(8,128)(2,1)S(1)}, bf16[8,32,2048]{2,1,0:T(8,128)(2,1)S(1)}, u32[]{:S(2)}, u32[]{:S(2)}) collective-permute-start(bf16[8,32,2048]{2,1,0:T(8,128)(2,1)S(1)} %collective-permute-done.1), channel_id=1, source_target_pairs={{0,2},{2,4},{4,6},{6,8},{8,10},{10,12},{12,14},{14,16},{16,18},{18... | collective-permute-start | bytes 3145736 | tf_op jit(solution)/shard_map/ppermute | solution.py:26
  70.1 19.7 %collective-permute-start.3 = (bf16[8,32,2048]{2,1,0:T(8,128)(2,1)S(1)}, bf16[8,32,2048]{2,1,0:T(8,128)(2,1)S(1)}, u32[]{:S(2)}, u32[]{:S(2)}) collective-permute-start(bf16[8,32,2048]{2,1,0:T(8,128)(2,1)S(1)} %collective-permute-done.2), channel_id=1, source_target_pairs={{0,2},{2,4},{4,6},{6,8},{8,10},{10,12},{12,14},{14,16},{16,18},{18... | collective-permute-start | bytes 3145736 | tf_op jit(solution)/shard_map/ppermute | solution.py:26
  93.6 67.4 %collective-permute-start.8 = (f32[32,4,257]{2,0,1:T(8,128)S(1)}, f32[32,4,257]{2,0,1:T(8,128)S(1)}, u32[]{:S(2)}, u32[]{:S(2)}) collective-permute-start(f32[32,4,257]{2,0,1:T(8,128)S(1)} %pad_maximum_fusion.5), channel_id=1, source_target_pairs={{0,1},{1,0},{2,3},{3,2},{4,5},{5,4},{6,7},{7,6},{8,9},{9,8},{10,11... | collective-permute-start | bytes 394760 | tf_op jit(solution)/shard_map/ppermute | solution.py:18
  95.6 41.9 %collective-permute-start.7 = (f32[32,257]{1,0:T(8,128)S(1)}, f32[32,257]{1,0:T(8,128)S(1)}, u32[]{:S(2)}, u32[]{:S(2)}) collective-permute-start(f32[32,257]{1,0:T(8,128)S(1)} %fusion.5), channel_id=1, source_target_pairs={{0,505},{2,507},{4,509},{6,511},{8,1},{10,3},{12,5},{14,7},{16,9},... | collective-permute-start | bytes 98696 | tf_op jit(solution)/shard_map/ppermute | solution.py:26
  97.5 41.9 %collective-permute-start.12 = (f32[32,257]{1,0:T(8,128)S(1)}, f32[32,257]{1,0:T(8,128)S(1)}, u32[]{:S(2)}, u32[]{:S(2)}) collective-permute-start(f32[32,257]{1,0:T(8,128)S(1)} %fusion.5), channel_id=1, source_target_pairs={{0,504},{2,506},{4,508},{6,510},{8,0},{10,2},{12,4},{14,6},{16,8},... | collective-permute-start | bytes 98696 | tf_op jit(solution)/shard_map/ppermute | solution.py:26
  100.1 41.3 %collective-permute-start.4 = (f32[32,257]{1,0:T(8,128)S(1)}, f32[32,257]{1,0:T(8,128)S(1)}, u32[]{:S(2)}, u32[]{:S(2)}) collective-permute-start(f32[32,257]{1,0:T(8,128)S(1)} %fusion.8), channel_id=1, source_target_pairs={{0,511},{2,1},{4,3},{6,5},{8,7},{10,9},{12,11},{14,13},{16,15},{18... | collective-permute-start | bytes 98696 | tf_op jit(solution)/shard_map/ppermute | solution.py:26
  135.5 13.4 %collective-permute-start.5 = (f32[32,257]{1,0:T(8,128)S(1)}, f32[32,257]{1,0:T(8,128)S(1)}, u32[]{:S(2)}, u32[]{:S(2)}) collective-permute-start(f32[32,257]{1,0:T(8,128)S(1)} %fusion.7), channel_id=1, source_target_pairs={{0,509},{2,511},{4,1},{6,3},{8,5},{10,7},{12,9},{14,11},{16,13},{1... | collective-permute-start | bytes 98696 | tf_op jit(solution)/shard_map/ppermute | solution.py:26
  137.5 13.4 %collective-permute-start.6 = (f32[32,257]{1,0:T(8,128)S(1)}, f32[32,257]{1,0:T(8,128)S(1)}, u32[]{:S(2)}, u32[]{:S(2)}) collective-permute-start(f32[32,257]{1,0:T(8,128)S(1)} %fusion.6), channel_id=1, source_target_pairs={{0,507},{2,509},{4,511},{6,1},{8,3},{10,5},{12,7},{14,9},{16,11},{... | collective-permute-start | bytes 98696 | tf_op jit(solution)/shard_map/ppermute | solution.py:26
  139.4 11.5 %collective-permute-start.9 = (f32[32,257]{1,0:T(8,128)S(1)}, f32[32,257]{1,0:T(8,128)S(1)}, u32[]{:S(2)}, u32[]{:S(2)}) collective-permute-start(f32[32,257]{1,0:T(8,128)S(1)} %fusion.8), channel_id=1, source_target_pairs={{0,510},{2,0},{4,2},{6,4},{8,6},{10,8},{12,10},{14,12},{16,14},{18... | collective-permute-start | bytes 98696 | tf_op jit(solution)/shard_map/ppermute | solution.py:26
  141.4 9.6 %collective-permute-start.10 = (f32[32,257]{1,0:T(8,128)S(1)}, f32[32,257]{1,0:T(8,128)S(1)}, u32[]{:S(2)}, u32[]{:S(2)}) collective-permute-start(f32[32,257]{1,0:T(8,128)S(1)} %fusion.7), channel_id=1, source_target_pairs={{0,508},{2,510},{4,0},{6,2},{8,4},{10,6},{12,8},{14,10},{16,12},{1... | collective-permute-start | bytes 98696 | tf_op jit(solution)/shard_map/ppermute | solution.py:26
  149.0 12.0 %collective-permute-start.11 = (f32[32,257]{1,0:T(8,128)S(1)}, f32[32,257]{1,0:T(8,128)S(1)}, u32[]{:S(2)}, u32[]{:S(2)}) collective-permute-start(f32[32,257]{1,0:T(8,128)S(1)} %fusion.6), channel_id=1, source_target_pairs={{0,506},{2,508},{4,510},{6,0},{8,2},{10,4},{12,6},{14,8},{16,10},{... | collective-permute-start | bytes 98696 | tf_op jit(solution)/shard_map/ppermute | solution.py:26

commit v11 on v7

--- a/solution.py
+++ b/solution.py
@@ -112,16 +112,31 @@
         + tuple(shifted(moving_behind, "blk", -d) for d in range(1, near + 1))
     )
     lags = [lags_of(d, first[d - 1], first[near + d - 1]) for d in range(1, near + 1)]
-    early = [
-        (shifted(piece[channels:], "blk", d), shifted(piece[:channels], "blk", -d)) for d, piece in enumerate(lags, 1)
-    ]
+    early = [(shifted(lags[0][channels:], "blk", 1), shifted(lags[0][:channels], "blk", -1))]
+
+    def packed(bulk, piece):
+        head = piece.astype(jnp.bfloat16)
+        rest = (piece - head.astype(jnp.float32)).astype(jnp.bfloat16)
+        flat = jnp.concatenate([head.reshape(-1), rest.reshape(-1)])
+        flat = jnp.pad(flat, (0, channels * length - flat.shape[0]))
+        return jnp.concatenate([bulk, flat.reshape(1, channels, length)], axis=0)
+
+    def unpacked(bulk):
+        flat = bulk[-1].reshape(-1)
+        size = channels * back_table.shape[1]
+        head = flat[:size].astype(jnp.float32) + flat[size:2 * size].astype(jnp.float32)
+        return bulk[:-1], head.reshape(channels, -1)
+
     far_ahead, far_behind, early = lax.optimization_barrier(
         (
-            shifted(jnp.concatenate(first[:near], axis=0), "blk", near),
-            shifted(jnp.concatenate(first[near:], axis=0), "blk", -near),
+            shifted(packed(jnp.concatenate(first[:near], axis=0), lags[1][channels:]), "blk", near),
+            shifted(packed(jnp.concatenate(first[near:], axis=0), lags[1][:channels]), "blk", -near),
             early,
         )
     )
+    far_ahead, from_two_earlier = unpacked(far_ahead)
+    far_behind, from_two_later = unpacked(far_behind)
+    early = early + [(from_two_earlier, from_two_later)]
     for d in range(near + 1, stops + 1):
         at = (d - near - 1) * split
         lags.append(lags_of(d, far_ahead[at:at + split], far_behind[at:at + split]))

time: 138 us -> 157 us (1.14)
  other arithmetic: 9.1 us -> 20.8 us
  starting transfers between devices: 64.9 us -> 54.4 us
  local copies, waits for them, and re-layouts: 4.05 us -> 13.3 us
  waiting for transfers between devices: 43.9 us -> 51.1 us
    ppermute x14 -> x12, starting transfers between devices: 62.7 us -> 52.1 us  [shifted(): lax.ppermute(x, axis, [(i, (i + by) % length) for i in range(length)])]
    ppermute x14 -> x12, waiting for transfers between devices: 36.1 us -> 44.2 us  [shifted(): lax.ppermute(x, axis, [(i, (i + by) % length) for i in range(length)])]
    concatenate x2 -> x4, other arithmetic: 0.19 us -> 5.34 us  [the longest x2 3.85 us: packed(): return jnp.concatenate([bulk, flat.reshape(1, channels, length)], axis=0)]
    reshape x0 -> x6, local copies, waits for them, and re-layouts: none -> 4.02 us  [the longest x4 2.09 us: packed(): flat = jnp.concatenate([head.reshape(-1), rest.reshape(-1)])]
    unnamed x8 -> x42, local copies, waits for them, and re-layouts: 3.71 us -> 6.76 us
    convert_element_type x2, other arithmetic: 0.29 us -> 2.46 us  [lags_of(): later = jnp.where(dc_imag, jnp.zeros_like(later), later).astype(jnp.float32)]
  transfers between devices with their start and end apart: 15 -> 13, of which waited for: 7 -> 6; matrix products, arithmetic and copies ran while one was open for 6% -> 8% of each run, Pallas kernels for 0% -> 0%
where the time goes in v11:
time: 157 us; the launch traced here: 154 us
  starting transfers between devices  54.4 us (35%)
  waiting for transfers between devices  51.1 us (33%)
  other arithmetic  20.8 us (13%)
  local copies, waits for them, and re-layouts  13.3 us (8%)
  matrix products  13 us (8%)
    ppermute x12, starting transfers between devices, shifted(): lax.ppermute(x, axis, [(i, (i + by) % length) for i in range(length)])  52.1 us
    ppermute x12, waiting for transfers between devices, shifted(): lax.ppermute(x, axis, [(i, (i + by) % length) for i in range(length)])  44.2 us
    dot_general x4, matrix products, lags_of(): jnp.dot(jnp.concatenate([own, later], axis=0), back_table, precision=lax....  7.76 us
    ppermute x1, waiting for transfers between devices, swapped(): return lax.ppermute(x, axis, [(i, i ^ 1) for i in range(length)])  6.92 us
    unnamed x42, local copies, waits for them, and re-layouts  6.76 us
    concatenate x2, other arithmetic, packed(): return jnp.concatenate([bulk, flat.reshape(1, channels, length)], axis=0)  3.85 us
  transfers between devices with their start and end apart: 13, of which 6 were waited for; matrix products, arithmetic and copies ran while one was open for 8% of the time, Pallas kernels for 0%

profile of v11, /device:TPU:1, one launch (start us, length us, event | category | flops | bytes accessed | tf_op | source)
XLA Modules:
  0.0 153.9 jit_solution(11880635993112784510)
XLA Ops:
  0.6 1.0 fusion.53
  2.3 1.8 %copy.8 = bf16[32,8,2048]{2,0,1:T(8,128)(2,1)S(1)} copy(bf16[32,8,2048]{2,1,0:T(8,128)(2,1)} %param.5) | data formatting | bytes 2097152 | tf_op args[0]
  4.1 3.0 %subtract_convert_fusion = (bf16[32,64,1024]{2,1,0:T(8,128)(2,1)S(1)}, bf16[32,64,1024]{2,1,0:T(8,128)(2,1)S(1)}) fusion(f32[64,1024]{1,0:T(8,128)S(1)} %get-tuple-element.103, f32[32,1024]{1,0:T(8,128)S(1)} %get-tuple-element.100, f32[64,1024]{1,0:T(8,128)S(1)} %get-tuple-element.104, f32[32,1024]{1,0:T(8,128)S(1)} %get-tuple-element.99), kind=kLoop, calls=%fused_computation.5 | loop fusion | flops 18874368 | bytes 9175040 | tf_op jit(solution)/shard_map/convert.7
  7.1 2.5 %fusion.4 = (f32[256]{0:T(256)S(1)}, f32[2048,256]{0,1:T(8,128)S(1)}) fusion(bf16[256,2048]{1,0:T(8,128)(2,1)S(1)} %bitcast.116, bf16[2048,1024]{1,0:T(8,128)(2,1)S(1)} %bitcast.114, bf16[2048,1024]{1,0:T(8,128)(2,1)S(1)} %bitcast.113), kind=kOutput, calls=%fused_computation.16 | convolution fusion | flops 2165309184 | bytes 11535360 | tf_op jit(solution)/shard_map/dot_general | solution.py:81
  10.2 1.6 %slice_convert_fusion.2 = (f32[4,32,2048]{2,1,0:T(8,128)}, bf16[4,32,2048]{2,1,0:T(8,128)(2,1)}, bf16[4,32,2048]{2,1,0:T(8,128)(2,1)}) fusion(bf16[8,32,2048]{2,1,0:T(8,128)(2,1)S(1)} %multiply_convert_fusion), kind=kLoop, calls=%fused_computation.194 | loop fusion | flops 262144 | bytes 3145728 | tf_op jit(solution)/shard_map/convert_element_type | solution.py:91
  12.0 1.4 scatter.4
  13.4 8.8 %collective-permute-start.2 = (bf16[4,32,2048]{2,1,0:T(8,128)(2,1)}, bf16[4,32,2048]{2,1,0:T(8,128)(2,1)S(1)}, u32[]{:S(2)}, u32[]{:S(2)}) collective-permute-start(bf16[4,32,2048]{2,1,0:T(8,128)(2,1)} %scatter.4), channel_id=1, source_target_pairs={{0,510},{2,0},{4,2},{6,4},{8,6},{10,8},{12,10},{14,12},{16,14},{18... | collective-permute-start | bytes 1572872 | tf_op jit(solution)/shard_map/ppermute | solution.py:13
  22.1 10.7 %collective-permute-start.3 = (bf16[4,32,2048]{2,1,0:T(8,128)(2,1)}, bf16[4,32,2048]{2,1,0:T(8,128)(2,1)S(1)}, u32[]{:S(2)}, u32[]{:S(2)}) collective-permute-start(bf16[4,32,2048]{2,1,0:T(8,128)(2,1)} %scatter.4), channel_id=1, source_target_pairs={{0,508},{2,510},{4,0},{6,2},{8,4},{10,6},{12,8},{14,10},{16,12},{1... | collective-permute-start | bytes 1572872 | tf_op jit(solution)/shard_map/ppermute | solution.py:13
  32.8 3.3 %collective-permute-start = (bf16[4,32,2048]{2,1,0:T(8,128)(2,1)}, bf16[4,32,2048]{2,1,0:T(8,128)(2,1)S(1)}, u32[]{:S(2)}, u32[]{:S(2)}) collective-permute-start(bf16[4,32,2048]{2,1,0:T(8,128)(2,1)} %get-tuple-element.64), channel_id=1, source_target_pairs={{0,2},{2,4},{4,6},{6,8},{8,10},{10,12},{12,14},{14,16},{16,18},{18... | collective-permute-start | bytes 1572872 | tf_op jit(solution)/shard_map/ppermute | solution.py:13
  36.1 1.9 %collective-permute-start.1 = (bf16[4,32,2048]{2,1,0:T(8,128)(2,1)}, bf16[4,32,2048]{2,1,0:T(8,128)(2,1)S(1)}, u32[]{:S(2)}, u32[]{:S(2)}) collective-permute-start(bf16[4,32,2048]{2,1,0:T(8,128)(2,1)} %get-tuple-element.64), channel_id=1, source_target_pairs={{0,4},{2,6},{4,8},{6,10},{8,12},{10,14},{12,16},{14,18},{16,20},{1... | collective-permute-start | bytes 1572872 | tf_op jit(solution)/shard_map/ppermute | solution.py:13
  39.0 5.9 %collective-permute-done.3 = bf16[4,32,2048]{2,1,0:T(8,128)(2,1)S(1)} collective-permute-done((bf16[4,32,2048]{2,1,0:T(8,128)(2,1)}, bf16[4,32,2048]{2,1,0:T(8,128)(2,1)S(1)}, u32[]{:S(2)}, u32[]{:S(2)}) %collective-permute-start.3) | collective-permute-done | bytes 524320 | tf_op jit(solution)/shard_map/ppermute | solution.py:13
  45.5 15.3 %collective-permute-done.1 = bf16[4,32,2048]{2,1,0:T(8,128)(2,1)S(1)} collective-permute-done((bf16[4,32,2048]{2,1,0:T(8,128)(2,1)}, bf16[4,32,2048]{2,1,0:T(8,128)(2,1)S(1)}, u32[]{:S(2)}, u32[]{:S(2)}) %collective-permute-start.1) | collective-permute-done | bytes 524320 | tf_op jit(solution)/shard_map/ppermute | solution.py:13
  61.3 1.1 select_convert_fusion.3
  64.8 1.9 %fusion.7 = f32[64,257]{1,0:T(8,128)S(1)} fusion(f32[1024,257]{1,0:T(8,128)S(1)} %bitcast.109, f32[1024,257]{1,0:T(8,128)S(1)} %bitcast.105, f32[32,1024]{1,0:T(8,128)S(1)} %get-tuple-element.49, f32[32,1024]{1,0:T(8,128)S(1)} %get-tuple-element.48, f32[32,1024]{1,0:T(8,128)S(1)} %get-tuple-element.54, f32[32,1024]{1,0:T(8,128)S(1)} %get-tuple-element.55), kind=kOutput, calls=%fused_computation.22 | convolution fusion | flops 405145600 | bytes 2695424 | tf_op jit(solution)/shard_map/dot_general | solution.py:102
  69.4 2.4 %pad_maximum_fusion.6 = bf16[9,32,2048]{2,1,0:T(8,128)(2,1)} fusion(bf16[1,32,2048]{2,1,0:T(8,128)(2,1)S(1)} %reshape.670, bf16[4,32,2048]{2,1,0:T(8,128)(2,1)} %copy-done.7, bf16[4,32,2048]{2,1,0:T(8,128)(2,1)} %copy-done.6), kind=kLoop, calls=%fused_computation.25 | loop fusion | flops 1179648 | bytes 2359296 | tf_op jit(solution)/shard_map/concatenate | solution.py:122
  71.8 2.1 %collective-permute-start.5 = (bf16[9,32,2048]{2,1,0:T(8,128)(2,1)}, bf16[9,32,2048]{2,1,0:T(8,128)(2,1)}, u32[]{:S(2)}, u32[]{:S(2)}) collective-permute-start(bf16[9,32,2048]{2,1,0:T(8,128)(2,1)} %pad_maximum_fusion.6), channel_id=1, source_target_pairs={{0,508},{2,510},{4,0},{6,2},{8,4},{10,6},{12,8},{14,10},{16,12},{1... | collective-permute-start | bytes 3538952 | tf_op jit(solution)/shard_map/ppermute | solution.py:13
  77.4 1.5 pad_maximum_fusion.5
  78.9 3.4 %collective-permute-start.4 = (bf16[9,32,2048]{2,1,0:T(8,128)(2,1)S(1)}, bf16[9,32,2048]{2,1,0:T(8,128)(2,1)S(1)}, u32[]{:S(2)}, u32[]{:S(2)}) collective-permute-start(bf16[9,32,2048]{2,1,0:T(8,128)(2,1)S(1)} %pad_maximum_fusion.5), channel_id=1, source_target_pairs={{0,4},{2,6},{4,8},{6,10},{8,12},{10,14},{12,16},{14,18},{16,20},{1... | collective-permute-start | bytes 3538952 | tf_op jit(solution)/shard_map/ppermute | solution.py:13
  83.7 1.9 %fusion.8 = f32[64,257]{1,0:T(8,128)S(1)} fusion(f32[1024,257]{1,0:T(8,128)S(1)} %bitcast.110, f32[1024,257]{1,0:T(8,128)S(1)} %bitcast.106, f32[32,1024]{1,0:T(8,128)S(1)} %get-tuple-element.45, f32[32,1024]{1,0:T(8,128)S(1)} %get-tuple-element.44, f32[32,1024]{1,0:T(8,128)S(1)} %get-tuple-element.43, f32[32,1024]{1,0:T(8,128)S(1)} %get-tuple-element.42), kind=kOutput, calls=%fused_computation.23 | convolution fusion | flops 405145600 | bytes 2695424 | tf_op jit(solution)/shard_map/dot_general | solution.py:102
  85.7 1.9 %collective-permute-start.6 = (f32[32,257]{1,0:T(8,128)S(1)}, f32[32,257]{1,0:T(8,128)S(1)}, u32[]{:S(2)}, u32[]{:S(2)}) collective-permute-start(f32[32,257]{1,0:T(8,128)S(1)} %get-tuple-element.81), channel_id=1, source_target_pairs={{0,2},{2,4},{4,6},{6,8},{8,10},{10,12},{12,14},{14,16},{16,18},{18... | collective-permute-start | bytes 98696 | tf_op jit(solution)/shard_map/ppermute | solution.py:13
  87.6 2.4 %collective-permute-start.7 = (f32[32,257]{1,0:T(8,128)S(1)}, f32[32,257]{1,0:T(8,128)S(1)}, u32[]{:S(2)}, u32[]{:S(2)}) collective-permute-start(f32[32,257]{1,0:T(8,128)S(1)} %get-tuple-element.82), channel_id=1, source_target_pairs={{0,510},{2,0},{4,2},{6,4},{8,6},{10,8},{12,10},{14,12},{16,14},{18... | collective-permute-start | bytes 98696 | tf_op jit(solution)/shard_map/ppermute | solution.py:13
  90.0 16.9 %collective-permute-done.6 = f32[32,257]{1,0:T(8,128)S(1)} collective-permute-done((f32[32,257]{1,0:T(8,128)S(1)}, f32[32,257]{1,0:T(8,128)S(1)}, u32[]{:S(2)}, u32[]{:S(2)}) %collective-permute-start.6) | collective-permute-done | bytes 32928 | tf_op jit(solution)/shard_map/ppermute | solution.py:13
  106.9 5.4 %collective-permute-done.4 = bf16[9,32,2048]{2,1,0:T(8,128)(2,1)S(1)} collective-permute-done((bf16[9,32,2048]{2,1,0:T(8,128)(2,1)S(1)}, bf16[9,32,2048]{2,1,0:T(8,128)(2,1)S(1)}, u32[]{:S(2)}, u32[]{:S(2)}) %collective-permute-start.4) | collective-permute-done | bytes 1179680 | tf_op jit(solution)/shard_map/ppermute | solution.py:13
  113.1 1.3 select_convert_fusion.1
  118.1 1.9 %fusion.6 = f32[64,257]{1,0:T(8,128)S(1)} fusion(f32[1024,257]{1,0:T(8,128)S(1)} %bitcast.111, f32[1024,257]{1,0:T(8,128)S(1)} %bitcast.107, f32[32,1024]{1,0:T(8,128)S(1)} %get-tuple-element.37, f32[32,1024]{1,0:T(8,128)S(1)} %get-tuple-element.36, f32[32,1024]{1,0:T(8,128)S(1)} %get-tuple-element.35, f32[32,1024]{1,0:T(8,128)S(1)} %get-tuple-element.34), kind=kOutput, calls=%fused_computation.21 | convolution fusion | flops 405145600 | bytes 2695424 | tf_op jit(solution)/shard_map/dot_general | solution.py:102
  120.7 1.9 %collective-permute-start.8 = (f32[32,257]{1,0:T(8,128)}, f32[32,257]{1,0:T(8,128)}, u32[]{:S(2)}, u32[]{:S(2)}) collective-permute-start(f32[32,257]{1,0:T(8,128)} %get-tuple-element.71), channel_id=1, source_target_pairs={{0,6},{2,8},{4,10},{6,12},{8,14},{10,16},{12,18},{14,20},{16,22},{... | collective-permute-start | bytes 98696 | tf_op jit(solution)/shard_map/ppermute | solution.py:13
  123.2 1.9 %fusion.5 = f32[64,257]{1,0:T(8,128)S(1)} fusion(f32[1024,257]{1,0:T(8,128)S(1)} %bitcast.112, f32[1024,257]{1,0:T(8,128)S(1)} %bitcast.108, f32[32,1024]{1,0:T(8,128)S(1)} %get-tuple-element.41, f32[32,1024]{1,0:T(8,128)S(1)} %get-tuple-element.40, f32[32,1024]{1,0:T(8,128)S(1)} %get-tuple-element.52, f32[32,1024]{1,0:T(8,128)S(1)} %get-tuple-element.53), kind=kOutput, calls=%fused_computation.20 | convolution fusion | flops 405145600 | bytes 2695424 | tf_op jit(solution)/shard_map/dot_general | solution.py:102
  125.2 1.9 %collective-permute-start.9 = (f32[32,257]{1,0:T(8,128)S(1)}, f32[32,257]{1,0:T(8,128)S(1)}, u32[]{:S(2)}, u32[]{:S(2)}) collective-permute-start(f32[32,257]{1,0:T(8,128)S(1)} %get-tuple-element.75), channel_id=1, source_target_pairs={{0,8},{2,10},{4,12},{6,14},{8,16},{10,18},{12,20},{14,22},{16,24},... | collective-permute-start | bytes 98696 | tf_op jit(solution)/shard_map/ppermute | solution.py:13
  127.4 9.4 %collective-permute-start.10 = (f32[32,257]{1,0:T(8,128)}, f32[32,257]{1,0:T(8,128)S(1)}, u32[]{:S(2)}, u32[]{:S(2)}) collective-permute-start(f32[32,257]{1,0:T(8,128)} %get-tuple-element.74), channel_id=1, source_target_pairs={{0,506},{2,508},{4,510},{6,0},{8,2},{10,4},{12,6},{14,8},{16,10},{... | collective-permute-start | bytes 98696 | tf_op jit(solution)/shard_map/ppermute | solution.py:13
  136.8 4.5 %collective-permute-start.11 = (f32[32,257]{1,0:T(8,128)S(1)}, f32[32,257]{1,0:T(8,128)S(1)}, u32[]{:S(2)}, u32[]{:S(2)}) collective-permute-start(f32[32,257]{1,0:T(8,128)S(1)} %get-tuple-element.78), channel_id=1, source_target_pairs={{0,504},{2,506},{4,508},{6,510},{8,0},{10,2},{12,4},{14,6},{16,8},... | collective-permute-start | bytes 98696 | tf_op jit(solution)/shard_map/ppermute | solution.py:13
  142.6 2.3 %collective-permute-start.12 = (f32[2,32,4,257]{3,1,2,0:T(8,128)S(1)}, f32[2,32,4,257]{3,1,2,0:T(8,128)S(1)}, u32[]{:S(2)}, u32[]{:S(2)}) collective-permute-start(f32[2,32,4,257]{3,1,2,0:T(8,128)S(1)} %pad_maximum_fusion.7), channel_id=1, source_target_pairs={{0,1},{1,0},{2,3},{3,2},{4,5},{5,4},{6,7},{7,6},{8,9},{9,8},{10,11... | collective-permute-start | bytes 789512 | tf_op jit(solution)/shard_map/ppermute | solution.py:18
  144.8 6.9 %collective-permute-done.12 = f32[2,32,4,257]{3,1,2,0:T(8,128)S(1)} collective-permute-done((f32[2,32,4,257]{3,1,2,0:T(8,128)S(1)}, f32[2,32,4,257]{3,1,2,0:T(8,128)S(1)}, u32[]{:S(2)}, u32[]{:S(2)}) %collective-permute-start.12) | collective-permute-done | bytes 263200 | tf_op jit(solution)/shard_map/ppermute | solution.py:18
  (102 shorter events, 22.5 us)
Async XLA Ops:
  7.0 2.6 %copy-start.16 = (s32[32]{0:T(128)S(1)}, s32[32]{0:T(128)}, u32[]{:S(2)}) copy-start(s32[32]{0:T(128)} %param.7) | copy-start | bytes 388
  10.1 1.7 %copy-start = (bf16[8,32,2048]{2,1,0:T(8,128)(2,1)}, bf16[8,32,2048]{2,1,0:T(8,128)(2,1)S(1)}, u32[]{:S(2)}) copy-start(bf16[8,32,2048]{2,1,0:T(8,128)(2,1)S(1)} %multiply_convert_fusion) | copy-start | bytes 3145732
  10.1 1.7 %copy-start.15 = (s32[4,32]{1,0:T(4,128)S(1)}, s32[4,32]{1,0:T(4,128)}, u32[]{:S(2)}) copy-start(s32[4,32]{1,0:T(4,128)} %param.6) | copy-start | bytes 1540
  13.4 25.6 %collective-permute-start.2 = (bf16[4,32,2048]{2,1,0:T(8,128)(2,1)}, bf16[4,32,2048]{2,1,0:T(8,128)(2,1)S(1)}, u32[]{:S(2)}, u32[]{:S(2)}) collective-permute-start(bf16[4,32,2048]{2,1,0:T(8,128)(2,1)} %scatter.4), channel_id=1, source_target_pairs={{0,510},{2,0},{4,2},{6,4},{8,6},{10,8},{12,10},{14,12},{16,14},{18... | collective-permute-start | bytes 1572872 | tf_op jit(solution)/shard_map/ppermute | solution.py:13
  22.1 22.8 %collective-permute-start.3 = (bf16[4,32,2048]{2,1,0:T(8,128)(2,1)}, bf16[4,32,2048]{2,1,0:T(8,128)(2,1)S(1)}, u32[]{:S(2)}, u32[]{:S(2)}) collective-permute-start(bf16[4,32,2048]{2,1,0:T(8,128)(2,1)} %scatter.4), channel_id=1, source_target_pairs={{0,508},{2,510},{4,0},{6,2},{8,4},{10,6},{12,8},{14,10},{16,12},{1... | collective-permute-start | bytes 1572872 | tf_op jit(solution)/shard_map/ppermute | solution.py:13
  32.8 12.7 %collective-permute-start = (bf16[4,32,2048]{2,1,0:T(8,128)(2,1)}, bf16[4,32,2048]{2,1,0:T(8,128)(2,1)S(1)}, u32[]{:S(2)}, u32[]{:S(2)}) collective-permute-start(bf16[4,32,2048]{2,1,0:T(8,128)(2,1)} %get-tuple-element.64), channel_id=1, source_target_pairs={{0,2},{2,4},{4,6},{6,8},{8,10},{10,12},{12,14},{14,16},{16,18},{18... | collective-permute-start | bytes 1572872 | tf_op jit(solution)/shard_map/ppermute | solution.py:13
  36.1 24.8 %collective-permute-start.1 = (bf16[4,32,2048]{2,1,0:T(8,128)(2,1)}, bf16[4,32,2048]{2,1,0:T(8,128)(2,1)S(1)}, u32[]{:S(2)}, u32[]{:S(2)}) collective-permute-start(bf16[4,32,2048]{2,1,0:T(8,128)(2,1)} %get-tuple-element.64), channel_id=1, source_target_pairs={{0,4},{2,6},{4,8},{6,10},{8,12},{10,14},{12,16},{14,18},{16,20},{1... | collective-permute-start | bytes 1572872 | tf_op jit(solution)/shard_map/ppermute | solution.py:13
  38.5 22.5 %copy-start.1 = (bf16[8,32,2048]{2,1,0:T(8,128)(2,1)S(1)}, bf16[8,32,2048]{2,1,0:T(8,128)(2,1)}, u32[]{:S(2)}) copy-start(bf16[8,32,2048]{2,1,0:T(8,128)(2,1)} %copy-done) | copy-start | bytes 3145732
  39.0 23.5 %copy-start.6 = (bf16[4,32,2048]{2,1,0:T(8,128)(2,1)}, bf16[4,32,2048]{2,1,0:T(8,128)(2,1)S(1)}, u32[]{:S(2)}) copy-start(bf16[4,32,2048]{2,1,0:T(8,128)(2,1)S(1)} %collective-permute-done.2) | copy-start | bytes 1572868
  44.9 17.5 %copy-start.7 = (bf16[4,32,2048]{2,1,0:T(8,128)(2,1)}, bf16[4,32,2048]{2,1,0:T(8,128)(2,1)S(1)}, u32[]{:S(2)}) copy-start(bf16[4,32,2048]{2,1,0:T(8,128)(2,1)S(1)} %collective-permute-done.3) | copy-start | bytes 1572868
  45.5 17.3 %copy-start.8 = (bf16[4,32,2048]{2,1,0:T(8,128)(2,1)}, bf16[4,32,2048]{2,1,0:T(8,128)(2,1)S(1)}, u32[]{:S(2)}) copy-start(bf16[4,32,2048]{2,1,0:T(8,128)(2,1)S(1)} %collective-permute-done) | copy-start | bytes 1572868
  60.9 1.6 %copy-start.9 = (bf16[4,32,2048]{2,1,0:T(8,128)(2,1)}, bf16[4,32,2048]{2,1,0:T(8,128)(2,1)S(1)}, u32[]{:S(2)}) copy-start(bf16[4,32,2048]{2,1,0:T(8,128)(2,1)S(1)} %collective-permute-done.1) | copy-start | bytes 1572868
  63.2 1.2 copy-start.3
  71.8 35.2 %collective-permute-start.5 = (bf16[9,32,2048]{2,1,0:T(8,128)(2,1)}, bf16[9,32,2048]{2,1,0:T(8,128)(2,1)}, u32[]{:S(2)}, u32[]{:S(2)}) collective-permute-start(bf16[9,32,2048]{2,1,0:T(8,128)(2,1)} %pad_maximum_fusion.6), channel_id=1, source_target_pairs={{0,508},{2,510},{4,0},{6,2},{8,4},{10,6},{12,8},{14,10},{16,12},{1... | collective-permute-start | bytes 3538952 | tf_op jit(solution)/shard_map/ppermute | solution.py:13
  77.4 5.7 %copy-start.2 = (bf16[8,32,2048]{2,1,0:T(8,128)(2,1)S(1)}, bf16[8,32,2048]{2,1,0:T(8,128)(2,1)}, u32[]{:S(2)}) copy-start(bf16[8,32,2048]{2,1,0:T(8,128)(2,1)} %copy-done) | copy-start | bytes 3145732
  77.4 6.0 %copy-start.5 = (f32[4,32,2048]{2,1,0:T(8,128)S(1)}, f32[4,32,2048]{2,1,0:T(8,128)}, u32[]{:S(2)}) copy-start(f32[4,32,2048]{2,1,0:T(8,128)} %get-tuple-element.95) | copy-start | bytes 3145732
  78.9 33.4 %collective-permute-start.4 = (bf16[9,32,2048]{2,1,0:T(8,128)(2,1)S(1)}, bf16[9,32,2048]{2,1,0:T(8,128)(2,1)S(1)}, u32[]{:S(2)}, u32[]{:S(2)}) collective-permute-start(bf16[9,32,2048]{2,1,0:T(8,128)(2,1)S(1)} %pad_maximum_fusion.5), channel_id=1, source_target_pairs={{0,4},{2,6},{4,8},{6,10},{8,12},{10,14},{12,16},{14,18},{16,20},{1... | collective-permute-start | bytes 3538952 | tf_op jit(solution)/shard_map/ppermute | solution.py:13
  85.7 21.3 %collective-permute-start.6 = (f32[32,257]{1,0:T(8,128)S(1)}, f32[32,257]{1,0:T(8,128)S(1)}, u32[]{:S(2)}, u32[]{:S(2)}) collective-permute-start(f32[32,257]{1,0:T(8,128)S(1)} %get-tuple-element.81), channel_id=1, source_target_pairs={{0,2},{2,4},{4,6},{6,8},{8,10},{10,12},{12,14},{14,16},{16,18},{18... | collective-permute-start | bytes 98696 | tf_op jit(solution)/shard_map/ppermute | solution.py:13
  87.6 19.3 %collective-permute-start.7 = (f32[32,257]{1,0:T(8,128)S(1)}, f32[32,257]{1,0:T(8,128)S(1)}, u32[]{:S(2)}, u32[]{:S(2)}) collective-permute-start(f32[32,257]{1,0:T(8,128)S(1)} %get-tuple-element.82), channel_id=1, source_target_pairs={{0,510},{2,0},{4,2},{6,4},{8,6},{10,8},{12,10},{14,12},{16,14},{18... | collective-permute-start | bytes 98696 | tf_op jit(solution)/shard_map/ppermute | solution.py:13
  106.9 6.2 %copy-start.14 = (f32[32,257]{1,0:T(8,128)}, f32[32,257]{1,0:T(8,128)S(1)}, u32[]{:S(2)}) copy-start(f32[32,257]{1,0:T(8,128)S(1)} %collective-permute-done.6) | copy-start | bytes 98692
  106.9 6.2 %copy-start.12 = (f32[32,257]{1,0:T(8,128)}, f32[32,257]{1,0:T(8,128)S(1)}, u32[]{:S(2)}) copy-start(f32[32,257]{1,0:T(8,128)S(1)} %collective-permute-done.7) | copy-start | bytes 98692
  116.5 1.2 copy-start.4
  120.7 20.9 %collective-permute-start.8 = (f32[32,257]{1,0:T(8,128)}, f32[32,257]{1,0:T(8,128)}, u32[]{:S(2)}, u32[]{:S(2)}) collective-permute-start(f32[32,257]{1,0:T(8,128)} %get-tuple-element.71), channel_id=1, source_target_pairs={{0,6},{2,8},{4,10},{6,12},{8,14},{10,16},{12,18},{14,20},{16,22},{... | collective-permute-start | bytes 98696 | tf_op jit(solution)/shard_map/ppermute | solution.py:13
  123.2 18.4 %copy-start.11 = (f32[1,32,1,257]{3,1,2,0:T(8,128)S(1)}, f32[1,32,1,257]{3,1,2,0:T(8,128)}, u32[]{:S(2)}) copy-start(f32[1,32,1,257]{3,1,2,0:T(8,128)} %get-tuple-element.86) | copy-start | bytes 98692
  125.2 17.3 %copy-start.10 = (f32[1,32,1,257]{3,1,2,0:T(8,128)S(1)}, f32[1,32,1,257]{3,1,2,0:T(8,128)}, u32[]{:S(2)}) copy-start(f32[1,32,1,257]{3,1,2,0:T(8,128)} %get-tuple-element.85) | copy-start | bytes 98692
  125.2 17.3 %copy-start.13 = (f32[32,257]{1,0:T(8,128)S(1)}, f32[32,257]{1,0:T(8,128)}, u32[]{:S(2)}) copy-start(f32[32,257]{1,0:T(8,128)} %copy-done.12) | copy-start | bytes 98692
  125.2 16.4 %collective-permute-start.9 = (f32[32,257]{1,0:T(8,128)S(1)}, f32[32,257]{1,0:T(8,128)S(1)}, u32[]{:S(2)}, u32[]{:S(2)}) collective-permute-start(f32[32,257]{1,0:T(8,128)S(1)} %get-tuple-element.75), channel_id=1, source_target_pairs={{0,8},{2,10},{4,12},{6,14},{8,16},{10,18},{12,20},{14,22},{16,24},... | collective-permute-start | bytes 98696 | tf_op jit(solution)/shard_map/ppermute | solution.py:13
  127.4 15.1 %collective-permute-start.10 = (f32[32,257]{1,0:T(8,128)}, f32[32,257]{1,0:T(8,128)S(1)}, u32[]{:S(2)}, u32[]{:S(2)}) collective-permute-start(f32[32,257]{1,0:T(8,128)} %get-tuple-element.74), channel_id=1, source_target_pairs={{0,506},{2,508},{4,510},{6,0},{8,2},{10,4},{12,6},{14,8},{16,10},{... | collective-permute-start | bytes 98696 | tf_op jit(solution)/shard_map/ppermute | solution.py:13
  136.8 5.7 %collective-permute-start.11 = (f32[32,257]{1,0:T(8,128)S(1)}, f32[32,257]{1,0:T(8,128)S(1)}, u32[]{:S(2)}, u32[]{:S(2)}) collective-permute-start(f32[32,257]{1,0:T(8,128)S(1)} %get-tuple-element.78), channel_id=1, source_target_pairs={{0,504},{2,506},{4,508},{6,510},{8,0},{10,2},{12,4},{14,6},{16,8},... | collective-permute-start | bytes 98696 | tf_op jit(solution)/shard_map/ppermute | solution.py:13
  142.6 9.2 %collective-permute-start.12 = (f32[2,32,4,257]{3,1,2,0:T(8,128)S(1)}, f32[2,32,4,257]{3,1,2,0:T(8,128)S(1)}, u32[]{:S(2)}, u32[]{:S(2)}) collective-permute-start(f32[2,32,4,257]{3,1,2,0:T(8,128)S(1)} %pad_maximum_fusion.7), channel_id=1, source_target_pairs={{0,1},{1,0},{2,3},{3,2},{4,5},{5,4},{6,7},{7,6},{8,9},{9,8},{10,11... | collective-permute-start | bytes 789512 | tf_op jit(solution)/shard_map/ppermute | solution.py:18

commit v12 on v10

--- a/solution.py
+++ b/solution.py
@@ -114,11 +114,11 @@
         )
     mine = jnp.stack(lags, axis=1)
     across = jnp.stack([along(piece, -d, d, flip=True) for d, piece in enumerate(lags, 1)], axis=1)
-    beside = jnp.stack([along(piece, -d, d) for d, piece in enumerate(lags, 1)], axis=1)
-    other = swapped(mine, "rep")
+    done_here = jnp.where(first_rep, mine + across, across + mine)
+    other = swapped(done_here, "rep")
     scale = 1.0 / math.sqrt(segments * lax.axis_size("rep") * half_len)
-    correlations = jnp.where(first_rep, mine + across, other + beside) * scale
-    mirrored = (jnp.where(first_rep, beside + other, across + mine) * scale)[:, :, ::-1]
+    correlations = jnp.where(first_rep, done_here, other) * scale
+    mirrored = (jnp.where(first_rep, other, done_here) * scale)[:, :, ::-1]
     return (correlations, mirrored)
 
 def solution(mesh):

time: 164 us -> 155 us (0.945)
  the two profiles are of different devices: /device:TPU:10 before, /device:TPU:1 now
where the time goes in v12:
time: 155 us
  waiting for transfers between devices  57.6 us (37%)
  starting transfers between devices  56.9 us (37%)
  other arithmetic  18 us (12%)
  matrix products  13.1 us (8%)
  local copies, waits for them, and re-layouts  8.21 us (5%)
    ppermute x8, starting transfers between devices, along(): return lax.ppermute(x, ('blk', 'rep'), perm)  54.9 us
    ppermute x8, waiting for transfers between devices, along(): return lax.ppermute(x, ('blk', 'rep'), perm)  51.6 us
    dot_general x4, matrix products, on_device(): jnp.dot(cross_spectrum(paired, partner, half_len), back_table, precision=...  7.28 us
    another operation x5, other arithmetic  7.11 us
    ppermute x1, waiting for transfers between devices, swapped(): return lax.ppermute(x, axis, [(i, i ^ 1) for i in range(length)])  5.93 us
    unnamed x11, local copies, waits for them, and re-layouts  4.7 us
    convert_element_type x4, other arithmetic, on_device(): paired = jnp.where(first_rep, white, arrived).astype(jnp.float32)  4.46 us
    dot_general x4, matrix products, pick_rows(): jnp.einsum('gp,spk->sgk', picks, block, preferred_element_type=jnp.float32)  3.29 us
  transfers between devices with their start and end apart: 9, of which 6 were waited for; matrix products, arithmetic and copies ran while one was open for 9% of the time, Pallas kernels for 0%

profile of v12, /device:TPU:1, one launch (start us, length us, event | category | flops | bytes accessed | tf_op | source)
XLA Modules:
  0.0 154.7 jit_solution(576682226882088431)
XLA Ops:
  0.6 1.0 fusion.42
  2.3 1.8 %copy.8 = bf16[32,8,2048]{2,0,1:T(8,128)(2,1)S(1)} copy(bf16[32,8,2048]{2,1,0:T(8,128)(2,1)} %param.5) | data formatting | bytes 2097152 | tf_op args[0]
  4.1 3.0 %subtract_convert_fusion = (bf16[32,64,1024]{2,1,0:T(8,128)(2,1)S(1)}, bf16[32,64,1024]{2,1,0:T(8,128)(2,1)S(1)}) fusion(f32[64,1024]{1,0:T(8,128)S(1)} %get-tuple-element.60, f32[32,1024]{1,0:T(8,128)S(1)} %get-tuple-element.57, f32[64,1024]{1,0:T(8,128)S(1)} %get-tuple-element.61, f32[32,1024]{1,0:T(8,128)S(1)} %get-tuple-element.56), kind=kLoop, calls=%fused_computation.5 | loop fusion | flops 18874368 | bytes 9175040 | tf_op jit(solution)/shard_map/convert.7
  7.1 2.5 %fusion.4 = (f32[256]{0:T(256)S(1)}, f32[2048,256]{0,1:T(8,128)S(1)}) fusion(bf16[256,2048]{1,0:T(8,128)(2,1)S(1)} %bitcast.70, bf16[2048,1024]{1,0:T(8,128)(2,1)S(1)} %bitcast.69, bf16[2048,1024]{1,0:T(8,128)(2,1)S(1)} %bitcast.68), kind=kOutput, calls=%fused_computation.12 | convolution fusion | flops 2165309184 | bytes 11535360 | tf_op jit(solution)/shard_map/dot_general | solution.py:89
  10.9 1.0 copy.12
  11.9 2.1 %and_reduce_fusion = pred[]{:T(512)} fusion(s32[3]{0:T(128)S(1)} %copy-done.1, s32[1]{0:T(128)} %get-tuple-element.54, s32[1]{0:T(128)} %constant.94.clone.1, s32[1]{0:T(128)} %get-tuple-element.55), kind=kLoop, calls=%fused_computation.129 | loop fusion | flops 17 | bytes 25 | tf_op jit(solution)/shard_map/reduce.1
  14.0 2.1 %dynamic-slice_select_fusion = bf16[4,32,1]{2,1,0:T(8,128)(2,1)S(1)} fusion(bf16[4,32,1]{2,1,0:T(8,128)(2,1)S(1)} %copy.9, bf16[8,32,2048]{2,1,0:T(8,128)(2,1)S(1)} %multiply_convert_fusion, s32[]{:T(128)} %bitcast.7, s32[]{:T(128)} %bitcast.8, pred[]{:T(512)} %and_reduce_fusion), kind=kLoop, calls=%fused_computation.103 | loop fusion | flops 128 | bytes 777 | tf_op jit(solution)/shard_map/select.1
  16.0 2.7 %scatter.4 = bf16[8,32,2048]{2,1,0:T(8,128)(2,1)} dynamic-update-slice(bf16[8,32,2048]{2,1,0:T(8,128)(2,1)} %copy.12, bf16[4,32,1]{2,1,0:T(8,128)(2,1)S(1)} %dynamic-slice_select_fusion, s32[]{:T(128)} %bitcast.7, s32[]{:T(128)} %constant.84.clone.1, s32[]{:T(128)} %bitcast.8) | dynamic-update-slice | bytes 516 | tf_op jit(solution)/shard_map/scatter | solution.py:98
  18.7 4.6 %collective-permute-start = (bf16[8,32,2048]{2,1,0:T(8,128)(2,1)}, bf16[8,32,2048]{2,1,0:T(8,128)(2,1)}, u32[]{:S(2)}, u32[]{:S(2)}) collective-permute-start(bf16[8,32,2048]{2,1,0:T(8,128)(2,1)} %scatter.4), channel_id=1, source_target_pairs={{0,2},{2,4},{4,6},{6,8},{8,10},{10,12},{12,14},{14,16},{16,18},{18... | collective-permute-start | bytes 3145736 | tf_op jit(solution)/shard_map/ppermute | solution.py:26
  24.3 11.1 %collective-permute-done = bf16[8,32,2048]{2,1,0:T(8,128)(2,1)} collective-permute-done((bf16[8,32,2048]{2,1,0:T(8,128)(2,1)}, bf16[8,32,2048]{2,1,0:T(8,128)(2,1)}, u32[]{:S(2)}, u32[]{:S(2)}) %collective-permute-start) | collective-permute-done | bytes 1048608 | tf_op jit(solution)/shard_map/ppermute | solution.py:26
  35.4 0.8 convert_reduce_fusion.3
  36.2 4.4 %collective-permute-start.1 = (bf16[8,32,2048]{2,1,0:T(8,128)(2,1)}, bf16[8,32,2048]{2,1,0:T(8,128)(2,1)S(1)}, u32[]{:S(2)}, u32[]{:S(2)}) collective-permute-start(bf16[8,32,2048]{2,1,0:T(8,128)(2,1)} %collective-permute-done), channel_id=1, source_target_pairs={{0,2},{2,4},{4,6},{6,8},{8,10},{10,12},{12,14},{14,16},{16,18},{18... | collective-permute-start | bytes 3145736 | tf_op jit(solution)/shard_map/ppermute | solution.py:26
  40.6 1.8 %convolution_bitcast_fusion.3 = f32[8,32,2048]{2,1,0:T(8,128)S(1)} fusion(bf16[8,32,2048]{2,1,0:T(8,128)(2,1)S(1)} %multiply_convert_fusion, pred[]{:T(512)S(6)} %eq.77, bf16[8,32,2048]{2,1,0:T(8,128)(2,1)} %collective-permute-done, pred[2048]{0:T(1024)(128)(4,1)S(1)} %iota_compare_fusion.4, s32[32]{0:T(128)S(1)} %broadcast_select_fusion.12), kind=kOutput, calls=%fused_computation.10 | convolution fusion | flops 34604032 | bytes 4196481 | tf_op jit(solution)/shard_map/gp,spk->sgk/dot_general | solution.py:82
  42.4 2.2 %select_convert_fusion.3 = f32[8,32,2048]{2,1,0:T(8,128)S(1)} fusion(pred[]{:T(512)S(6)} %eq.77, bf16[8,32,2048]{2,1,0:T(8,128)(2,1)} %collective-permute-done, pred[2048]{0:T(1024)(128)(4,1)S(1)} %iota_compare_fusion.4, f32[32]{0:T(128)S(1)} %subtract_convert_fusion.1, f32[8,32,2048]{2,1,0:T(8,128)S(1)} %bitcast.56, f32[8,32]{1,0:T(8,128)S(1)} %rsqrt.12), kind=kLoop, calls=%fused_computation.35 | loop fusion | flops 3145728 | bytes 5246081 | tf_op jit(solution)/shard_map/convert_element_type | solution.py:105
  45.1 1.8 %fusion.8 = f32[32,257]{1,0:T(8,128)S(1)} fusion(f32[1024,257]{1,0:T(8,128)S(1)} %bitcast.64, f32[1024,257]{1,0:T(8,128)S(1)} %bitcast.60, f32[32,1024]{1,0:T(8,128)S(1)} %get-tuple-element.43, f32[32,1024]{1,0:T(8,128)S(1)} %get-tuple-element.42), kind=kOutput, calls=%fused_computation.19 | convolution fusion | flops 202704896 | bytes 2400384 | tf_op jit(solution)/shard_map/dot_general | solution.py:108
  46.9 7.0 %collective-permute-done.1 = bf16[8,32,2048]{2,1,0:T(8,128)(2,1)S(1)} collective-permute-done((bf16[8,32,2048]{2,1,0:T(8,128)(2,1)}, bf16[8,32,2048]{2,1,0:T(8,128)(2,1)S(1)}, u32[]{:S(2)}, u32[]{:S(2)}) %collective-permute-start.1) | collective-permute-done | bytes 1048608 | tf_op jit(solution)/shard_map/ppermute | solution.py:26
  54.0 3.2 %collective-permute-start.2 = (bf16[8,32,2048]{2,1,0:T(8,128)(2,1)S(1)}, bf16[8,32,2048]{2,1,0:T(8,128)(2,1)S(1)}, u32[]{:S(2)}, u32[]{:S(2)}) collective-permute-start(bf16[8,32,2048]{2,1,0:T(8,128)(2,1)S(1)} %collective-permute-done.1), channel_id=1, source_target_pairs={{0,2},{2,4},{4,6},{6,8},{8,10},{10,12},{12,14},{14,16},{16,18},{18... | collective-permute-start | bytes 3145736 | tf_op jit(solution)/shard_map/ppermute | solution.py:26
  59.0 1.8 %fusion.7 = f32[32,257]{1,0:T(8,128)S(1)} fusion(f32[1024,257]{1,0:T(8,128)S(1)} %bitcast.65, f32[1024,257]{1,0:T(8,128)S(1)} %bitcast.61, f32[32,1024]{1,0:T(8,128)S(1)} %get-tuple-element.41, f32[32,1024]{1,0:T(8,128)S(1)} %get-tuple-element.40), kind=kOutput, calls=%fused_computation.18 | convolution fusion | flops 202704896 | bytes 2400384 | tf_op jit(solution)/shard_map/dot_general | solution.py:108
  60.8 15.0 %collective-permute-done.2 = bf16[8,32,2048]{2,1,0:T(8,128)(2,1)S(1)} collective-permute-done((bf16[8,32,2048]{2,1,0:T(8,128)(2,1)S(1)}, bf16[8,32,2048]{2,1,0:T(8,128)(2,1)S(1)}, u32[]{:S(2)}, u32[]{:S(2)}) %collective-permute-start.2) | collective-permute-done | bytes 1048608 | tf_op jit(solution)/shard_map/ppermute | solution.py:26
  75.9 1.9 %collective-permute-start.3 = (bf16[8,32,2048]{2,1,0:T(8,128)(2,1)S(1)}, bf16[8,32,2048]{2,1,0:T(8,128)(2,1)S(1)}, u32[]{:S(2)}, u32[]{:S(2)}) collective-permute-start(bf16[8,32,2048]{2,1,0:T(8,128)(2,1)S(1)} %collective-permute-done.2), channel_id=1, source_target_pairs={{0,2},{2,4},{4,6},{6,8},{8,10},{10,12},{12,14},{14,16},{16,18},{18... | collective-permute-start | bytes 3145736 | tf_op jit(solution)/shard_map/ppermute | solution.py:26
  79.7 1.8 %fusion.6 = f32[32,257]{1,0:T(8,128)S(1)} fusion(f32[1024,257]{1,0:T(8,128)S(1)} %bitcast.66, f32[1024,257]{1,0:T(8,128)S(1)} %bitcast.62, f32[32,1024]{1,0:T(8,128)S(1)} %get-tuple-element.39, f32[32,1024]{1,0:T(8,128)S(1)} %get-tuple-element.38), kind=kOutput, calls=%fused_computation.17 | convolution fusion | flops 202704896 | bytes 2400384 | tf_op jit(solution)/shard_map/dot_general | solution.py:108
  81.5 16.3 %collective-permute-done.3 = bf16[8,32,2048]{2,1,0:T(8,128)(2,1)S(1)} collective-permute-done((bf16[8,32,2048]{2,1,0:T(8,128)(2,1)S(1)}, bf16[8,32,2048]{2,1,0:T(8,128)(2,1)S(1)}, u32[]{:S(2)}, u32[]{:S(2)}) %collective-permute-start.3) | collective-permute-done | bytes 1048608 | tf_op jit(solution)/shard_map/ppermute | solution.py:26
  99.7 1.8 %fusion.5 = f32[32,257]{1,0:T(8,128)S(1)} fusion(f32[1024,257]{1,0:T(8,128)S(1)} %bitcast.67, f32[1024,257]{1,0:T(8,128)S(1)} %bitcast.63, f32[32,1024]{1,0:T(8,128)S(1)} %get-tuple-element.37, f32[32,1024]{1,0:T(8,128)S(1)} %get-tuple-element.36), kind=kOutput, calls=%fused_computation.16 | convolution fusion | flops 202704896 | bytes 2400384 | tf_op jit(solution)/shard_map/dot_general | solution.py:108
  101.5 4.4 %collective-permute-start.7 = (f32[32,257]{1,0:T(8,128)S(1)}, f32[32,257]{1,0:T(8,128)S(1)}, u32[]{:S(2)}, u32[]{:S(2)}) collective-permute-start(f32[32,257]{1,0:T(8,128)S(1)} %fusion.5), channel_id=1, source_target_pairs={{0,505},{2,507},{4,509},{6,511},{8,1},{10,3},{12,5},{14,7},{16,9},... | collective-permute-start | bytes 98696 | tf_op jit(solution)/shard_map/ppermute | solution.py:26
  105.9 17.7 %collective-permute-start.4 = (f32[32,257]{1,0:T(8,128)S(1)}, f32[32,257]{1,0:T(8,128)S(1)}, u32[]{:S(2)}, u32[]{:S(2)}) collective-permute-start(f32[32,257]{1,0:T(8,128)S(1)} %fusion.8), channel_id=1, source_target_pairs={{0,511},{2,1},{4,3},{6,5},{8,7},{10,9},{12,11},{14,13},{16,15},{18... | collective-permute-start | bytes 98696 | tf_op jit(solution)/shard_map/ppermute | solution.py:26
  123.6 9.4 %collective-permute-start.5 = (f32[32,257]{1,0:T(8,128)S(1)}, f32[32,257]{1,0:T(8,128)S(1)}, u32[]{:S(2)}, u32[]{:S(2)}) collective-permute-start(f32[32,257]{1,0:T(8,128)S(1)} %fusion.7), channel_id=1, source_target_pairs={{0,509},{2,511},{4,1},{6,3},{8,5},{10,7},{12,9},{14,11},{16,13},{1... | collective-permute-start | bytes 98696 | tf_op jit(solution)/shard_map/ppermute | solution.py:26
  133.0 9.4 %collective-permute-start.6 = (f32[32,257]{1,0:T(8,128)S(1)}, f32[32,257]{1,0:T(8,128)S(1)}, u32[]{:S(2)}, u32[]{:S(2)}) collective-permute-start(f32[32,257]{1,0:T(8,128)S(1)} %fusion.6), channel_id=1, source_target_pairs={{0,507},{2,509},{4,511},{6,1},{8,3},{10,5},{12,7},{14,9},{16,11},{... | collective-permute-start | bytes 98696 | tf_op jit(solution)/shard_map/ppermute | solution.py:26
  142.4 2.3 %collective-permute-done.6 = f32[32,257]{1,0:T(8,128)S(1)} collective-permute-done((f32[32,257]{1,0:T(8,128)S(1)}, f32[32,257]{1,0:T(8,128)S(1)}, u32[]{:S(2)}, u32[]{:S(2)}) %collective-permute-start.6) | collective-permute-done | bytes 32928 | tf_op jit(solution)/shard_map/ppermute | solution.py:26
  144.8 1.9 %collective-permute-start.8 = (f32[32,4,257]{2,0,1:T(8,128)S(1)}, f32[32,4,257]{2,0,1:T(8,128)S(1)}, u32[]{:S(2)}, u32[]{:S(2)}) collective-permute-start(f32[32,4,257]{2,0,1:T(8,128)S(1)} %maximum_add_fusion), channel_id=1, source_target_pairs={{0,1},{1,0},{2,3},{3,2},{4,5},{5,4},{6,7},{7,6},{8,9},{9,8},{10,11... | collective-permute-start | bytes 394760 | tf_op jit(solution)/shard_map/ppermute | solution.py:18
  146.7 5.9 %collective-permute-done.8 = f32[32,4,257]{2,0,1:T(8,128)S(1)} collective-permute-done((f32[32,4,257]{2,0,1:T(8,128)S(1)}, f32[32,4,257]{2,0,1:T(8,128)S(1)}, u32[]{:S(2)}, u32[]{:S(2)}) %collective-permute-start.8) | collective-permute-done | bytes 131616 | tf_op jit(solution)/shard_map/ppermute | solution.py:18
  153.1 0.8 copy.11
  153.9 0.8 copy.10
  (45 shorter events, 9.5 us)
Async XLA Ops:
  7.1 2.6 %copy-start.2 = (s32[32]{0:T(128)S(1)}, s32[32]{0:T(128)}, u32[]{:S(2)}) copy-start(s32[32]{0:T(128)} %param.7) | copy-start | bytes 388
  7.1 3.2 %copy-start = (s32[4,32]{1,0:T(4,128)S(1)}, s32[4,32]{1,0:T(4,128)}, u32[]{:S(2)}) copy-start(s32[4,32]{1,0:T(4,128)} %param.6) | copy-start | bytes 1540
  10.4 1.5 copy-start.1
  18.7 16.6 %collective-permute-start = (bf16[8,32,2048]{2,1,0:T(8,128)(2,1)}, bf16[8,32,2048]{2,1,0:T(8,128)(2,1)}, u32[]{:S(2)}, u32[]{:S(2)}) collective-permute-start(bf16[8,32,2048]{2,1,0:T(8,128)(2,1)} %scatter.4), channel_id=1, source_target_pairs={{0,2},{2,4},{4,6},{6,8},{8,10},{10,12},{12,14},{14,16},{16,18},{18... | collective-permute-start | bytes 3145736 | tf_op jit(solution)/shard_map/ppermute | solution.py:26
  36.2 17.7 %collective-permute-start.1 = (bf16[8,32,2048]{2,1,0:T(8,128)(2,1)}, bf16[8,32,2048]{2,1,0:T(8,128)(2,1)S(1)}, u32[]{:S(2)}, u32[]{:S(2)}) collective-permute-start(bf16[8,32,2048]{2,1,0:T(8,128)(2,1)} %collective-permute-done), channel_id=1, source_target_pairs={{0,2},{2,4},{4,6},{6,8},{8,10},{10,12},{12,14},{14,16},{16,18},{18... | collective-permute-start | bytes 3145736 | tf_op jit(solution)/shard_map/ppermute | solution.py:26
  54.0 21.8 %collective-permute-start.2 = (bf16[8,32,2048]{2,1,0:T(8,128)(2,1)S(1)}, bf16[8,32,2048]{2,1,0:T(8,128)(2,1)S(1)}, u32[]{:S(2)}, u32[]{:S(2)}) collective-permute-start(bf16[8,32,2048]{2,1,0:T(8,128)(2,1)S(1)} %collective-permute-done.1), channel_id=1, source_target_pairs={{0,2},{2,4},{4,6},{6,8},{8,10},{10,12},{12,14},{14,16},{16,18},{18... | collective-permute-start | bytes 3145736 | tf_op jit(solution)/shard_map/ppermute | solution.py:26
  75.9 21.8 %collective-permute-start.3 = (bf16[8,32,2048]{2,1,0:T(8,128)(2,1)S(1)}, bf16[8,32,2048]{2,1,0:T(8,128)(2,1)S(1)}, u32[]{:S(2)}, u32[]{:S(2)}) collective-permute-start(bf16[8,32,2048]{2,1,0:T(8,128)(2,1)S(1)} %collective-permute-done.2), channel_id=1, source_target_pairs={{0,2},{2,4},{4,6},{6,8},{8,10},{10,12},{12,14},{14,16},{16,18},{18... | collective-permute-start | bytes 3145736 | tf_op jit(solution)/shard_map/ppermute | solution.py:26
  101.5 40.9 %collective-permute-start.7 = (f32[32,257]{1,0:T(8,128)S(1)}, f32[32,257]{1,0:T(8,128)S(1)}, u32[]{:S(2)}, u32[]{:S(2)}) collective-permute-start(f32[32,257]{1,0:T(8,128)S(1)} %fusion.5), channel_id=1, source_target_pairs={{0,505},{2,507},{4,509},{6,511},{8,1},{10,3},{12,5},{14,7},{16,9},... | collective-permute-start | bytes 98696 | tf_op jit(solution)/shard_map/ppermute | solution.py:26
  105.9 36.5 %collective-permute-start.4 = (f32[32,257]{1,0:T(8,128)S(1)}, f32[32,257]{1,0:T(8,128)S(1)}, u32[]{:S(2)}, u32[]{:S(2)}) collective-permute-start(f32[32,257]{1,0:T(8,128)S(1)} %fusion.8), channel_id=1, source_target_pairs={{0,511},{2,1},{4,3},{6,5},{8,7},{10,9},{12,11},{14,13},{16,15},{18... | collective-permute-start | bytes 98696 | tf_op jit(solution)/shard_map/ppermute | solution.py:26
  123.6 18.8 %collective-permute-start.5 = (f32[32,257]{1,0:T(8,128)S(1)}, f32[32,257]{1,0:T(8,128)S(1)}, u32[]{:S(2)}, u32[]{:S(2)}) collective-permute-start(f32[32,257]{1,0:T(8,128)S(1)} %fusion.7), channel_id=1, source_target_pairs={{0,509},{2,511},{4,1},{6,3},{8,5},{10,7},{12,9},{14,11},{16,13},{1... | collective-permute-start | bytes 98696 | tf_op jit(solution)/shard_map/ppermute | solution.py:26
  133.0 11.7 %collective-permute-start.6 = (f32[32,257]{1,0:T(8,128)S(1)}, f32[32,257]{1,0:T(8,128)S(1)}, u32[]{:S(2)}, u32[]{:S(2)}) collective-permute-start(f32[32,257]{1,0:T(8,128)S(1)} %fusion.6), channel_id=1, source_target_pairs={{0,507},{2,509},{4,511},{6,1},{8,3},{10,5},{12,7},{14,9},{16,11},{... | collective-permute-start | bytes 98696 | tf_op jit(solution)/shard_map/ppermute | solution.py:26
  144.8 7.9 %collective-permute-start.8 = (f32[32,4,257]{2,0,1:T(8,128)S(1)}, f32[32,4,257]{2,0,1:T(8,128)S(1)}, u32[]{:S(2)}, u32[]{:S(2)}) collective-permute-start(f32[32,4,257]{2,0,1:T(8,128)S(1)} %maximum_add_fusion), channel_id=1, source_target_pairs={{0,1},{1,0},{2,3},{3,2},{4,5},{5,4},{6,7},{7,6},{8,9},{9,8},{10,11... | collective-permute-start | bytes 394760 | tf_op jit(solution)/shard_map/ppermute | solution.py:18

commit v13 on v7

--- a/solution.py
+++ b/solution.py
@@ -99,19 +99,24 @@
         later_offsets = later[stop - 1, :, half_len].astype(jnp.int32)
         later = jnp.where(dc_imag, jnp.zeros_like(later), later).astype(jnp.float32)
         later = cross_spectrum(later, pick_rows(later_offsets, behind), half_len)
-        return jnp.dot(
-            jnp.concatenate([own, later], axis=0),
+        return jnp.concatenate([own, later], axis=0)
+
+    def lags_of_stops(crosses):
+        rows = crosses[0].shape[0]
+        lags = jnp.dot(
+            jnp.concatenate(crosses, axis=0),
             back_table,
-            precision=lax.Precision.HIGHEST,
+            precision=lax.Precision.HIGH,
             preferred_element_type=jnp.float32,
         )
+        return [lags[i * rows:(i + 1) * rows] for i in range(len(crosses))]
 
     near = stops // 2
     first = lax.optimization_barrier(
         tuple(shifted(moving_ahead, "blk", d) for d in range(1, near + 1))
         + tuple(shifted(moving_behind, "blk", -d) for d in range(1, near + 1))
     )
-    lags = [lags_of(d, first[d - 1], first[near + d - 1]) for d in range(1, near + 1)]
+    lags = lags_of_stops([lags_of(d, first[d - 1], first[near + d - 1]) for d in range(1, near + 1)])
     early = [
         (shifted(piece[channels:], "blk", d), shifted(piece[:channels], "blk", -d)) for d, piece in enumerate(lags, 1)
     ]
@@ -122,9 +127,12 @@
             early,
         )
     )
-    for d in range(near + 1, stops + 1):
-        at = (d - near - 1) * split
-        lags.append(lags_of(d, far_ahead[at:at + split], far_behind[at:at + split]))
+    lags += lags_of_stops(
+        [
+            lags_of(d, far_ahead[(d - near - 1) * split:(d - near) * split], far_behind[(d - near - 1) * split:(d - near) * split])
+            for d in range(near + 1, stops + 1)
+        ]
+    )
     late = [(shifted(lags[d - 1][channels:], "blk", d), shifted(lags[d - 1][:channels], "blk", -d)) for d in
             range(near + 1, stops + 1)]
     own_parts = [piece[:channels] for piece in lags]

time: 138 us -> 144 us (1.043)
  the two profiles are of different devices: /device:TPU:1 before, /device:TPU:8 now
where the time goes in v13:
time: 144 us; the launch traced here: 143 us
  starting transfers between devices  71.8 us (50%)
  waiting for transfers between devices  44.8 us (31%)
  matrix products  10.5 us (7%)
  other arithmetic  9.11 us (6%)
  local copies, waits for them, and re-layouts  6.03 us (4%)
    ppermute x14, starting transfers between devices, shifted(): lax.ppermute(x, axis, [(i, (i + by) % length) for i in range(length)])  69.3 us
    ppermute x14, waiting for transfers between devices, shifted(): lax.ppermute(x, axis, [(i, (i + by) % length) for i in range(length)])  34.6 us
    ppermute x1, waiting for transfers between devices, swapped(): return lax.ppermute(x, axis, [(i, i ^ 1) for i in range(length)])  10.2 us
    dot_general x2, matrix products, lags_of_stops(): jnp.dot(jnp.concatenate(crosses, axis=0), back_table, precision=lax.Preci...  5.31 us
    unnamed x8, local copies, waits for them, and re-layouts  3.71 us
    another operation x2, other arithmetic  2.96 us
  transfers between devices with their start and end apart: 15, of which 8 were waited for; matrix products, arithmetic and copies ran while one was open for 5% of the time, Pallas kernels for 0%

profile of v13, /device:TPU:8, one launch (start us, length us, event | category | flops | bytes accessed | tf_op | source)
XLA Modules:
  0.0 143.3 jit_solution(6077940796027309209)
XLA Ops:
  0.6 1.0 fusion.47
  1.7 0.6 fusion.53
  2.3 1.8 %copy.12 = bf16[32,8,2048]{2,0,1:T(8,128)(2,1)S(1)} copy(bf16[32,8,2048]{2,1,0:T(8,128)(2,1)} %param.5) | data formatting | bytes 2097152 | tf_op args[0]
  4.1 3.0 %subtract_convert_fusion = (bf16[32,64,1024]{2,1,0:T(8,128)(2,1)S(1)}, bf16[32,64,1024]{2,1,0:T(8,128)(2,1)S(1)}) fusion(f32[64,1024]{1,0:T(8,128)S(1)} %get-tuple-element.103, f32[32,1024]{1,0:T(8,128)S(1)} %get-tuple-element.100, f32[64,1024]{1,0:T(8,128)S(1)} %get-tuple-element.104, f32[32,1024]{1,0:T(8,128)S(1)} %get-tuple-element.99), kind=kLoop, calls=%fused_computation.5 | loop fusion | flops 18874368 | bytes 9175040 | tf_op jit(solution)/shard_map/convert.7
  7.1 2.5 %fusion.6 = (f32[256]{0:T(256)S(1)}, f32[2048,256]{0,1:T(8,128)S(1)}) fusion(bf16[256,2048]{1,0:T(8,128)(2,1)S(1)} %bitcast.108, bf16[2048,1024]{1,0:T(8,128)(2,1)S(1)} %bitcast.102, bf16[2048,1024]{1,0:T(8,128)(2,1)S(1)} %bitcast.101), kind=kOutput, calls=%fused_computation.18 | convolution fusion | flops 2165309184 | bytes 11535360 | tf_op jit(solution)/shard_map/dot_general | solution.py:81
  10.6 1.9 %collective-permute-start.2 = (bf16[4,32,2048]{2,1,0:T(8,128)(2,1)S(1)}, bf16[4,32,2048]{2,1,0:T(8,128)(2,1)S(1)}, u32[]{:S(2)}, u32[]{:S(2)}) collective-permute-start(bf16[4,32,2048]{2,1,0:T(8,128)(2,1)S(1)} %scatter.4), channel_id=1, source_target_pairs={{0,510},{2,0},{4,2},{6,4},{8,6},{10,8},{12,10},{14,12},{16,14},{18... | collective-permute-start | bytes 1572872 | tf_op jit(solution)/shard_map/ppermute | solution.py:13
  12.5 16.2 %collective-permute-start.3 = (bf16[4,32,2048]{2,1,0:T(8,128)(2,1)S(1)}, bf16[4,32,2048]{2,1,0:T(8,128)(2,1)S(1)}, u32[]{:S(2)}, u32[]{:S(2)}) collective-permute-start(bf16[4,32,2048]{2,1,0:T(8,128)(2,1)S(1)} %scatter.4), channel_id=1, source_target_pairs={{0,508},{2,510},{4,0},{6,2},{8,4},{10,6},{12,8},{14,10},{16,12},{1... | collective-permute-start | bytes 1572872 | tf_op jit(solution)/shard_map/ppermute | solution.py:13
  28.7 1.9 %collective-permute-start = (bf16[4,32,2048]{2,1,0:T(8,128)(2,1)S(1)}, bf16[4,32,2048]{2,1,0:T(8,128)(2,1)S(1)}, u32[]{:S(2)}, u32[]{:S(2)}) collective-permute-start(bf16[4,32,2048]{2,1,0:T(8,128)(2,1)S(1)} %get-tuple-element.66), channel_id=1, source_target_pairs={{0,2},{2,4},{4,6},{6,8},{8,10},{10,12},{12,14},{14,16},{16,18},{18... | collective-permute-start | bytes 1572872 | tf_op jit(solution)/shard_map/ppermute | solution.py:13
  30.6 1.9 %collective-permute-start.1 = (bf16[4,32,2048]{2,1,0:T(8,128)(2,1)S(1)}, bf16[4,32,2048]{2,1,0:T(8,128)(2,1)S(1)}, u32[]{:S(2)}, u32[]{:S(2)}) collective-permute-start(bf16[4,32,2048]{2,1,0:T(8,128)(2,1)S(1)} %get-tuple-element.66), channel_id=1, source_target_pairs={{0,4},{2,6},{4,8},{6,10},{8,12},{10,14},{12,16},{14,18},{16,20},{1... | collective-permute-start | bytes 1572872 | tf_op jit(solution)/shard_map/ppermute | solution.py:13
  33.5 1.9 %collective-permute-done.3 = bf16[4,32,2048]{2,1,0:T(8,128)(2,1)S(1)} collective-permute-done((bf16[4,32,2048]{2,1,0:T(8,128)(2,1)S(1)}, bf16[4,32,2048]{2,1,0:T(8,128)(2,1)S(1)}, u32[]{:S(2)}, u32[]{:S(2)}) %collective-permute-start.3) | collective-permute-done | bytes 524320 | tf_op jit(solution)/shard_map/ppermute | solution.py:13
  35.4 6.9 %collective-permute-done = bf16[4,32,2048]{2,1,0:T(8,128)(2,1)S(1)} collective-permute-done((bf16[4,32,2048]{2,1,0:T(8,128)(2,1)S(1)}, bf16[4,32,2048]{2,1,0:T(8,128)(2,1)S(1)}, u32[]{:S(2)}, u32[]{:S(2)}) %collective-permute-start) | collective-permute-done | bytes 524320 | tf_op jit(solution)/shard_map/ppermute | solution.py:13
  42.2 5.1 %collective-permute-done.1 = bf16[4,32,2048]{2,1,0:T(8,128)(2,1)S(1)} collective-permute-done((bf16[4,32,2048]{2,1,0:T(8,128)(2,1)S(1)}, bf16[4,32,2048]{2,1,0:T(8,128)(2,1)S(1)}, u32[]{:S(2)}, u32[]{:S(2)}) %collective-permute-start.1) | collective-permute-done | bytes 524320 | tf_op jit(solution)/shard_map/ppermute | solution.py:13
  48.5 9.0 %collective-permute-start.5 = (bf16[8,32,2048]{2,1,0:T(8,128)(2,1)S(1)}, bf16[8,32,2048]{2,1,0:T(8,128)(2,1)S(1)}, u32[]{:S(2)}, u32[]{:S(2)}) collective-permute-start(bf16[8,32,2048]{2,1,0:T(8,128)(2,1)S(1)} %pad_maximum_fusion.4), channel_id=1, source_target_pairs={{0,508},{2,510},{4,0},{6,2},{8,4},{10,6},{12,8},{14,10},{16,12},{1... | collective-permute-start | bytes 3145736 | tf_op jit(solution)/shard_map/ppermute | solution.py:13
  58.0 2.1 %collective-permute-start.4 = (bf16[8,32,2048]{2,1,0:T(8,128)(2,1)S(1)}, bf16[8,32,2048]{2,1,0:T(8,128)(2,1)S(1)}, u32[]{:S(2)}, u32[]{:S(2)}) collective-permute-start(bf16[8,32,2048]{2,1,0:T(8,128)(2,1)S(1)} %pad_maximum_fusion.3), channel_id=1, source_target_pairs={{0,4},{2,6},{4,8},{6,10},{8,12},{10,14},{12,16},{14,18},{16,20},{1... | collective-permute-start | bytes 3145736 | tf_op jit(solution)/shard_map/ppermute | solution.py:13
  61.4 2.7 %fusion.5 = f32[128,257]{0,1:T(8,128)S(1)} fusion(f32[1024,257]{1,0:T(8,128)S(1)} %bitcast.106, f32[1024,257]{1,0:T(8,128)S(1)} %bitcast.104, f32[32,1024]{1,0:T(8,128)S(1)} %get-tuple-element.55, f32[32,1024]{1,0:T(8,128)S(1)} %get-tuple-element.54, f32[32,1024]{1,0:T(8,128)S(1)} %get-tuple-element.60, f32[32,1024]{1,0:T(8,128)S(1)} %get-tuple-element.61, ...), kind=kOutput, calls=%fused_computation.8 | convolution fusion | flops 406587392 | bytes 3285504 | tf_op jit(solution)/shard_map/dot_general | solution.py:106
  64.2 4.5 %collective-permute-start.6 = (f32[32,257]{0,1:T(8,128)S(1)}, f32[32,257]{0,1:T(8,128)S(1)}, u32[]{:S(2)}, u32[]{:S(2)}) collective-permute-start(f32[32,257]{0,1:T(8,128)S(1)} %get-tuple-element.86), channel_id=1, source_target_pairs={{0,2},{2,4},{4,6},{6,8},{8,10},{10,12},{12,14},{14,16},{16,18},{18... | collective-permute-start | bytes 98696 | tf_op jit(solution)/shard_map/ppermute | solution.py:13
  68.7 3.2 %collective-permute-start.7 = (f32[32,257]{0,1:T(8,128)S(1)}, f32[32,257]{0,1:T(8,128)S(1)}, u32[]{:S(2)}, u32[]{:S(2)}) collective-permute-start(f32[32,257]{0,1:T(8,128)S(1)} %get-tuple-element.88), channel_id=1, source_target_pairs={{0,510},{2,0},{4,2},{6,4},{8,6},{10,8},{12,10},{14,12},{16,14},{18... | collective-permute-start | bytes 98696 | tf_op jit(solution)/shard_map/ppermute | solution.py:13
  72.0 2.2 %collective-permute-start.8 = (f32[32,257]{0,1:T(8,128)S(1)}, f32[32,257]{0,1:T(8,128)S(1)}, u32[]{:S(2)}, u32[]{:S(2)}) collective-permute-start(f32[32,257]{0,1:T(8,128)S(1)} %get-tuple-element.85), channel_id=1, source_target_pairs={{0,4},{2,6},{4,8},{6,10},{8,12},{10,14},{12,16},{14,18},{16,20},{1... | collective-permute-start | bytes 98696 | tf_op jit(solution)/shard_map/ppermute | solution.py:13
  74.2 14.6 %collective-permute-done.6 = f32[32,257]{0,1:T(8,128)S(1)} collective-permute-done((f32[32,257]{0,1:T(8,128)S(1)}, f32[32,257]{0,1:T(8,128)S(1)}, u32[]{:S(2)}, u32[]{:S(2)}) %collective-permute-start.6) | collective-permute-done | bytes 32928 | tf_op jit(solution)/shard_map/ppermute | solution.py:13
  88.8 7.6 %collective-permute-start.9 = (f32[32,257]{0,1:T(8,128)S(1)}, f32[32,257]{0,1:T(8,128)S(1)}, u32[]{:S(2)}, u32[]{:S(2)}) collective-permute-start(f32[32,257]{0,1:T(8,128)S(1)} %get-tuple-element.87), channel_id=1, source_target_pairs={{0,508},{2,510},{4,0},{6,2},{8,4},{10,6},{12,8},{14,10},{16,12},{1... | collective-permute-start | bytes 98696 | tf_op jit(solution)/shard_map/ppermute | solution.py:13
  96.5 2.5 %collective-permute-done.9 = f32[32,257]{0,1:T(8,128)S(1)} collective-permute-done((f32[32,257]{0,1:T(8,128)S(1)}, f32[32,257]{0,1:T(8,128)S(1)}, u32[]{:S(2)}, u32[]{:S(2)}) %collective-permute-start.9) | collective-permute-done | bytes 32928 | tf_op jit(solution)/shard_map/ppermute | solution.py:13
  101.6 2.7 %fusion.4 = f32[128,257]{0,1:T(8,128)S(1)} fusion(f32[1024,257]{1,0:T(8,128)S(1)} %bitcast.107, f32[1024,257]{1,0:T(8,128)S(1)} %bitcast.105, f32[32,1024]{1,0:T(8,128)S(1)} %get-tuple-element.47, f32[32,1024]{1,0:T(8,128)S(1)} %get-tuple-element.46, f32[32,1024]{1,0:T(8,128)S(1)} %get-tuple-element.56, f32[32,1024]{1,0:T(8,128)S(1)} %get-tuple-element.57, ...), kind=kOutput, calls=%fused_computation.7 | convolution fusion | flops 406587392 | bytes 3285504 | tf_op jit(solution)/shard_map/dot_general | solution.py:106
  104.5 1.9 %collective-permute-start.10 = (f32[32,257]{0,1:T(8,128)S(1)}, f32[32,257]{0,1:T(8,128)S(1)}, u32[]{:S(2)}, u32[]{:S(2)}) collective-permute-start(f32[32,257]{0,1:T(8,128)S(1)} %get-tuple-element.73), channel_id=1, source_target_pairs={{0,6},{2,8},{4,10},{6,12},{8,14},{10,16},{12,18},{14,20},{16,22},{... | collective-permute-start | bytes 98696 | tf_op jit(solution)/shard_map/ppermute | solution.py:13
  106.4 1.9 %collective-permute-start.11 = (f32[32,257]{0,1:T(8,128)S(1)}, f32[32,257]{0,1:T(8,128)S(1)}, u32[]{:S(2)}, u32[]{:S(2)}) collective-permute-start(f32[32,257]{0,1:T(8,128)S(1)} %get-tuple-element.78), channel_id=1, source_target_pairs={{0,8},{2,10},{4,12},{6,14},{8,16},{10,18},{12,20},{14,22},{16,24},... | collective-permute-start | bytes 98696 | tf_op jit(solution)/shard_map/ppermute | solution.py:13
  108.3 10.3 %collective-permute-start.12 = (f32[32,257]{0,1:T(8,128)S(1)}, f32[32,257]{0,1:T(8,128)S(1)}, u32[]{:S(2)}, u32[]{:S(2)}) collective-permute-start(f32[32,257]{0,1:T(8,128)S(1)} %get-tuple-element.80), channel_id=1, source_target_pairs={{0,506},{2,508},{4,510},{6,0},{8,2},{10,4},{12,6},{14,8},{16,10},{... | collective-permute-start | bytes 98696 | tf_op jit(solution)/shard_map/ppermute | solution.py:13
  118.6 4.5 %collective-permute-start.13 = (f32[32,257]{0,1:T(8,128)S(1)}, f32[32,257]{0,1:T(8,128)S(1)}, u32[]{:S(2)}, u32[]{:S(2)}) collective-permute-start(f32[32,257]{0,1:T(8,128)S(1)} %get-tuple-element.79), channel_id=1, source_target_pairs={{0,504},{2,506},{4,508},{6,510},{8,0},{10,2},{12,4},{14,6},{16,8},... | collective-permute-start | bytes 98696 | tf_op jit(solution)/shard_map/ppermute | solution.py:13
  124.5 0.8 collective-permute-done.11
  125.6 2.8 %collective-permute-done.13 = f32[32,257]{0,1:T(8,128)S(1)} collective-permute-done((f32[32,257]{0,1:T(8,128)S(1)}, f32[32,257]{0,1:T(8,128)S(1)}, u32[]{:S(2)}, u32[]{:S(2)}) %collective-permute-start.13) | collective-permute-done | bytes 32928 | tf_op jit(solution)/shard_map/ppermute | solution.py:13
  128.5 2.5 %collective-permute-start.14 = (f32[2,32,4,257]{3,1,2,0:T(8,128)S(1)}, f32[2,32,4,257]{3,1,2,0:T(8,128)S(1)}, u32[]{:S(2)}, u32[]{:S(2)}) collective-permute-start(f32[2,32,4,257]{3,1,2,0:T(8,128)S(1)} %pad_maximum_fusion.5), channel_id=1, source_target_pairs={{0,1},{1,0},{2,3},{3,2},{4,5},{5,4},{6,7},{7,6},{8,9},{9,8},{10,11... | collective-permute-start | bytes 789512 | tf_op jit(solution)/shard_map/ppermute | solution.py:18
  131.0 10.2 %collective-permute-done.14 = f32[2,32,4,257]{3,1,2,0:T(8,128)S(1)} collective-permute-done((f32[2,32,4,257]{3,1,2,0:T(8,128)S(1)}, f32[2,32,4,257]{3,1,2,0:T(8,128)S(1)}, u32[]{:S(2)}, u32[]{:S(2)}) %collective-permute-start.14) | collective-permute-done | bytes 263200 | tf_op jit(solution)/shard_map/ppermute | solution.py:18
  141.7 0.8 copy.31
  142.5 0.8 copy.30
  (72 shorter events, 9.9 us)
Async XLA Ops:
  7.0 2.6 %copy-start.1 = (s32[32]{0:T(128)S(1)}, s32[32]{0:T(128)}, u32[]{:S(2)}) copy-start(s32[32]{0:T(128)} %param.7) | copy-start | bytes 388
  9.6 0.7 copy-start
  10.6 22.9 %collective-permute-start.2 = (bf16[4,32,2048]{2,1,0:T(8,128)(2,1)S(1)}, bf16[4,32,2048]{2,1,0:T(8,128)(2,1)S(1)}, u32[]{:S(2)}, u32[]{:S(2)}) collective-permute-start(bf16[4,32,2048]{2,1,0:T(8,128)(2,1)S(1)} %scatter.4), channel_id=1, source_target_pairs={{0,510},{2,0},{4,2},{6,4},{8,6},{10,8},{12,10},{14,12},{16,14},{18... | collective-permute-start | bytes 1572872 | tf_op jit(solution)/shard_map/ppermute | solution.py:13
  12.5 22.9 %collective-permute-start.3 = (bf16[4,32,2048]{2,1,0:T(8,128)(2,1)S(1)}, bf16[4,32,2048]{2,1,0:T(8,128)(2,1)S(1)}, u32[]{:S(2)}, u32[]{:S(2)}) collective-permute-start(bf16[4,32,2048]{2,1,0:T(8,128)(2,1)S(1)} %scatter.4), channel_id=1, source_target_pairs={{0,508},{2,510},{4,0},{6,2},{8,4},{10,6},{12,8},{14,10},{16,12},{1... | collective-permute-start | bytes 1572872 | tf_op jit(solution)/shard_map/ppermute | solution.py:13
  28.7 13.5 %collective-permute-start = (bf16[4,32,2048]{2,1,0:T(8,128)(2,1)S(1)}, bf16[4,32,2048]{2,1,0:T(8,128)(2,1)S(1)}, u32[]{:S(2)}, u32[]{:S(2)}) collective-permute-start(bf16[4,32,2048]{2,1,0:T(8,128)(2,1)S(1)} %get-tuple-element.66), channel_id=1, source_target_pairs={{0,2},{2,4},{4,6},{6,8},{8,10},{10,12},{12,14},{14,16},{16,18},{18... | collective-permute-start | bytes 1572872 | tf_op jit(solution)/shard_map/ppermute | solution.py:13
  30.6 16.8 %collective-permute-start.1 = (bf16[4,32,2048]{2,1,0:T(8,128)(2,1)S(1)}, bf16[4,32,2048]{2,1,0:T(8,128)(2,1)S(1)}, u32[]{:S(2)}, u32[]{:S(2)}) collective-permute-start(bf16[4,32,2048]{2,1,0:T(8,128)(2,1)S(1)} %get-tuple-element.66), channel_id=1, source_target_pairs={{0,4},{2,6},{4,8},{6,10},{8,12},{10,14},{12,16},{14,18},{16,20},{1... | collective-permute-start | bytes 1572872 | tf_op jit(solution)/shard_map/ppermute | solution.py:13
  48.5 50.5 %collective-permute-start.5 = (bf16[8,32,2048]{2,1,0:T(8,128)(2,1)S(1)}, bf16[8,32,2048]{2,1,0:T(8,128)(2,1)S(1)}, u32[]{:S(2)}, u32[]{:S(2)}) collective-permute-start(bf16[8,32,2048]{2,1,0:T(8,128)(2,1)S(1)} %pad_maximum_fusion.4), channel_id=1, source_target_pairs={{0,508},{2,510},{4,0},{6,2},{8,4},{10,6},{12,8},{14,10},{16,12},{1... | collective-permute-start | bytes 3145736 | tf_op jit(solution)/shard_map/ppermute | solution.py:13
  58.0 41.0 %collective-permute-start.4 = (bf16[8,32,2048]{2,1,0:T(8,128)(2,1)S(1)}, bf16[8,32,2048]{2,1,0:T(8,128)(2,1)S(1)}, u32[]{:S(2)}, u32[]{:S(2)}) collective-permute-start(bf16[8,32,2048]{2,1,0:T(8,128)(2,1)S(1)} %pad_maximum_fusion.3), channel_id=1, source_target_pairs={{0,4},{2,6},{4,8},{6,10},{8,12},{10,14},{12,16},{14,18},{16,20},{1... | collective-permute-start | bytes 3145736 | tf_op jit(solution)/shard_map/ppermute | solution.py:13
  64.2 24.6 %collective-permute-start.6 = (f32[32,257]{0,1:T(8,128)S(1)}, f32[32,257]{0,1:T(8,128)S(1)}, u32[]{:S(2)}, u32[]{:S(2)}) collective-permute-start(f32[32,257]{0,1:T(8,128)S(1)} %get-tuple-element.86), channel_id=1, source_target_pairs={{0,2},{2,4},{4,6},{6,8},{8,10},{10,12},{12,14},{14,16},{16,18},{18... | collective-permute-start | bytes 98696 | tf_op jit(solution)/shard_map/ppermute | solution.py:13
  68.7 27.8 %collective-permute-start.7 = (f32[32,257]{0,1:T(8,128)S(1)}, f32[32,257]{0,1:T(8,128)S(1)}, u32[]{:S(2)}, u32[]{:S(2)}) collective-permute-start(f32[32,257]{0,1:T(8,128)S(1)} %get-tuple-element.88), channel_id=1, source_target_pairs={{0,510},{2,0},{4,2},{6,4},{8,6},{10,8},{12,10},{14,12},{16,14},{18... | collective-permute-start | bytes 98696 | tf_op jit(solution)/shard_map/ppermute | solution.py:13
  72.0 24.5 %collective-permute-start.8 = (f32[32,257]{0,1:T(8,128)S(1)}, f32[32,257]{0,1:T(8,128)S(1)}, u32[]{:S(2)}, u32[]{:S(2)}) collective-permute-start(f32[32,257]{0,1:T(8,128)S(1)} %get-tuple-element.85), channel_id=1, source_target_pairs={{0,4},{2,6},{4,8},{6,10},{8,12},{10,14},{12,16},{14,18},{16,20},{1... | collective-permute-start | bytes 98696 | tf_op jit(solution)/shard_map/ppermute | solution.py:13
  88.8 10.2 %collective-permute-start.9 = (f32[32,257]{0,1:T(8,128)S(1)}, f32[32,257]{0,1:T(8,128)S(1)}, u32[]{:S(2)}, u32[]{:S(2)}) collective-permute-start(f32[32,257]{0,1:T(8,128)S(1)} %get-tuple-element.87), channel_id=1, source_target_pairs={{0,508},{2,510},{4,0},{6,2},{8,4},{10,6},{12,8},{14,10},{16,12},{1... | collective-permute-start | bytes 98696 | tf_op jit(solution)/shard_map/ppermute | solution.py:13
  104.5 20.0 %collective-permute-start.10 = (f32[32,257]{0,1:T(8,128)S(1)}, f32[32,257]{0,1:T(8,128)S(1)}, u32[]{:S(2)}, u32[]{:S(2)}) collective-permute-start(f32[32,257]{0,1:T(8,128)S(1)} %get-tuple-element.73), channel_id=1, source_target_pairs={{0,6},{2,8},{4,10},{6,12},{8,14},{10,16},{12,18},{14,20},{16,22},{... | collective-permute-start | bytes 98696 | tf_op jit(solution)/shard_map/ppermute | solution.py:13
  106.4 19.0 %collective-permute-start.11 = (f32[32,257]{0,1:T(8,128)S(1)}, f32[32,257]{0,1:T(8,128)S(1)}, u32[]{:S(2)}, u32[]{:S(2)}) collective-permute-start(f32[32,257]{0,1:T(8,128)S(1)} %get-tuple-element.78), channel_id=1, source_target_pairs={{0,8},{2,10},{4,12},{6,14},{8,16},{10,18},{12,20},{14,22},{16,24},... | collective-permute-start | bytes 98696 | tf_op jit(solution)/shard_map/ppermute | solution.py:13
  108.3 17.1 %collective-permute-start.12 = (f32[32,257]{0,1:T(8,128)S(1)}, f32[32,257]{0,1:T(8,128)S(1)}, u32[]{:S(2)}, u32[]{:S(2)}) collective-permute-start(f32[32,257]{0,1:T(8,128)S(1)} %get-tuple-element.80), channel_id=1, source_target_pairs={{0,506},{2,508},{4,510},{6,0},{8,2},{10,4},{12,6},{14,8},{16,10},{... | collective-permute-start | bytes 98696 | tf_op jit(solution)/shard_map/ppermute | solution.py:13
  118.6 9.7 %collective-permute-start.13 = (f32[32,257]{0,1:T(8,128)S(1)}, f32[32,257]{0,1:T(8,128)S(1)}, u32[]{:S(2)}, u32[]{:S(2)}) collective-permute-start(f32[32,257]{0,1:T(8,128)S(1)} %get-tuple-element.79), channel_id=1, source_target_pairs={{0,504},{2,506},{4,508},{6,510},{8,0},{10,2},{12,4},{14,6},{16,8},... | collective-permute-start | bytes 98696 | tf_op jit(solution)/shard_map/ppermute | solution.py:13
  128.5 12.7 %collective-permute-start.14 = (f32[2,32,4,257]{3,1,2,0:T(8,128)S(1)}, f32[2,32,4,257]{3,1,2,0:T(8,128)S(1)}, u32[]{:S(2)}, u32[]{:S(2)}) collective-permute-start(f32[2,32,4,257]{3,1,2,0:T(8,128)S(1)} %pad_maximum_fusion.5), channel_id=1, source_target_pairs={{0,1},{1,0},{2,3},{3,2},{4,5},{5,4},{6,7},{7,6},{8,9},{9,8},{10,11... | collective-permute-start | bytes 789512 | tf_op jit(solution)/shard_map/ppermute | solution.py:18

commit v14 on v7

--- a/solution.py
+++ b/solution.py
@@ -102,7 +102,7 @@
         return jnp.dot(
             jnp.concatenate([own, later], axis=0),
             back_table,
-            precision=lax.Precision.HIGHEST,
+            precision=lax.Precision.HIGH,
             preferred_element_type=jnp.float32,
         )
 

time: 138 us -> 136 us (0.986)
  matrix products: 13 us -> 9.74 us
  waiting for transfers between devices: 43.9 us -> 45.5 us
    dot_general x4, matrix products: 7.78 us -> 4.55 us  [lags_of(): jnp.dot(jnp.concatenate([own, later], axis=0), back_table, precision=lax....]
    ppermute x14, waiting for transfers between devices: 36.1 us -> 37.7 us  [shifted(): lax.ppermute(x, axis, [(i, (i + by) % length) for i in range(length)])]
  transfers between devices with their start and end apart: 15 -> 15, of which waited for: 7 -> 7; matrix products, arithmetic and copies ran while one was open for 6% -> 5% of each run, Pallas kernels for 0% -> 0%
where the time goes in v14:
time: 136 us; the launch traced here: 134 us
  starting transfers between devices  64.9 us (48%)
  waiting for transfers between devices  45.5 us (33%)
  matrix products  9.74 us (7%)
  other arithmetic  9.1 us (7%)
  local copies, waits for them, and re-layouts  4.05 us (3%)
    ppermute x14, starting transfers between devices, shifted(): lax.ppermute(x, axis, [(i, (i + by) % length) for i in range(length)])  62.7 us
    ppermute x14, waiting for transfers between devices, shifted(): lax.ppermute(x, axis, [(i, (i + by) % length) for i in range(length)])  37.7 us
    ppermute x1, waiting for transfers between devices, swapped(): return lax.ppermute(x, axis, [(i, i ^ 1) for i in range(length)])  7.74 us
    dot_general x4, matrix products, lags_of(): jnp.dot(jnp.concatenate([own, later], axis=0), back_table, precision=lax....  4.55 us
    unnamed x8, local copies, waits for them, and re-layouts  3.71 us
    another operation x2, other arithmetic  2.96 us
  transfers between devices with their start and end apart: 15, of which 7 were waited for; matrix products, arithmetic and copies ran while one was open for 5% of the time, Pallas kernels for 0%

profile of v14, /device:TPU:1, one launch (start us, length us, event | category | flops | bytes accessed | tf_op | source)
XLA Modules:
  0.0 134.4 jit_solution(3437409594050487678)
XLA Ops:
  0.6 1.0 fusion.47
  2.3 1.8 %copy.8 = bf16[32,8,2048]{2,0,1:T(8,128)(2,1)S(1)} copy(bf16[32,8,2048]{2,1,0:T(8,128)(2,1)} %param.5) | data formatting | bytes 2097152 | tf_op args[0]
  4.1 3.0 %subtract_convert_fusion = (bf16[32,64,1024]{2,1,0:T(8,128)(2,1)S(1)}, bf16[32,64,1024]{2,1,0:T(8,128)(2,1)S(1)}) fusion(f32[64,1024]{1,0:T(8,128)S(1)} %get-tuple-element.101, f32[32,1024]{1,0:T(8,128)S(1)} %get-tuple-element.98, f32[64,1024]{1,0:T(8,128)S(1)} %get-tuple-element.102, f32[32,1024]{1,0:T(8,128)S(1)} %get-tuple-element.97), kind=kLoop, calls=%fused_computation.5 | loop fusion | flops 18874368 | bytes 9175040 | tf_op jit(solution)/shard_map/convert.7
  7.1 2.5 %fusion.4 = (f32[256]{0:T(256)S(1)}, f32[2048,256]{0,1:T(8,128)S(1)}) fusion(bf16[256,2048]{1,0:T(8,128)(2,1)S(1)} %bitcast.112, bf16[2048,1024]{1,0:T(8,128)(2,1)S(1)} %bitcast.110, bf16[2048,1024]{1,0:T(8,128)(2,1)S(1)} %bitcast.109), kind=kOutput, calls=%fused_computation.16 | convolution fusion | flops 2165309184 | bytes 11535360 | tf_op jit(solution)/shard_map/dot_general | solution.py:81
  10.6 8.8 %collective-permute-start.2 = (bf16[4,32,2048]{2,1,0:T(8,128)(2,1)S(1)}, bf16[4,32,2048]{2,1,0:T(8,128)(2,1)S(1)}, u32[]{:S(2)}, u32[]{:S(2)}) collective-permute-start(bf16[4,32,2048]{2,1,0:T(8,128)(2,1)S(1)} %scatter.4), channel_id=1, source_target_pairs={{0,510},{2,0},{4,2},{6,4},{8,6},{10,8},{12,10},{14,12},{16,14},{18... | collective-permute-start | bytes 1572872 | tf_op jit(solution)/shard_map/ppermute | solution.py:13
  19.4 10.7 %collective-permute-start.3 = (bf16[4,32,2048]{2,1,0:T(8,128)(2,1)S(1)}, bf16[4,32,2048]{2,1,0:T(8,128)(2,1)S(1)}, u32[]{:S(2)}, u32[]{:S(2)}) collective-permute-start(bf16[4,32,2048]{2,1,0:T(8,128)(2,1)S(1)} %scatter.4), channel_id=1, source_target_pairs={{0,508},{2,510},{4,0},{6,2},{8,4},{10,6},{12,8},{14,10},{16,12},{1... | collective-permute-start | bytes 1572872 | tf_op jit(solution)/shard_map/ppermute | solution.py:13
  30.0 3.3 %collective-permute-start = (bf16[4,32,2048]{2,1,0:T(8,128)(2,1)S(1)}, bf16[4,32,2048]{2,1,0:T(8,128)(2,1)S(1)}, u32[]{:S(2)}, u32[]{:S(2)}) collective-permute-start(bf16[4,32,2048]{2,1,0:T(8,128)(2,1)S(1)} %get-tuple-element.64), channel_id=1, source_target_pairs={{0,2},{2,4},{4,6},{6,8},{8,10},{10,12},{12,14},{14,16},{16,18},{18... | collective-permute-start | bytes 1572872 | tf_op jit(solution)/shard_map/ppermute | solution.py:13
  33.3 1.9 %collective-permute-start.1 = (bf16[4,32,2048]{2,1,0:T(8,128)(2,1)S(1)}, bf16[4,32,2048]{2,1,0:T(8,128)(2,1)S(1)}, u32[]{:S(2)}, u32[]{:S(2)}) collective-permute-start(bf16[4,32,2048]{2,1,0:T(8,128)(2,1)S(1)} %get-tuple-element.64), channel_id=1, source_target_pairs={{0,4},{2,6},{4,8},{6,10},{8,12},{10,14},{12,16},{14,18},{16,20},{1... | collective-permute-start | bytes 1572872 | tf_op jit(solution)/shard_map/ppermute | solution.py:13
  36.2 5.6 %collective-permute-done.3 = bf16[4,32,2048]{2,1,0:T(8,128)(2,1)S(1)} collective-permute-done((bf16[4,32,2048]{2,1,0:T(8,128)(2,1)S(1)}, bf16[4,32,2048]{2,1,0:T(8,128)(2,1)S(1)}, u32[]{:S(2)}, u32[]{:S(2)}) %collective-permute-start.3) | collective-permute-done | bytes 524320 | tf_op jit(solution)/shard_map/ppermute | solution.py:13
  41.8 0.6 collective-permute-done
  42.4 15.4 %collective-permute-done.1 = bf16[4,32,2048]{2,1,0:T(8,128)(2,1)S(1)} collective-permute-done((bf16[4,32,2048]{2,1,0:T(8,128)(2,1)S(1)}, bf16[4,32,2048]{2,1,0:T(8,128)(2,1)S(1)}, u32[]{:S(2)}, u32[]{:S(2)}) %collective-permute-start.1) | collective-permute-done | bytes 524320 | tf_op jit(solution)/shard_map/ppermute | solution.py:13
  59.4 1.9 %collective-permute-start.5 = (bf16[8,32,2048]{2,1,0:T(8,128)(2,1)S(1)}, bf16[8,32,2048]{2,1,0:T(8,128)(2,1)S(1)}, u32[]{:S(2)}, u32[]{:S(2)}) collective-permute-start(bf16[8,32,2048]{2,1,0:T(8,128)(2,1)S(1)} %pad_maximum_fusion.6), channel_id=1, source_target_pairs={{0,508},{2,510},{4,0},{6,2},{8,4},{10,6},{12,8},{14,10},{16,12},{1... | collective-permute-start | bytes 3145736 | tf_op jit(solution)/shard_map/ppermute | solution.py:13
  61.3 3.4 %collective-permute-start.4 = (bf16[8,32,2048]{2,1,0:T(8,128)(2,1)S(1)}, bf16[8,32,2048]{2,1,0:T(8,128)(2,1)S(1)}, u32[]{:S(2)}, u32[]{:S(2)}) collective-permute-start(bf16[8,32,2048]{2,1,0:T(8,128)(2,1)S(1)} %pad_maximum_fusion.5), channel_id=1, source_target_pairs={{0,4},{2,6},{4,8},{6,10},{8,12},{10,14},{12,16},{14,18},{16,20},{1... | collective-permute-start | bytes 3145736 | tf_op jit(solution)/shard_map/ppermute | solution.py:13
  65.4 1.1 fusion.7
  66.5 1.9 %collective-permute-start.8 = (f32[32,257]{1,0:T(8,128)S(1)}, f32[32,257]{1,0:T(8,128)S(1)}, u32[]{:S(2)}, u32[]{:S(2)}) collective-permute-start(f32[32,257]{1,0:T(8,128)S(1)} %get-tuple-element.85), channel_id=1, source_target_pairs={{0,4},{2,6},{4,8},{6,10},{8,12},{10,14},{12,16},{14,18},{16,20},{1... | collective-permute-start | bytes 98696 | tf_op jit(solution)/shard_map/ppermute | solution.py:13
  68.4 9.3 %collective-permute-start.9 = (f32[32,257]{1,0:T(8,128)S(1)}, f32[32,257]{1,0:T(8,128)S(1)}, u32[]{:S(2)}, u32[]{:S(2)}) collective-permute-start(f32[32,257]{1,0:T(8,128)S(1)} %get-tuple-element.86), channel_id=1, source_target_pairs={{0,508},{2,510},{4,0},{6,2},{8,4},{10,6},{12,8},{14,10},{16,12},{1... | collective-permute-start | bytes 98696 | tf_op jit(solution)/shard_map/ppermute | solution.py:13
  78.4 1.1 fusion.8
  79.6 1.9 %collective-permute-start.6 = (f32[32,257]{1,0:T(8,128)S(1)}, f32[32,257]{1,0:T(8,128)S(1)}, u32[]{:S(2)}, u32[]{:S(2)}) collective-permute-start(f32[32,257]{1,0:T(8,128)S(1)} %get-tuple-element.81), channel_id=1, source_target_pairs={{0,2},{2,4},{4,6},{6,8},{8,10},{10,12},{12,14},{14,16},{16,18},{18... | collective-permute-start | bytes 98696 | tf_op jit(solution)/shard_map/ppermute | solution.py:13
  81.5 11.5 %collective-permute-done.8 = f32[32,257]{1,0:T(8,128)S(1)} collective-permute-done((f32[32,257]{1,0:T(8,128)S(1)}, f32[32,257]{1,0:T(8,128)S(1)}, u32[]{:S(2)}, u32[]{:S(2)}) %collective-permute-start.8) | collective-permute-done | bytes 32928 | tf_op jit(solution)/shard_map/ppermute | solution.py:13
  93.0 1.9 %collective-permute-start.7 = (f32[32,257]{1,0:T(8,128)S(1)}, f32[32,257]{1,0:T(8,128)S(1)}, u32[]{:S(2)}, u32[]{:S(2)}) collective-permute-start(f32[32,257]{1,0:T(8,128)S(1)} %get-tuple-element.82), channel_id=1, source_target_pairs={{0,510},{2,0},{4,2},{6,4},{8,6},{10,8},{12,10},{14,12},{16,14},{18... | collective-permute-start | bytes 98696 | tf_op jit(solution)/shard_map/ppermute | solution.py:13
  94.9 3.5 %collective-permute-done.7 = f32[32,257]{1,0:T(8,128)S(1)} collective-permute-done((f32[32,257]{1,0:T(8,128)S(1)}, f32[32,257]{1,0:T(8,128)S(1)}, u32[]{:S(2)}, u32[]{:S(2)}) %collective-permute-start.7) | collective-permute-done | bytes 32928 | tf_op jit(solution)/shard_map/ppermute | solution.py:13
  100.4 1.1 fusion.6
  101.5 1.9 %collective-permute-start.10 = (f32[32,257]{1,0:T(8,128)S(1)}, f32[32,257]{1,0:T(8,128)S(1)}, u32[]{:S(2)}, u32[]{:S(2)}) collective-permute-start(f32[32,257]{1,0:T(8,128)S(1)} %get-tuple-element.71), channel_id=1, source_target_pairs={{0,6},{2,8},{4,10},{6,12},{8,14},{10,16},{12,18},{14,20},{16,22},{... | collective-permute-start | bytes 98696 | tf_op jit(solution)/shard_map/ppermute | solution.py:13
  104.1 1.1 fusion.5
  105.2 1.9 %collective-permute-start.11 = (f32[32,257]{1,0:T(8,128)S(1)}, f32[32,257]{1,0:T(8,128)S(1)}, u32[]{:S(2)}, u32[]{:S(2)}) collective-permute-start(f32[32,257]{1,0:T(8,128)S(1)} %get-tuple-element.75), channel_id=1, source_target_pairs={{0,8},{2,10},{4,12},{6,14},{8,16},{10,18},{12,20},{14,22},{16,24},... | collective-permute-start | bytes 98696 | tf_op jit(solution)/shard_map/ppermute | solution.py:13
  107.1 9.4 %collective-permute-start.12 = (f32[32,257]{1,0:T(8,128)S(1)}, f32[32,257]{1,0:T(8,128)S(1)}, u32[]{:S(2)}, u32[]{:S(2)}) collective-permute-start(f32[32,257]{1,0:T(8,128)S(1)} %get-tuple-element.74), channel_id=1, source_target_pairs={{0,506},{2,508},{4,510},{6,0},{8,2},{10,4},{12,6},{14,8},{16,10},{... | collective-permute-start | bytes 98696 | tf_op jit(solution)/shard_map/ppermute | solution.py:13
  116.5 4.5 %collective-permute-start.13 = (f32[32,257]{1,0:T(8,128)S(1)}, f32[32,257]{1,0:T(8,128)S(1)}, u32[]{:S(2)}, u32[]{:S(2)}) collective-permute-start(f32[32,257]{1,0:T(8,128)S(1)} %get-tuple-element.78), channel_id=1, source_target_pairs={{0,504},{2,506},{4,508},{6,510},{8,0},{10,2},{12,4},{14,6},{16,8},... | collective-permute-start | bytes 98696 | tf_op jit(solution)/shard_map/ppermute | solution.py:13
  121.2 1.1 collective-permute-done.13
  122.3 2.2 %collective-permute-start.14 = (f32[2,32,4,257]{3,1,2,0:T(8,128)S(1)}, f32[2,32,4,257]{3,1,2,0:T(8,128)S(1)}, u32[]{:S(2)}, u32[]{:S(2)}) collective-permute-start(f32[2,32,4,257]{3,1,2,0:T(8,128)S(1)} %pad_maximum_fusion.7), channel_id=1, source_target_pairs={{0,1},{1,0},{2,3},{3,2},{4,5},{5,4},{6,7},{7,6},{8,9},{9,8},{10,11... | collective-permute-start | bytes 789512 | tf_op jit(solution)/shard_map/ppermute | solution.py:18
  124.6 7.7 %collective-permute-done.14 = f32[2,32,4,257]{3,1,2,0:T(8,128)S(1)} collective-permute-done((f32[2,32,4,257]{3,1,2,0:T(8,128)S(1)}, f32[2,32,4,257]{3,1,2,0:T(8,128)S(1)}, u32[]{:S(2)}, u32[]{:S(2)}) %collective-permute-start.14) | collective-permute-done | bytes 263200 | tf_op jit(solution)/shard_map/ppermute | solution.py:18
  132.8 0.8 copy.11
  133.6 0.8 copy.10
  (60 shorter events, 8.5 us)
Async XLA Ops:
  7.0 2.6 %copy-start.1 = (s32[32]{0:T(128)S(1)}, s32[32]{0:T(128)}, u32[]{:S(2)}) copy-start(s32[32]{0:T(128)} %param.7) | copy-start | bytes 388
  9.6 0.7 copy-start
  10.6 25.6 %collective-permute-start.2 = (bf16[4,32,2048]{2,1,0:T(8,128)(2,1)S(1)}, bf16[4,32,2048]{2,1,0:T(8,128)(2,1)S(1)}, u32[]{:S(2)}, u32[]{:S(2)}) collective-permute-start(bf16[4,32,2048]{2,1,0:T(8,128)(2,1)S(1)} %scatter.4), channel_id=1, source_target_pairs={{0,510},{2,0},{4,2},{6,4},{8,6},{10,8},{12,10},{14,12},{16,14},{18... | collective-permute-start | bytes 1572872 | tf_op jit(solution)/shard_map/ppermute | solution.py:13
  19.4 22.5 %collective-permute-start.3 = (bf16[4,32,2048]{2,1,0:T(8,128)(2,1)S(1)}, bf16[4,32,2048]{2,1,0:T(8,128)(2,1)S(1)}, u32[]{:S(2)}, u32[]{:S(2)}) collective-permute-start(bf16[4,32,2048]{2,1,0:T(8,128)(2,1)S(1)} %scatter.4), channel_id=1, source_target_pairs={{0,508},{2,510},{4,0},{6,2},{8,4},{10,6},{12,8},{14,10},{16,12},{1... | collective-permute-start | bytes 1572872 | tf_op jit(solution)/shard_map/ppermute | solution.py:13
  30.0 12.4 %collective-permute-start = (bf16[4,32,2048]{2,1,0:T(8,128)(2,1)S(1)}, bf16[4,32,2048]{2,1,0:T(8,128)(2,1)S(1)}, u32[]{:S(2)}, u32[]{:S(2)}) collective-permute-start(bf16[4,32,2048]{2,1,0:T(8,128)(2,1)S(1)} %get-tuple-element.64), channel_id=1, source_target_pairs={{0,2},{2,4},{4,6},{6,8},{8,10},{10,12},{12,14},{14,16},{16,18},{18... | collective-permute-start | bytes 1572872 | tf_op jit(solution)/shard_map/ppermute | solution.py:13
  33.3 24.6 %collective-permute-start.1 = (bf16[4,32,2048]{2,1,0:T(8,128)(2,1)S(1)}, bf16[4,32,2048]{2,1,0:T(8,128)(2,1)S(1)}, u32[]{:S(2)}, u32[]{:S(2)}) collective-permute-start(bf16[4,32,2048]{2,1,0:T(8,128)(2,1)S(1)} %get-tuple-element.64), channel_id=1, source_target_pairs={{0,4},{2,6},{4,8},{6,10},{8,12},{10,14},{12,16},{14,18},{16,20},{1... | collective-permute-start | bytes 1572872 | tf_op jit(solution)/shard_map/ppermute | solution.py:13
  59.4 39.0 %collective-permute-start.5 = (bf16[8,32,2048]{2,1,0:T(8,128)(2,1)S(1)}, bf16[8,32,2048]{2,1,0:T(8,128)(2,1)S(1)}, u32[]{:S(2)}, u32[]{:S(2)}) collective-permute-start(bf16[8,32,2048]{2,1,0:T(8,128)(2,1)S(1)} %pad_maximum_fusion.6), channel_id=1, source_target_pairs={{0,508},{2,510},{4,0},{6,2},{8,4},{10,6},{12,8},{14,10},{16,12},{1... | collective-permute-start | bytes 3145736 | tf_op jit(solution)/shard_map/ppermute | solution.py:13
  61.3 37.1 %collective-permute-start.4 = (bf16[8,32,2048]{2,1,0:T(8,128)(2,1)S(1)}, bf16[8,32,2048]{2,1,0:T(8,128)(2,1)S(1)}, u32[]{:S(2)}, u32[]{:S(2)}) collective-permute-start(bf16[8,32,2048]{2,1,0:T(8,128)(2,1)S(1)} %pad_maximum_fusion.5), channel_id=1, source_target_pairs={{0,4},{2,6},{4,8},{6,10},{8,12},{10,14},{12,16},{14,18},{16,20},{1... | collective-permute-start | bytes 3145736 | tf_op jit(solution)/shard_map/ppermute | solution.py:13
  66.5 26.5 %collective-permute-start.8 = (f32[32,257]{1,0:T(8,128)S(1)}, f32[32,257]{1,0:T(8,128)S(1)}, u32[]{:S(2)}, u32[]{:S(2)}) collective-permute-start(f32[32,257]{1,0:T(8,128)S(1)} %get-tuple-element.85), channel_id=1, source_target_pairs={{0,4},{2,6},{4,8},{6,10},{8,12},{10,14},{12,16},{14,18},{16,20},{1... | collective-permute-start | bytes 98696 | tf_op jit(solution)/shard_map/ppermute | solution.py:13
  68.4 26.5 %collective-permute-start.9 = (f32[32,257]{1,0:T(8,128)S(1)}, f32[32,257]{1,0:T(8,128)S(1)}, u32[]{:S(2)}, u32[]{:S(2)}) collective-permute-start(f32[32,257]{1,0:T(8,128)S(1)} %get-tuple-element.86), channel_id=1, source_target_pairs={{0,508},{2,510},{4,0},{6,2},{8,4},{10,6},{12,8},{14,10},{16,12},{1... | collective-permute-start | bytes 98696 | tf_op jit(solution)/shard_map/ppermute | solution.py:13
  79.6 15.3 %collective-permute-start.6 = (f32[32,257]{1,0:T(8,128)S(1)}, f32[32,257]{1,0:T(8,128)S(1)}, u32[]{:S(2)}, u32[]{:S(2)}) collective-permute-start(f32[32,257]{1,0:T(8,128)S(1)} %get-tuple-element.81), channel_id=1, source_target_pairs={{0,2},{2,4},{4,6},{6,8},{8,10},{10,12},{12,14},{14,16},{16,18},{18... | collective-permute-start | bytes 98696 | tf_op jit(solution)/shard_map/ppermute | solution.py:13
  93.0 5.4 %collective-permute-start.7 = (f32[32,257]{1,0:T(8,128)S(1)}, f32[32,257]{1,0:T(8,128)S(1)}, u32[]{:S(2)}, u32[]{:S(2)}) collective-permute-start(f32[32,257]{1,0:T(8,128)S(1)} %get-tuple-element.82), channel_id=1, source_target_pairs={{0,510},{2,0},{4,2},{6,4},{8,6},{10,8},{12,10},{14,12},{16,14},{18... | collective-permute-start | bytes 98696 | tf_op jit(solution)/shard_map/ppermute | solution.py:13
  101.5 19.5 %collective-permute-start.10 = (f32[32,257]{1,0:T(8,128)S(1)}, f32[32,257]{1,0:T(8,128)S(1)}, u32[]{:S(2)}, u32[]{:S(2)}) collective-permute-start(f32[32,257]{1,0:T(8,128)S(1)} %get-tuple-element.71), channel_id=1, source_target_pairs={{0,6},{2,8},{4,10},{6,12},{8,14},{10,16},{12,18},{14,20},{16,22},{... | collective-permute-start | bytes 98696 | tf_op jit(solution)/shard_map/ppermute | solution.py:13
  105.2 15.9 %collective-permute-start.11 = (f32[32,257]{1,0:T(8,128)S(1)}, f32[32,257]{1,0:T(8,128)S(1)}, u32[]{:S(2)}, u32[]{:S(2)}) collective-permute-start(f32[32,257]{1,0:T(8,128)S(1)} %get-tuple-element.75), channel_id=1, source_target_pairs={{0,8},{2,10},{4,12},{6,14},{8,16},{10,18},{12,20},{14,22},{16,24},... | collective-permute-start | bytes 98696 | tf_op jit(solution)/shard_map/ppermute | solution.py:13
  107.1 14.0 %collective-permute-start.12 = (f32[32,257]{1,0:T(8,128)S(1)}, f32[32,257]{1,0:T(8,128)S(1)}, u32[]{:S(2)}, u32[]{:S(2)}) collective-permute-start(f32[32,257]{1,0:T(8,128)S(1)} %get-tuple-element.74), channel_id=1, source_target_pairs={{0,506},{2,508},{4,510},{6,0},{8,2},{10,4},{12,6},{14,8},{16,10},{... | collective-permute-start | bytes 98696 | tf_op jit(solution)/shard_map/ppermute | solution.py:13
  116.5 5.7 %collective-permute-start.13 = (f32[32,257]{1,0:T(8,128)S(1)}, f32[32,257]{1,0:T(8,128)S(1)}, u32[]{:S(2)}, u32[]{:S(2)}) collective-permute-start(f32[32,257]{1,0:T(8,128)S(1)} %get-tuple-element.78), channel_id=1, source_target_pairs={{0,504},{2,506},{4,508},{6,510},{8,0},{10,2},{12,4},{14,6},{16,8},... | collective-permute-start | bytes 98696 | tf_op jit(solution)/shard_map/ppermute | solution.py:13
  122.3 10.0 %collective-permute-start.14 = (f32[2,32,4,257]{3,1,2,0:T(8,128)S(1)}, f32[2,32,4,257]{3,1,2,0:T(8,128)S(1)}, u32[]{:S(2)}, u32[]{:S(2)}) collective-permute-start(f32[2,32,4,257]{3,1,2,0:T(8,128)S(1)} %pad_maximum_fusion.7), channel_id=1, source_target_pairs={{0,1},{1,0},{2,3},{3,2},{4,5},{5,4},{6,7},{7,6},{8,9},{9,8},{10,11... | collective-permute-start | bytes 789512 | tf_op jit(solution)/shard_map/ppermute | solution.py:18

commit v15 on v13

--- a/solution.py
+++ b/solution.py
@@ -116,7 +116,7 @@
         tuple(shifted(moving_ahead, "blk", d) for d in range(1, near + 1))
         + tuple(shifted(moving_behind, "blk", -d) for d in range(1, near + 1))
     )
-    lags = lags_of_stops([lags_of(d, first[d - 1], first[near + d - 1]) for d in range(1, near + 1)])
+    lags = [lags_of_stops([lags_of(d, first[d - 1], first[near + d - 1])])[0] for d in range(1, near + 1)]
     early = [
         (shifted(piece[channels:], "blk", d), shifted(piece[:channels], "blk", -d)) for d, piece in enumerate(lags, 1)
     ]

time: 144 us -> 135 us (0.938)
  the two profiles are of different devices: /device:TPU:8 before, /device:TPU:1 now
where the time goes in v15:
time: 135 us; the launch traced here: 133 us
  starting transfers between devices  64.9 us (48%)
  waiting for transfers between devices  45.5 us (34%)
  other arithmetic  9.1 us (7%)
  matrix products  8.75 us (6%)
  local copies, waits for them, and re-layouts  4.05 us (3%)
    ppermute x14, starting transfers between devices, shifted(): lax.ppermute(x, axis, [(i, (i + by) % length) for i in range(length)])  62.7 us
    ppermute x14, waiting for transfers between devices, shifted(): lax.ppermute(x, axis, [(i, (i + by) % length) for i in range(length)])  37.7 us
    ppermute x1, waiting for transfers between devices, swapped(): return lax.ppermute(x, axis, [(i, i ^ 1) for i in range(length)])  7.75 us
    unnamed x8, local copies, waits for them, and re-layouts  3.71 us
    dot_general x3, matrix products, lags_of_stops(): jnp.dot(jnp.concatenate(crosses, axis=0), back_table, precision=lax.Preci...  3.56 us
    another operation x2, other arithmetic  2.96 us
    dot_general x8, matrix products, pick_rows(): jnp.einsum('gp,spk->sgk', picks, block, preferred_element_type=jnp.float32)  2.71 us
  transfers between devices with their start and end apart: 15, of which 7 were waited for; matrix products, arithmetic and copies ran while one was open for 3% of the time, Pallas kernels for 0%

profile of v15, /device:TPU:1, one launch (start us, length us, event | category | flops | bytes accessed | tf_op | source)
XLA Modules:
  0.0 133.4 jit_solution(18071121185112908033)
XLA Ops:
  0.6 1.0 fusion.47
  1.7 0.6 fusion.53
  2.3 1.8 %copy.12 = bf16[32,8,2048]{2,0,1:T(8,128)(2,1)S(1)} copy(bf16[32,8,2048]{2,1,0:T(8,128)(2,1)} %param.5) | data formatting | bytes 2097152 | tf_op args[0]
  4.1 3.0 %subtract_convert_fusion = (bf16[32,64,1024]{2,1,0:T(8,128)(2,1)S(1)}, bf16[32,64,1024]{2,1,0:T(8,128)(2,1)S(1)}) fusion(f32[64,1024]{1,0:T(8,128)S(1)} %get-tuple-element.101, f32[32,1024]{1,0:T(8,128)S(1)} %get-tuple-element.98, f32[64,1024]{1,0:T(8,128)S(1)} %get-tuple-element.102, f32[32,1024]{1,0:T(8,128)S(1)} %get-tuple-element.97), kind=kLoop, calls=%fused_computation.5 | loop fusion | flops 18874368 | bytes 9175040 | tf_op jit(solution)/shard_map/convert.7
  7.1 2.5 %fusion.4 = (f32[256]{0:T(256)S(1)}, f32[2048,256]{0,1:T(8,128)S(1)}) fusion(bf16[256,2048]{1,0:T(8,128)(2,1)S(1)} %bitcast.110, bf16[2048,1024]{1,0:T(8,128)(2,1)S(1)} %bitcast.108, bf16[2048,1024]{1,0:T(8,128)(2,1)S(1)} %bitcast.107), kind=kOutput, calls=%fused_computation.16 | convolution fusion | flops 2165309184 | bytes 11535360 | tf_op jit(solution)/shard_map/dot_general | solution.py:81
  10.6 8.8 %collective-permute-start.2 = (bf16[4,32,2048]{2,1,0:T(8,128)(2,1)S(1)}, bf16[4,32,2048]{2,1,0:T(8,128)(2,1)S(1)}, u32[]{:S(2)}, u32[]{:S(2)}) collective-permute-start(bf16[4,32,2048]{2,1,0:T(8,128)(2,1)S(1)} %scatter.4), channel_id=1, source_target_pairs={{0,510},{2,0},{4,2},{6,4},{8,6},{10,8},{12,10},{14,12},{16,14},{18... | collective-permute-start | bytes 1572872 | tf_op jit(solution)/shard_map/ppermute | solution.py:13
  19.4 10.7 %collective-permute-start.3 = (bf16[4,32,2048]{2,1,0:T(8,128)(2,1)S(1)}, bf16[4,32,2048]{2,1,0:T(8,128)(2,1)S(1)}, u32[]{:S(2)}, u32[]{:S(2)}) collective-permute-start(bf16[4,32,2048]{2,1,0:T(8,128)(2,1)S(1)} %scatter.4), channel_id=1, source_target_pairs={{0,508},{2,510},{4,0},{6,2},{8,4},{10,6},{12,8},{14,10},{16,12},{1... | collective-permute-start | bytes 1572872 | tf_op jit(solution)/shard_map/ppermute | solution.py:13
  30.0 3.3 %collective-permute-start = (bf16[4,32,2048]{2,1,0:T(8,128)(2,1)S(1)}, bf16[4,32,2048]{2,1,0:T(8,128)(2,1)S(1)}, u32[]{:S(2)}, u32[]{:S(2)}) collective-permute-start(bf16[4,32,2048]{2,1,0:T(8,128)(2,1)S(1)} %get-tuple-element.64), channel_id=1, source_target_pairs={{0,2},{2,4},{4,6},{6,8},{8,10},{10,12},{12,14},{14,16},{16,18},{18... | collective-permute-start | bytes 1572872 | tf_op jit(solution)/shard_map/ppermute | solution.py:13
  33.3 1.9 %collective-permute-start.1 = (bf16[4,32,2048]{2,1,0:T(8,128)(2,1)S(1)}, bf16[4,32,2048]{2,1,0:T(8,128)(2,1)S(1)}, u32[]{:S(2)}, u32[]{:S(2)}) collective-permute-start(bf16[4,32,2048]{2,1,0:T(8,128)(2,1)S(1)} %get-tuple-element.64), channel_id=1, source_target_pairs={{0,4},{2,6},{4,8},{6,10},{8,12},{10,14},{12,16},{14,18},{16,20},{1... | collective-permute-start | bytes 1572872 | tf_op jit(solution)/shard_map/ppermute | solution.py:13
  36.2 5.6 %collective-permute-done.3 = bf16[4,32,2048]{2,1,0:T(8,128)(2,1)S(1)} collective-permute-done((bf16[4,32,2048]{2,1,0:T(8,128)(2,1)S(1)}, bf16[4,32,2048]{2,1,0:T(8,128)(2,1)S(1)}, u32[]{:S(2)}, u32[]{:S(2)}) %collective-permute-start.3) | collective-permute-done | bytes 524320 | tf_op jit(solution)/shard_map/ppermute | solution.py:13
  41.8 0.6 collective-permute-done
  42.4 15.4 %collective-permute-done.1 = bf16[4,32,2048]{2,1,0:T(8,128)(2,1)S(1)} collective-permute-done((bf16[4,32,2048]{2,1,0:T(8,128)(2,1)S(1)}, bf16[4,32,2048]{2,1,0:T(8,128)(2,1)S(1)}, u32[]{:S(2)}, u32[]{:S(2)}) %collective-permute-start.1) | collective-permute-done | bytes 524320 | tf_op jit(solution)/shard_map/ppermute | solution.py:13
  59.4 1.9 %collective-permute-start.5 = (bf16[8,32,2048]{2,1,0:T(8,128)(2,1)S(1)}, bf16[8,32,2048]{2,1,0:T(8,128)(2,1)S(1)}, u32[]{:S(2)}, u32[]{:S(2)}) collective-permute-start(bf16[8,32,2048]{2,1,0:T(8,128)(2,1)S(1)} %pad_maximum_fusion.5), channel_id=1, source_target_pairs={{0,508},{2,510},{4,0},{6,2},{8,4},{10,6},{12,8},{14,10},{16,12},{1... | collective-permute-start | bytes 3145736 | tf_op jit(solution)/shard_map/ppermute | solution.py:13
  61.3 3.4 %collective-permute-start.4 = (bf16[8,32,2048]{2,1,0:T(8,128)(2,1)S(1)}, bf16[8,32,2048]{2,1,0:T(8,128)(2,1)S(1)}, u32[]{:S(2)}, u32[]{:S(2)}) collective-permute-start(bf16[8,32,2048]{2,1,0:T(8,128)(2,1)S(1)} %pad_maximum_fusion.4), channel_id=1, source_target_pairs={{0,4},{2,6},{4,8},{6,10},{8,12},{10,14},{12,16},{14,18},{16,20},{1... | collective-permute-start | bytes 3145736 | tf_op jit(solution)/shard_map/ppermute | solution.py:13
  65.4 1.1 fusion.6
  66.5 1.9 %collective-permute-start.8 = (f32[32,257]{1,0:T(8,128)S(1)}, f32[32,257]{1,0:T(8,128)S(1)}, u32[]{:S(2)}, u32[]{:S(2)}) collective-permute-start(f32[32,257]{1,0:T(8,128)S(1)} %get-tuple-element.85), channel_id=1, source_target_pairs={{0,4},{2,6},{4,8},{6,10},{8,12},{10,14},{12,16},{14,18},{16,20},{1... | collective-permute-start | bytes 98696 | tf_op jit(solution)/shard_map/ppermute | solution.py:13
  68.5 9.3 %collective-permute-start.9 = (f32[32,257]{1,0:T(8,128)S(1)}, f32[32,257]{1,0:T(8,128)S(1)}, u32[]{:S(2)}, u32[]{:S(2)}) collective-permute-start(f32[32,257]{1,0:T(8,128)S(1)} %get-tuple-element.86), channel_id=1, source_target_pairs={{0,508},{2,510},{4,0},{6,2},{8,4},{10,6},{12,8},{14,10},{16,12},{1... | collective-permute-start | bytes 98696 | tf_op jit(solution)/shard_map/ppermute | solution.py:13
  78.4 1.1 fusion.7
  79.6 1.9 %collective-permute-start.6 = (f32[32,257]{1,0:T(8,128)S(1)}, f32[32,257]{1,0:T(8,128)S(1)}, u32[]{:S(2)}, u32[]{:S(2)}) collective-permute-start(f32[32,257]{1,0:T(8,128)S(1)} %get-tuple-element.81), channel_id=1, source_target_pairs={{0,2},{2,4},{4,6},{6,8},{8,10},{10,12},{12,14},{14,16},{16,18},{18... | collective-permute-start | bytes 98696 | tf_op jit(solution)/shard_map/ppermute | solution.py:13
  81.5 11.4 %collective-permute-done.8 = f32[32,257]{1,0:T(8,128)S(1)} collective-permute-done((f32[32,257]{1,0:T(8,128)S(1)}, f32[32,257]{1,0:T(8,128)S(1)}, u32[]{:S(2)}, u32[]{:S(2)}) %collective-permute-start.8) | collective-permute-done | bytes 32928 | tf_op jit(solution)/shard_map/ppermute | solution.py:13
  93.0 1.9 %collective-permute-start.7 = (f32[32,257]{1,0:T(8,128)S(1)}, f32[32,257]{1,0:T(8,128)S(1)}, u32[]{:S(2)}, u32[]{:S(2)}) collective-permute-start(f32[32,257]{1,0:T(8,128)S(1)} %get-tuple-element.82), channel_id=1, source_target_pairs={{0,510},{2,0},{4,2},{6,4},{8,6},{10,8},{12,10},{14,12},{16,14},{18... | collective-permute-start | bytes 98696 | tf_op jit(solution)/shard_map/ppermute | solution.py:13
  94.9 3.5 %collective-permute-done.7 = f32[32,257]{1,0:T(8,128)S(1)} collective-permute-done((f32[32,257]{1,0:T(8,128)S(1)}, f32[32,257]{1,0:T(8,128)S(1)}, u32[]{:S(2)}, u32[]{:S(2)}) %collective-permute-start.7) | collective-permute-done | bytes 32928 | tf_op jit(solution)/shard_map/ppermute | solution.py:13
  101.0 1.3 fusion.5
  102.3 1.9 %collective-permute-start.10 = (f32[32,257]{1,0:T(8,128)S(1)}, f32[32,257]{1,0:T(8,128)S(1)}, u32[]{:S(2)}, u32[]{:S(2)}) collective-permute-start(f32[32,257]{1,0:T(8,128)S(1)} %get-tuple-element.69), channel_id=1, source_target_pairs={{0,6},{2,8},{4,10},{6,12},{8,14},{10,16},{12,18},{14,20},{16,22},{... | collective-permute-start | bytes 98696 | tf_op jit(solution)/shard_map/ppermute | solution.py:13
  104.2 1.9 %collective-permute-start.11 = (f32[32,257]{1,0:T(8,128)S(1)}, f32[32,257]{1,0:T(8,128)S(1)}, u32[]{:S(2)}, u32[]{:S(2)}) collective-permute-start(f32[32,257]{1,0:T(8,128)S(1)} %get-tuple-element.76), channel_id=1, source_target_pairs={{0,8},{2,10},{4,12},{6,14},{8,16},{10,18},{12,20},{14,22},{16,24},... | collective-permute-start | bytes 98696 | tf_op jit(solution)/shard_map/ppermute | solution.py:13
  106.1 9.4 %collective-permute-start.12 = (f32[32,257]{1,0:T(8,128)S(1)}, f32[32,257]{1,0:T(8,128)S(1)}, u32[]{:S(2)}, u32[]{:S(2)}) collective-permute-start(f32[32,257]{1,0:T(8,128)S(1)} %get-tuple-element.75), channel_id=1, source_target_pairs={{0,506},{2,508},{4,510},{6,0},{8,2},{10,4},{12,6},{14,8},{16,10},{... | collective-permute-start | bytes 98696 | tf_op jit(solution)/shard_map/ppermute | solution.py:13
  115.5 4.5 %collective-permute-start.13 = (f32[32,257]{1,0:T(8,128)S(1)}, f32[32,257]{1,0:T(8,128)S(1)}, u32[]{:S(2)}, u32[]{:S(2)}) collective-permute-start(f32[32,257]{1,0:T(8,128)S(1)} %get-tuple-element.74), channel_id=1, source_target_pairs={{0,504},{2,506},{4,508},{6,510},{8,0},{10,2},{12,4},{14,6},{16,8},... | collective-permute-start | bytes 98696 | tf_op jit(solution)/shard_map/ppermute | solution.py:13
  120.1 1.1 collective-permute-done.13
  121.3 2.2 %collective-permute-start.14 = (f32[2,32,4,257]{3,1,2,0:T(8,128)S(1)}, f32[2,32,4,257]{3,1,2,0:T(8,128)S(1)}, u32[]{:S(2)}, u32[]{:S(2)}) collective-permute-start(f32[2,32,4,257]{3,1,2,0:T(8,128)S(1)} %pad_maximum_fusion.6), channel_id=1, source_target_pairs={{0,1},{1,0},{2,3},{3,2},{4,5},{5,4},{6,7},{7,6},{8,9},{9,8},{10,11... | collective-permute-start | bytes 789512 | tf_op jit(solution)/shard_map/ppermute | solution.py:18
  123.5 7.7 %collective-permute-done.14 = f32[2,32,4,257]{3,1,2,0:T(8,128)S(1)} collective-permute-done((f32[2,32,4,257]{3,1,2,0:T(8,128)S(1)}, f32[2,32,4,257]{3,1,2,0:T(8,128)S(1)}, u32[]{:S(2)}, u32[]{:S(2)}) %collective-permute-start.14) | collective-permute-done | bytes 263200 | tf_op jit(solution)/shard_map/ppermute | solution.py:18
  131.8 0.8 copy.19
  132.6 0.8 copy.18
  (58 shorter events, 7.9 us)
Async XLA Ops:
  7.0 2.6 %copy-start.1 = (s32[32]{0:T(128)S(1)}, s32[32]{0:T(128)}, u32[]{:S(2)}) copy-start(s32[32]{0:T(128)} %param.7) | copy-start | bytes 388
  9.6 0.7 copy-start
  10.6 25.6 %collective-permute-start.2 = (bf16[4,32,2048]{2,1,0:T(8,128)(2,1)S(1)}, bf16[4,32,2048]{2,1,0:T(8,128)(2,1)S(1)}, u32[]{:S(2)}, u32[]{:S(2)}) collective-permute-start(bf16[4,32,2048]{2,1,0:T(8,128)(2,1)S(1)} %scatter.4), channel_id=1, source_target_pairs={{0,510},{2,0},{4,2},{6,4},{8,6},{10,8},{12,10},{14,12},{16,14},{18... | collective-permute-start | bytes 1572872 | tf_op jit(solution)/shard_map/ppermute | solution.py:13
  19.4 22.5 %collective-permute-start.3 = (bf16[4,32,2048]{2,1,0:T(8,128)(2,1)S(1)}, bf16[4,32,2048]{2,1,0:T(8,128)(2,1)S(1)}, u32[]{:S(2)}, u32[]{:S(2)}) collective-permute-start(bf16[4,32,2048]{2,1,0:T(8,128)(2,1)S(1)} %scatter.4), channel_id=1, source_target_pairs={{0,508},{2,510},{4,0},{6,2},{8,4},{10,6},{12,8},{14,10},{16,12},{1... | collective-permute-start | bytes 1572872 | tf_op jit(solution)/shard_map/ppermute | solution.py:13
  30.0 12.4 %collective-permute-start = (bf16[4,32,2048]{2,1,0:T(8,128)(2,1)S(1)}, bf16[4,32,2048]{2,1,0:T(8,128)(2,1)S(1)}, u32[]{:S(2)}, u32[]{:S(2)}) collective-permute-start(bf16[4,32,2048]{2,1,0:T(8,128)(2,1)S(1)} %get-tuple-element.64), channel_id=1, source_target_pairs={{0,2},{2,4},{4,6},{6,8},{8,10},{10,12},{12,14},{14,16},{16,18},{18... | collective-permute-start | bytes 1572872 | tf_op jit(solution)/shard_map/ppermute | solution.py:13
  33.3 24.6 %collective-permute-start.1 = (bf16[4,32,2048]{2,1,0:T(8,128)(2,1)S(1)}, bf16[4,32,2048]{2,1,0:T(8,128)(2,1)S(1)}, u32[]{:S(2)}, u32[]{:S(2)}) collective-permute-start(bf16[4,32,2048]{2,1,0:T(8,128)(2,1)S(1)} %get-tuple-element.64), channel_id=1, source_target_pairs={{0,4},{2,6},{4,8},{6,10},{8,12},{10,14},{12,16},{14,18},{16,20},{1... | collective-permute-start | bytes 1572872 | tf_op jit(solution)/shard_map/ppermute | solution.py:13
  59.4 39.0 %collective-permute-start.5 = (bf16[8,32,2048]{2,1,0:T(8,128)(2,1)S(1)}, bf16[8,32,2048]{2,1,0:T(8,128)(2,1)S(1)}, u32[]{:S(2)}, u32[]{:S(2)}) collective-permute-start(bf16[8,32,2048]{2,1,0:T(8,128)(2,1)S(1)} %pad_maximum_fusion.5), channel_id=1, source_target_pairs={{0,508},{2,510},{4,0},{6,2},{8,4},{10,6},{12,8},{14,10},{16,12},{1... | collective-permute-start | bytes 3145736 | tf_op jit(solution)/shard_map/ppermute | solution.py:13
  61.3 37.1 %collective-permute-start.4 = (bf16[8,32,2048]{2,1,0:T(8,128)(2,1)S(1)}, bf16[8,32,2048]{2,1,0:T(8,128)(2,1)S(1)}, u32[]{:S(2)}, u32[]{:S(2)}) collective-permute-start(bf16[8,32,2048]{2,1,0:T(8,128)(2,1)S(1)} %pad_maximum_fusion.4), channel_id=1, source_target_pairs={{0,4},{2,6},{4,8},{6,10},{8,12},{10,14},{12,16},{14,18},{16,20},{1... | collective-permute-start | bytes 3145736 | tf_op jit(solution)/shard_map/ppermute | solution.py:13
  66.5 26.5 %collective-permute-start.8 = (f32[32,257]{1,0:T(8,128)S(1)}, f32[32,257]{1,0:T(8,128)S(1)}, u32[]{:S(2)}, u32[]{:S(2)}) collective-permute-start(f32[32,257]{1,0:T(8,128)S(1)} %get-tuple-element.85), channel_id=1, source_target_pairs={{0,4},{2,6},{4,8},{6,10},{8,12},{10,14},{12,16},{14,18},{16,20},{1... | collective-permute-start | bytes 98696 | tf_op jit(solution)/shard_map/ppermute | solution.py:13
  68.5 26.4 %collective-permute-start.9 = (f32[32,257]{1,0:T(8,128)S(1)}, f32[32,257]{1,0:T(8,128)S(1)}, u32[]{:S(2)}, u32[]{:S(2)}) collective-permute-start(f32[32,257]{1,0:T(8,128)S(1)} %get-tuple-element.86), channel_id=1, source_target_pairs={{0,508},{2,510},{4,0},{6,2},{8,4},{10,6},{12,8},{14,10},{16,12},{1... | collective-permute-start | bytes 98696 | tf_op jit(solution)/shard_map/ppermute | solution.py:13
  79.6 15.3 %collective-permute-start.6 = (f32[32,257]{1,0:T(8,128)S(1)}, f32[32,257]{1,0:T(8,128)S(1)}, u32[]{:S(2)}, u32[]{:S(2)}) collective-permute-start(f32[32,257]{1,0:T(8,128)S(1)} %get-tuple-element.81), channel_id=1, source_target_pairs={{0,2},{2,4},{4,6},{6,8},{8,10},{10,12},{12,14},{14,16},{16,18},{18... | collective-permute-start | bytes 98696 | tf_op jit(solution)/shard_map/ppermute | solution.py:13
  93.0 5.4 %collective-permute-start.7 = (f32[32,257]{1,0:T(8,128)S(1)}, f32[32,257]{1,0:T(8,128)S(1)}, u32[]{:S(2)}, u32[]{:S(2)}) collective-permute-start(f32[32,257]{1,0:T(8,128)S(1)} %get-tuple-element.82), channel_id=1, source_target_pairs={{0,510},{2,0},{4,2},{6,4},{8,6},{10,8},{12,10},{14,12},{16,14},{18... | collective-permute-start | bytes 98696 | tf_op jit(solution)/shard_map/ppermute | solution.py:13
  102.3 17.8 %collective-permute-start.10 = (f32[32,257]{1,0:T(8,128)S(1)}, f32[32,257]{1,0:T(8,128)S(1)}, u32[]{:S(2)}, u32[]{:S(2)}) collective-permute-start(f32[32,257]{1,0:T(8,128)S(1)} %get-tuple-element.69), channel_id=1, source_target_pairs={{0,6},{2,8},{4,10},{6,12},{8,14},{10,16},{12,18},{14,20},{16,22},{... | collective-permute-start | bytes 98696 | tf_op jit(solution)/shard_map/ppermute | solution.py:13
  104.2 15.9 %collective-permute-start.11 = (f32[32,257]{1,0:T(8,128)S(1)}, f32[32,257]{1,0:T(8,128)S(1)}, u32[]{:S(2)}, u32[]{:S(2)}) collective-permute-start(f32[32,257]{1,0:T(8,128)S(1)} %get-tuple-element.76), channel_id=1, source_target_pairs={{0,8},{2,10},{4,12},{6,14},{8,16},{10,18},{12,20},{14,22},{16,24},... | collective-permute-start | bytes 98696 | tf_op jit(solution)/shard_map/ppermute | solution.py:13
  106.1 14.0 %collective-permute-start.12 = (f32[32,257]{1,0:T(8,128)S(1)}, f32[32,257]{1,0:T(8,128)S(1)}, u32[]{:S(2)}, u32[]{:S(2)}) collective-permute-start(f32[32,257]{1,0:T(8,128)S(1)} %get-tuple-element.75), channel_id=1, source_target_pairs={{0,506},{2,508},{4,510},{6,0},{8,2},{10,4},{12,6},{14,8},{16,10},{... | collective-permute-start | bytes 98696 | tf_op jit(solution)/shard_map/ppermute | solution.py:13
  115.5 5.7 %collective-permute-start.13 = (f32[32,257]{1,0:T(8,128)S(1)}, f32[32,257]{1,0:T(8,128)S(1)}, u32[]{:S(2)}, u32[]{:S(2)}) collective-permute-start(f32[32,257]{1,0:T(8,128)S(1)} %get-tuple-element.74), channel_id=1, source_target_pairs={{0,504},{2,506},{4,508},{6,510},{8,0},{10,2},{12,4},{14,6},{16,8},... | collective-permute-start | bytes 98696 | tf_op jit(solution)/shard_map/ppermute | solution.py:13
  121.3 10.0 %collective-permute-start.14 = (f32[2,32,4,257]{3,1,2,0:T(8,128)S(1)}, f32[2,32,4,257]{3,1,2,0:T(8,128)S(1)}, u32[]{:S(2)}, u32[]{:S(2)}) collective-permute-start(f32[2,32,4,257]{3,1,2,0:T(8,128)S(1)} %pad_maximum_fusion.6), channel_id=1, source_target_pairs={{0,1},{1,0},{2,3},{3,2},{4,5},{5,4},{6,7},{7,6},{8,9},{9,8},{10,11... | collective-permute-start | bytes 789512 | tf_op jit(solution)/shard_map/ppermute | solution.py:18

commit v16 on v15

--- a/solution.py
+++ b/solution.py
@@ -78,11 +78,7 @@
     channels, segments, length = samples.shape
     half_len = length // 2
     stops = offsets.shape[0]
-    spectrum = jnp.dot(
-        jnp.swapaxes(samples, 0, 1).reshape(segments * channels, length),
-        forward_table(length),
-        preferred_element_type=jnp.float32,
-    ).reshape(segments, channels, length)
+    spectrum = jnp.einsum("csn,nk->sck", samples, forward_table(length), preferred_element_type=jnp.float32)
     keep = (1 - bad_mask).astype(jnp.float32)
     white = whiten(spectrum, keep[None, :, None], half_len)
     split = segments // 2

time: 135 us -> 136 us (level)
    unnamed x8 -> x9, local copies, waits for them, and re-layouts: 3.71 us -> 1.91 us
where the time goes in v16:
time: 136 us; the launch traced here: 134 us
  starting transfers between devices  64.9 us (48%)
  waiting for transfers between devices  45.7 us (34%)
  other arithmetic  10.1 us (7%)
  matrix products  8.9 us (7%)
  local copies, waits for them, and re-layouts  3.52 us (3%)
    ppermute x14, starting transfers between devices, shifted(): lax.ppermute(x, axis, [(i, (i + by) % length) for i in range(length)])  62.7 us
    ppermute x14, waiting for transfers between devices, shifted(): lax.ppermute(x, axis, [(i, (i + by) % length) for i in range(length)])  37.9 us
    ppermute x1, waiting for transfers between devices, swapped(): return lax.ppermute(x, axis, [(i, i ^ 1) for i in range(length)])  7.81 us
    dot_general x3, matrix products, lags_of_stops(): jnp.dot(jnp.concatenate(crosses, axis=0), back_table, precision=lax.Preci...  3.55 us
    another operation x2, other arithmetic  2.96 us
    dot_general x8, matrix products, pick_rows(): jnp.einsum('gp,spk->sgk', picks, block, preferred_element_type=jnp.float32)  2.72 us
  transfers between devices with their start and end apart: 15, of which 7 were waited for; matrix products, arithmetic and copies ran while one was open for 3% of the time, Pallas kernels for 0%

profile of v16, /device:TPU:1, one launch (start us, length us, event | category | flops | bytes accessed | tf_op | source)
XLA Modules:
  0.0 134.2 jit_solution(2449146843691817308)
XLA Ops:
  0.6 1.0 fusion.47
  2.3 3.0 %subtract_convert_fusion = (bf16[32,64,1024]{2,1,0:T(8,128)(2,1)S(1)}, bf16[32,64,1024]{2,1,0:T(8,128)(2,1)S(1)}) fusion(f32[64,1024]{1,0:T(8,128)S(1)} %get-tuple-element.101, f32[32,1024]{1,0:T(8,128)S(1)} %get-tuple-element.98, f32[64,1024]{1,0:T(8,128)S(1)} %get-tuple-element.102, f32[32,1024]{1,0:T(8,128)S(1)} %get-tuple-element.97), kind=kLoop, calls=%fused_computation.5 | loop fusion | flops 18874368 | bytes 9175040 | tf_op jit(solution)/shard_map/convert.7
  5.3 2.6 %multiply_reduce_fusion = (f32[8,32]{1,0:T(8,128)S(1)}, f32[8,32,2048]{2,1,0:T(8,128)S(1)}) fusion(bf16[32,8,2048]{2,1,0:T(8,128)(2,1)S(1)} %copy-done, bf16[2048,1024]{1,0:T(8,128)(2,1)S(1)} %bitcast.107, bf16[2048,1024]{1,0:T(8,128)(2,1)S(1)} %bitcast.106), kind=kOutput, calls=%fused_computation.17 | convolution fusion | flops 2165309184 | bytes 11535360 | tf_op jit(solution)/shard_map/csn,nk->sck/dot_general | solution.py:81
  8.4 1.2 slice_convert_fusion
  9.7 1.4 %scatter.4 = bf16[4,32,2048]{2,1,0:T(8,128)(2,1)} dynamic-update-slice(bf16[4,32,2048]{2,1,0:T(8,128)(2,1)} %get-tuple-element.63, bf16[4,32,1]{2,1,0:T(8,128)(2,1)S(1)} %copy.14, s32[]{:T(128)} %constant.84.clone.1, s32[]{:T(128)} %constant.84.clone.1, s32[]{:T(128)} %constant.92.clone.1) | dynamic-update-slice | bytes 516 | tf_op jit(solution)/shard_map/scatter | solution.py:90
  11.2 8.8 %collective-permute-start.2 = (bf16[4,32,2048]{2,1,0:T(8,128)(2,1)}, bf16[4,32,2048]{2,1,0:T(8,128)(2,1)S(1)}, u32[]{:S(2)}, u32[]{:S(2)}) collective-permute-start(bf16[4,32,2048]{2,1,0:T(8,128)(2,1)} %scatter.4), channel_id=1, source_target_pairs={{0,510},{2,0},{4,2},{6,4},{8,6},{10,8},{12,10},{14,12},{16,14},{18... | collective-permute-start | bytes 1572872 | tf_op jit(solution)/shard_map/ppermute | solution.py:13
  19.9 10.7 %collective-permute-start.3 = (bf16[4,32,2048]{2,1,0:T(8,128)(2,1)}, bf16[4,32,2048]{2,1,0:T(8,128)(2,1)S(1)}, u32[]{:S(2)}, u32[]{:S(2)}) collective-permute-start(bf16[4,32,2048]{2,1,0:T(8,128)(2,1)} %scatter.4), channel_id=1, source_target_pairs={{0,508},{2,510},{4,0},{6,2},{8,4},{10,6},{12,8},{14,10},{16,12},{1... | collective-permute-start | bytes 1572872 | tf_op jit(solution)/shard_map/ppermute | solution.py:13
  30.6 3.3 %collective-permute-start = (bf16[4,32,2048]{2,1,0:T(8,128)(2,1)}, bf16[4,32,2048]{2,1,0:T(8,128)(2,1)S(1)}, u32[]{:S(2)}, u32[]{:S(2)}) collective-permute-start(bf16[4,32,2048]{2,1,0:T(8,128)(2,1)} %get-tuple-element.64), channel_id=1, source_target_pairs={{0,2},{2,4},{4,6},{6,8},{8,10},{10,12},{12,14},{14,16},{16,18},{18... | collective-permute-start | bytes 1572872 | tf_op jit(solution)/shard_map/ppermute | solution.py:13
  33.9 1.9 %collective-permute-start.1 = (bf16[4,32,2048]{2,1,0:T(8,128)(2,1)}, bf16[4,32,2048]{2,1,0:T(8,128)(2,1)S(1)}, u32[]{:S(2)}, u32[]{:S(2)}) collective-permute-start(bf16[4,32,2048]{2,1,0:T(8,128)(2,1)} %get-tuple-element.64), channel_id=1, source_target_pairs={{0,4},{2,6},{4,8},{6,10},{8,12},{10,14},{12,16},{14,18},{16,20},{1... | collective-permute-start | bytes 1572872 | tf_op jit(solution)/shard_map/ppermute | solution.py:13
  36.7 6.0 %collective-permute-done.3 = bf16[4,32,2048]{2,1,0:T(8,128)(2,1)S(1)} collective-permute-done((bf16[4,32,2048]{2,1,0:T(8,128)(2,1)}, bf16[4,32,2048]{2,1,0:T(8,128)(2,1)S(1)}, u32[]{:S(2)}, u32[]{:S(2)}) %collective-permute-start.3) | collective-permute-done | bytes 524320 | tf_op jit(solution)/shard_map/ppermute | solution.py:13
  42.7 0.6 collective-permute-done
  43.3 15.3 %collective-permute-done.1 = bf16[4,32,2048]{2,1,0:T(8,128)(2,1)S(1)} collective-permute-done((bf16[4,32,2048]{2,1,0:T(8,128)(2,1)}, bf16[4,32,2048]{2,1,0:T(8,128)(2,1)S(1)}, u32[]{:S(2)}, u32[]{:S(2)}) %collective-permute-start.1) | collective-permute-done | bytes 524320 | tf_op jit(solution)/shard_map/ppermute | solution.py:13
  60.2 1.9 %collective-permute-start.5 = (bf16[8,32,2048]{2,1,0:T(8,128)(2,1)S(1)}, bf16[8,32,2048]{2,1,0:T(8,128)(2,1)S(1)}, u32[]{:S(2)}, u32[]{:S(2)}) collective-permute-start(bf16[8,32,2048]{2,1,0:T(8,128)(2,1)S(1)} %pad_maximum_fusion.5), channel_id=1, source_target_pairs={{0,508},{2,510},{4,0},{6,2},{8,4},{10,6},{12,8},{14,10},{16,12},{1... | collective-permute-start | bytes 3145736 | tf_op jit(solution)/shard_map/ppermute | solution.py:13
  62.1 3.4 %collective-permute-start.4 = (bf16[8,32,2048]{2,1,0:T(8,128)(2,1)S(1)}, bf16[8,32,2048]{2,1,0:T(8,128)(2,1)S(1)}, u32[]{:S(2)}, u32[]{:S(2)}) collective-permute-start(bf16[8,32,2048]{2,1,0:T(8,128)(2,1)S(1)} %pad_maximum_fusion.4), channel_id=1, source_target_pairs={{0,4},{2,6},{4,8},{6,10},{8,12},{10,14},{12,16},{14,18},{16,20},{1... | collective-permute-start | bytes 3145736 | tf_op jit(solution)/shard_map/ppermute | solution.py:13
  66.1 1.1 fusion.5
  67.3 1.9 %collective-permute-start.8 = (f32[32,257]{1,0:T(8,128)S(1)}, f32[32,257]{1,0:T(8,128)S(1)}, u32[]{:S(2)}, u32[]{:S(2)}) collective-permute-start(f32[32,257]{1,0:T(8,128)S(1)} %get-tuple-element.85), channel_id=1, source_target_pairs={{0,4},{2,6},{4,8},{6,10},{8,12},{10,14},{12,16},{14,18},{16,20},{1... | collective-permute-start | bytes 98696 | tf_op jit(solution)/shard_map/ppermute | solution.py:13
  69.2 9.3 %collective-permute-start.9 = (f32[32,257]{1,0:T(8,128)S(1)}, f32[32,257]{1,0:T(8,128)S(1)}, u32[]{:S(2)}, u32[]{:S(2)}) collective-permute-start(f32[32,257]{1,0:T(8,128)S(1)} %get-tuple-element.86), channel_id=1, source_target_pairs={{0,508},{2,510},{4,0},{6,2},{8,4},{10,6},{12,8},{14,10},{16,12},{1... | collective-permute-start | bytes 98696 | tf_op jit(solution)/shard_map/ppermute | solution.py:13
  79.2 1.1 fusion.6
  80.4 1.9 %collective-permute-start.6 = (f32[32,257]{1,0:T(8,128)S(1)}, f32[32,257]{1,0:T(8,128)S(1)}, u32[]{:S(2)}, u32[]{:S(2)}) collective-permute-start(f32[32,257]{1,0:T(8,128)S(1)} %get-tuple-element.81), channel_id=1, source_target_pairs={{0,2},{2,4},{4,6},{6,8},{8,10},{10,12},{12,14},{14,16},{16,18},{18... | collective-permute-start | bytes 98696 | tf_op jit(solution)/shard_map/ppermute | solution.py:13
  82.3 11.4 %collective-permute-done.8 = f32[32,257]{1,0:T(8,128)S(1)} collective-permute-done((f32[32,257]{1,0:T(8,128)S(1)}, f32[32,257]{1,0:T(8,128)S(1)}, u32[]{:S(2)}, u32[]{:S(2)}) %collective-permute-start.8) | collective-permute-done | bytes 32928 | tf_op jit(solution)/shard_map/ppermute | solution.py:13
  93.8 1.9 %collective-permute-start.7 = (f32[32,257]{1,0:T(8,128)S(1)}, f32[32,257]{1,0:T(8,128)S(1)}, u32[]{:S(2)}, u32[]{:S(2)}) collective-permute-start(f32[32,257]{1,0:T(8,128)S(1)} %get-tuple-element.82), channel_id=1, source_target_pairs={{0,510},{2,0},{4,2},{6,4},{8,6},{10,8},{12,10},{14,12},{16,14},{18... | collective-permute-start | bytes 98696 | tf_op jit(solution)/shard_map/ppermute | solution.py:13
  95.7 3.5 %collective-permute-done.7 = f32[32,257]{1,0:T(8,128)S(1)} collective-permute-done((f32[32,257]{1,0:T(8,128)S(1)}, f32[32,257]{1,0:T(8,128)S(1)}, u32[]{:S(2)}, u32[]{:S(2)}) %collective-permute-start.7) | collective-permute-done | bytes 32928 | tf_op jit(solution)/shard_map/ppermute | solution.py:13
  101.8 1.3 fusion.4
  103.1 1.9 %collective-permute-start.10 = (f32[32,257]{1,0:T(8,128)S(1)}, f32[32,257]{1,0:T(8,128)S(1)}, u32[]{:S(2)}, u32[]{:S(2)}) collective-permute-start(f32[32,257]{1,0:T(8,128)S(1)} %get-tuple-element.69), channel_id=1, source_target_pairs={{0,6},{2,8},{4,10},{6,12},{8,14},{10,16},{12,18},{14,20},{16,22},{... | collective-permute-start | bytes 98696 | tf_op jit(solution)/shard_map/ppermute | solution.py:13
  105.0 1.9 %collective-permute-start.11 = (f32[32,257]{1,0:T(8,128)S(1)}, f32[32,257]{1,0:T(8,128)S(1)}, u32[]{:S(2)}, u32[]{:S(2)}) collective-permute-start(f32[32,257]{1,0:T(8,128)S(1)} %get-tuple-element.76), channel_id=1, source_target_pairs={{0,8},{2,10},{4,12},{6,14},{8,16},{10,18},{12,20},{14,22},{16,24},... | collective-permute-start | bytes 98696 | tf_op jit(solution)/shard_map/ppermute | solution.py:13
  106.9 9.4 %collective-permute-start.12 = (f32[32,257]{1,0:T(8,128)S(1)}, f32[32,257]{1,0:T(8,128)S(1)}, u32[]{:S(2)}, u32[]{:S(2)}) collective-permute-start(f32[32,257]{1,0:T(8,128)S(1)} %get-tuple-element.75), channel_id=1, source_target_pairs={{0,506},{2,508},{4,510},{6,0},{8,2},{10,4},{12,6},{14,8},{16,10},{... | collective-permute-start | bytes 98696 | tf_op jit(solution)/shard_map/ppermute | solution.py:13
  116.3 4.5 %collective-permute-start.13 = (f32[32,257]{1,0:T(8,128)S(1)}, f32[32,257]{1,0:T(8,128)S(1)}, u32[]{:S(2)}, u32[]{:S(2)}) collective-permute-start(f32[32,257]{1,0:T(8,128)S(1)} %get-tuple-element.74), channel_id=1, source_target_pairs={{0,504},{2,506},{4,508},{6,510},{8,0},{10,2},{12,4},{14,6},{16,8},... | collective-permute-start | bytes 98696 | tf_op jit(solution)/shard_map/ppermute | solution.py:13
  120.9 1.1 collective-permute-done.13
  122.1 2.2 %collective-permute-start.14 = (f32[2,32,4,257]{3,1,2,0:T(8,128)S(1)}, f32[2,32,4,257]{3,1,2,0:T(8,128)S(1)}, u32[]{:S(2)}, u32[]{:S(2)}) collective-permute-start(f32[2,32,4,257]{3,1,2,0:T(8,128)S(1)} %pad_maximum_fusion.6), channel_id=1, source_target_pairs={{0,1},{1,0},{2,3},{3,2},{4,5},{5,4},{6,7},{7,6},{8,9},{9,8},{10,11... | collective-permute-start | bytes 789512 | tf_op jit(solution)/shard_map/ppermute | solution.py:18
  124.3 7.8 %collective-permute-done.14 = f32[2,32,4,257]{3,1,2,0:T(8,128)S(1)} collective-permute-done((f32[2,32,4,257]{3,1,2,0:T(8,128)S(1)}, f32[2,32,4,257]{3,1,2,0:T(8,128)S(1)}, u32[]{:S(2)}, u32[]{:S(2)}) %collective-permute-start.14) | collective-permute-done | bytes 263200 | tf_op jit(solution)/shard_map/ppermute | solution.py:18
  132.6 0.8 copy.20
  133.4 0.8 copy.19
  (58 shorter events, 8.1 us)
Async XLA Ops:
  0.6 4.6 %copy-start = (bf16[32,8,2048]{2,1,0:T(8,128)(2,1)S(1)}, bf16[32,8,2048]{2,1,0:T(8,128)(2,1)}, u32[]{:S(2)}) copy-start(bf16[32,8,2048]{2,1,0:T(8,128)(2,1)} %param.5) | copy-start | bytes 3145732
  5.3 2.6 %copy-start.2 = (s32[32]{0:T(128)S(1)}, s32[32]{0:T(128)}, u32[]{:S(2)}) copy-start(s32[32]{0:T(128)} %param.7) | copy-start | bytes 388
  7.9 1.7 %copy-start.1 = (s32[4,32]{1,0:T(4,128)S(1)}, s32[4,32]{1,0:T(4,128)}, u32[]{:S(2)}) copy-start(s32[4,32]{1,0:T(4,128)} %param.6) | copy-start | bytes 1540
  11.2 25.6 %collective-permute-start.2 = (bf16[4,32,2048]{2,1,0:T(8,128)(2,1)}, bf16[4,32,2048]{2,1,0:T(8,128)(2,1)S(1)}, u32[]{:S(2)}, u32[]{:S(2)}) collective-permute-start(bf16[4,32,2048]{2,1,0:T(8,128)(2,1)} %scatter.4), channel_id=1, source_target_pairs={{0,510},{2,0},{4,2},{6,4},{8,6},{10,8},{12,10},{14,12},{16,14},{18... | collective-permute-start | bytes 1572872 | tf_op jit(solution)/shard_map/ppermute | solution.py:13
  19.9 22.8 %collective-permute-start.3 = (bf16[4,32,2048]{2,1,0:T(8,128)(2,1)}, bf16[4,32,2048]{2,1,0:T(8,128)(2,1)S(1)}, u32[]{:S(2)}, u32[]{:S(2)}) collective-permute-start(bf16[4,32,2048]{2,1,0:T(8,128)(2,1)} %scatter.4), channel_id=1, source_target_pairs={{0,508},{2,510},{4,0},{6,2},{8,4},{10,6},{12,8},{14,10},{16,12},{1... | collective-permute-start | bytes 1572872 | tf_op jit(solution)/shard_map/ppermute | solution.py:13
  30.6 12.7 %collective-permute-start = (bf16[4,32,2048]{2,1,0:T(8,128)(2,1)}, bf16[4,32,2048]{2,1,0:T(8,128)(2,1)S(1)}, u32[]{:S(2)}, u32[]{:S(2)}) collective-permute-start(bf16[4,32,2048]{2,1,0:T(8,128)(2,1)} %get-tuple-element.64), channel_id=1, source_target_pairs={{0,2},{2,4},{4,6},{6,8},{8,10},{10,12},{12,14},{14,16},{16,18},{18... | collective-permute-start | bytes 1572872 | tf_op jit(solution)/shard_map/ppermute | solution.py:13
  33.9 24.8 %collective-permute-start.1 = (bf16[4,32,2048]{2,1,0:T(8,128)(2,1)}, bf16[4,32,2048]{2,1,0:T(8,128)(2,1)S(1)}, u32[]{:S(2)}, u32[]{:S(2)}) collective-permute-start(bf16[4,32,2048]{2,1,0:T(8,128)(2,1)} %get-tuple-element.64), channel_id=1, source_target_pairs={{0,4},{2,6},{4,8},{6,10},{8,12},{10,14},{12,16},{14,18},{16,20},{1... | collective-permute-start | bytes 1572872 | tf_op jit(solution)/shard_map/ppermute | solution.py:13
  60.2 39.0 %collective-permute-start.5 = (bf16[8,32,2048]{2,1,0:T(8,128)(2,1)S(1)}, bf16[8,32,2048]{2,1,0:T(8,128)(2,1)S(1)}, u32[]{:S(2)}, u32[]{:S(2)}) collective-permute-start(bf16[8,32,2048]{2,1,0:T(8,128)(2,1)S(1)} %pad_maximum_fusion.5), channel_id=1, source_target_pairs={{0,508},{2,510},{4,0},{6,2},{8,4},{10,6},{12,8},{14,10},{16,12},{1... | collective-permute-start | bytes 3145736 | tf_op jit(solution)/shard_map/ppermute | solution.py:13
  62.1 37.1 %collective-permute-start.4 = (bf16[8,32,2048]{2,1,0:T(8,128)(2,1)S(1)}, bf16[8,32,2048]{2,1,0:T(8,128)(2,1)S(1)}, u32[]{:S(2)}, u32[]{:S(2)}) collective-permute-start(bf16[8,32,2048]{2,1,0:T(8,128)(2,1)S(1)} %pad_maximum_fusion.4), channel_id=1, source_target_pairs={{0,4},{2,6},{4,8},{6,10},{8,12},{10,14},{12,16},{14,18},{16,20},{1... | collective-permute-start | bytes 3145736 | tf_op jit(solution)/shard_map/ppermute | solution.py:13
  67.3 26.5 %collective-permute-start.8 = (f32[32,257]{1,0:T(8,128)S(1)}, f32[32,257]{1,0:T(8,128)S(1)}, u32[]{:S(2)}, u32[]{:S(2)}) collective-permute-start(f32[32,257]{1,0:T(8,128)S(1)} %get-tuple-element.85), channel_id=1, source_target_pairs={{0,4},{2,6},{4,8},{6,10},{8,12},{10,14},{12,16},{14,18},{16,20},{1... | collective-permute-start | bytes 98696 | tf_op jit(solution)/shard_map/ppermute | solution.py:13
  69.2 26.4 %collective-permute-start.9 = (f32[32,257]{1,0:T(8,128)S(1)}, f32[32,257]{1,0:T(8,128)S(1)}, u32[]{:S(2)}, u32[]{:S(2)}) collective-permute-start(f32[32,257]{1,0:T(8,128)S(1)} %get-tuple-element.86), channel_id=1, source_target_pairs={{0,508},{2,510},{4,0},{6,2},{8,4},{10,6},{12,8},{14,10},{16,12},{1... | collective-permute-start | bytes 98696 | tf_op jit(solution)/shard_map/ppermute | solution.py:13
  80.4 15.3 %collective-permute-start.6 = (f32[32,257]{1,0:T(8,128)S(1)}, f32[32,257]{1,0:T(8,128)S(1)}, u32[]{:S(2)}, u32[]{:S(2)}) collective-permute-start(f32[32,257]{1,0:T(8,128)S(1)} %get-tuple-element.81), channel_id=1, source_target_pairs={{0,2},{2,4},{4,6},{6,8},{8,10},{10,12},{12,14},{14,16},{16,18},{18... | collective-permute-start | bytes 98696 | tf_op jit(solution)/shard_map/ppermute | solution.py:13
  93.8 5.4 %collective-permute-start.7 = (f32[32,257]{1,0:T(8,128)S(1)}, f32[32,257]{1,0:T(8,128)S(1)}, u32[]{:S(2)}, u32[]{:S(2)}) collective-permute-start(f32[32,257]{1,0:T(8,128)S(1)} %get-tuple-element.82), channel_id=1, source_target_pairs={{0,510},{2,0},{4,2},{6,4},{8,6},{10,8},{12,10},{14,12},{16,14},{18... | collective-permute-start | bytes 98696 | tf_op jit(solution)/shard_map/ppermute | solution.py:13
  103.1 17.8 %collective-permute-start.10 = (f32[32,257]{1,0:T(8,128)S(1)}, f32[32,257]{1,0:T(8,128)S(1)}, u32[]{:S(2)}, u32[]{:S(2)}) collective-permute-start(f32[32,257]{1,0:T(8,128)S(1)} %get-tuple-element.69), channel_id=1, source_target_pairs={{0,6},{2,8},{4,10},{6,12},{8,14},{10,16},{12,18},{14,20},{16,22},{... | collective-permute-start | bytes 98696 | tf_op jit(solution)/shard_map/ppermute | solution.py:13
  105.0 15.9 %collective-permute-start.11 = (f32[32,257]{1,0:T(8,128)S(1)}, f32[32,257]{1,0:T(8,128)S(1)}, u32[]{:S(2)}, u32[]{:S(2)}) collective-permute-start(f32[32,257]{1,0:T(8,128)S(1)} %get-tuple-element.76), channel_id=1, source_target_pairs={{0,8},{2,10},{4,12},{6,14},{8,16},{10,18},{12,20},{14,22},{16,24},... | collective-permute-start | bytes 98696 | tf_op jit(solution)/shard_map/ppermute | solution.py:13
  106.9 14.0 %collective-permute-start.12 = (f32[32,257]{1,0:T(8,128)S(1)}, f32[32,257]{1,0:T(8,128)S(1)}, u32[]{:S(2)}, u32[]{:S(2)}) collective-permute-start(f32[32,257]{1,0:T(8,128)S(1)} %get-tuple-element.75), channel_id=1, source_target_pairs={{0,506},{2,508},{4,510},{6,0},{8,2},{10,4},{12,6},{14,8},{16,10},{... | collective-permute-start | bytes 98696 | tf_op jit(solution)/shard_map/ppermute | solution.py:13
  116.3 5.7 %collective-permute-start.13 = (f32[32,257]{1,0:T(8,128)S(1)}, f32[32,257]{1,0:T(8,128)S(1)}, u32[]{:S(2)}, u32[]{:S(2)}) collective-permute-start(f32[32,257]{1,0:T(8,128)S(1)} %get-tuple-element.74), channel_id=1, source_target_pairs={{0,504},{2,506},{4,508},{6,510},{8,0},{10,2},{12,4},{14,6},{16,8},... | collective-permute-start | bytes 98696 | tf_op jit(solution)/shard_map/ppermute | solution.py:13
  122.1 10.0 %collective-permute-start.14 = (f32[2,32,4,257]{3,1,2,0:T(8,128)S(1)}, f32[2,32,4,257]{3,1,2,0:T(8,128)S(1)}, u32[]{:S(2)}, u32[]{:S(2)}) collective-permute-start(f32[2,32,4,257]{3,1,2,0:T(8,128)S(1)} %pad_maximum_fusion.6), channel_id=1, source_target_pairs={{0,1},{1,0},{2,3},{3,2},{4,5},{5,4},{6,7},{7,6},{8,9},{9,8},{10,11... | collective-permute-start | bytes 789512 | tf_op jit(solution)/shard_map/ppermute | solution.py:18

commit v17 on v15

--- a/solution.py
+++ b/solution.py
@@ -139,14 +139,12 @@
     later_parts = [piece[channels:] for piece in lags]
     from_earlier = [pair[0] for pair in early + late]
     from_later = [pair[1] for pair in early + late]
-    corr_part = jnp.stack(own_parts, axis=1) + jnp.stack(from_earlier, axis=1)
-    mirror_part = jnp.stack(from_later, axis=1) + jnp.stack(later_parts, axis=1)
+    scale = 1.0 / math.sqrt(segments * lax.axis_size("rep") * half_len)
+    corr_part = (jnp.stack(own_parts, axis=1) + jnp.stack(from_earlier, axis=1)) * scale
+    mirror_part = ((jnp.stack(from_later, axis=1) + jnp.stack(later_parts, axis=1)) * scale)[:, :, ::-1]
     parts = jnp.stack([corr_part, mirror_part], axis=0)
-    summed = parts + swapped(parts, "rep")
-    scale = 1.0 / math.sqrt(segments * lax.axis_size("rep") * half_len)
-    correlations = summed[0] * scale
-    mirrored = (summed[1] * scale)[:, :, ::-1]
-    return (correlations, mirrored)
+    other = swapped(parts, "rep")
+    return (parts[0] + other[0], parts[1] + other[1])
 
 
 def solution(mesh):

time: 135 us -> 141 us (1.044)
  the two profiles are of different devices: /device:TPU:1 before, /device:TPU:9 now
where the time goes in v17:
time: 141 us; the launch traced here: 140 us
  waiting for transfers between devices  60.3 us (43%)
  starting transfers between devices  57 us (40%)
  other arithmetic  9.1 us (6%)
  matrix products  8.8 us (6%)
  local copies, waits for them, and re-layouts  4.07 us (3%)
    ppermute x14, starting transfers between devices, shifted(): lax.ppermute(x, axis, [(i, (i + by) % length) for i in range(length)])  54.8 us
    ppermute x14, waiting for transfers between devices, shifted(): lax.ppermute(x, axis, [(i, (i + by) % length) for i in range(length)])  50.8 us
    ppermute x1, waiting for transfers between devices, swapped(): return lax.ppermute(x, axis, [(i, i ^ 1) for i in range(length)])  9.52 us
    unnamed x8, local copies, waits for them, and re-layouts  3.71 us
    dot_general x3, matrix products, lags_of_stops(): jnp.dot(jnp.concatenate(crosses, axis=0), back_table, precision=lax.Preci...  3.57 us
    another operation x2, other arithmetic  2.96 us
  transfers between devices with their start and end apart: 15, of which 7 were waited for; matrix products, arithmetic and copies ran while one was open for 4% of the time, Pallas kernels for 0%

profile of v17, /device:TPU:9, one launch (start us, length us, event | category | flops | bytes accessed | tf_op | source)
XLA Modules:
  0.0 140.4 jit_solution(13841593902969188165)
XLA Ops:
  0.6 1.0 fusion.50
  1.7 0.6 fusion.56
  2.3 1.8 %copy.12 = bf16[32,8,2048]{2,0,1:T(8,128)(2,1)S(1)} copy(bf16[32,8,2048]{2,1,0:T(8,128)(2,1)} %param.5) | data formatting | bytes 2097152 | tf_op args[0]
  4.1 3.0 %subtract_convert_fusion = (bf16[32,64,1024]{2,1,0:T(8,128)(2,1)S(1)}, bf16[32,64,1024]{2,1,0:T(8,128)(2,1)S(1)}) fusion(f32[64,1024]{1,0:T(8,128)S(1)} %get-tuple-element.107, f32[32,1024]{1,0:T(8,128)S(1)} %get-tuple-element.104, f32[64,1024]{1,0:T(8,128)S(1)} %get-tuple-element.108, f32[32,1024]{1,0:T(8,128)S(1)} %get-tuple-element.103), kind=kLoop, calls=%fused_computation.5 | loop fusion | flops 18874368 | bytes 9175040 | tf_op jit(solution)/shard_map/convert.7
  7.1 2.5 %fusion.4 = (f32[256]{0:T(256)S(1)}, f32[2048,256]{0,1:T(8,128)S(1)}) fusion(bf16[256,2048]{1,0:T(8,128)(2,1)S(1)} %bitcast.128, bf16[2048,1024]{1,0:T(8,128)(2,1)S(1)} %bitcast.126, bf16[2048,1024]{1,0:T(8,128)(2,1)S(1)} %bitcast.125), kind=kOutput, calls=%fused_computation.16 | convolution fusion | flops 2165309184 | bytes 11535360 | tf_op jit(solution)/shard_map/dot_general | solution.py:81
  10.6 2.6 %collective-permute-start.2 = (bf16[4,32,2048]{2,1,0:T(8,128)(2,1)S(1)}, bf16[4,32,2048]{2,1,0:T(8,128)(2,1)S(1)}, u32[]{:S(2)}, u32[]{:S(2)}) collective-permute-start(bf16[4,32,2048]{2,1,0:T(8,128)(2,1)S(1)} %scatter.4), channel_id=1, source_target_pairs={{0,510},{2,0},{4,2},{6,4},{8,6},{10,8},{12,10},{14,12},{16,14},{18... | collective-permute-start | bytes 1572872 | tf_op jit(solution)/shard_map/ppermute | solution.py:13
  13.2 7.5 %collective-permute-start.3 = (bf16[4,32,2048]{2,1,0:T(8,128)(2,1)S(1)}, bf16[4,32,2048]{2,1,0:T(8,128)(2,1)S(1)}, u32[]{:S(2)}, u32[]{:S(2)}) collective-permute-start(bf16[4,32,2048]{2,1,0:T(8,128)(2,1)S(1)} %scatter.4), channel_id=1, source_target_pairs={{0,508},{2,510},{4,0},{6,2},{8,4},{10,6},{12,8},{14,10},{16,12},{1... | collective-permute-start | bytes 1572872 | tf_op jit(solution)/shard_map/ppermute | solution.py:13
  20.6 1.9 %collective-permute-start = (bf16[4,32,2048]{2,1,0:T(8,128)(2,1)S(1)}, bf16[4,32,2048]{2,1,0:T(8,128)(2,1)S(1)}, u32[]{:S(2)}, u32[]{:S(2)}) collective-permute-start(bf16[4,32,2048]{2,1,0:T(8,128)(2,1)S(1)} %get-tuple-element.66), channel_id=1, source_target_pairs={{0,2},{2,4},{4,6},{6,8},{8,10},{10,12},{12,14},{14,16},{16,18},{18... | collective-permute-start | bytes 1572872 | tf_op jit(solution)/shard_map/ppermute | solution.py:13
  22.5 1.9 %collective-permute-start.1 = (bf16[4,32,2048]{2,1,0:T(8,128)(2,1)S(1)}, bf16[4,32,2048]{2,1,0:T(8,128)(2,1)S(1)}, u32[]{:S(2)}, u32[]{:S(2)}) collective-permute-start(bf16[4,32,2048]{2,1,0:T(8,128)(2,1)S(1)} %get-tuple-element.66), channel_id=1, source_target_pairs={{0,4},{2,6},{4,8},{6,10},{8,12},{10,14},{12,16},{14,18},{16,20},{1... | collective-permute-start | bytes 1572872 | tf_op jit(solution)/shard_map/ppermute | solution.py:13
  25.4 3.6 %collective-permute-done.3 = bf16[4,32,2048]{2,1,0:T(8,128)(2,1)S(1)} collective-permute-done((bf16[4,32,2048]{2,1,0:T(8,128)(2,1)S(1)}, bf16[4,32,2048]{2,1,0:T(8,128)(2,1)S(1)}, u32[]{:S(2)}, u32[]{:S(2)}) %collective-permute-start.3) | collective-permute-done | bytes 524320 | tf_op jit(solution)/shard_map/ppermute | solution.py:13
  29.1 3.6 %collective-permute-done = bf16[4,32,2048]{2,1,0:T(8,128)(2,1)S(1)} collective-permute-done((bf16[4,32,2048]{2,1,0:T(8,128)(2,1)S(1)}, bf16[4,32,2048]{2,1,0:T(8,128)(2,1)S(1)}, u32[]{:S(2)}, u32[]{:S(2)}) %collective-permute-start) | collective-permute-done | bytes 524320 | tf_op jit(solution)/shard_map/ppermute | solution.py:13
  32.7 17.7 %collective-permute-done.1 = bf16[4,32,2048]{2,1,0:T(8,128)(2,1)S(1)} collective-permute-done((bf16[4,32,2048]{2,1,0:T(8,128)(2,1)S(1)}, bf16[4,32,2048]{2,1,0:T(8,128)(2,1)S(1)}, u32[]{:S(2)}, u32[]{:S(2)}) %collective-permute-start.1) | collective-permute-done | bytes 524320 | tf_op jit(solution)/shard_map/ppermute | solution.py:13
  51.9 8.7 %collective-permute-start.5 = (bf16[8,32,2048]{2,1,0:T(8,128)(2,1)S(1)}, bf16[8,32,2048]{2,1,0:T(8,128)(2,1)S(1)}, u32[]{:S(2)}, u32[]{:S(2)}) collective-permute-start(bf16[8,32,2048]{2,1,0:T(8,128)(2,1)S(1)} %pad_maximum_fusion.5), channel_id=1, source_target_pairs={{0,508},{2,510},{4,0},{6,2},{8,4},{10,6},{12,8},{14,10},{16,12},{1... | collective-permute-start | bytes 3145736 | tf_op jit(solution)/shard_map/ppermute | solution.py:13
  60.6 1.9 %collective-permute-start.4 = (bf16[8,32,2048]{2,1,0:T(8,128)(2,1)S(1)}, bf16[8,32,2048]{2,1,0:T(8,128)(2,1)S(1)}, u32[]{:S(2)}, u32[]{:S(2)}) collective-permute-start(bf16[8,32,2048]{2,1,0:T(8,128)(2,1)S(1)} %pad_maximum_fusion.4), channel_id=1, source_target_pairs={{0,4},{2,6},{4,8},{6,10},{8,12},{10,14},{12,16},{14,18},{16,20},{1... | collective-permute-start | bytes 3145736 | tf_op jit(solution)/shard_map/ppermute | solution.py:13
  63.2 1.1 fusion.6
  64.4 1.9 %collective-permute-start.8 = (f32[32,257]{1,0:T(8,128)S(1)}, f32[32,257]{1,0:T(8,128)S(1)}, u32[]{:S(2)}, u32[]{:S(2)}) collective-permute-start(f32[32,257]{1,0:T(8,128)S(1)} %get-tuple-element.91), channel_id=1, source_target_pairs={{0,4},{2,6},{4,8},{6,10},{8,12},{10,14},{12,16},{14,18},{16,20},{1... | collective-permute-start | bytes 98696 | tf_op jit(solution)/shard_map/ppermute | solution.py:13
  66.4 3.5 %collective-permute-start.9 = (f32[32,257]{1,0:T(8,128)S(1)}, f32[32,257]{1,0:T(8,128)S(1)}, u32[]{:S(2)}, u32[]{:S(2)}) collective-permute-start(f32[32,257]{1,0:T(8,128)S(1)} %get-tuple-element.92), channel_id=1, source_target_pairs={{0,508},{2,510},{4,0},{6,2},{8,4},{10,6},{12,8},{14,10},{16,12},{1... | collective-permute-start | bytes 98696 | tf_op jit(solution)/shard_map/ppermute | solution.py:13
  70.6 1.1 fusion.7
  71.8 1.9 %collective-permute-start.6 = (f32[32,257]{1,0:T(8,128)S(1)}, f32[32,257]{1,0:T(8,128)S(1)}, u32[]{:S(2)}, u32[]{:S(2)}) collective-permute-start(f32[32,257]{1,0:T(8,128)S(1)} %get-tuple-element.86), channel_id=1, source_target_pairs={{0,2},{2,4},{4,6},{6,8},{8,10},{10,12},{12,14},{14,16},{16,18},{18... | collective-permute-start | bytes 98696 | tf_op jit(solution)/shard_map/ppermute | solution.py:13
  73.7 13.1 %collective-permute-done.8 = f32[32,257]{1,0:T(8,128)S(1)} collective-permute-done((f32[32,257]{1,0:T(8,128)S(1)}, f32[32,257]{1,0:T(8,128)S(1)}, u32[]{:S(2)}, u32[]{:S(2)}) %collective-permute-start.8) | collective-permute-done | bytes 32928 | tf_op jit(solution)/shard_map/ppermute | solution.py:13
  86.9 1.9 %collective-permute-start.7 = (f32[32,257]{1,0:T(8,128)S(1)}, f32[32,257]{1,0:T(8,128)S(1)}, u32[]{:S(2)}, u32[]{:S(2)}) collective-permute-start(f32[32,257]{1,0:T(8,128)S(1)} %get-tuple-element.87), channel_id=1, source_target_pairs={{0,510},{2,0},{4,2},{6,4},{8,6},{10,8},{12,10},{14,12},{16,14},{18... | collective-permute-start | bytes 98696 | tf_op jit(solution)/shard_map/ppermute | solution.py:13
  88.8 3.5 %collective-permute-done.7 = f32[32,257]{1,0:T(8,128)S(1)} collective-permute-done((f32[32,257]{1,0:T(8,128)S(1)}, f32[32,257]{1,0:T(8,128)S(1)}, u32[]{:S(2)}, u32[]{:S(2)}) %collective-permute-start.7) | collective-permute-done | bytes 32928 | tf_op jit(solution)/shard_map/ppermute | solution.py:13
  94.9 1.3 fusion.5
  96.2 5.4 %collective-permute-start.12 = (f32[32,257]{1,0:T(8,128)S(1)}, f32[32,257]{1,0:T(8,128)S(1)}, u32[]{:S(2)}, u32[]{:S(2)}) collective-permute-start(f32[32,257]{1,0:T(8,128)S(1)} %get-tuple-element.79), channel_id=1, source_target_pairs={{0,506},{2,508},{4,510},{6,0},{8,2},{10,4},{12,6},{14,8},{16,10},{... | collective-permute-start | bytes 98696 | tf_op jit(solution)/shard_map/ppermute | solution.py:13
  101.6 8.8 %collective-permute-start.13 = (f32[32,257]{1,0:T(8,128)S(1)}, f32[32,257]{1,0:T(8,128)S(1)}, u32[]{:S(2)}, u32[]{:S(2)}) collective-permute-start(f32[32,257]{1,0:T(8,128)S(1)} %get-tuple-element.78), channel_id=1, source_target_pairs={{0,504},{2,506},{4,508},{6,510},{8,0},{10,2},{12,4},{14,6},{16,8},... | collective-permute-start | bytes 98696 | tf_op jit(solution)/shard_map/ppermute | solution.py:13
  110.5 4.8 %collective-permute-start.10 = (f32[32,257]{1,0:T(8,128)S(1)}, f32[32,257]{1,0:T(8,128)S(1)}, u32[]{:S(2)}, u32[]{:S(2)}) collective-permute-start(f32[32,257]{1,0:T(8,128)S(1)} %get-tuple-element.77), channel_id=1, source_target_pairs={{0,6},{2,8},{4,10},{6,12},{8,14},{10,16},{12,18},{14,20},{16,22},{... | collective-permute-start | bytes 98696 | tf_op jit(solution)/shard_map/ppermute | solution.py:13
  115.3 1.9 %collective-permute-start.11 = (f32[32,257]{1,0:T(8,128)S(1)}, f32[32,257]{1,0:T(8,128)S(1)}, u32[]{:S(2)}, u32[]{:S(2)}) collective-permute-start(f32[32,257]{1,0:T(8,128)S(1)} %get-tuple-element.80), channel_id=1, source_target_pairs={{0,8},{2,10},{4,12},{6,14},{8,16},{10,18},{12,20},{14,22},{16,24},... | collective-permute-start | bytes 98696 | tf_op jit(solution)/shard_map/ppermute | solution.py:13
  117.7 9.1 %collective-permute-done.11 = f32[32,257]{1,0:T(8,128)S(1)} collective-permute-done((f32[32,257]{1,0:T(8,128)S(1)}, f32[32,257]{1,0:T(8,128)S(1)}, u32[]{:S(2)}, u32[]{:S(2)}) %collective-permute-start.11) | collective-permute-done | bytes 32928 | tf_op jit(solution)/shard_map/ppermute | solution.py:13
  127.0 2.2 %collective-permute-start.14 = (f32[2,32,4,257]{3,1,2,0:T(8,128)S(1)}, f32[2,32,4,257]{3,1,2,0:T(8,128)S(1)}, u32[]{:S(2)}, u32[]{:S(2)}) collective-permute-start(f32[2,32,4,257]{3,1,2,0:T(8,128)S(1)} %pad_maximum_fusion.6), channel_id=1, source_target_pairs={{0,1},{1,0},{2,3},{3,2},{4,5},{5,4},{6,7},{7,6},{8,9},{9,8},{10,11... | collective-permute-start | bytes 789512 | tf_op jit(solution)/shard_map/ppermute | solution.py:18
  129.2 9.5 %collective-permute-done.14 = f32[2,32,4,257]{3,1,2,0:T(8,128)S(1)} collective-permute-done((f32[2,32,4,257]{3,1,2,0:T(8,128)S(1)}, f32[2,32,4,257]{3,1,2,0:T(8,128)S(1)}, u32[]{:S(2)}, u32[]{:S(2)}) %collective-permute-start.14) | collective-permute-done | bytes 263200 | tf_op jit(solution)/shard_map/ppermute | solution.py:18
  138.8 0.8 copy.18
  139.6 0.8 copy.19
  (57 shorter events, 7.9 us)
Async XLA Ops:
  7.0 2.6 %copy-start.1 = (s32[32]{0:T(128)S(1)}, s32[32]{0:T(128)}, u32[]{:S(2)}) copy-start(s32[32]{0:T(128)} %param.7) | copy-start | bytes 388
  9.6 0.7 copy-start
  10.6 14.8 %collective-permute-start.2 = (bf16[4,32,2048]{2,1,0:T(8,128)(2,1)S(1)}, bf16[4,32,2048]{2,1,0:T(8,128)(2,1)S(1)}, u32[]{:S(2)}, u32[]{:S(2)}) collective-permute-start(bf16[4,32,2048]{2,1,0:T(8,128)(2,1)S(1)} %scatter.4), channel_id=1, source_target_pairs={{0,510},{2,0},{4,2},{6,4},{8,6},{10,8},{12,10},{14,12},{16,14},{18... | collective-permute-start | bytes 1572872 | tf_op jit(solution)/shard_map/ppermute | solution.py:13
  13.2 15.9 %collective-permute-start.3 = (bf16[4,32,2048]{2,1,0:T(8,128)(2,1)S(1)}, bf16[4,32,2048]{2,1,0:T(8,128)(2,1)S(1)}, u32[]{:S(2)}, u32[]{:S(2)}) collective-permute-start(bf16[4,32,2048]{2,1,0:T(8,128)(2,1)S(1)} %scatter.4), channel_id=1, source_target_pairs={{0,508},{2,510},{4,0},{6,2},{8,4},{10,6},{12,8},{14,10},{16,12},{1... | collective-permute-start | bytes 1572872 | tf_op jit(solution)/shard_map/ppermute | solution.py:13
  20.6 12.1 %collective-permute-start = (bf16[4,32,2048]{2,1,0:T(8,128)(2,1)S(1)}, bf16[4,32,2048]{2,1,0:T(8,128)(2,1)S(1)}, u32[]{:S(2)}, u32[]{:S(2)}) collective-permute-start(bf16[4,32,2048]{2,1,0:T(8,128)(2,1)S(1)} %get-tuple-element.66), channel_id=1, source_target_pairs={{0,2},{2,4},{4,6},{6,8},{8,10},{10,12},{12,14},{14,16},{16,18},{18... | collective-permute-start | bytes 1572872 | tf_op jit(solution)/shard_map/ppermute | solution.py:13
  22.5 27.9 %collective-permute-start.1 = (bf16[4,32,2048]{2,1,0:T(8,128)(2,1)S(1)}, bf16[4,32,2048]{2,1,0:T(8,128)(2,1)S(1)}, u32[]{:S(2)}, u32[]{:S(2)}) collective-permute-start(bf16[4,32,2048]{2,1,0:T(8,128)(2,1)S(1)} %get-tuple-element.66), channel_id=1, source_target_pairs={{0,4},{2,6},{4,8},{6,10},{8,12},{10,14},{12,16},{14,18},{16,20},{1... | collective-permute-start | bytes 1572872 | tf_op jit(solution)/shard_map/ppermute | solution.py:13
  51.9 40.3 %collective-permute-start.5 = (bf16[8,32,2048]{2,1,0:T(8,128)(2,1)S(1)}, bf16[8,32,2048]{2,1,0:T(8,128)(2,1)S(1)}, u32[]{:S(2)}, u32[]{:S(2)}) collective-permute-start(bf16[8,32,2048]{2,1,0:T(8,128)(2,1)S(1)} %pad_maximum_fusion.5), channel_id=1, source_target_pairs={{0,508},{2,510},{4,0},{6,2},{8,4},{10,6},{12,8},{14,10},{16,12},{1... | collective-permute-start | bytes 3145736 | tf_op jit(solution)/shard_map/ppermute | solution.py:13
  60.6 31.6 %collective-permute-start.4 = (bf16[8,32,2048]{2,1,0:T(8,128)(2,1)S(1)}, bf16[8,32,2048]{2,1,0:T(8,128)(2,1)S(1)}, u32[]{:S(2)}, u32[]{:S(2)}) collective-permute-start(bf16[8,32,2048]{2,1,0:T(8,128)(2,1)S(1)} %pad_maximum_fusion.4), channel_id=1, source_target_pairs={{0,4},{2,6},{4,8},{6,10},{8,12},{10,14},{12,16},{14,18},{16,20},{1... | collective-permute-start | bytes 3145736 | tf_op jit(solution)/shard_map/ppermute | solution.py:13
  64.4 22.4 %collective-permute-start.8 = (f32[32,257]{1,0:T(8,128)S(1)}, f32[32,257]{1,0:T(8,128)S(1)}, u32[]{:S(2)}, u32[]{:S(2)}) collective-permute-start(f32[32,257]{1,0:T(8,128)S(1)} %get-tuple-element.91), channel_id=1, source_target_pairs={{0,4},{2,6},{4,8},{6,10},{8,12},{10,14},{12,16},{14,18},{16,20},{1... | collective-permute-start | bytes 98696 | tf_op jit(solution)/shard_map/ppermute | solution.py:13
  66.4 22.4 %collective-permute-start.9 = (f32[32,257]{1,0:T(8,128)S(1)}, f32[32,257]{1,0:T(8,128)S(1)}, u32[]{:S(2)}, u32[]{:S(2)}) collective-permute-start(f32[32,257]{1,0:T(8,128)S(1)} %get-tuple-element.92), channel_id=1, source_target_pairs={{0,508},{2,510},{4,0},{6,2},{8,4},{10,6},{12,8},{14,10},{16,12},{1... | collective-permute-start | bytes 98696 | tf_op jit(solution)/shard_map/ppermute | solution.py:13
  71.8 17.0 %collective-permute-start.6 = (f32[32,257]{1,0:T(8,128)S(1)}, f32[32,257]{1,0:T(8,128)S(1)}, u32[]{:S(2)}, u32[]{:S(2)}) collective-permute-start(f32[32,257]{1,0:T(8,128)S(1)} %get-tuple-element.86), channel_id=1, source_target_pairs={{0,2},{2,4},{4,6},{6,8},{8,10},{10,12},{12,14},{14,16},{16,18},{18... | collective-permute-start | bytes 98696 | tf_op jit(solution)/shard_map/ppermute | solution.py:13
  86.9 5.4 %collective-permute-start.7 = (f32[32,257]{1,0:T(8,128)S(1)}, f32[32,257]{1,0:T(8,128)S(1)}, u32[]{:S(2)}, u32[]{:S(2)}) collective-permute-start(f32[32,257]{1,0:T(8,128)S(1)} %get-tuple-element.87), channel_id=1, source_target_pairs={{0,510},{2,0},{4,2},{6,4},{8,6},{10,8},{12,10},{14,12},{16,14},{18... | collective-permute-start | bytes 98696 | tf_op jit(solution)/shard_map/ppermute | solution.py:13
  96.2 21.1 %collective-permute-start.12 = (f32[32,257]{1,0:T(8,128)S(1)}, f32[32,257]{1,0:T(8,128)S(1)}, u32[]{:S(2)}, u32[]{:S(2)}) collective-permute-start(f32[32,257]{1,0:T(8,128)S(1)} %get-tuple-element.79), channel_id=1, source_target_pairs={{0,506},{2,508},{4,510},{6,0},{8,2},{10,4},{12,6},{14,8},{16,10},{... | collective-permute-start | bytes 98696 | tf_op jit(solution)/shard_map/ppermute | solution.py:13
  101.6 15.6 %collective-permute-start.13 = (f32[32,257]{1,0:T(8,128)S(1)}, f32[32,257]{1,0:T(8,128)S(1)}, u32[]{:S(2)}, u32[]{:S(2)}) collective-permute-start(f32[32,257]{1,0:T(8,128)S(1)} %get-tuple-element.78), channel_id=1, source_target_pairs={{0,504},{2,506},{4,508},{6,510},{8,0},{10,2},{12,4},{14,6},{16,8},... | collective-permute-start | bytes 98696 | tf_op jit(solution)/shard_map/ppermute | solution.py:13
  110.5 7.2 %collective-permute-start.10 = (f32[32,257]{1,0:T(8,128)S(1)}, f32[32,257]{1,0:T(8,128)S(1)}, u32[]{:S(2)}, u32[]{:S(2)}) collective-permute-start(f32[32,257]{1,0:T(8,128)S(1)} %get-tuple-element.77), channel_id=1, source_target_pairs={{0,6},{2,8},{4,10},{6,12},{8,14},{10,16},{12,18},{14,20},{16,22},{... | collective-permute-start | bytes 98696 | tf_op jit(solution)/shard_map/ppermute | solution.py:13
  115.3 11.6 %collective-permute-start.11 = (f32[32,257]{1,0:T(8,128)S(1)}, f32[32,257]{1,0:T(8,128)S(1)}, u32[]{:S(2)}, u32[]{:S(2)}) collective-permute-start(f32[32,257]{1,0:T(8,128)S(1)} %get-tuple-element.80), channel_id=1, source_target_pairs={{0,8},{2,10},{4,12},{6,14},{8,16},{10,18},{12,20},{14,22},{16,24},... | collective-permute-start | bytes 98696 | tf_op jit(solution)/shard_map/ppermute | solution.py:13
  127.0 11.7 %collective-permute-start.14 = (f32[2,32,4,257]{3,1,2,0:T(8,128)S(1)}, f32[2,32,4,257]{3,1,2,0:T(8,128)S(1)}, u32[]{:S(2)}, u32[]{:S(2)}) collective-permute-start(f32[2,32,4,257]{3,1,2,0:T(8,128)S(1)} %pad_maximum_fusion.6), channel_id=1, source_target_pairs={{0,1},{1,0},{2,3},{3,2},{4,5},{5,4},{6,7},{7,6},{8,9},{9,8},{10,11... | collective-permute-start | bytes 789512 | tf_op jit(solution)/shard_map/ppermute | solution.py:18

commit v18 on v15

--- a/solution.py
+++ b/solution.py
@@ -112,10 +112,11 @@
         return [lags[i * rows:(i + 1) * rows] for i in range(len(crosses))]
 
     near = stops // 2
-    first = lax.optimization_barrier(
-        tuple(shifted(moving_ahead, "blk", d) for d in range(1, near + 1))
-        + tuple(shifted(moving_behind, "blk", -d) for d in range(1, near + 1))
+    far_first = lax.optimization_barrier(
+        tuple(shifted(moving_ahead, "blk", d) for d in range(near, 0, -1))
+        + tuple(shifted(moving_behind, "blk", -d) for d in range(near, 0, -1))
     )
+    first = far_first[:near][::-1] + far_first[near:][::-1]
     lags = [lags_of_stops([lags_of(d, first[d - 1], first[near + d - 1])])[0] for d in range(1, near + 1)]
     early = [
         (shifted(piece[channels:], "blk", d), shifted(piece[:channels], "blk", -d)) for d, piece in enumerate(lags, 1)

time: 135 us -> 135 us (level)
  the two profiles are of different devices: /device:TPU:1 before, /device:TPU:8 now
where the time goes in v18:
time: 135 us; the launch traced here: 134 us
  starting transfers between devices  70 us (52%)
  waiting for transfers between devices  41.1 us (30%)
  other arithmetic  9.1 us (7%)
  matrix products  8.77 us (6%)
  local copies, waits for them, and re-layouts  4.05 us (3%)
    ppermute x14, starting transfers between devices, shifted(): lax.ppermute(x, axis, [(i, (i + by) % length) for i in range(length)])  67.5 us
    ppermute x14, waiting for transfers between devices, shifted(): lax.ppermute(x, axis, [(i, (i + by) % length) for i in range(length)])  32.8 us
    ppermute x1, waiting for transfers between devices, swapped(): return lax.ppermute(x, axis, [(i, i ^ 1) for i in range(length)])  8.32 us
    unnamed x8, local copies, waits for them, and re-layouts  3.71 us
    dot_general x3, matrix products, lags_of_stops(): jnp.dot(jnp.concatenate(crosses, axis=0), back_table, precision=lax.Preci...  3.56 us
    another operation x2, other arithmetic  2.96 us
    dot_general x8, matrix products, pick_rows(): jnp.einsum('gp,spk->sgk', picks, block, preferred_element_type=jnp.float32)  2.71 us
  transfers between devices with their start and end apart: 15, of which 7 were waited for; matrix products, arithmetic and copies ran while one was open for 3% of the time, Pallas kernels for 0%

profile of v18, /device:TPU:8, one launch (start us, length us, event | category | flops | bytes accessed | tf_op | source)
XLA Modules:
  0.0 134.1 jit_solution(7477080517114553010)
XLA Ops:
  0.6 1.0 fusion.47
  1.7 0.6 fusion.53
  2.3 1.8 %copy.12 = bf16[32,8,2048]{2,0,1:T(8,128)(2,1)S(1)} copy(bf16[32,8,2048]{2,1,0:T(8,128)(2,1)} %param.5) | data formatting | bytes 2097152 | tf_op args[0]
  4.1 3.0 %subtract_convert_fusion = (bf16[32,64,1024]{2,1,0:T(8,128)(2,1)S(1)}, bf16[32,64,1024]{2,1,0:T(8,128)(2,1)S(1)}) fusion(f32[64,1024]{1,0:T(8,128)S(1)} %get-tuple-element.101, f32[32,1024]{1,0:T(8,128)S(1)} %get-tuple-element.98, f32[64,1024]{1,0:T(8,128)S(1)} %get-tuple-element.102, f32[32,1024]{1,0:T(8,128)S(1)} %get-tuple-element.97), kind=kLoop, calls=%fused_computation.5 | loop fusion | flops 18874368 | bytes 9175040 | tf_op jit(solution)/shard_map/convert.7
  7.1 2.5 %fusion.4 = (f32[256]{0:T(256)S(1)}, f32[2048,256]{0,1:T(8,128)S(1)}) fusion(bf16[256,2048]{1,0:T(8,128)(2,1)S(1)} %bitcast.110, bf16[2048,1024]{1,0:T(8,128)(2,1)S(1)} %bitcast.108, bf16[2048,1024]{1,0:T(8,128)(2,1)S(1)} %bitcast.107), kind=kOutput, calls=%fused_computation.16 | convolution fusion | flops 2165309184 | bytes 11535360 | tf_op jit(solution)/shard_map/dot_general | solution.py:81
  10.6 7.7 %collective-permute-start.2 = (bf16[4,32,2048]{2,1,0:T(8,128)(2,1)S(1)}, bf16[4,32,2048]{2,1,0:T(8,128)(2,1)S(1)}, u32[]{:S(2)}, u32[]{:S(2)}) collective-permute-start(bf16[4,32,2048]{2,1,0:T(8,128)(2,1)S(1)} %scatter.4), channel_id=1, source_target_pairs={{0,508},{2,510},{4,0},{6,2},{8,4},{10,6},{12,8},{14,10},{16,12},{1... | collective-permute-start | bytes 1572872 | tf_op jit(solution)/shard_map/ppermute | solution.py:13
  18.3 10.1 %collective-permute-start.3 = (bf16[4,32,2048]{2,1,0:T(8,128)(2,1)S(1)}, bf16[4,32,2048]{2,1,0:T(8,128)(2,1)S(1)}, u32[]{:S(2)}, u32[]{:S(2)}) collective-permute-start(bf16[4,32,2048]{2,1,0:T(8,128)(2,1)S(1)} %scatter.4), channel_id=1, source_target_pairs={{0,510},{2,0},{4,2},{6,4},{8,6},{10,8},{12,10},{14,12},{16,14},{18... | collective-permute-start | bytes 1572872 | tf_op jit(solution)/shard_map/ppermute | solution.py:13
  28.4 1.9 %collective-permute-start = (bf16[4,32,2048]{2,1,0:T(8,128)(2,1)S(1)}, bf16[4,32,2048]{2,1,0:T(8,128)(2,1)S(1)}, u32[]{:S(2)}, u32[]{:S(2)}) collective-permute-start(bf16[4,32,2048]{2,1,0:T(8,128)(2,1)S(1)} %get-tuple-element.64), channel_id=1, source_target_pairs={{0,4},{2,6},{4,8},{6,10},{8,12},{10,14},{12,16},{14,18},{16,20},{1... | collective-permute-start | bytes 1572872 | tf_op jit(solution)/shard_map/ppermute | solution.py:13
  30.3 1.9 %collective-permute-start.1 = (bf16[4,32,2048]{2,1,0:T(8,128)(2,1)S(1)}, bf16[4,32,2048]{2,1,0:T(8,128)(2,1)S(1)}, u32[]{:S(2)}, u32[]{:S(2)}) collective-permute-start(bf16[4,32,2048]{2,1,0:T(8,128)(2,1)S(1)} %get-tuple-element.64), channel_id=1, source_target_pairs={{0,2},{2,4},{4,6},{6,8},{8,10},{10,12},{12,14},{14,16},{16,18},{18... | collective-permute-start | bytes 1572872 | tf_op jit(solution)/shard_map/ppermute | solution.py:13
  33.2 1.9 %collective-permute-done.3 = bf16[4,32,2048]{2,1,0:T(8,128)(2,1)S(1)} collective-permute-done((bf16[4,32,2048]{2,1,0:T(8,128)(2,1)S(1)}, bf16[4,32,2048]{2,1,0:T(8,128)(2,1)S(1)}, u32[]{:S(2)}, u32[]{:S(2)}) %collective-permute-start.3) | collective-permute-done | bytes 524320 | tf_op jit(solution)/shard_map/ppermute | solution.py:13
  35.1 10.1 %collective-permute-done = bf16[4,32,2048]{2,1,0:T(8,128)(2,1)S(1)} collective-permute-done((bf16[4,32,2048]{2,1,0:T(8,128)(2,1)S(1)}, bf16[4,32,2048]{2,1,0:T(8,128)(2,1)S(1)}, u32[]{:S(2)}, u32[]{:S(2)}) %collective-permute-start) | collective-permute-done | bytes 524320 | tf_op jit(solution)/shard_map/ppermute | solution.py:13
  45.2 4.2 %collective-permute-done.1 = bf16[4,32,2048]{2,1,0:T(8,128)(2,1)S(1)} collective-permute-done((bf16[4,32,2048]{2,1,0:T(8,128)(2,1)S(1)}, bf16[4,32,2048]{2,1,0:T(8,128)(2,1)S(1)}, u32[]{:S(2)}, u32[]{:S(2)}) %collective-permute-start.1) | collective-permute-done | bytes 524320 | tf_op jit(solution)/shard_map/ppermute | solution.py:13
  50.9 9.4 %collective-permute-start.5 = (bf16[8,32,2048]{2,1,0:T(8,128)(2,1)S(1)}, bf16[8,32,2048]{2,1,0:T(8,128)(2,1)S(1)}, u32[]{:S(2)}, u32[]{:S(2)}) collective-permute-start(bf16[8,32,2048]{2,1,0:T(8,128)(2,1)S(1)} %pad_maximum_fusion.5), channel_id=1, source_target_pairs={{0,508},{2,510},{4,0},{6,2},{8,4},{10,6},{12,8},{14,10},{16,12},{1... | collective-permute-start | bytes 3145736 | tf_op jit(solution)/shard_map/ppermute | solution.py:13
  60.3 1.9 %collective-permute-start.4 = (bf16[8,32,2048]{2,1,0:T(8,128)(2,1)S(1)}, bf16[8,32,2048]{2,1,0:T(8,128)(2,1)S(1)}, u32[]{:S(2)}, u32[]{:S(2)}) collective-permute-start(bf16[8,32,2048]{2,1,0:T(8,128)(2,1)S(1)} %pad_maximum_fusion.4), channel_id=1, source_target_pairs={{0,4},{2,6},{4,8},{6,10},{8,12},{10,14},{12,16},{14,18},{16,20},{1... | collective-permute-start | bytes 3145736 | tf_op jit(solution)/shard_map/ppermute | solution.py:13
  62.9 1.1 fusion.6
  64.1 1.9 %collective-permute-start.8 = (f32[32,257]{1,0:T(8,128)S(1)}, f32[32,257]{1,0:T(8,128)S(1)}, u32[]{:S(2)}, u32[]{:S(2)}) collective-permute-start(f32[32,257]{1,0:T(8,128)S(1)} %get-tuple-element.85), channel_id=1, source_target_pairs={{0,4},{2,6},{4,8},{6,10},{8,12},{10,14},{12,16},{14,18},{16,20},{1... | collective-permute-start | bytes 98696 | tf_op jit(solution)/shard_map/ppermute | solution.py:13
  66.0 4.1 %collective-permute-start.9 = (f32[32,257]{1,0:T(8,128)S(1)}, f32[32,257]{1,0:T(8,128)S(1)}, u32[]{:S(2)}, u32[]{:S(2)}) collective-permute-start(f32[32,257]{1,0:T(8,128)S(1)} %get-tuple-element.86), channel_id=1, source_target_pairs={{0,508},{2,510},{4,0},{6,2},{8,4},{10,6},{12,8},{14,10},{16,12},{1... | collective-permute-start | bytes 98696 | tf_op jit(solution)/shard_map/ppermute | solution.py:13
  70.8 1.1 fusion.7
  72.0 1.9 %collective-permute-start.6 = (f32[32,257]{1,0:T(8,128)S(1)}, f32[32,257]{1,0:T(8,128)S(1)}, u32[]{:S(2)}, u32[]{:S(2)}) collective-permute-start(f32[32,257]{1,0:T(8,128)S(1)} %get-tuple-element.81), channel_id=1, source_target_pairs={{0,2},{2,4},{4,6},{6,8},{8,10},{10,12},{12,14},{14,16},{16,18},{18... | collective-permute-start | bytes 98696 | tf_op jit(solution)/shard_map/ppermute | solution.py:13
  73.9 12.5 %collective-permute-done.8 = f32[32,257]{1,0:T(8,128)S(1)} collective-permute-done((f32[32,257]{1,0:T(8,128)S(1)}, f32[32,257]{1,0:T(8,128)S(1)}, u32[]{:S(2)}, u32[]{:S(2)}) %collective-permute-start.8) | collective-permute-done | bytes 32928 | tf_op jit(solution)/shard_map/ppermute | solution.py:13
  86.4 6.9 %collective-permute-start.7 = (f32[32,257]{1,0:T(8,128)S(1)}, f32[32,257]{1,0:T(8,128)S(1)}, u32[]{:S(2)}, u32[]{:S(2)}) collective-permute-start(f32[32,257]{1,0:T(8,128)S(1)} %get-tuple-element.82), channel_id=1, source_target_pairs={{0,510},{2,0},{4,2},{6,4},{8,6},{10,8},{12,10},{14,12},{16,14},{18... | collective-permute-start | bytes 98696 | tf_op jit(solution)/shard_map/ppermute | solution.py:13
  93.3 1.7 %collective-permute-done.7 = f32[32,257]{1,0:T(8,128)S(1)} collective-permute-done((f32[32,257]{1,0:T(8,128)S(1)}, f32[32,257]{1,0:T(8,128)S(1)}, u32[]{:S(2)}, u32[]{:S(2)}) %collective-permute-start.7) | collective-permute-done | bytes 32928 | tf_op jit(solution)/shard_map/ppermute | solution.py:13
  97.6 1.3 fusion.5
  98.9 1.9 %collective-permute-start.10 = (f32[32,257]{1,0:T(8,128)S(1)}, f32[32,257]{1,0:T(8,128)S(1)}, u32[]{:S(2)}, u32[]{:S(2)}) collective-permute-start(f32[32,257]{1,0:T(8,128)S(1)} %get-tuple-element.69), channel_id=1, source_target_pairs={{0,6},{2,8},{4,10},{6,12},{8,14},{10,16},{12,18},{14,20},{16,22},{... | collective-permute-start | bytes 98696 | tf_op jit(solution)/shard_map/ppermute | solution.py:13
  100.8 1.9 %collective-permute-start.11 = (f32[32,257]{1,0:T(8,128)S(1)}, f32[32,257]{1,0:T(8,128)S(1)}, u32[]{:S(2)}, u32[]{:S(2)}) collective-permute-start(f32[32,257]{1,0:T(8,128)S(1)} %get-tuple-element.76), channel_id=1, source_target_pairs={{0,8},{2,10},{4,12},{6,14},{8,16},{10,18},{12,20},{14,22},{16,24},... | collective-permute-start | bytes 98696 | tf_op jit(solution)/shard_map/ppermute | solution.py:13
  102.8 11.3 %collective-permute-start.12 = (f32[32,257]{1,0:T(8,128)S(1)}, f32[32,257]{1,0:T(8,128)S(1)}, u32[]{:S(2)}, u32[]{:S(2)}) collective-permute-start(f32[32,257]{1,0:T(8,128)S(1)} %get-tuple-element.75), channel_id=1, source_target_pairs={{0,506},{2,508},{4,510},{6,0},{8,2},{10,4},{12,6},{14,8},{16,10},{... | collective-permute-start | bytes 98696 | tf_op jit(solution)/shard_map/ppermute | solution.py:13
  114.1 4.5 %collective-permute-start.13 = (f32[32,257]{1,0:T(8,128)S(1)}, f32[32,257]{1,0:T(8,128)S(1)}, u32[]{:S(2)}, u32[]{:S(2)}) collective-permute-start(f32[32,257]{1,0:T(8,128)S(1)} %get-tuple-element.74), channel_id=1, source_target_pairs={{0,504},{2,506},{4,508},{6,510},{8,0},{10,2},{12,4},{14,6},{16,8},... | collective-permute-start | bytes 98696 | tf_op jit(solution)/shard_map/ppermute | solution.py:13
  118.7 2.4 %collective-permute-done.13 = f32[32,257]{1,0:T(8,128)S(1)} collective-permute-done((f32[32,257]{1,0:T(8,128)S(1)}, f32[32,257]{1,0:T(8,128)S(1)}, u32[]{:S(2)}, u32[]{:S(2)}) %collective-permute-start.13) | collective-permute-done | bytes 32928 | tf_op jit(solution)/shard_map/ppermute | solution.py:13
  121.2 2.5 %collective-permute-start.14 = (f32[2,32,4,257]{3,1,2,0:T(8,128)S(1)}, f32[2,32,4,257]{3,1,2,0:T(8,128)S(1)}, u32[]{:S(2)}, u32[]{:S(2)}) collective-permute-start(f32[2,32,4,257]{3,1,2,0:T(8,128)S(1)} %pad_maximum_fusion.6), channel_id=1, source_target_pairs={{0,1},{1,0},{2,3},{3,2},{4,5},{5,4},{6,7},{7,6},{8,9},{9,8},{10,11... | collective-permute-start | bytes 789512 | tf_op jit(solution)/shard_map/ppermute | solution.py:18
  123.7 8.3 %collective-permute-done.14 = f32[2,32,4,257]{3,1,2,0:T(8,128)S(1)} collective-permute-done((f32[2,32,4,257]{3,1,2,0:T(8,128)S(1)}, f32[2,32,4,257]{3,1,2,0:T(8,128)S(1)}, u32[]{:S(2)}, u32[]{:S(2)}) %collective-permute-start.14) | collective-permute-done | bytes 263200 | tf_op jit(solution)/shard_map/ppermute | solution.py:18
  132.5 0.8 copy.19
  133.3 0.8 copy.18
  (58 shorter events, 7.9 us)
Async XLA Ops:
  7.0 2.6 %copy-start.1 = (s32[32]{0:T(128)S(1)}, s32[32]{0:T(128)}, u32[]{:S(2)}) copy-start(s32[32]{0:T(128)} %param.7) | copy-start | bytes 388
  9.6 0.7 copy-start
  10.6 22.6 %collective-permute-start.2 = (bf16[4,32,2048]{2,1,0:T(8,128)(2,1)S(1)}, bf16[4,32,2048]{2,1,0:T(8,128)(2,1)S(1)}, u32[]{:S(2)}, u32[]{:S(2)}) collective-permute-start(bf16[4,32,2048]{2,1,0:T(8,128)(2,1)S(1)} %scatter.4), channel_id=1, source_target_pairs={{0,508},{2,510},{4,0},{6,2},{8,4},{10,6},{12,8},{14,10},{16,12},{1... | collective-permute-start | bytes 1572872 | tf_op jit(solution)/shard_map/ppermute | solution.py:13
  18.3 16.8 %collective-permute-start.3 = (bf16[4,32,2048]{2,1,0:T(8,128)(2,1)S(1)}, bf16[4,32,2048]{2,1,0:T(8,128)(2,1)S(1)}, u32[]{:S(2)}, u32[]{:S(2)}) collective-permute-start(bf16[4,32,2048]{2,1,0:T(8,128)(2,1)S(1)} %scatter.4), channel_id=1, source_target_pairs={{0,510},{2,0},{4,2},{6,4},{8,6},{10,8},{12,10},{14,12},{16,14},{18... | collective-permute-start | bytes 1572872 | tf_op jit(solution)/shard_map/ppermute | solution.py:13
  28.4 16.7 %collective-permute-start = (bf16[4,32,2048]{2,1,0:T(8,128)(2,1)S(1)}, bf16[4,32,2048]{2,1,0:T(8,128)(2,1)S(1)}, u32[]{:S(2)}, u32[]{:S(2)}) collective-permute-start(bf16[4,32,2048]{2,1,0:T(8,128)(2,1)S(1)} %get-tuple-element.64), channel_id=1, source_target_pairs={{0,4},{2,6},{4,8},{6,10},{8,12},{10,14},{12,16},{14,18},{16,20},{1... | collective-permute-start | bytes 1572872 | tf_op jit(solution)/shard_map/ppermute | solution.py:13
  30.3 19.0 %collective-permute-start.1 = (bf16[4,32,2048]{2,1,0:T(8,128)(2,1)S(1)}, bf16[4,32,2048]{2,1,0:T(8,128)(2,1)S(1)}, u32[]{:S(2)}, u32[]{:S(2)}) collective-permute-start(bf16[4,32,2048]{2,1,0:T(8,128)(2,1)S(1)} %get-tuple-element.64), channel_id=1, source_target_pairs={{0,2},{2,4},{4,6},{6,8},{8,10},{10,12},{12,14},{14,16},{16,18},{18... | collective-permute-start | bytes 1572872 | tf_op jit(solution)/shard_map/ppermute | solution.py:13
  50.9 44.1 %collective-permute-start.5 = (bf16[8,32,2048]{2,1,0:T(8,128)(2,1)S(1)}, bf16[8,32,2048]{2,1,0:T(8,128)(2,1)S(1)}, u32[]{:S(2)}, u32[]{:S(2)}) collective-permute-start(bf16[8,32,2048]{2,1,0:T(8,128)(2,1)S(1)} %pad_maximum_fusion.5), channel_id=1, source_target_pairs={{0,508},{2,510},{4,0},{6,2},{8,4},{10,6},{12,8},{14,10},{16,12},{1... | collective-permute-start | bytes 3145736 | tf_op jit(solution)/shard_map/ppermute | solution.py:13
  60.3 34.8 %collective-permute-start.4 = (bf16[8,32,2048]{2,1,0:T(8,128)(2,1)S(1)}, bf16[8,32,2048]{2,1,0:T(8,128)(2,1)S(1)}, u32[]{:S(2)}, u32[]{:S(2)}) collective-permute-start(bf16[8,32,2048]{2,1,0:T(8,128)(2,1)S(1)} %pad_maximum_fusion.4), channel_id=1, source_target_pairs={{0,4},{2,6},{4,8},{6,10},{8,12},{10,14},{12,16},{14,18},{16,20},{1... | collective-permute-start | bytes 3145736 | tf_op jit(solution)/shard_map/ppermute | solution.py:13
  64.1 22.4 %collective-permute-start.8 = (f32[32,257]{1,0:T(8,128)S(1)}, f32[32,257]{1,0:T(8,128)S(1)}, u32[]{:S(2)}, u32[]{:S(2)}) collective-permute-start(f32[32,257]{1,0:T(8,128)S(1)} %get-tuple-element.85), channel_id=1, source_target_pairs={{0,4},{2,6},{4,8},{6,10},{8,12},{10,14},{12,16},{14,18},{16,20},{1... | collective-permute-start | bytes 98696 | tf_op jit(solution)/shard_map/ppermute | solution.py:13
  66.0 27.3 %collective-permute-start.9 = (f32[32,257]{1,0:T(8,128)S(1)}, f32[32,257]{1,0:T(8,128)S(1)}, u32[]{:S(2)}, u32[]{:S(2)}) collective-permute-start(f32[32,257]{1,0:T(8,128)S(1)} %get-tuple-element.86), channel_id=1, source_target_pairs={{0,508},{2,510},{4,0},{6,2},{8,4},{10,6},{12,8},{14,10},{16,12},{1... | collective-permute-start | bytes 98696 | tf_op jit(solution)/shard_map/ppermute | solution.py:13
  72.0 21.3 %collective-permute-start.6 = (f32[32,257]{1,0:T(8,128)S(1)}, f32[32,257]{1,0:T(8,128)S(1)}, u32[]{:S(2)}, u32[]{:S(2)}) collective-permute-start(f32[32,257]{1,0:T(8,128)S(1)} %get-tuple-element.81), channel_id=1, source_target_pairs={{0,2},{2,4},{4,6},{6,8},{8,10},{10,12},{12,14},{14,16},{16,18},{18... | collective-permute-start | bytes 98696 | tf_op jit(solution)/shard_map/ppermute | solution.py:13
  86.4 8.6 %collective-permute-start.7 = (f32[32,257]{1,0:T(8,128)S(1)}, f32[32,257]{1,0:T(8,128)S(1)}, u32[]{:S(2)}, u32[]{:S(2)}) collective-permute-start(f32[32,257]{1,0:T(8,128)S(1)} %get-tuple-element.82), channel_id=1, source_target_pairs={{0,510},{2,0},{4,2},{6,4},{8,6},{10,8},{12,10},{14,12},{16,14},{18... | collective-permute-start | bytes 98696 | tf_op jit(solution)/shard_map/ppermute | solution.py:13
  98.9 19.8 %collective-permute-start.10 = (f32[32,257]{1,0:T(8,128)S(1)}, f32[32,257]{1,0:T(8,128)S(1)}, u32[]{:S(2)}, u32[]{:S(2)}) collective-permute-start(f32[32,257]{1,0:T(8,128)S(1)} %get-tuple-element.69), channel_id=1, source_target_pairs={{0,6},{2,8},{4,10},{6,12},{8,14},{10,16},{12,18},{14,20},{16,22},{... | collective-permute-start | bytes 98696 | tf_op jit(solution)/shard_map/ppermute | solution.py:13
  100.8 17.8 %collective-permute-start.11 = (f32[32,257]{1,0:T(8,128)S(1)}, f32[32,257]{1,0:T(8,128)S(1)}, u32[]{:S(2)}, u32[]{:S(2)}) collective-permute-start(f32[32,257]{1,0:T(8,128)S(1)} %get-tuple-element.76), channel_id=1, source_target_pairs={{0,8},{2,10},{4,12},{6,14},{8,16},{10,18},{12,20},{14,22},{16,24},... | collective-permute-start | bytes 98696 | tf_op jit(solution)/shard_map/ppermute | solution.py:13
  102.8 16.0 %collective-permute-start.12 = (f32[32,257]{1,0:T(8,128)S(1)}, f32[32,257]{1,0:T(8,128)S(1)}, u32[]{:S(2)}, u32[]{:S(2)}) collective-permute-start(f32[32,257]{1,0:T(8,128)S(1)} %get-tuple-element.75), channel_id=1, source_target_pairs={{0,506},{2,508},{4,510},{6,0},{8,2},{10,4},{12,6},{14,8},{16,10},{... | collective-permute-start | bytes 98696 | tf_op jit(solution)/shard_map/ppermute | solution.py:13
  114.1 7.0 %collective-permute-start.13 = (f32[32,257]{1,0:T(8,128)S(1)}, f32[32,257]{1,0:T(8,128)S(1)}, u32[]{:S(2)}, u32[]{:S(2)}) collective-permute-start(f32[32,257]{1,0:T(8,128)S(1)} %get-tuple-element.74), channel_id=1, source_target_pairs={{0,504},{2,506},{4,508},{6,510},{8,0},{10,2},{12,4},{14,6},{16,8},... | collective-permute-start | bytes 98696 | tf_op jit(solution)/shard_map/ppermute | solution.py:13
  121.2 10.9 %collective-permute-start.14 = (f32[2,32,4,257]{3,1,2,0:T(8,128)S(1)}, f32[2,32,4,257]{3,1,2,0:T(8,128)S(1)}, u32[]{:S(2)}, u32[]{:S(2)}) collective-permute-start(f32[2,32,4,257]{3,1,2,0:T(8,128)S(1)} %pad_maximum_fusion.6), channel_id=1, source_target_pairs={{0,1},{1,0},{2,3},{3,2},{4,5},{5,4},{6,7},{7,6},{8,9},{9,8},{10,11... | collective-permute-start | bytes 789512 | tf_op jit(solution)/shard_map/ppermute | solution.py:18

commit v19 on v18

--- a/solution.py
+++ b/solution.py
@@ -121,10 +121,10 @@
     early = [
         (shifted(piece[channels:], "blk", d), shifted(piece[:channels], "blk", -d)) for d, piece in enumerate(lags, 1)
     ]
-    far_ahead, far_behind, early = lax.optimization_barrier(
+    far_behind, far_ahead, early = lax.optimization_barrier(
         (
+            shifted(jnp.concatenate(first[near:], axis=0), "blk", -near),
             shifted(jnp.concatenate(first[:near], axis=0), "blk", near),
-            shifted(jnp.concatenate(first[near:], axis=0), "blk", -near),
             early,
         )
     )

time: 135 us -> 136 us (level)
  starting transfers between devices: 70 us -> 83.5 us
  waiting for transfers between devices: 41.1 us -> 28.6 us
    ppermute x14, starting transfers between devices: 67.5 us -> 80.9 us  [shifted(): lax.ppermute(x, axis, [(i, (i + by) % length) for i in range(length)])]
    ppermute x14, waiting for transfers between devices: 32.8 us -> 20.3 us  [shifted(): lax.ppermute(x, axis, [(i, (i + by) % length) for i in range(length)])]
  transfers between devices with their start and end apart: 15 -> 15, of which waited for: 7 -> 6; matrix products, arithmetic and copies ran while one was open for 3% -> 3% of each run, Pallas kernels for 0% -> 0%
where the time goes in v19:
time: 136 us; the launch traced here: 135 us
  starting transfers between devices  83.5 us (61%)
  waiting for transfers between devices  28.6 us (21%)
  other arithmetic  9.1 us (7%)
  matrix products  8.79 us (6%)
  local copies, waits for them, and re-layouts  4.05 us (3%)
    ppermute x14, starting transfers between devices, shifted(): lax.ppermute(x, axis, [(i, (i + by) % length) for i in range(length)])  80.9 us
    ppermute x14, waiting for transfers between devices, shifted(): lax.ppermute(x, axis, [(i, (i + by) % length) for i in range(length)])  20.3 us
    ppermute x1, waiting for transfers between devices, swapped(): return lax.ppermute(x, axis, [(i, i ^ 1) for i in range(length)])  8.33 us
    unnamed x8, local copies, waits for them, and re-layouts  3.71 us
    dot_general x3, matrix products, lags_of_stops(): jnp.dot(jnp.concatenate(crosses, axis=0), back_table, precision=lax.Preci...  3.56 us
    another operation x2, other arithmetic  2.96 us
    dot_general x8, matrix products, pick_rows(): jnp.einsum('gp,spk->sgk', picks, block, preferred_element_type=jnp.float32)  2.74 us
  transfers between devices with their start and end apart: 15, of which 6 were waited for; matrix products, arithmetic and copies ran while one was open for 3% of the time, Pallas kernels for 0%

profile of v19, /device:TPU:8, one launch (start us, length us, event | category | flops | bytes accessed | tf_op | source)
XLA Modules:
  0.0 135.1 jit_solution(11532184183205092876)
XLA Ops:
  0.6 1.0 fusion.47
  1.7 0.6 fusion.53
  2.3 1.8 %copy.12 = bf16[32,8,2048]{2,0,1:T(8,128)(2,1)S(1)} copy(bf16[32,8,2048]{2,1,0:T(8,128)(2,1)} %param.5) | data formatting | bytes 2097152 | tf_op args[0]
  4.1 3.0 %subtract_convert_fusion = (bf16[32,64,1024]{2,1,0:T(8,128)(2,1)S(1)}, bf16[32,64,1024]{2,1,0:T(8,128)(2,1)S(1)}) fusion(f32[64,1024]{1,0:T(8,128)S(1)} %get-tuple-element.101, f32[32,1024]{1,0:T(8,128)S(1)} %get-tuple-element.98, f32[64,1024]{1,0:T(8,128)S(1)} %get-tuple-element.102, f32[32,1024]{1,0:T(8,128)S(1)} %get-tuple-element.97), kind=kLoop, calls=%fused_computation.5 | loop fusion | flops 18874368 | bytes 9175040 | tf_op jit(solution)/shard_map/convert.7
  7.1 2.5 %fusion.4 = (f32[256]{0:T(256)S(1)}, f32[2048,256]{0,1:T(8,128)S(1)}) fusion(bf16[256,2048]{1,0:T(8,128)(2,1)S(1)} %bitcast.110, bf16[2048,1024]{1,0:T(8,128)(2,1)S(1)} %bitcast.108, bf16[2048,1024]{1,0:T(8,128)(2,1)S(1)} %bitcast.107), kind=kOutput, calls=%fused_computation.16 | convolution fusion | flops 2165309184 | bytes 11535360 | tf_op jit(solution)/shard_map/dot_general | solution.py:81
  9.7 0.5 multiply_convert_fusion
  10.6 7.7 %collective-permute-start.2 = (bf16[4,32,2048]{2,1,0:T(8,128)(2,1)S(1)}, bf16[4,32,2048]{2,1,0:T(8,128)(2,1)S(1)}, u32[]{:S(2)}, u32[]{:S(2)}) collective-permute-start(bf16[4,32,2048]{2,1,0:T(8,128)(2,1)S(1)} %scatter.4), channel_id=1, source_target_pairs={{0,508},{2,510},{4,0},{6,2},{8,4},{10,6},{12,8},{14,10},{16,12},{1... | collective-permute-start | bytes 1572872 | tf_op jit(solution)/shard_map/ppermute | solution.py:13
  18.3 10.1 %collective-permute-start.3 = (bf16[4,32,2048]{2,1,0:T(8,128)(2,1)S(1)}, bf16[4,32,2048]{2,1,0:T(8,128)(2,1)S(1)}, u32[]{:S(2)}, u32[]{:S(2)}) collective-permute-start(bf16[4,32,2048]{2,1,0:T(8,128)(2,1)S(1)} %scatter.4), channel_id=1, source_target_pairs={{0,510},{2,0},{4,2},{6,4},{8,6},{10,8},{12,10},{14,12},{16,14},{18... | collective-permute-start | bytes 1572872 | tf_op jit(solution)/shard_map/ppermute | solution.py:13
  28.4 1.9 %collective-permute-start = (bf16[4,32,2048]{2,1,0:T(8,128)(2,1)S(1)}, bf16[4,32,2048]{2,1,0:T(8,128)(2,1)S(1)}, u32[]{:S(2)}, u32[]{:S(2)}) collective-permute-start(bf16[4,32,2048]{2,1,0:T(8,128)(2,1)S(1)} %get-tuple-element.64), channel_id=1, source_target_pairs={{0,4},{2,6},{4,8},{6,10},{8,12},{10,14},{12,16},{14,18},{16,20},{1... | collective-permute-start | bytes 1572872 | tf_op jit(solution)/shard_map/ppermute | solution.py:13
  30.3 1.9 %collective-permute-start.1 = (bf16[4,32,2048]{2,1,0:T(8,128)(2,1)S(1)}, bf16[4,32,2048]{2,1,0:T(8,128)(2,1)S(1)}, u32[]{:S(2)}, u32[]{:S(2)}) collective-permute-start(bf16[4,32,2048]{2,1,0:T(8,128)(2,1)S(1)} %get-tuple-element.64), channel_id=1, source_target_pairs={{0,2},{2,4},{4,6},{6,8},{8,10},{10,12},{12,14},{14,16},{16,18},{18... | collective-permute-start | bytes 1572872 | tf_op jit(solution)/shard_map/ppermute | solution.py:13
  33.2 1.9 %collective-permute-done.3 = bf16[4,32,2048]{2,1,0:T(8,128)(2,1)S(1)} collective-permute-done((bf16[4,32,2048]{2,1,0:T(8,128)(2,1)S(1)}, bf16[4,32,2048]{2,1,0:T(8,128)(2,1)S(1)}, u32[]{:S(2)}, u32[]{:S(2)}) %collective-permute-start.3) | collective-permute-done | bytes 524320 | tf_op jit(solution)/shard_map/ppermute | solution.py:13
  35.1 10.1 %collective-permute-done = bf16[4,32,2048]{2,1,0:T(8,128)(2,1)S(1)} collective-permute-done((bf16[4,32,2048]{2,1,0:T(8,128)(2,1)S(1)}, bf16[4,32,2048]{2,1,0:T(8,128)(2,1)S(1)}, u32[]{:S(2)}, u32[]{:S(2)}) %collective-permute-start) | collective-permute-done | bytes 524320 | tf_op jit(solution)/shard_map/ppermute | solution.py:13
  45.2 4.2 %collective-permute-done.1 = bf16[4,32,2048]{2,1,0:T(8,128)(2,1)S(1)} collective-permute-done((bf16[4,32,2048]{2,1,0:T(8,128)(2,1)S(1)}, bf16[4,32,2048]{2,1,0:T(8,128)(2,1)S(1)}, u32[]{:S(2)}, u32[]{:S(2)}) %collective-permute-start.1) | collective-permute-done | bytes 524320 | tf_op jit(solution)/shard_map/ppermute | solution.py:13
  50.9 1.9 %collective-permute-start.5 = (bf16[8,32,2048]{2,1,0:T(8,128)(2,1)S(1)}, bf16[8,32,2048]{2,1,0:T(8,128)(2,1)S(1)}, u32[]{:S(2)}, u32[]{:S(2)}) collective-permute-start(bf16[8,32,2048]{2,1,0:T(8,128)(2,1)S(1)} %pad_maximum_fusion.5), channel_id=1, source_target_pairs={{0,4},{2,6},{4,8},{6,10},{8,12},{10,14},{12,16},{14,18},{16,20},{1... | collective-permute-start | bytes 3145736 | tf_op jit(solution)/shard_map/ppermute | solution.py:13
  52.8 9.4 %collective-permute-start.4 = (bf16[8,32,2048]{2,1,0:T(8,128)(2,1)S(1)}, bf16[8,32,2048]{2,1,0:T(8,128)(2,1)S(1)}, u32[]{:S(2)}, u32[]{:S(2)}) collective-permute-start(bf16[8,32,2048]{2,1,0:T(8,128)(2,1)S(1)} %pad_maximum_fusion.4), channel_id=1, source_target_pairs={{0,508},{2,510},{4,0},{6,2},{8,4},{10,6},{12,8},{14,10},{16,12},{1... | collective-permute-start | bytes 3145736 | tf_op jit(solution)/shard_map/ppermute | solution.py:13
  62.9 1.1 fusion.6
  64.1 1.9 %collective-permute-start.8 = (f32[32,257]{1,0:T(8,128)S(1)}, f32[32,257]{1,0:T(8,128)S(1)}, u32[]{:S(2)}, u32[]{:S(2)}) collective-permute-start(f32[32,257]{1,0:T(8,128)S(1)} %get-tuple-element.85), channel_id=1, source_target_pairs={{0,4},{2,6},{4,8},{6,10},{8,12},{10,14},{12,16},{14,18},{16,20},{1... | collective-permute-start | bytes 98696 | tf_op jit(solution)/shard_map/ppermute | solution.py:13
  66.0 9.8 %collective-permute-start.9 = (f32[32,257]{1,0:T(8,128)S(1)}, f32[32,257]{1,0:T(8,128)S(1)}, u32[]{:S(2)}, u32[]{:S(2)}) collective-permute-start(f32[32,257]{1,0:T(8,128)S(1)} %get-tuple-element.86), channel_id=1, source_target_pairs={{0,508},{2,510},{4,0},{6,2},{8,4},{10,6},{12,8},{14,10},{16,12},{1... | collective-permute-start | bytes 98696 | tf_op jit(solution)/shard_map/ppermute | solution.py:13
  76.5 1.1 fusion.7
  77.7 1.9 %collective-permute-start.6 = (f32[32,257]{1,0:T(8,128)S(1)}, f32[32,257]{1,0:T(8,128)S(1)}, u32[]{:S(2)}, u32[]{:S(2)}) collective-permute-start(f32[32,257]{1,0:T(8,128)S(1)} %get-tuple-element.81), channel_id=1, source_target_pairs={{0,2},{2,4},{4,6},{6,8},{8,10},{10,12},{12,14},{14,16},{16,18},{18... | collective-permute-start | bytes 98696 | tf_op jit(solution)/shard_map/ppermute | solution.py:13
  79.6 3.6 %collective-permute-start.7 = (f32[32,257]{1,0:T(8,128)S(1)}, f32[32,257]{1,0:T(8,128)S(1)}, u32[]{:S(2)}, u32[]{:S(2)}) collective-permute-start(f32[32,257]{1,0:T(8,128)S(1)} %get-tuple-element.82), channel_id=1, source_target_pairs={{0,510},{2,0},{4,2},{6,4},{8,6},{10,8},{12,10},{14,12},{16,14},{18... | collective-permute-start | bytes 98696 | tf_op jit(solution)/shard_map/ppermute | solution.py:13
  83.3 1.7 %collective-permute-done.7 = f32[32,257]{1,0:T(8,128)S(1)} collective-permute-done((f32[32,257]{1,0:T(8,128)S(1)}, f32[32,257]{1,0:T(8,128)S(1)}, u32[]{:S(2)}, u32[]{:S(2)}) %collective-permute-start.7) | collective-permute-done | bytes 32928 | tf_op jit(solution)/shard_map/ppermute | solution.py:13
  87.6 1.3 fusion.5
  88.9 1.9 %collective-permute-start.10 = (f32[32,257]{1,0:T(8,128)S(1)}, f32[32,257]{1,0:T(8,128)S(1)}, u32[]{:S(2)}, u32[]{:S(2)}) collective-permute-start(f32[32,257]{1,0:T(8,128)S(1)} %get-tuple-element.69), channel_id=1, source_target_pairs={{0,6},{2,8},{4,10},{6,12},{8,14},{10,16},{12,18},{14,20},{16,22},{... | collective-permute-start | bytes 98696 | tf_op jit(solution)/shard_map/ppermute | solution.py:13
  90.9 1.9 %collective-permute-start.11 = (f32[32,257]{1,0:T(8,128)S(1)}, f32[32,257]{1,0:T(8,128)S(1)}, u32[]{:S(2)}, u32[]{:S(2)}) collective-permute-start(f32[32,257]{1,0:T(8,128)S(1)} %get-tuple-element.76), channel_id=1, source_target_pairs={{0,8},{2,10},{4,12},{6,14},{8,16},{10,18},{12,20},{14,22},{16,24},... | collective-permute-start | bytes 98696 | tf_op jit(solution)/shard_map/ppermute | solution.py:13
  92.8 22.3 %collective-permute-start.12 = (f32[32,257]{1,0:T(8,128)S(1)}, f32[32,257]{1,0:T(8,128)S(1)}, u32[]{:S(2)}, u32[]{:S(2)}) collective-permute-start(f32[32,257]{1,0:T(8,128)S(1)} %get-tuple-element.75), channel_id=1, source_target_pairs={{0,506},{2,508},{4,510},{6,0},{8,2},{10,4},{12,6},{14,8},{16,10},{... | collective-permute-start | bytes 98696 | tf_op jit(solution)/shard_map/ppermute | solution.py:13
  115.1 4.5 %collective-permute-start.13 = (f32[32,257]{1,0:T(8,128)S(1)}, f32[32,257]{1,0:T(8,128)S(1)}, u32[]{:S(2)}, u32[]{:S(2)}) collective-permute-start(f32[32,257]{1,0:T(8,128)S(1)} %get-tuple-element.74), channel_id=1, source_target_pairs={{0,504},{2,506},{4,508},{6,510},{8,0},{10,2},{12,4},{14,6},{16,8},... | collective-permute-start | bytes 98696 | tf_op jit(solution)/shard_map/ppermute | solution.py:13
  119.7 2.4 %collective-permute-done.13 = f32[32,257]{1,0:T(8,128)S(1)} collective-permute-done((f32[32,257]{1,0:T(8,128)S(1)}, f32[32,257]{1,0:T(8,128)S(1)}, u32[]{:S(2)}, u32[]{:S(2)}) %collective-permute-start.13) | collective-permute-done | bytes 32928 | tf_op jit(solution)/shard_map/ppermute | solution.py:13
  122.1 2.5 %collective-permute-start.14 = (f32[2,32,4,257]{3,1,2,0:T(8,128)S(1)}, f32[2,32,4,257]{3,1,2,0:T(8,128)S(1)}, u32[]{:S(2)}, u32[]{:S(2)}) collective-permute-start(f32[2,32,4,257]{3,1,2,0:T(8,128)S(1)} %pad_maximum_fusion.6), channel_id=1, source_target_pairs={{0,1},{1,0},{2,3},{3,2},{4,5},{5,4},{6,7},{7,6},{8,9},{9,8},{10,11... | collective-permute-start | bytes 789512 | tf_op jit(solution)/shard_map/ppermute | solution.py:18
  124.7 8.3 %collective-permute-done.14 = f32[2,32,4,257]{3,1,2,0:T(8,128)S(1)} collective-permute-done((f32[2,32,4,257]{3,1,2,0:T(8,128)S(1)}, f32[2,32,4,257]{3,1,2,0:T(8,128)S(1)}, u32[]{:S(2)}, u32[]{:S(2)}) %collective-permute-start.14) | collective-permute-done | bytes 263200 | tf_op jit(solution)/shard_map/ppermute | solution.py:18
  133.5 0.8 copy.19
  134.3 0.8 copy.18
  (58 shorter events, 7.4 us)
Async XLA Ops:
  7.0 2.6 %copy-start.1 = (s32[32]{0:T(128)S(1)}, s32[32]{0:T(128)}, u32[]{:S(2)}) copy-start(s32[32]{0:T(128)} %param.7) | copy-start | bytes 388
  9.6 0.7 copy-start
  10.6 22.6 %collective-permute-start.2 = (bf16[4,32,2048]{2,1,0:T(8,128)(2,1)S(1)}, bf16[4,32,2048]{2,1,0:T(8,128)(2,1)S(1)}, u32[]{:S(2)}, u32[]{:S(2)}) collective-permute-start(bf16[4,32,2048]{2,1,0:T(8,128)(2,1)S(1)} %scatter.4), channel_id=1, source_target_pairs={{0,508},{2,510},{4,0},{6,2},{8,4},{10,6},{12,8},{14,10},{16,12},{1... | collective-permute-start | bytes 1572872 | tf_op jit(solution)/shard_map/ppermute | solution.py:13
  18.3 16.8 %collective-permute-start.3 = (bf16[4,32,2048]{2,1,0:T(8,128)(2,1)S(1)}, bf16[4,32,2048]{2,1,0:T(8,128)(2,1)S(1)}, u32[]{:S(2)}, u32[]{:S(2)}) collective-permute-start(bf16[4,32,2048]{2,1,0:T(8,128)(2,1)S(1)} %scatter.4), channel_id=1, source_target_pairs={{0,510},{2,0},{4,2},{6,4},{8,6},{10,8},{12,10},{14,12},{16,14},{18... | collective-permute-start | bytes 1572872 | tf_op jit(solution)/shard_map/ppermute | solution.py:13
  28.4 16.7 %collective-permute-start = (bf16[4,32,2048]{2,1,0:T(8,128)(2,1)S(1)}, bf16[4,32,2048]{2,1,0:T(8,128)(2,1)S(1)}, u32[]{:S(2)}, u32[]{:S(2)}) collective-permute-start(bf16[4,32,2048]{2,1,0:T(8,128)(2,1)S(1)} %get-tuple-element.64), channel_id=1, source_target_pairs={{0,4},{2,6},{4,8},{6,10},{8,12},{10,14},{12,16},{14,18},{16,20},{1... | collective-permute-start | bytes 1572872 | tf_op jit(solution)/shard_map/ppermute | solution.py:13
  30.3 19.0 %collective-permute-start.1 = (bf16[4,32,2048]{2,1,0:T(8,128)(2,1)S(1)}, bf16[4,32,2048]{2,1,0:T(8,128)(2,1)S(1)}, u32[]{:S(2)}, u32[]{:S(2)}) collective-permute-start(bf16[4,32,2048]{2,1,0:T(8,128)(2,1)S(1)} %get-tuple-element.64), channel_id=1, source_target_pairs={{0,2},{2,4},{4,6},{6,8},{8,10},{10,12},{12,14},{14,16},{16,18},{18... | collective-permute-start | bytes 1572872 | tf_op jit(solution)/shard_map/ppermute | solution.py:13
  50.9 34.1 %collective-permute-start.5 = (bf16[8,32,2048]{2,1,0:T(8,128)(2,1)S(1)}, bf16[8,32,2048]{2,1,0:T(8,128)(2,1)S(1)}, u32[]{:S(2)}, u32[]{:S(2)}) collective-permute-start(bf16[8,32,2048]{2,1,0:T(8,128)(2,1)S(1)} %pad_maximum_fusion.5), channel_id=1, source_target_pairs={{0,4},{2,6},{4,8},{6,10},{8,12},{10,14},{12,16},{14,18},{16,20},{1... | collective-permute-start | bytes 3145736 | tf_op jit(solution)/shard_map/ppermute | solution.py:13
  52.8 32.2 %collective-permute-start.4 = (bf16[8,32,2048]{2,1,0:T(8,128)(2,1)S(1)}, bf16[8,32,2048]{2,1,0:T(8,128)(2,1)S(1)}, u32[]{:S(2)}, u32[]{:S(2)}) collective-permute-start(bf16[8,32,2048]{2,1,0:T(8,128)(2,1)S(1)} %pad_maximum_fusion.4), channel_id=1, source_target_pairs={{0,508},{2,510},{4,0},{6,2},{8,4},{10,6},{12,8},{14,10},{16,12},{1... | collective-permute-start | bytes 3145736 | tf_op jit(solution)/shard_map/ppermute | solution.py:13
  64.1 15.6 %collective-permute-start.8 = (f32[32,257]{1,0:T(8,128)S(1)}, f32[32,257]{1,0:T(8,128)S(1)}, u32[]{:S(2)}, u32[]{:S(2)}) collective-permute-start(f32[32,257]{1,0:T(8,128)S(1)} %get-tuple-element.85), channel_id=1, source_target_pairs={{0,4},{2,6},{4,8},{6,10},{8,12},{10,14},{12,16},{14,18},{16,20},{1... | collective-permute-start | bytes 98696 | tf_op jit(solution)/shard_map/ppermute | solution.py:13
  66.0 17.3 %collective-permute-start.9 = (f32[32,257]{1,0:T(8,128)S(1)}, f32[32,257]{1,0:T(8,128)S(1)}, u32[]{:S(2)}, u32[]{:S(2)}) collective-permute-start(f32[32,257]{1,0:T(8,128)S(1)} %get-tuple-element.86), channel_id=1, source_target_pairs={{0,508},{2,510},{4,0},{6,2},{8,4},{10,6},{12,8},{14,10},{16,12},{1... | collective-permute-start | bytes 98696 | tf_op jit(solution)/shard_map/ppermute | solution.py:13
  77.7 5.6 %collective-permute-start.6 = (f32[32,257]{1,0:T(8,128)S(1)}, f32[32,257]{1,0:T(8,128)S(1)}, u32[]{:S(2)}, u32[]{:S(2)}) collective-permute-start(f32[32,257]{1,0:T(8,128)S(1)} %get-tuple-element.81), channel_id=1, source_target_pairs={{0,2},{2,4},{4,6},{6,8},{8,10},{10,12},{12,14},{14,16},{16,18},{18... | collective-permute-start | bytes 98696 | tf_op jit(solution)/shard_map/ppermute | solution.py:13
  79.6 5.4 %collective-permute-start.7 = (f32[32,257]{1,0:T(8,128)S(1)}, f32[32,257]{1,0:T(8,128)S(1)}, u32[]{:S(2)}, u32[]{:S(2)}) collective-permute-start(f32[32,257]{1,0:T(8,128)S(1)} %get-tuple-element.82), channel_id=1, source_target_pairs={{0,510},{2,0},{4,2},{6,4},{8,6},{10,8},{12,10},{14,12},{16,14},{18... | collective-permute-start | bytes 98696 | tf_op jit(solution)/shard_map/ppermute | solution.py:13
  88.9 30.7 %collective-permute-start.10 = (f32[32,257]{1,0:T(8,128)S(1)}, f32[32,257]{1,0:T(8,128)S(1)}, u32[]{:S(2)}, u32[]{:S(2)}) collective-permute-start(f32[32,257]{1,0:T(8,128)S(1)} %get-tuple-element.69), channel_id=1, source_target_pairs={{0,6},{2,8},{4,10},{6,12},{8,14},{10,16},{12,18},{14,20},{16,22},{... | collective-permute-start | bytes 98696 | tf_op jit(solution)/shard_map/ppermute | solution.py:13
  90.9 28.8 %collective-permute-start.11 = (f32[32,257]{1,0:T(8,128)S(1)}, f32[32,257]{1,0:T(8,128)S(1)}, u32[]{:S(2)}, u32[]{:S(2)}) collective-permute-start(f32[32,257]{1,0:T(8,128)S(1)} %get-tuple-element.76), channel_id=1, source_target_pairs={{0,8},{2,10},{4,12},{6,14},{8,16},{10,18},{12,20},{14,22},{16,24},... | collective-permute-start | bytes 98696 | tf_op jit(solution)/shard_map/ppermute | solution.py:13
  92.8 26.9 %collective-permute-start.12 = (f32[32,257]{1,0:T(8,128)S(1)}, f32[32,257]{1,0:T(8,128)S(1)}, u32[]{:S(2)}, u32[]{:S(2)}) collective-permute-start(f32[32,257]{1,0:T(8,128)S(1)} %get-tuple-element.75), channel_id=1, source_target_pairs={{0,506},{2,508},{4,510},{6,0},{8,2},{10,4},{12,6},{14,8},{16,10},{... | collective-permute-start | bytes 98696 | tf_op jit(solution)/shard_map/ppermute | solution.py:13
  115.1 7.0 %collective-permute-start.13 = (f32[32,257]{1,0:T(8,128)S(1)}, f32[32,257]{1,0:T(8,128)S(1)}, u32[]{:S(2)}, u32[]{:S(2)}) collective-permute-start(f32[32,257]{1,0:T(8,128)S(1)} %get-tuple-element.74), channel_id=1, source_target_pairs={{0,504},{2,506},{4,508},{6,510},{8,0},{10,2},{12,4},{14,6},{16,8},... | collective-permute-start | bytes 98696 | tf_op jit(solution)/shard_map/ppermute | solution.py:13
  122.1 10.9 %collective-permute-start.14 = (f32[2,32,4,257]{3,1,2,0:T(8,128)S(1)}, f32[2,32,4,257]{3,1,2,0:T(8,128)S(1)}, u32[]{:S(2)}, u32[]{:S(2)}) collective-permute-start(f32[2,32,4,257]{3,1,2,0:T(8,128)S(1)} %pad_maximum_fusion.6), channel_id=1, source_target_pairs={{0,1},{1,0},{2,3},{3,2},{4,5},{5,4},{6,7},{7,6},{8,9},{9,8},{10,11... | collective-permute-start | bytes 789512 | tf_op jit(solution)/shard_map/ppermute | solution.py:18

commit v20 on v18

--- a/solution.py
+++ b/solution.py
@@ -78,11 +78,7 @@
     channels, segments, length = samples.shape
     half_len = length // 2
     stops = offsets.shape[0]
-    spectrum = jnp.dot(
-        jnp.swapaxes(samples, 0, 1).reshape(segments * channels, length),
-        forward_table(length),
-        preferred_element_type=jnp.float32,
-    ).reshape(segments, channels, length)
+    spectrum = jnp.einsum("csn,nk->sck", samples, forward_table(length), preferred_element_type=jnp.float32)
     keep = (1 - bad_mask).astype(jnp.float32)
     white = whiten(spectrum, keep[None, :, None], half_len)
     split = segments // 2

time: 135 us -> 136 us (level)
  the two profiles are of different devices: /device:TPU:8 before, /device:TPU:1 now
where the time goes in v20:
time: 136 us; the launch traced here: 133 us
  starting transfers between devices  71.5 us (53%)
  waiting for transfers between devices  37.8 us (28%)
  other arithmetic  10.1 us (7%)
  matrix products  8.91 us (7%)
  local copies, waits for them, and re-layouts  3.52 us (3%)
    ppermute x14, starting transfers between devices, shifted(): lax.ppermute(x, axis, [(i, (i + by) % length) for i in range(length)])  69.3 us
    ppermute x14, waiting for transfers between devices, shifted(): lax.ppermute(x, axis, [(i, (i + by) % length) for i in range(length)])  30.9 us
    ppermute x1, waiting for transfers between devices, swapped(): return lax.ppermute(x, axis, [(i, i ^ 1) for i in range(length)])  6.97 us
    dot_general x3, matrix products, lags_of_stops(): jnp.dot(jnp.concatenate(crosses, axis=0), back_table, precision=lax.Preci...  3.55 us
    another operation x2, other arithmetic  2.96 us
    dot_general x8, matrix products, pick_rows(): jnp.einsum('gp,spk->sgk', picks, block, preferred_element_type=jnp.float32)  2.74 us
  transfers between devices with their start and end apart: 15, of which 6 were waited for; matrix products, arithmetic and copies ran while one was open for 3% of the time, Pallas kernels for 0%

profile of v20, /device:TPU:1, one launch (start us, length us, event | category | flops | bytes accessed | tf_op | source)
XLA Modules:
  0.0 133.0 jit_solution(10803896727672498601)
XLA Ops:
  0.6 1.0 fusion.47
  1.7 0.6 fusion.53
  2.3 3.0 %subtract_convert_fusion = (bf16[32,64,1024]{2,1,0:T(8,128)(2,1)S(1)}, bf16[32,64,1024]{2,1,0:T(8,128)(2,1)S(1)}) fusion(f32[64,1024]{1,0:T(8,128)S(1)} %get-tuple-element.101, f32[32,1024]{1,0:T(8,128)S(1)} %get-tuple-element.98, f32[64,1024]{1,0:T(8,128)S(1)} %get-tuple-element.102, f32[32,1024]{1,0:T(8,128)S(1)} %get-tuple-element.97), kind=kLoop, calls=%fused_computation.5 | loop fusion | flops 18874368 | bytes 9175040 | tf_op jit(solution)/shard_map/convert.7
  5.3 2.6 %multiply_reduce_fusion = (f32[8,32]{1,0:T(8,128)S(1)}, f32[8,32,2048]{2,1,0:T(8,128)S(1)}) fusion(bf16[32,8,2048]{2,1,0:T(8,128)(2,1)S(1)} %copy-done, bf16[2048,1024]{1,0:T(8,128)(2,1)S(1)} %bitcast.107, bf16[2048,1024]{1,0:T(8,128)(2,1)S(1)} %bitcast.106), kind=kOutput, calls=%fused_computation.17 | convolution fusion | flops 2165309184 | bytes 11535360 | tf_op jit(solution)/shard_map/csn,nk->sck/dot_general | solution.py:81
  8.4 1.2 slice_convert_fusion
  9.7 1.4 %scatter.4 = bf16[4,32,2048]{2,1,0:T(8,128)(2,1)} dynamic-update-slice(bf16[4,32,2048]{2,1,0:T(8,128)(2,1)} %get-tuple-element.63, bf16[4,32,1]{2,1,0:T(8,128)(2,1)S(1)} %copy.14, s32[]{:T(128)} %constant.84.clone.1, s32[]{:T(128)} %constant.84.clone.1, s32[]{:T(128)} %constant.92.clone.1) | dynamic-update-slice | bytes 516 | tf_op jit(solution)/shard_map/scatter | solution.py:90
  11.2 16.9 %collective-permute-start.2 = (bf16[4,32,2048]{2,1,0:T(8,128)(2,1)}, bf16[4,32,2048]{2,1,0:T(8,128)(2,1)S(1)}, u32[]{:S(2)}, u32[]{:S(2)}) collective-permute-start(bf16[4,32,2048]{2,1,0:T(8,128)(2,1)} %scatter.4), channel_id=1, source_target_pairs={{0,508},{2,510},{4,0},{6,2},{8,4},{10,6},{12,8},{14,10},{16,12},{1... | collective-permute-start | bytes 1572872 | tf_op jit(solution)/shard_map/ppermute | solution.py:13
  28.0 2.9 %collective-permute-start.3 = (bf16[4,32,2048]{2,1,0:T(8,128)(2,1)}, bf16[4,32,2048]{2,1,0:T(8,128)(2,1)S(1)}, u32[]{:S(2)}, u32[]{:S(2)}) collective-permute-start(bf16[4,32,2048]{2,1,0:T(8,128)(2,1)} %scatter.4), channel_id=1, source_target_pairs={{0,510},{2,0},{4,2},{6,4},{8,6},{10,8},{12,10},{14,12},{16,14},{18... | collective-permute-start | bytes 1572872 | tf_op jit(solution)/shard_map/ppermute | solution.py:13
  30.9 1.9 %collective-permute-start = (bf16[4,32,2048]{2,1,0:T(8,128)(2,1)}, bf16[4,32,2048]{2,1,0:T(8,128)(2,1)S(1)}, u32[]{:S(2)}, u32[]{:S(2)}) collective-permute-start(bf16[4,32,2048]{2,1,0:T(8,128)(2,1)} %get-tuple-element.64), channel_id=1, source_target_pairs={{0,4},{2,6},{4,8},{6,10},{8,12},{10,14},{12,16},{14,18},{16,20},{1... | collective-permute-start | bytes 1572872 | tf_op jit(solution)/shard_map/ppermute | solution.py:13
  32.8 2.7 %collective-permute-start.1 = (bf16[4,32,2048]{2,1,0:T(8,128)(2,1)}, bf16[4,32,2048]{2,1,0:T(8,128)(2,1)S(1)}, u32[]{:S(2)}, u32[]{:S(2)}) collective-permute-start(bf16[4,32,2048]{2,1,0:T(8,128)(2,1)} %get-tuple-element.64), channel_id=1, source_target_pairs={{0,2},{2,4},{4,6},{6,8},{8,10},{10,12},{12,14},{14,16},{16,18},{18... | collective-permute-start | bytes 1572872 | tf_op jit(solution)/shard_map/ppermute | solution.py:13
  36.5 2.4 %collective-permute-done.2 = bf16[4,32,2048]{2,1,0:T(8,128)(2,1)S(1)} collective-permute-done((bf16[4,32,2048]{2,1,0:T(8,128)(2,1)}, bf16[4,32,2048]{2,1,0:T(8,128)(2,1)S(1)}, u32[]{:S(2)}, u32[]{:S(2)}) %collective-permute-start.2) | collective-permute-done | bytes 524320 | tf_op jit(solution)/shard_map/ppermute | solution.py:13
  38.9 12.8 %collective-permute-done = bf16[4,32,2048]{2,1,0:T(8,128)(2,1)S(1)} collective-permute-done((bf16[4,32,2048]{2,1,0:T(8,128)(2,1)}, bf16[4,32,2048]{2,1,0:T(8,128)(2,1)S(1)}, u32[]{:S(2)}, u32[]{:S(2)}) %collective-permute-start) | collective-permute-done | bytes 524320 | tf_op jit(solution)/shard_map/ppermute | solution.py:13
  53.2 7.9 %collective-permute-start.5 = (bf16[8,32,2048]{2,1,0:T(8,128)(2,1)S(1)}, bf16[8,32,2048]{2,1,0:T(8,128)(2,1)S(1)}, u32[]{:S(2)}, u32[]{:S(2)}) collective-permute-start(bf16[8,32,2048]{2,1,0:T(8,128)(2,1)S(1)} %pad_maximum_fusion.5), channel_id=1, source_target_pairs={{0,508},{2,510},{4,0},{6,2},{8,4},{10,6},{12,8},{14,10},{16,12},{1... | collective-permute-start | bytes 3145736 | tf_op jit(solution)/shard_map/ppermute | solution.py:13
  61.1 1.9 %collective-permute-start.4 = (bf16[8,32,2048]{2,1,0:T(8,128)(2,1)S(1)}, bf16[8,32,2048]{2,1,0:T(8,128)(2,1)S(1)}, u32[]{:S(2)}, u32[]{:S(2)}) collective-permute-start(bf16[8,32,2048]{2,1,0:T(8,128)(2,1)S(1)} %pad_maximum_fusion.4), channel_id=1, source_target_pairs={{0,4},{2,6},{4,8},{6,10},{8,12},{10,14},{12,16},{14,18},{16,20},{1... | collective-permute-start | bytes 3145736 | tf_op jit(solution)/shard_map/ppermute | solution.py:13
  63.7 1.1 fusion.5
  64.9 1.9 %collective-permute-start.8 = (f32[32,257]{1,0:T(8,128)S(1)}, f32[32,257]{1,0:T(8,128)S(1)}, u32[]{:S(2)}, u32[]{:S(2)}) collective-permute-start(f32[32,257]{1,0:T(8,128)S(1)} %get-tuple-element.85), channel_id=1, source_target_pairs={{0,4},{2,6},{4,8},{6,10},{8,12},{10,14},{12,16},{14,18},{16,20},{1... | collective-permute-start | bytes 98696 | tf_op jit(solution)/shard_map/ppermute | solution.py:13
  66.8 9.3 %collective-permute-start.9 = (f32[32,257]{1,0:T(8,128)S(1)}, f32[32,257]{1,0:T(8,128)S(1)}, u32[]{:S(2)}, u32[]{:S(2)}) collective-permute-start(f32[32,257]{1,0:T(8,128)S(1)} %get-tuple-element.86), channel_id=1, source_target_pairs={{0,508},{2,510},{4,0},{6,2},{8,4},{10,6},{12,8},{14,10},{16,12},{1... | collective-permute-start | bytes 98696 | tf_op jit(solution)/shard_map/ppermute | solution.py:13
  76.8 1.1 fusion.6
  78.0 1.9 %collective-permute-start.6 = (f32[32,257]{1,0:T(8,128)S(1)}, f32[32,257]{1,0:T(8,128)S(1)}, u32[]{:S(2)}, u32[]{:S(2)}) collective-permute-start(f32[32,257]{1,0:T(8,128)S(1)} %get-tuple-element.81), channel_id=1, source_target_pairs={{0,2},{2,4},{4,6},{6,8},{8,10},{10,12},{12,14},{14,16},{16,18},{18... | collective-permute-start | bytes 98696 | tf_op jit(solution)/shard_map/ppermute | solution.py:13
  79.9 13.5 %collective-permute-done.8 = f32[32,257]{1,0:T(8,128)S(1)} collective-permute-done((f32[32,257]{1,0:T(8,128)S(1)}, f32[32,257]{1,0:T(8,128)S(1)}, u32[]{:S(2)}, u32[]{:S(2)}) %collective-permute-start.8) | collective-permute-done | bytes 32928 | tf_op jit(solution)/shard_map/ppermute | solution.py:13
  93.4 4.4 %collective-permute-start.7 = (f32[32,257]{1,0:T(8,128)S(1)}, f32[32,257]{1,0:T(8,128)S(1)}, u32[]{:S(2)}, u32[]{:S(2)}) collective-permute-start(f32[32,257]{1,0:T(8,128)S(1)} %get-tuple-element.82), channel_id=1, source_target_pairs={{0,510},{2,0},{4,2},{6,4},{8,6},{10,8},{12,10},{14,12},{16,14},{18... | collective-permute-start | bytes 98696 | tf_op jit(solution)/shard_map/ppermute | solution.py:13
  97.8 1.0 collective-permute-done.7
  101.4 1.3 fusion.4
  102.7 1.9 %collective-permute-start.10 = (f32[32,257]{1,0:T(8,128)S(1)}, f32[32,257]{1,0:T(8,128)S(1)}, u32[]{:S(2)}, u32[]{:S(2)}) collective-permute-start(f32[32,257]{1,0:T(8,128)S(1)} %get-tuple-element.69), channel_id=1, source_target_pairs={{0,6},{2,8},{4,10},{6,12},{8,14},{10,16},{12,18},{14,20},{16,22},{... | collective-permute-start | bytes 98696 | tf_op jit(solution)/shard_map/ppermute | solution.py:13
  104.6 1.9 %collective-permute-start.11 = (f32[32,257]{1,0:T(8,128)S(1)}, f32[32,257]{1,0:T(8,128)S(1)}, u32[]{:S(2)}, u32[]{:S(2)}) collective-permute-start(f32[32,257]{1,0:T(8,128)S(1)} %get-tuple-element.76), channel_id=1, source_target_pairs={{0,8},{2,10},{4,12},{6,14},{8,16},{10,18},{12,20},{14,22},{16,24},... | collective-permute-start | bytes 98696 | tf_op jit(solution)/shard_map/ppermute | solution.py:13
  106.5 9.4 %collective-permute-start.12 = (f32[32,257]{1,0:T(8,128)S(1)}, f32[32,257]{1,0:T(8,128)S(1)}, u32[]{:S(2)}, u32[]{:S(2)}) collective-permute-start(f32[32,257]{1,0:T(8,128)S(1)} %get-tuple-element.75), channel_id=1, source_target_pairs={{0,506},{2,508},{4,510},{6,0},{8,2},{10,4},{12,6},{14,8},{16,10},{... | collective-permute-start | bytes 98696 | tf_op jit(solution)/shard_map/ppermute | solution.py:13
  115.9 4.5 %collective-permute-start.13 = (f32[32,257]{1,0:T(8,128)S(1)}, f32[32,257]{1,0:T(8,128)S(1)}, u32[]{:S(2)}, u32[]{:S(2)}) collective-permute-start(f32[32,257]{1,0:T(8,128)S(1)} %get-tuple-element.74), channel_id=1, source_target_pairs={{0,504},{2,506},{4,508},{6,510},{8,0},{10,2},{12,4},{14,6},{16,8},... | collective-permute-start | bytes 98696 | tf_op jit(solution)/shard_map/ppermute | solution.py:13
  120.5 1.1 collective-permute-done.13
  121.7 2.2 %collective-permute-start.14 = (f32[2,32,4,257]{3,1,2,0:T(8,128)S(1)}, f32[2,32,4,257]{3,1,2,0:T(8,128)S(1)}, u32[]{:S(2)}, u32[]{:S(2)}) collective-permute-start(f32[2,32,4,257]{3,1,2,0:T(8,128)S(1)} %pad_maximum_fusion.6), channel_id=1, source_target_pairs={{0,1},{1,0},{2,3},{3,2},{4,5},{5,4},{6,7},{7,6},{8,9},{9,8},{10,11... | collective-permute-start | bytes 789512 | tf_op jit(solution)/shard_map/ppermute | solution.py:18
  123.9 7.0 %collective-permute-done.14 = f32[2,32,4,257]{3,1,2,0:T(8,128)S(1)} collective-permute-done((f32[2,32,4,257]{3,1,2,0:T(8,128)S(1)}, f32[2,32,4,257]{3,1,2,0:T(8,128)S(1)}, u32[]{:S(2)}, u32[]{:S(2)}) %collective-permute-start.14) | collective-permute-done | bytes 263200 | tf_op jit(solution)/shard_map/ppermute | solution.py:18
  131.3 0.8 copy.20
  132.2 0.8 copy.19
  (58 shorter events, 7.6 us)
Async XLA Ops:
  0.6 4.6 %copy-start = (bf16[32,8,2048]{2,1,0:T(8,128)(2,1)S(1)}, bf16[32,8,2048]{2,1,0:T(8,128)(2,1)}, u32[]{:S(2)}) copy-start(bf16[32,8,2048]{2,1,0:T(8,128)(2,1)} %param.5) | copy-start | bytes 3145732
  5.3 2.6 %copy-start.2 = (s32[32]{0:T(128)S(1)}, s32[32]{0:T(128)}, u32[]{:S(2)}) copy-start(s32[32]{0:T(128)} %param.7) | copy-start | bytes 388
  7.9 1.7 %copy-start.1 = (s32[4,32]{1,0:T(4,128)S(1)}, s32[4,32]{1,0:T(4,128)}, u32[]{:S(2)}) copy-start(s32[4,32]{1,0:T(4,128)} %param.6) | copy-start | bytes 1540
  11.2 27.7 %collective-permute-start.2 = (bf16[4,32,2048]{2,1,0:T(8,128)(2,1)}, bf16[4,32,2048]{2,1,0:T(8,128)(2,1)S(1)}, u32[]{:S(2)}, u32[]{:S(2)}) collective-permute-start(bf16[4,32,2048]{2,1,0:T(8,128)(2,1)} %scatter.4), channel_id=1, source_target_pairs={{0,508},{2,510},{4,0},{6,2},{8,4},{10,6},{12,8},{14,10},{16,12},{1... | collective-permute-start | bytes 1572872 | tf_op jit(solution)/shard_map/ppermute | solution.py:13
  28.0 10.9 %collective-permute-start.3 = (bf16[4,32,2048]{2,1,0:T(8,128)(2,1)}, bf16[4,32,2048]{2,1,0:T(8,128)(2,1)S(1)}, u32[]{:S(2)}, u32[]{:S(2)}) collective-permute-start(bf16[4,32,2048]{2,1,0:T(8,128)(2,1)} %scatter.4), channel_id=1, source_target_pairs={{0,510},{2,0},{4,2},{6,4},{8,6},{10,8},{12,10},{14,12},{16,14},{18... | collective-permute-start | bytes 1572872 | tf_op jit(solution)/shard_map/ppermute | solution.py:13
  30.9 20.8 %collective-permute-start = (bf16[4,32,2048]{2,1,0:T(8,128)(2,1)}, bf16[4,32,2048]{2,1,0:T(8,128)(2,1)S(1)}, u32[]{:S(2)}, u32[]{:S(2)}) collective-permute-start(bf16[4,32,2048]{2,1,0:T(8,128)(2,1)} %get-tuple-element.64), channel_id=1, source_target_pairs={{0,4},{2,6},{4,8},{6,10},{8,12},{10,14},{12,16},{14,18},{16,20},{1... | collective-permute-start | bytes 1572872 | tf_op jit(solution)/shard_map/ppermute | solution.py:13
  32.8 18.9 %collective-permute-start.1 = (bf16[4,32,2048]{2,1,0:T(8,128)(2,1)}, bf16[4,32,2048]{2,1,0:T(8,128)(2,1)S(1)}, u32[]{:S(2)}, u32[]{:S(2)}) collective-permute-start(bf16[4,32,2048]{2,1,0:T(8,128)(2,1)} %get-tuple-element.64), channel_id=1, source_target_pairs={{0,2},{2,4},{4,6},{6,8},{8,10},{10,12},{12,14},{14,16},{16,18},{18... | collective-permute-start | bytes 1572872 | tf_op jit(solution)/shard_map/ppermute | solution.py:13
  53.2 45.6 %collective-permute-start.5 = (bf16[8,32,2048]{2,1,0:T(8,128)(2,1)S(1)}, bf16[8,32,2048]{2,1,0:T(8,128)(2,1)S(1)}, u32[]{:S(2)}, u32[]{:S(2)}) collective-permute-start(bf16[8,32,2048]{2,1,0:T(8,128)(2,1)S(1)} %pad_maximum_fusion.5), channel_id=1, source_target_pairs={{0,508},{2,510},{4,0},{6,2},{8,4},{10,6},{12,8},{14,10},{16,12},{1... | collective-permute-start | bytes 3145736 | tf_op jit(solution)/shard_map/ppermute | solution.py:13
  61.1 37.7 %collective-permute-start.4 = (bf16[8,32,2048]{2,1,0:T(8,128)(2,1)S(1)}, bf16[8,32,2048]{2,1,0:T(8,128)(2,1)S(1)}, u32[]{:S(2)}, u32[]{:S(2)}) collective-permute-start(bf16[8,32,2048]{2,1,0:T(8,128)(2,1)S(1)} %pad_maximum_fusion.4), channel_id=1, source_target_pairs={{0,4},{2,6},{4,8},{6,10},{8,12},{10,14},{12,16},{14,18},{16,20},{1... | collective-permute-start | bytes 3145736 | tf_op jit(solution)/shard_map/ppermute | solution.py:13
  64.9 28.5 %collective-permute-start.8 = (f32[32,257]{1,0:T(8,128)S(1)}, f32[32,257]{1,0:T(8,128)S(1)}, u32[]{:S(2)}, u32[]{:S(2)}) collective-permute-start(f32[32,257]{1,0:T(8,128)S(1)} %get-tuple-element.85), channel_id=1, source_target_pairs={{0,4},{2,6},{4,8},{6,10},{8,12},{10,14},{12,16},{14,18},{16,20},{1... | collective-permute-start | bytes 98696 | tf_op jit(solution)/shard_map/ppermute | solution.py:13
  66.8 31.0 %collective-permute-start.9 = (f32[32,257]{1,0:T(8,128)S(1)}, f32[32,257]{1,0:T(8,128)S(1)}, u32[]{:S(2)}, u32[]{:S(2)}) collective-permute-start(f32[32,257]{1,0:T(8,128)S(1)} %get-tuple-element.86), channel_id=1, source_target_pairs={{0,508},{2,510},{4,0},{6,2},{8,4},{10,6},{12,8},{14,10},{16,12},{1... | collective-permute-start | bytes 98696 | tf_op jit(solution)/shard_map/ppermute | solution.py:13
  78.0 19.8 %collective-permute-start.6 = (f32[32,257]{1,0:T(8,128)S(1)}, f32[32,257]{1,0:T(8,128)S(1)}, u32[]{:S(2)}, u32[]{:S(2)}) collective-permute-start(f32[32,257]{1,0:T(8,128)S(1)} %get-tuple-element.81), channel_id=1, source_target_pairs={{0,2},{2,4},{4,6},{6,8},{8,10},{10,12},{12,14},{14,16},{16,18},{18... | collective-permute-start | bytes 98696 | tf_op jit(solution)/shard_map/ppermute | solution.py:13
  93.4 5.4 %collective-permute-start.7 = (f32[32,257]{1,0:T(8,128)S(1)}, f32[32,257]{1,0:T(8,128)S(1)}, u32[]{:S(2)}, u32[]{:S(2)}) collective-permute-start(f32[32,257]{1,0:T(8,128)S(1)} %get-tuple-element.82), channel_id=1, source_target_pairs={{0,510},{2,0},{4,2},{6,4},{8,6},{10,8},{12,10},{14,12},{16,14},{18... | collective-permute-start | bytes 98696 | tf_op jit(solution)/shard_map/ppermute | solution.py:13
  102.7 17.8 %collective-permute-start.10 = (f32[32,257]{1,0:T(8,128)S(1)}, f32[32,257]{1,0:T(8,128)S(1)}, u32[]{:S(2)}, u32[]{:S(2)}) collective-permute-start(f32[32,257]{1,0:T(8,128)S(1)} %get-tuple-element.69), channel_id=1, source_target_pairs={{0,6},{2,8},{4,10},{6,12},{8,14},{10,16},{12,18},{14,20},{16,22},{... | collective-permute-start | bytes 98696 | tf_op jit(solution)/shard_map/ppermute | solution.py:13
  104.6 15.9 %collective-permute-start.11 = (f32[32,257]{1,0:T(8,128)S(1)}, f32[32,257]{1,0:T(8,128)S(1)}, u32[]{:S(2)}, u32[]{:S(2)}) collective-permute-start(f32[32,257]{1,0:T(8,128)S(1)} %get-tuple-element.76), channel_id=1, source_target_pairs={{0,8},{2,10},{4,12},{6,14},{8,16},{10,18},{12,20},{14,22},{16,24},... | collective-permute-start | bytes 98696 | tf_op jit(solution)/shard_map/ppermute | solution.py:13
  106.5 14.0 %collective-permute-start.12 = (f32[32,257]{1,0:T(8,128)S(1)}, f32[32,257]{1,0:T(8,128)S(1)}, u32[]{:S(2)}, u32[]{:S(2)}) collective-permute-start(f32[32,257]{1,0:T(8,128)S(1)} %get-tuple-element.75), channel_id=1, source_target_pairs={{0,506},{2,508},{4,510},{6,0},{8,2},{10,4},{12,6},{14,8},{16,10},{... | collective-permute-start | bytes 98696 | tf_op jit(solution)/shard_map/ppermute | solution.py:13
  115.9 5.7 %collective-permute-start.13 = (f32[32,257]{1,0:T(8,128)S(1)}, f32[32,257]{1,0:T(8,128)S(1)}, u32[]{:S(2)}, u32[]{:S(2)}) collective-permute-start(f32[32,257]{1,0:T(8,128)S(1)} %get-tuple-element.74), channel_id=1, source_target_pairs={{0,504},{2,506},{4,508},{6,510},{8,0},{10,2},{12,4},{14,6},{16,8},... | collective-permute-start | bytes 98696 | tf_op jit(solution)/shard_map/ppermute | solution.py:13
  121.7 9.1 %collective-permute-start.14 = (f32[2,32,4,257]{3,1,2,0:T(8,128)S(1)}, f32[2,32,4,257]{3,1,2,0:T(8,128)S(1)}, u32[]{:S(2)}, u32[]{:S(2)}) collective-permute-start(f32[2,32,4,257]{3,1,2,0:T(8,128)S(1)} %pad_maximum_fusion.6), channel_id=1, source_target_pairs={{0,1},{1,0},{2,3},{3,2},{4,5},{5,4},{6,7},{7,6},{8,9},{9,8},{10,11... | collective-permute-start | bytes 789512 | tf_op jit(solution)/shard_map/ppermute | solution.py:18
